TPU v7x, 128 devices: a whole 4x4x4 slice. The times are simulated.
128 devices in a mesh: dp: 8 (over x, y_lo), expert: 16 (over z, y_hi, core).
Axes of the slice: x: 4, y: 4 (y_hi: 2, y_lo: 2; y = y_hi * 2 + y_lo), z: 4, core: 2. Of those that a mesh axis runs over, the one named last changes fastest.
Arguments:
- tokens: bfloat16 [16384, 3072], P(('dp', 'expert')), parts along dimension 0, may hold values from -6 to 6
- expert_ids: int32 [16384, 4], P(('dp', 'expert')), parts along dimension 0, may hold values from 0 to 15, as said below
- gate_weights: float32 [16384, 4], P(('dp', 'expert')), parts along dimension 0, may hold values from 0.05 to 0.5
- slot_rows: int32 [128, 16, 64], P(('dp', 'expert')), parts along dimension 0, may hold values from 0 to 128, as said below
- w_in: bfloat16 [16, 3072, 2560], P('expert'), may hold values from -0.109375 to 0.109375
- w_out: bfloat16 [16, 1280, 3072], P('expert'), may hold values from -0.15625 to 0.15625
Outputs:
- mixed: bfloat16 [16384, 3072], P(('dp', 'expert')), parts along dimension 0
There are 8 independent parts, one for each index of `dp`. A program takes and returns all parts, laid end to end along the dimension named above; an argument that names none is the same for every part. Nothing has to cross between parts.
Inputs may be any that keep to these rules, and one draw needn't show every extreme that they name: `expert_ids`: each row names 4 different experts. slot_rows[s, e] lists, in increasing order, the rows of shard s whose tokens name expert e, the first 64 of them, then 128 in the remaining slots; in every draw some expert has all 64 slots filled by every shard.
All inputs are finite; a program needn't handle non-finite values.
Results may differ from a plain program's by a relative error of at most 0.0063.
Values may be sent and summed in bfloat16 or wider, within the bound.
No kernel may reach another device: no remote copies, remote signals or barrier semaphores. Data moves between devices by JAX's collectives and lax.ppermute only.
A program may use at most 128 MiB of HBM per device.

v0:
```python
import jax
import jax.numpy as jnp
from jax import lax
from jax.sharding import PartitionSpec as P


def expert_block(rows_in, w_first, w_second):
    features = rows_in.shape[-1]
    hidden_units = w_second.shape[0]
    flat = rows_in.reshape(-1, features)
    projected = jnp.dot(flat, w_first, preferred_element_type=jnp.float32)
    intermediate_activation = (
        jax.nn.silu(projected[:, :hidden_units]) * projected[:, hidden_units:]
    ).astype(jnp.bfloat16)
    result = jnp.dot(intermediate_activation, w_second, preferred_element_type=jnp.float32).astype(
        jnp.bfloat16
    )
    return result.reshape(rows_in.shape)


def shards(tokens, expert_ids, gate_weights, slot_rows, w_in, w_out):
    tok_rows, features = tokens.shape
    experts = slot_rows.shape[1]
    capacity = slot_rows.shape[2]
    w_first = w_in[0]
    w_second = w_out[0]
    own_rows = slot_rows[0]
    occupied = own_rows < tok_rows
    clipped = jnp.minimum(own_rows, tok_rows - 1)
    matches = (
        expert_ids[:, :, None] == jnp.arange(experts, dtype=jnp.int32)[None, None, :]
    ).astype(jnp.float32)
    gate_of = jnp.einsum("tk,tke->et", gate_weights, matches)
    slot_gate = jnp.where(occupied, jnp.take_along_axis(gate_of, clipped, axis=1), 0.0).astype(
        jnp.bfloat16
    )
    this_device = lax.axis_index("expert")
    gathered, all_lists = (
        lax.all_gather(tokens, "expert", axis=0, tiled=True),
        lax.all_gather(slot_rows, "expert", axis=0, tiled=True),
    )
    own_lists = lax.dynamic_index_in_dim(all_lists, this_device, axis=1, keepdims=False)
    offsets = jnp.arange(experts, dtype=jnp.int32)[:, None] * tok_rows
    positions = jnp.where(own_lists < tok_rows, own_lists + offsets, gathered.shape[0])
    selected = jnp.take(gathered, positions.reshape(-1), axis=0, mode="fill", fill_value=0)
    layer_response = expert_block(selected.reshape(experts, capacity, features), w_first, w_second)
    returned = lax.all_to_all(layer_response, "expert", split_axis=0, concat_axis=0, tiled=True)
    expert_onehot = own_rows.reshape(-1)[None, :] == jnp.arange(tok_rows, dtype=jnp.int32)[:, None]
    mixing = jnp.where(expert_onehot, slot_gate.reshape(-1)[None, :], jnp.zeros((), jnp.bfloat16))
    summed = jnp.dot(mixing, returned.reshape(-1, features), preferred_element_type=jnp.float32)
    return summed.astype(jnp.bfloat16)


def solution(mesh):
    in_specs = (
        P(("dp", "expert"), None),
        P(("dp", "expert"), None),
        P(("dp", "expert"), None),
        P(("dp", "expert"), None, None),
        P("expert", None, None),
        P("expert", None, None),
    )
    out_specs = P(("dp", "expert"), None)
    return jax.shard_map(shards, mesh=mesh, in_specs=in_specs, out_specs=out_specs, check_vma=False)
```

profile of v0, /device:TPU:0, one launch (start us, length us, event | category | flops | bytes accessed | tf_op | source)
XLA Modules:
  0.0 243.8 jit_solution(8252859320478719966)
XLA Ops:
  6.5 0.0 all-gather.2.cloned.1.call-start
  6.5 0.7 all-gather.2.cloned.1.call-update
  7.3 0.1 add.75
  7.3 0.1 add.79
  7.4 0.1 add.76
  7.5 26.9 %all_gather.6 = s32[16,16,64]{2,1,0:T(8,128)S(1)} all-gather(s32[1,16,64]{2,1,0:T(8,128)} %param.9), channel_id=1, replica_groups=mesh['dp'=8,'expert'=16] {'expert'}, dimensions={0}, use_global_device_ids=true | all-gather | bytes 69632 | tf_op jit(solution)/shard_map/all_gather | solution.py:40
  34.4 0.5 broadcast.165
  34.9 0.7 fusion.26
  35.5 0.1 squeeze.13
  35.6 0.1 squeeze.14
  35.7 67.6 %all-gather.2.cloned.1.call-done = bf16[2048,3072]{1,0:T(8,128)(2,1)} async-done(((bf16[128,3072]{1,0:T(8,128)(2,1)}), bf16[2048,3072]{1,0:T(8,128)(2,1)}) %all-gather.2.cloned.1.call-update) | async-done | bytes 12582928 | tf_op jit(solution)/shard_map/all_gather | solution.py:39
  103.3 18.4 %gather_fusion = bf16[1024,3072]{1,0:T(8,128)(2,1)} fusion(bf16[2048,3072]{1,0:T(8,128)(2,1)} %all-gather.2.cloned.1.call-done, s32[1024]{0:T(1024)S(1)} %broadcast_clamp_fusion), kind=kCustom, calls=%fused_computation | custom fusion | bytes 12587008 | tf_op jit(solution)/shard_map/jit(_take)/gather | solution.py:45
  121.7 0.0 copy-start.3
  121.7 21.2 %fusion = f32[1024,2560]{1,0:T(8,128)S(1)} fusion(bf16[1,3072,2560]{2,1,0:T(8,128)(2,1)} %param.10, bf16[1024,3072]{1,0:T(8,128)(2,1)} %gather_fusion, pred[1024]{0:T(1024)(128)(4,1)S(1)} %compare_and_fusion), kind=kOutput, calls=%fused_computation.2 | convolution fusion | flops 16109273088 | bytes 32506880 | tf_op jit(solution)/shard_map/dot_general | solution.py:11
  142.9 0.0 copy-done.3
  142.9 10.2 %fusion.6 = bf16[1024,3072]{1,0:T(8,128)(2,1)} fusion(bf16[1,1280,3072]{2,1,0:T(8,128)(2,1)S(1)} %copy-done.3, f32[1024,2560]{1,0:T(8,128)S(1)} %fusion), kind=kOutput, calls=%fused_computation.8 | convolution fusion | flops 8064073728 | bytes 24641536 | tf_op jit(solution)/shard_map/dot_general | solution.py:15
  153.2 0.0 copy-start
  153.2 0.0 copy-start.1
  153.2 0.0 copy-start.2
  153.2 4.8 %all-to-all-start = ((bf16[16,64,3072]{2,1,0:T(8,128)(2,1)}), bf16[16,64,3072]{2,1,0:T(8,128)(2,1)}, u32[]{:S(2)}, u32[]{:S(2)}) async-start(bf16[16,64,3072]{2,1,0:T(8,128)(2,1)} %bitcast.24), calls=%async_computation | async-start | bytes 12582912 | tf_op jit(solution)/shard_map/all_to_all | solution.py:47
  158.0 0.0 copy-done
  158.0 0.1 eq.28
  158.1 0.1 reshape.124
  158.1 0.0 copy-done.1
  158.1 0.1 copy.9
  158.2 0.0 copy-done.2
  158.2 0.2 copy.10
  158.4 0.4 fusion.16
  158.8 7.3 %gather_fusion.1 = bf16[1024]{0:T(1024)(128)(2,1)S(1)} fusion(f32[16,128]{0,1:T(8,128)S(1)} %bitcast.23, s32[1024]{0:T(1024)S(1)} %reshape.124), kind=kCustom, calls=%fused_computation.1 | custom fusion | bytes 12288 | tf_op jit(solution)/shard_map/jit(take_along_axis)/gather | solution.py:34
  166.0 66.2 %all-to-all-done = bf16[16,64,3072]{2,1,0:T(8,128)(2,1)} async-done(((bf16[16,64,3072]{2,1,0:T(8,128)(2,1)}), bf16[16,64,3072]{2,1,0:T(8,128)(2,1)}, u32[]{:S(2)}, u32[]{:S(2)}) %all-to-all-start) | async-done | bytes 6291488 | tf_op jit(solution)/shard_map/all_to_all | solution.py:47
  232.3 4.7 %convolution_convert_fusion = bf16[128,3072]{1,0:T(8,128)(2,1)} fusion(bf16[1024,3072]{1,0:T(8,128)(2,1)} %bitcast.9, s32[1024]{0:T(1024)S(1)} %eq.28, bf16[1024]{0:T(1024)(128)(2,1)S(1)} %select_convert_fusion), kind=kOutput, calls=%fused_computation.11 | convolution fusion | flops 805961728 | bytes 7084032 | tf_op jit(solution)/shard_map/dot_general | solution.py:50
  (6 shorter events, 0.0 us)
Async XLA Ops:
  6.5 96.8 %all-gather.2.cloned.1.call-start = ((), (), s32[]{:S(2)}) async-start(), calls=%async_computation.1 | async-start | bytes 13369344 | tf_op jit(solution)/shard_map/all_gather | solution.py:39
  121.7 21.2 %copy-start.3 = (bf16[1,1280,3072]{2,1,0:T(8,128)(2,1)S(1)}, bf16[1,1280,3072]{2,1,0:T(8,128)(2,1)}, u32[]{:S(2)}) copy-start(bf16[1,1280,3072]{2,1,0:T(8,128)(2,1)} %param.11) | copy-start | bytes 23592964
  153.2 4.8 %copy-start = (s32[1,16,64]{2,1,0:T(8,128)S(1)}, s32[1,16,64]{2,1,0:T(8,128)}, u32[]{:S(2)}) copy-start(s32[1,16,64]{2,1,0:T(8,128)} %param.9) | copy-start | bytes 12292
  153.2 4.9 %copy-start.1 = (s32[128,4]{0,1:T(4,128)S(1)}, s32[128,4]{0,1:T(4,128)}, u32[]{:S(2)}) copy-start(s32[128,4]{0,1:T(4,128)} %param.7) | copy-start | bytes 6148
  153.2 5.1 %copy-start.2 = (f32[128,4]{0,1:T(4,128)S(1)}, f32[128,4]{0,1:T(4,128)}, u32[]{:S(2)}) copy-start(f32[128,4]{0,1:T(4,128)} %param.8) | copy-start | bytes 6148
  153.2 79.1 %all-to-all-start = ((bf16[16,64,3072]{2,1,0:T(8,128)(2,1)}), bf16[16,64,3072]{2,1,0:T(8,128)(2,1)}, u32[]{:S(2)}, u32[]{:S(2)}) async-start(bf16[16,64,3072]{2,1,0:T(8,128)(2,1)} %bitcast.24), calls=%async_computation | async-start | bytes 12582912 | tf_op jit(solution)/shard_map/all_to_all | solution.py:47
Sparse Core Ops, SparseCore 0:
  9.8 93.4 all-gather.1
where the time goes:
time: 245 us; the launch traced here: 244 us
  waiting for transfers between devices  135 us (55%)
  matrix products  36.5 us (15%)
  local copies, waits for them, and re-layouts  27.6 us (11%)
  blocking collectives  26.9 us (11%)
  between operations  13.5 us (6%)
  starting transfers between devices  4.77 us (2%)
    all_gather x1, waiting for transfers between devices, shards(): lax.all_gather(tokens, 'expert', axis=0, tiled=True)  67.6 us
    all_to_all x1, waiting for transfers between devices, shards(): lax.all_to_all(layer_response, 'expert', split_axis=0, concat_axis=0, til...  66.2 us
    all_gather x1, blocking collectives, shards(): lax.all_gather(slot_rows, 'expert', axis=0, tiled=True)  26.9 us
    dot_general x1, matrix products, expert_block(): projected = jnp.dot(flat, w_first, preferred_element_type=jnp.float32)  21.2 us
    gather x1, local copies, waits for them, and re-layouts, shards(): jnp.take(gathered, positions.reshape(-1), axis=0, mode='fill', fill_value=0)  18.4 us
    dot_general x1, matrix products, expert_block(): jnp.dot(intermediate_activation, w_second, preferred_element_type=jnp.flo...  10.2 us
    gather x2, local copies, waits for them, and re-layouts, shards(): jnp.take_along_axis(gate_of, clipped, axis=1)  7.32 us
  transfers between devices with their start and end apart: 2, of which 2 were waited for; matrix products, arithmetic and copies ran while one was open for 4% of the time, Pallas kernels for 0%

commit v1 on v0

v1 whole, which is shorter than its diff:
```python
import jax
import jax.numpy as jnp
from jax import lax
from jax.sharding import PartitionSpec as P

CHUNKS = 2


def expert_block(rows_in, w_first, w_second):
    features = rows_in.shape[-1]
    hidden_units = w_second.shape[0]
    flat = rows_in.reshape(-1, features)
    projected = jnp.dot(flat, w_first, preferred_element_type=jnp.float32)
    intermediate_activation = (
        jax.nn.silu(projected[:, :hidden_units]) * projected[:, hidden_units:]
    ).astype(jnp.bfloat16)
    result = jnp.dot(intermediate_activation, w_second, preferred_element_type=jnp.float32).astype(
        jnp.bfloat16
    )
    return result.reshape(rows_in.shape)


def shards(tokens, expert_ids, gate_weights, slot_rows, w_in, w_out):
    tok_rows, features = tokens.shape
    experts = slot_rows.shape[1]
    capacity = slot_rows.shape[2]
    w_first = w_in[0]
    w_second = w_out[0]
    own_rows = slot_rows[0]
    token_iota = jnp.arange(tok_rows, dtype=jnp.int32)
    picks = own_rows[:, :, None] == token_iota[None, None, :]
    matches = (
        expert_ids[:, :, None] == jnp.arange(experts, dtype=jnp.int32)[None, None, :]
    ).astype(jnp.float32)
    gate_of = jnp.einsum("tk,tke->et", gate_weights, matches).astype(jnp.bfloat16)
    mixing = jnp.where(picks, gate_of[:, None, :], jnp.zeros((), jnp.bfloat16))
    dispatched = jnp.einsum(
        "ect,td->ecd", picks.astype(jnp.bfloat16), tokens, preferred_element_type=jnp.float32
    ).astype(jnp.bfloat16)
    piece = capacity // CHUNKS
    summed = None
    for k in range(CHUNKS):
        part = dispatched[:, k * piece:(k + 1) * piece]
        arrived = lax.all_to_all(part, "expert", split_axis=0, concat_axis=0, tiled=True)
        response = expert_block(arrived, w_first, w_second)
        returned = lax.all_to_all(response, "expert", split_axis=0, concat_axis=0, tiled=True)
        weights = mixing[:, k * piece:(k + 1) * piece].reshape(-1, tok_rows)
        contrib = jnp.dot(
            weights.T, returned.reshape(-1, features), preferred_element_type=jnp.float32
        )
        summed = contrib if summed is None else summed + contrib
    return summed.astype(jnp.bfloat16)


def solution(mesh):
    in_specs = (
        P(("dp", "expert"), None),
        P(("dp", "expert"), None),
        P(("dp", "expert"), None),
        P(("dp", "expert"), None, None),
        P("expert", None, None),
        P("expert", None, None),
    )
    out_specs = P(("dp", "expert"), None)
    return jax.shard_map(shards, mesh=mesh, in_specs=in_specs, out_specs=out_specs, check_vma=False)
```

time: 245 us -> 194 us (0.79)
  waiting for transfers between devices: 135 us -> 74.6 us
  local copies, waits for them, and re-layouts: 27.6 us -> 3.77 us
  blocking collectives: 26.9 us -> 48.5 us
  matrix products: 36.5 us -> 52 us
  between operations: 13.5 us -> 0.08 us
  starting transfers between devices: 4.77 us -> 13.7 us
    all_gather x1 -> x0, waiting for transfers between devices: 67.6 us -> none  [shards(): lax.all_gather(tokens, 'expert', axis=0, tiled=True)]
    all_to_all x0 -> x1, blocking collectives: none -> 48.5 us  [shards(): lax.all_to_all(part, 'expert', split_axis=0, concat_axis=0, tiled=True)]
    all_gather x1 -> x0, blocking collectives: 26.9 us -> none  [shards(): lax.all_gather(slot_rows, 'expert', axis=0, tiled=True)]
    gather x3 -> x0, local copies, waits for them, and re-layouts: 25.7 us -> none  [the longest x1 18.4 us: shards(): jnp.take(gathered, positions.reshape(-1), axis=0, mode='fill', fill_value=0)]
    all_to_all x1 -> x3, starting transfers between devices: 4.76 us -> 13.7 us  [the longest x2 9.26 us: shards(): lax.all_to_all(response, 'expert', split_axis=0, concat_axis=0, tiled=True)]
    all_to_all x1 -> x3, waiting for transfers between devices: 66.2 us -> 74.6 us  [the longest x2 55.8 us: shards(): lax.all_to_all(response, 'expert', split_axis=0, concat_axis=0, tiled=True)]
    dot_general x1 -> x2, matrix products: 10.2 us -> 18.2 us  [expert_block(): jnp.dot(intermediate_activation, w_second, preferred_element_type=jnp.flo...]
    dot_general x1 -> x2, matrix products: 21.2 us -> 25.3 us  [expert_block(): projected = jnp.dot(flat, w_first, preferred_element_type=jnp.float32)]
  transfers between devices with their start and end apart: 2 -> 3, of which waited for: 2 -> 3; matrix products, arithmetic and copies ran while one was open for 4% -> 24% of each run, Pallas kernels for 0% -> 0%
where the time goes in v1:
time: 194 us; the launch traced here: 193 us
  waiting for transfers between devices  74.6 us (38%)
  matrix products  52 us (27%)
  blocking collectives  48.5 us (25%)
  starting transfers between devices  13.7 us (7%)
  local copies, waits for them, and re-layouts  3.77 us (2%)
    all_to_all x2, waiting for transfers between devices, shards(): lax.all_to_all(response, 'expert', split_axis=0, concat_axis=0, tiled=True)  55.8 us
    all_to_all x1, blocking collectives, shards(): lax.all_to_all(part, 'expert', split_axis=0, concat_axis=0, tiled=True)  48.5 us
    dot_general x2, matrix products, expert_block(): projected = jnp.dot(flat, w_first, preferred_element_type=jnp.float32)  25.3 us
    all_to_all x1, waiting for transfers between devices, shards(): lax.all_to_all(part, 'expert', split_axis=0, concat_axis=0, tiled=True)  18.8 us
    dot_general x2, matrix products, expert_block(): jnp.dot(intermediate_activation, w_second, preferred_element_type=jnp.flo...  18.2 us
    all_to_all x2, starting transfers between devices, shards(): lax.all_to_all(response, 'expert', split_axis=0, concat_axis=0, tiled=True)  9.26 us
    dot_general x2, matrix products, shards(): jnp.dot(weights.T, returned.reshape(-1, features), preferred_element_type...  5.95 us
    all_to_all x1, starting transfers between devices, shards(): lax.all_to_all(part, 'expert', split_axis=0, concat_axis=0, tiled=True)  4.48 us
  transfers between devices with their start and end apart: 3, of which 3 were waited for; matrix products, arithmetic and copies ran while one was open for 24% of the time, Pallas kernels for 0%

profile of v1, /device:TPU:0, one launch (start us, length us, event | category | flops | bytes accessed | tf_op | source)
XLA Modules:
  0.0 193.3 jit_solution(9537694105707587873)
XLA Ops:
  0.0 0.0 copy-start
  0.0 1.1 copy-done
  1.1 2.5 %convolution_convert_fusion = bf16[16,64,3072]{2,1,0:T(8,128)(2,1)S(1)} fusion(bf16[128,3072]{1,0:T(8,128)(2,1)S(1)} %copy-done, s32[16,64]{1,0:T(8,128)} %bitcast.40), kind=kOutput, calls=%fused_computation.8 | convolution fusion | flops 808583168 | bytes 7081984 | tf_op jit(solution)/shard_map/ect,td->ecd/dot_general | solution.py:37
  3.7 2.3 %fusion.29 = (bf16[16,32,3072]{2,1,0:T(8,128)(2,1)}, bf16[16,32,3072]{2,1,0:T(8,128)(2,1)S(1)}) fusion(bf16[16,64,3072]{2,1,0:T(8,128)(2,1)S(1)} %convolution_convert_fusion), kind=kLoop, calls=%fused_computation.32 | loop fusion | bytes 12582912 | tf_op jit(solution)/shard_map/slice | solution.py:43
  6.0 48.5 %all_to_all.20 = bf16[16,32,3072]{2,1,0:T(8,128)(2,1)} all-to-all(bf16[16,32,3072]{2,1,0:T(8,128)(2,1)S(1)} %get-tuple-element.6), channel_id=1, replica_groups=mesh['dp'=8,'expert'=16] {'expert'}, dimensions={0} | all-to-all | bytes 6291456 | tf_op jit(solution)/shard_map/all_to_all | solution.py:44
  54.5 4.5 %all-to-all-start = ((bf16[16,32,3072]{2,1,0:T(8,128)(2,1)}), bf16[16,32,3072]{2,1,0:T(8,128)(2,1)}, u32[]{:S(2)}, u32[]{:S(2)}) async-start(bf16[16,32,3072]{2,1,0:T(8,128)(2,1)} %get-tuple-element.5), calls=%async_computation | async-start | bytes 6291456 | tf_op jit(solution)/shard_map/all_to_all | solution.py:44
  59.0 12.7 %fusion = f32[512,2560]{1,0:T(8,128)S(1)} fusion(bf16[512,3072]{1,0:T(8,128)(2,1)} %bitcast.39, bf16[1,3072,2560]{2,1,0:T(8,128)(2,1)} %param.10), kind=kOutput, calls=%fused_computation | convolution fusion | flops 8053063680 | bytes 24117248 | tf_op jit(solution)/shard_map/dot_general | solution.py:13
  71.6 9.2 %fusion.11 = bf16[512,3072]{1,0:T(8,128)(2,1)} fusion(bf16[1,1280,3072]{2,1,0:T(8,128)(2,1)} %param.11, f32[512,2560]{1,0:T(8,128)S(1)} %fusion), kind=kOutput, calls=%fused_computation.10 | convolution fusion | flops 4032036864 | bytes 16252928 | tf_op jit(solution)/shard_map/dot_general | solution.py:17
  80.8 18.8 %all-to-all-done = bf16[16,32,3072]{2,1,0:T(8,128)(2,1)} async-done(((bf16[16,32,3072]{2,1,0:T(8,128)(2,1)}), bf16[16,32,3072]{2,1,0:T(8,128)(2,1)}, u32[]{:S(2)}, u32[]{:S(2)}) %all-to-all-start) | async-done | bytes 3145760 | tf_op jit(solution)/shard_map/all_to_all | solution.py:44
  99.6 4.7 %all-to-all-start.3 = ((bf16[16,32,3072]{2,1,0:T(8,128)(2,1)}), bf16[16,32,3072]{2,1,0:T(8,128)(2,1)}, u32[]{:S(2)}, u32[]{:S(2)}) async-start(bf16[16,32,3072]{2,1,0:T(8,128)(2,1)} %bitcast.38), calls=%async_computation.3 | async-start | bytes 6291456 | tf_op jit(solution)/shard_map/all_to_all | solution.py:46
  104.2 12.6 %fusion.2 = f32[512,2560]{1,0:T(8,128)S(1)} fusion(bf16[512,3072]{1,0:T(8,128)(2,1)} %bitcast.3, bf16[1,3072,2560]{2,1,0:T(8,128)(2,1)} %param.10), kind=kOutput, calls=%fused_computation.2 | convolution fusion | flops 8053063680 | bytes 24117248 | tf_op jit(solution)/shard_map/dot_general | solution.py:13
  116.9 9.1 %fusion.8 = bf16[512,3072]{1,0:T(8,128)(2,1)} fusion(bf16[1,1280,3072]{2,1,0:T(8,128)(2,1)} %param.11, f32[512,2560]{1,0:T(8,128)S(1)} %fusion.2), kind=kOutput, calls=%fused_computation.9 | convolution fusion | flops 4032036864 | bytes 16252928 | tf_op jit(solution)/shard_map/dot_general | solution.py:17
  125.9 18.7 %all-to-all-done.3 = bf16[16,32,3072]{2,1,0:T(8,128)(2,1)} async-done(((bf16[16,32,3072]{2,1,0:T(8,128)(2,1)}), bf16[16,32,3072]{2,1,0:T(8,128)(2,1)}, u32[]{:S(2)}, u32[]{:S(2)}) %all-to-all-start.3) | async-done | bytes 3145760 | tf_op jit(solution)/shard_map/all_to_all | solution.py:46
  144.7 0.0 copy-start.3
  144.7 0.0 copy-start.4
  144.7 0.0 copy-start.2
  144.7 4.6 %all-to-all-start.1 = ((bf16[16,32,3072]{2,1,0:T(8,128)(2,1)}), bf16[16,32,3072]{2,1,0:T(8,128)(2,1)}, u32[]{:S(2)}, u32[]{:S(2)}) async-start(bf16[16,32,3072]{2,1,0:T(8,128)(2,1)} %bitcast.37), calls=%async_computation.1 | async-start | bytes 6291456 | tf_op jit(solution)/shard_map/all_to_all | solution.py:46
  149.3 0.0 copy-done.3
  149.3 0.1 copy.12
  149.4 0.0 copy-done.4
  149.4 0.1 copy.7
  149.5 0.4 select_reduce_fusion
  149.9 0.1 copy.11
  149.9 0.0 copy-done.2
  149.9 0.2 fusion.23
  150.2 0.0 copy-start.1
  150.2 2.6 %convolution_bitcast_fusion = f32[128,3072]{1,0:T(8,128)S(1)} fusion(bf16[16,32,3072]{2,1,0:T(8,128)(2,1)} %all-to-all-done.3, bf16[16,64,128]{2,1,0:T(8,128)(2,1)S(1)} %fusion.23), kind=kOutput, calls=%fused_computation.11 | convolution fusion | flops 402653184 | bytes 4849664 | tf_op jit(solution)/shard_map/dot_general | solution.py:48
  152.8 37.1 %all-to-all-done.1 = bf16[16,32,3072]{2,1,0:T(8,128)(2,1)} async-done(((bf16[16,32,3072]{2,1,0:T(8,128)(2,1)}), bf16[16,32,3072]{2,1,0:T(8,128)(2,1)}, u32[]{:S(2)}, u32[]{:S(2)}) %all-to-all-start.1) | async-done | bytes 3145760 | tf_op jit(solution)/shard_map/all_to_all | solution.py:46
  189.9 3.4 %fusion.15 = bf16[128,3072]{1,0:T(8,128)(2,1)} fusion(f32[128,3072]{1,0:T(8,128)S(1)} %convolution_bitcast_fusion, bf16[16,32,3072]{2,1,0:T(8,128)(2,1)} %all-to-all-done.1, bf16[16,64,128]{2,1,0:T(8,128)(2,1)S(1)} %fusion.23), kind=kOutput, calls=%fused_computation.14 | convolution fusion | flops 403439616 | bytes 5636096 | tf_op jit(solution)/shard_map/dot_general | solution.py:48
  193.2 0.0 copy-done.1
Async XLA Ops:
  0.0 1.1 copy-start
  54.5 45.1 %all-to-all-start = ((bf16[16,32,3072]{2,1,0:T(8,128)(2,1)}), bf16[16,32,3072]{2,1,0:T(8,128)(2,1)}, u32[]{:S(2)}, u32[]{:S(2)}) async-start(bf16[16,32,3072]{2,1,0:T(8,128)(2,1)} %get-tuple-element.5), calls=%async_computation | async-start | bytes 6291456 | tf_op jit(solution)/shard_map/all_to_all | solution.py:44
  99.6 45.1 %all-to-all-start.3 = ((bf16[16,32,3072]{2,1,0:T(8,128)(2,1)}), bf16[16,32,3072]{2,1,0:T(8,128)(2,1)}, u32[]{:S(2)}, u32[]{:S(2)}) async-start(bf16[16,32,3072]{2,1,0:T(8,128)(2,1)} %bitcast.38), calls=%async_computation.3 | async-start | bytes 6291456 | tf_op jit(solution)/shard_map/all_to_all | solution.py:46
  144.7 4.6 %copy-start.3 = (f32[128,4]{0,1:T(4,128)S(1)}, f32[128,4]{0,1:T(4,128)}, u32[]{:S(2)}) copy-start(f32[128,4]{0,1:T(4,128)} %param.8) | copy-start | bytes 6148
  144.7 4.7 %copy-start.4 = (s32[128,4]{0,1:T(4,128)S(1)}, s32[128,4]{0,1:T(4,128)}, u32[]{:S(2)}) copy-start(s32[128,4]{0,1:T(4,128)} %param.7) | copy-start | bytes 6148
  144.7 5.3 %copy-start.2 = (s32[1,16,64]{2,1,0:T(8,128)S(1)}, s32[1,16,64]{2,1,0:T(8,128)}, u32[]{:S(2)}) copy-start(s32[1,16,64]{2,1,0:T(8,128)} %param.9) | copy-start | bytes 12292
  144.7 45.2 %all-to-all-start.1 = ((bf16[16,32,3072]{2,1,0:T(8,128)(2,1)}), bf16[16,32,3072]{2,1,0:T(8,128)(2,1)}, u32[]{:S(2)}, u32[]{:S(2)}) async-start(bf16[16,32,3072]{2,1,0:T(8,128)(2,1)} %bitcast.37), calls=%async_computation.1 | async-start | bytes 6291456 | tf_op jit(solution)/shard_map/all_to_all | solution.py:46
  150.2 43.1 %copy-start.1 = (bf16[128,3072]{1,0:T(8,128)(2,1)S(1)}, bf16[128,3072]{1,0:T(8,128)(2,1)}, u32[]{:S(2)}) copy-start(bf16[128,3072]{1,0:T(8,128)(2,1)} %param.6) | copy-start | bytes 2359300

commit v2 on v1

--- a/solution.py
+++ b/solution.py
@@ -3,7 +3,7 @@
 from jax import lax
 from jax.sharding import PartitionSpec as P
 
-CHUNKS = 2
+CHUNKS = 1
 
 
 def expert_block(rows_in, w_first, w_second):

time: 194 us -> 204 us (1.052)
  blocking collectives: 48.5 us -> 82.4 us
  matrix products: 52 us -> 40.9 us
  starting transfers between devices: 13.7 us -> 4.77 us
  local copies, waits for them, and re-layouts: 3.77 us -> 1.45 us
    all_to_all x1, blocking collectives: 48.5 us -> 82.4 us  [shards(): lax.all_to_all(part, 'expert', split_axis=0, concat_axis=0, tiled=True)]
    all_to_all x1 -> x0, waiting for transfers between devices: 18.8 us -> none  [shards(): lax.all_to_all(part, 'expert', split_axis=0, concat_axis=0, tiled=True)]
    all_to_all x2 -> x1, waiting for transfers between devices: 55.8 us -> 73.6 us  [shards(): lax.all_to_all(response, 'expert', split_axis=0, concat_axis=0, tiled=True)]
    dot_general x2 -> x1, matrix products: 25.3 us -> 19 us  [expert_block(): projected = jnp.dot(flat, w_first, preferred_element_type=jnp.float32)]
    all_to_all x2 -> x1, starting transfers between devices: 9.26 us -> 4.77 us  [shards(): lax.all_to_all(response, 'expert', split_axis=0, concat_axis=0, tiled=True)]
    all_to_all x1 -> x0, starting transfers between devices: 4.48 us -> none  [shards(): lax.all_to_all(part, 'expert', split_axis=0, concat_axis=0, tiled=True)]
    dot_general x2 -> x1, matrix products: 18.2 us -> 14.5 us  [expert_block(): jnp.dot(intermediate_activation, w_second, preferred_element_type=jnp.flo...]
    slice x1 -> x0, local copies, waits for them, and re-layouts: 2.33 us -> none  [shards(): part = dispatched[:, k * piece:(k + 1) * piece]]
  transfers between devices with their start and end apart: 3 -> 1, of which waited for: 3 -> 1; matrix products, arithmetic and copies ran while one was open for 24% -> 0% of each run, Pallas kernels for 0% -> 0%
where the time goes in v2:
time: 204 us
  blocking collectives  82.4 us (40%)
  waiting for transfers between devices  73.6 us (36%)
  matrix products  40.9 us (20%)
  starting transfers between devices  4.77 us (2%)
    all_to_all x1, blocking collectives, shards(): lax.all_to_all(part, 'expert', split_axis=0, concat_axis=0, tiled=True)  82.4 us
    all_to_all x1, waiting for transfers between devices, shards(): lax.all_to_all(response, 'expert', split_axis=0, concat_axis=0, tiled=True)  73.6 us
    dot_general x1, matrix products, expert_block(): projected = jnp.dot(flat, w_first, preferred_element_type=jnp.float32)  19 us
    dot_general x1, matrix products, expert_block(): jnp.dot(intermediate_activation, w_second, preferred_element_type=jnp.flo...  14.5 us
    dot_general x1, matrix products, shards(): jnp.dot(weights.T, returned.reshape(-1, features), preferred_element_type...  4.77 us
    all_to_all x1, starting transfers between devices, shards(): lax.all_to_all(response, 'expert', split_axis=0, concat_axis=0, tiled=True)  4.77 us
  transfers between devices with their start and end apart: 1, of which 1 were waited for; matrix products, arithmetic and copies ran while one was open for 0% of the time, Pallas kernels for 0%

profile of v2, /device:TPU:0, one launch (start us, length us, event | category | flops | bytes accessed | tf_op | source)
XLA Modules:
  0.0 203.5 jit_solution(9343511935879701298)
XLA Ops:
  0.0 0.0 copy-start
  0.0 1.1 copy-done
  1.1 0.0 copy-start.4
  1.1 2.7 %convolution_convert_fusion = bf16[16,64,3072]{2,1,0:T(8,128)(2,1)S(1)} fusion(bf16[128,3072]{1,0:T(8,128)(2,1)S(1)} %copy-done, s32[16,64]{1,0:T(8,128)} %bitcast.25), kind=kOutput, calls=%fused_computation.4 | convolution fusion | flops 808583168 | bytes 7081984 | tf_op jit(solution)/shard_map/ect,td->ecd/dot_general | solution.py:37
  3.8 0.0 slice-start
  3.8 82.4 %all_to_all.10 = bf16[16,64,3072]{2,1,0:T(8,128)(2,1)S(1)} all-to-all(bf16[16,64,3072]{2,1,0:T(8,128)(2,1)S(1)} %convolution_convert_fusion), channel_id=1, replica_groups=mesh['dp'=8,'expert'=16] {'expert'}, dimensions={0} | all-to-all | bytes 12582912 | tf_op jit(solution)/shard_map/all_to_all | solution.py:44
  86.2 0.0 copy-done.4
  86.2 0.0 slice-start.1
  86.2 19.0 %fusion = f32[1024,2560]{1,0:T(8,128)} fusion(bf16[1024,3072]{1,0:T(8,128)(2,1)S(1)} %bitcast.24, bf16[1,3072,2560]{2,1,0:T(8,128)(2,1)S(1)} %copy-done.4), kind=kOutput, calls=%fused_computation | convolution fusion | flops 16106127360 | bytes 32505856 | tf_op jit(solution)/shard_map/dot_general | solution.py:13
  105.2 0.0 slice-done
  105.2 0.0 slice-done.1
  105.2 14.5 %fusion.4 = bf16[1024,3072]{1,0:T(8,128)(2,1)} fusion(bf16[1,1280,3072]{2,1,0:T(8,128)(2,1)S(1)} %bitcast.29, f32[1024,2560]{1,0:T(8,128)} %fusion), kind=kOutput, calls=%fused_computation.5 | convolution fusion | flops 8064073728 | bytes 24641536 | tf_op jit(solution)/shard_map/dot_general | solution.py:17
  119.7 0.0 copy-start.2
  119.7 0.0 copy-start.3
  119.7 0.0 copy-start.1
  119.7 4.8 %all-to-all-start.1 = ((bf16[16,64,3072]{2,1,0:T(8,128)(2,1)}), bf16[16,64,3072]{2,1,0:T(8,128)(2,1)}, u32[]{:S(2)}, u32[]{:S(2)}) async-start(bf16[16,64,3072]{2,1,0:T(8,128)(2,1)} %bitcast.23), calls=%async_computation.1 | async-start | bytes 12582912 | tf_op jit(solution)/shard_map/all_to_all | solution.py:46
  124.4 0.0 copy-done.2
  124.5 0.1 copy.12
  124.6 0.0 copy-done.3
  124.6 0.1 copy.7
  124.7 0.4 select_reduce_fusion
  125.1 0.1 copy.11
  125.1 73.6 %all-to-all-done.1 = bf16[16,64,3072]{2,1,0:T(8,128)(2,1)} async-done(((bf16[16,64,3072]{2,1,0:T(8,128)(2,1)}), bf16[16,64,3072]{2,1,0:T(8,128)(2,1)}, u32[]{:S(2)}, u32[]{:S(2)}) %all-to-all-start.1) | async-done | bytes 6291488 | tf_op jit(solution)/shard_map/all_to_all | solution.py:46
  198.8 0.0 copy-done.1
  198.8 4.8 %fusion.8 = bf16[128,3072]{1,0:T(8,128)(2,1)} fusion(bf16[16,64,3072]{2,1,0:T(8,128)(2,1)} %all-to-all-done.1, s32[16,64]{1,0:T(8,128)S(1)} %bitcast.26, bf16[16,128]{1,0:T(8,128)(2,1)S(1)} %bitcast.27), kind=kOutput, calls=%fused_computation.9 | convolution fusion | flops 805961728 | bytes 7086080 | tf_op jit(solution)/shard_map/dot_general | solution.py:48
  (1 shorter events, 0.0 us)
Async XLA Ops:
  0.0 1.1 copy-start
  1.1 85.1 %copy-start.4 = (bf16[1,3072,2560]{2,1,0:T(8,128)(2,1)S(1)}, bf16[1,3072,2560]{2,1,0:T(8,128)(2,1)}, u32[]{:S(2)}) copy-start(bf16[1,3072,2560]{2,1,0:T(8,128)(2,1)} %param.10) | copy-start | bytes 47185924
  3.8 101.4 %slice-start = ((s8[7864320]{0:T(1024)(128)(4,1)}), s8[3670016]{0:T(1024)(128)(4,1)S(1)}, s32[]{:S(2)}) async-start(s8[7864320]{0:T(1024)(128)(4,1)} %bitcast.28), calls=%async_computation.2 | async-start | bytes 7340032
  86.2 19.0 %slice-start.1 = ((s8[7864320]{0:T(1024)(128)(4,1)}), s8[4194304]{0:T(1024)(128)(4,1)S(1)}, s32[]{:S(2)}) async-start(s8[7864320]{0:T(1024)(128)(4,1)} %bitcast.28), calls=%async_computation.3 | async-start | bytes 8388608
  119.7 4.8 %copy-start.2 = (f32[128,4]{0,1:T(4,128)S(1)}, f32[128,4]{0,1:T(4,128)}, u32[]{:S(2)}) copy-start(f32[128,4]{0,1:T(4,128)} %param.8) | copy-start | bytes 6148
  119.7 4.9 %copy-start.3 = (s32[128,4]{0,1:T(4,128)S(1)}, s32[128,4]{0,1:T(4,128)}, u32[]{:S(2)}) copy-start(s32[128,4]{0,1:T(4,128)} %param.7) | copy-start | bytes 6148
  119.7 79.1 %copy-start.1 = (s32[1,16,64]{2,1,0:T(8,128)S(1)}, s32[1,16,64]{2,1,0:T(8,128)}, u32[]{:S(2)}) copy-start(s32[1,16,64]{2,1,0:T(8,128)} %param.9) | copy-start | bytes 12292
  119.7 79.1 %all-to-all-start.1 = ((bf16[16,64,3072]{2,1,0:T(8,128)(2,1)}), bf16[16,64,3072]{2,1,0:T(8,128)(2,1)}, u32[]{:S(2)}, u32[]{:S(2)}) async-start(bf16[16,64,3072]{2,1,0:T(8,128)(2,1)} %bitcast.23), calls=%async_computation.1 | async-start | bytes 12582912 | tf_op jit(solution)/shard_map/all_to_all | solution.py:46

commit v3 on v1

--- a/solution.py
+++ b/solution.py
@@ -34,13 +34,16 @@
     ).astype(jnp.float32)
     gate_of = jnp.einsum("tk,tke->et", gate_weights, matches).astype(jnp.bfloat16)
     mixing = jnp.where(picks, gate_of[:, None, :], jnp.zeros((), jnp.bfloat16))
-    dispatched = jnp.einsum(
-        "ect,td->ecd", picks.astype(jnp.bfloat16), tokens, preferred_element_type=jnp.float32
-    ).astype(jnp.bfloat16)
+    one_hot = picks.astype(jnp.bfloat16)
     piece = capacity // CHUNKS
     summed = None
     for k in range(CHUNKS):
-        part = dispatched[:, k * piece:(k + 1) * piece]
+        part = jnp.einsum(
+            "ect,td->ecd",
+            one_hot[:, k * piece:(k + 1) * piece],
+            tokens,
+            preferred_element_type=jnp.float32,
+        ).astype(jnp.bfloat16)
         arrived = lax.all_to_all(part, "expert", split_axis=0, concat_axis=0, tiled=True)
         response = expert_block(arrived, w_first, w_second)
         returned = lax.all_to_all(response, "expert", split_axis=0, concat_axis=0, tiled=True)

time: 194 us -> 192 us (0.990)
  blocking collectives: 48.5 us -> 0 us
  waiting for transfers between devices: 74.6 us -> 113 us
  starting transfers between devices: 13.7 us -> 21.9 us
  local copies, waits for them, and re-layouts: 3.77 us -> 0.47 us
  matrix products: 52 us -> 54.6 us
    all_to_all x1 -> x0, blocking collectives: 48.5 us -> none  [shards(): lax.all_to_all(part, 'expert', split_axis=0, concat_axis=0, tiled=True)]
    all_to_all x1 -> x2, waiting for transfers between devices: 18.8 us -> 56.8 us  [shards(): lax.all_to_all(part, 'expert', split_axis=0, concat_axis=0, tiled=True)]
    all_to_all x1 -> x2, starting transfers between devices: 4.48 us -> 12.7 us  [shards(): lax.all_to_all(part, 'expert', split_axis=0, concat_axis=0, tiled=True)]
    dot_general x1 -> x2, matrix products: 2.53 us -> 5.26 us  [shards(): jnp.einsum('ect,td->ecd', one_hot[:, k * piece:(k + 1) * piece], tokens,...]
    slice x1 -> x0, local copies, waits for them, and re-layouts: 2.33 us -> none  [shards(): part = dispatched[:, k * piece:(k + 1) * piece]]
  transfers between devices with their start and end apart: 3 -> 4, of which waited for: 3 -> 4; matrix products, arithmetic and copies ran while one was open for 24% -> 26% of each run, Pallas kernels for 0% -> 0%
where the time goes in v3:
time: 192 us; the launch traced here: 191 us
  waiting for transfers between devices  113 us (59%)
  matrix products  54.6 us (28%)
  starting transfers between devices  21.9 us (11%)
    all_to_all x2, waiting for transfers between devices, shards(): lax.all_to_all(part, 'expert', split_axis=0, concat_axis=0, tiled=True)  56.8 us
    all_to_all x2, waiting for transfers between devices, shards(): lax.all_to_all(response, 'expert', split_axis=0, concat_axis=0, tiled=True)  55.9 us
    dot_general x2, matrix products, expert_block(): projected = jnp.dot(flat, w_first, preferred_element_type=jnp.float32)  25.3 us
    dot_general x2, matrix products, expert_block(): jnp.dot(intermediate_activation, w_second, preferred_element_type=jnp.flo...  18.2 us
    all_to_all x2, starting transfers between devices, shards(): lax.all_to_all(part, 'expert', split_axis=0, concat_axis=0, tiled=True)  12.7 us
    all_to_all x2, starting transfers between devices, shards(): lax.all_to_all(response, 'expert', split_axis=0, concat_axis=0, tiled=True)  9.26 us
    dot_general x2, matrix products, shards(): jnp.dot(weights.T, returned.reshape(-1, features), preferred_element_type...  5.87 us
    dot_general x2, matrix products, shards(): jnp.einsum('ect,td->ecd', one_hot[:, k * piece:(k + 1) * piece], tokens,...  5.26 us
  transfers between devices with their start and end apart: 4, of which 4 were waited for; matrix products, arithmetic and copies ran while one was open for 26% of the time, Pallas kernels for 0%

profile of v3, /device:TPU:0, one launch (start us, length us, event | category | flops | bytes accessed | tf_op | source)
XLA Modules:
  0.0 191.3 jit_solution(2339938296168230956)
XLA Ops:
  0.0 0.0 copy-start
  0.0 1.0 iota_compare_fusion
  1.0 0.2 copy-done
  1.2 2.6 %convolution_convert_fusion = bf16[16,32,3072]{2,1,0:T(8,128)(2,1)} fusion(bf16[128,3072]{1,0:T(8,128)(2,1)S(1)} %copy-done, pred[16,64,128]{2,1,0:T(32,128)(4,1)S(1)} %iota_compare_fusion), kind=kOutput, calls=%fused_computation.8 | convolution fusion | flops 404226048 | bytes 3997696 | tf_op jit(solution)/shard_map/ect,td->ecd/dot_general | solution.py:41
  3.8 8.2 %all-to-all-start.2 = ((bf16[16,32,3072]{2,1,0:T(8,128)(2,1)}), bf16[16,32,3072]{2,1,0:T(8,128)(2,1)}, u32[]{:S(2)}, u32[]{:S(2)}) async-start(bf16[16,32,3072]{2,1,0:T(8,128)(2,1)} %convolution_convert_fusion), calls=%async_computation.2 | async-start | bytes 6291456 | tf_op jit(solution)/shard_map/all_to_all | solution.py:47
  11.9 2.7 %convolution_convert_fusion.1 = bf16[16,32,3072]{2,1,0:T(8,128)(2,1)} fusion(bf16[128,3072]{1,0:T(8,128)(2,1)S(1)} %copy-done, pred[16,64,128]{2,1,0:T(32,128)(4,1)S(1)} %iota_compare_fusion), kind=kOutput, calls=%fused_computation.9 | convolution fusion | flops 404226048 | bytes 3997696 | tf_op jit(solution)/shard_map/ect,td->ecd/dot_general | solution.py:41
  14.6 38.0 %all-to-all-done.2 = bf16[16,32,3072]{2,1,0:T(8,128)(2,1)} async-done(((bf16[16,32,3072]{2,1,0:T(8,128)(2,1)}), bf16[16,32,3072]{2,1,0:T(8,128)(2,1)}, u32[]{:S(2)}, u32[]{:S(2)}) %all-to-all-start.2) | async-done | bytes 3145760 | tf_op jit(solution)/shard_map/all_to_all | solution.py:47
  52.6 4.5 %all-to-all-start = ((bf16[16,32,3072]{2,1,0:T(8,128)(2,1)}), bf16[16,32,3072]{2,1,0:T(8,128)(2,1)}, u32[]{:S(2)}, u32[]{:S(2)}) async-start(bf16[16,32,3072]{2,1,0:T(8,128)(2,1)} %convolution_convert_fusion.1), calls=%async_computation | async-start | bytes 6291456 | tf_op jit(solution)/shard_map/all_to_all | solution.py:47
  57.1 12.6 %fusion = f32[512,2560]{1,0:T(8,128)S(1)} fusion(bf16[512,3072]{1,0:T(8,128)(2,1)} %bitcast.8, bf16[1,3072,2560]{2,1,0:T(8,128)(2,1)} %param.10), kind=kOutput, calls=%fused_computation | convolution fusion | flops 8053063680 | bytes 24117248 | tf_op jit(solution)/shard_map/dot_general | solution.py:13
  69.7 9.2 %fusion.11 = bf16[512,3072]{1,0:T(8,128)(2,1)} fusion(bf16[1,1280,3072]{2,1,0:T(8,128)(2,1)} %param.11, f32[512,2560]{1,0:T(8,128)S(1)} %fusion), kind=kOutput, calls=%fused_computation.11 | convolution fusion | flops 4032036864 | bytes 16252928 | tf_op jit(solution)/shard_map/dot_general | solution.py:17
  78.9 18.8 %all-to-all-done = bf16[16,32,3072]{2,1,0:T(8,128)(2,1)} async-done(((bf16[16,32,3072]{2,1,0:T(8,128)(2,1)}), bf16[16,32,3072]{2,1,0:T(8,128)(2,1)}, u32[]{:S(2)}, u32[]{:S(2)}) %all-to-all-start) | async-done | bytes 3145760 | tf_op jit(solution)/shard_map/all_to_all | solution.py:47
  97.7 4.7 %all-to-all-start.3 = ((bf16[16,32,3072]{2,1,0:T(8,128)(2,1)}), bf16[16,32,3072]{2,1,0:T(8,128)(2,1)}, u32[]{:S(2)}, u32[]{:S(2)}) async-start(bf16[16,32,3072]{2,1,0:T(8,128)(2,1)} %bitcast.40), calls=%async_computation.3 | async-start | bytes 6291456 | tf_op jit(solution)/shard_map/all_to_all | solution.py:49
  102.3 12.6 %fusion.2 = f32[512,2560]{1,0:T(8,128)S(1)} fusion(bf16[512,3072]{1,0:T(8,128)(2,1)} %bitcast.3, bf16[1,3072,2560]{2,1,0:T(8,128)(2,1)} %param.10), kind=kOutput, calls=%fused_computation.2 | convolution fusion | flops 8053063680 | bytes 24117248 | tf_op jit(solution)/shard_map/dot_general | solution.py:13
  115.0 9.1 %fusion.8 = bf16[512,3072]{1,0:T(8,128)(2,1)} fusion(bf16[1,1280,3072]{2,1,0:T(8,128)(2,1)} %param.11, f32[512,2560]{1,0:T(8,128)S(1)} %fusion.2), kind=kOutput, calls=%fused_computation.10 | convolution fusion | flops 4032036864 | bytes 16252928 | tf_op jit(solution)/shard_map/dot_general | solution.py:17
  124.0 18.7 %all-to-all-done.3 = bf16[16,32,3072]{2,1,0:T(8,128)(2,1)} async-done(((bf16[16,32,3072]{2,1,0:T(8,128)(2,1)}), bf16[16,32,3072]{2,1,0:T(8,128)(2,1)}, u32[]{:S(2)}, u32[]{:S(2)}) %all-to-all-start.3) | async-done | bytes 3145760 | tf_op jit(solution)/shard_map/all_to_all | solution.py:49
  142.8 0.0 copy-start.2
  142.8 0.0 copy-start.3
  142.8 0.0 copy-start.1
  142.8 4.6 %all-to-all-start.1 = ((bf16[16,32,3072]{2,1,0:T(8,128)(2,1)}), bf16[16,32,3072]{2,1,0:T(8,128)(2,1)}, u32[]{:S(2)}, u32[]{:S(2)}) async-start(bf16[16,32,3072]{2,1,0:T(8,128)(2,1)} %bitcast.39), calls=%async_computation.1 | async-start | bytes 6291456 | tf_op jit(solution)/shard_map/all_to_all | solution.py:49
  147.4 0.0 copy-done.2
  147.4 0.1 copy.12
  147.5 0.0 copy-done.3
  147.5 0.1 copy.7
  147.6 0.4 select_reduce_fusion
  148.0 0.1 copy.11
  148.0 0.0 copy-done.1
  148.0 0.2 broadcast_select_fusion
  148.3 2.5 %convolution_bitcast_fusion = f32[128,3072]{1,0:T(8,128)S(1)} fusion(bf16[16,32,3072]{2,1,0:T(8,128)(2,1)} %all-to-all-done.3, bf16[16,64,128]{2,1,0:T(8,128)(2,1)S(1)} %broadcast_select_fusion), kind=kOutput, calls=%fused_computation.12 | convolution fusion | flops 402653184 | bytes 4849664 | tf_op jit(solution)/shard_map/dot_general | solution.py:51
  150.8 37.2 %all-to-all-done.1 = bf16[16,32,3072]{2,1,0:T(8,128)(2,1)} async-done(((bf16[16,32,3072]{2,1,0:T(8,128)(2,1)}), bf16[16,32,3072]{2,1,0:T(8,128)(2,1)}, u32[]{:S(2)}, u32[]{:S(2)}) %all-to-all-start.1) | async-done | bytes 3145760 | tf_op jit(solution)/shard_map/all_to_all | solution.py:49
  188.0 3.4 %fusion.15 = bf16[128,3072]{1,0:T(8,128)(2,1)} fusion(f32[128,3072]{1,0:T(8,128)S(1)} %convolution_bitcast_fusion, bf16[16,32,3072]{2,1,0:T(8,128)(2,1)} %all-to-all-done.1, bf16[16,64,128]{2,1,0:T(8,128)(2,1)S(1)} %broadcast_select_fusion), kind=kOutput, calls=%fused_computation.15 | convolution fusion | flops 403439616 | bytes 5636096 | tf_op jit(solution)/shard_map/dot_general | solution.py:51
Async XLA Ops:
  0.0 1.1 copy-start
  3.8 48.8 %all-to-all-start.2 = ((bf16[16,32,3072]{2,1,0:T(8,128)(2,1)}), bf16[16,32,3072]{2,1,0:T(8,128)(2,1)}, u32[]{:S(2)}, u32[]{:S(2)}) async-start(bf16[16,32,3072]{2,1,0:T(8,128)(2,1)} %convolution_convert_fusion), calls=%async_computation.2 | async-start | bytes 6291456 | tf_op jit(solution)/shard_map/all_to_all | solution.py:47
  52.6 45.1 %all-to-all-start = ((bf16[16,32,3072]{2,1,0:T(8,128)(2,1)}), bf16[16,32,3072]{2,1,0:T(8,128)(2,1)}, u32[]{:S(2)}, u32[]{:S(2)}) async-start(bf16[16,32,3072]{2,1,0:T(8,128)(2,1)} %convolution_convert_fusion.1), calls=%async_computation | async-start | bytes 6291456 | tf_op jit(solution)/shard_map/all_to_all | solution.py:47
  97.7 45.1 %all-to-all-start.3 = ((bf16[16,32,3072]{2,1,0:T(8,128)(2,1)}), bf16[16,32,3072]{2,1,0:T(8,128)(2,1)}, u32[]{:S(2)}, u32[]{:S(2)}) async-start(bf16[16,32,3072]{2,1,0:T(8,128)(2,1)} %bitcast.40), calls=%async_computation.3 | async-start | bytes 6291456 | tf_op jit(solution)/shard_map/all_to_all | solution.py:49
  142.8 4.6 %copy-start.2 = (f32[128,4]{0,1:T(4,128)S(1)}, f32[128,4]{0,1:T(4,128)}, u32[]{:S(2)}) copy-start(f32[128,4]{0,1:T(4,128)} %param.8) | copy-start | bytes 6148
  142.8 4.7 %copy-start.3 = (s32[128,4]{0,1:T(4,128)S(1)}, s32[128,4]{0,1:T(4,128)}, u32[]{:S(2)}) copy-start(s32[128,4]{0,1:T(4,128)} %param.7) | copy-start | bytes 6148
  142.8 5.3 %copy-start.1 = (s32[1,16,64]{2,1,0:T(8,128)S(1)}, s32[1,16,64]{2,1,0:T(8,128)}, u32[]{:S(2)}) copy-start(s32[1,16,64]{2,1,0:T(8,128)} %param.9) | copy-start | bytes 12292
  142.8 45.2 %all-to-all-start.1 = ((bf16[16,32,3072]{2,1,0:T(8,128)(2,1)}), bf16[16,32,3072]{2,1,0:T(8,128)(2,1)}, u32[]{:S(2)}, u32[]{:S(2)}) async-start(bf16[16,32,3072]{2,1,0:T(8,128)(2,1)} %bitcast.39), calls=%async_computation.1 | async-start | bytes 6291456 | tf_op jit(solution)/shard_map/all_to_all | solution.py:49

commit v4 on v2

v4 whole, which is shorter than its diff:
```python
import jax
import jax.numpy as jnp
import numpy as np
from jax import lax
from jax.sharding import Mesh
from jax.sharding import PartitionSpec as P

AXES = ("z", "yh", "core")
RING = 4


def expert_block(rows_in, w_first, w_second):
    features = rows_in.shape[-1]
    hidden_units = w_second.shape[0]
    flat = rows_in.reshape(-1, features)
    projected = jnp.dot(flat, w_first, preferred_element_type=jnp.float32)
    intermediate_activation = (
        jax.nn.silu(projected[:, :hidden_units]) * projected[:, hidden_units:]
    ).astype(jnp.bfloat16)
    result = jnp.dot(intermediate_activation, w_second, preferred_element_type=jnp.float32).astype(
        jnp.bfloat16
    )
    return result.reshape(rows_in.shape)


def shift_z(x, step):
    return lax.ppermute(x, "z", [(i, (i + step) % RING) for i in range(RING)])


def swap(x, axis):
    return lax.ppermute(x, axis, [(0, 1), (1, 0)])


def shards(tokens, expert_ids, gate_weights, slot_rows, w_in, w_out):
    tok_rows, features = tokens.shape
    experts = slot_rows.shape[1]
    capacity = slot_rows.shape[2]
    w_first = w_in[0]
    w_second = w_out[0]
    own_rows = slot_rows[0]
    zi = lax.axis_index("z")
    yi = lax.axis_index("yh")
    ki = lax.axis_index("core")
    n_y = 2
    blocks = RING * n_y

    meta = jnp.zeros((1, features), jnp.bfloat16)
    meta = meta.at[0, : experts * capacity].set(own_rows.reshape(-1).astype(jnp.bfloat16))
    block = jnp.concatenate([tokens, meta], axis=0)

    half = (tok_rows + 1) // 2
    partner = swap(block, "yh")
    from_below = shift_z(block, 1)
    from_above = shift_z(block, -1)
    p_below = shift_z(partner, 1)
    p_above = shift_z(partner, -1)
    far = jnp.concatenate(
        [shift_z(from_below[:half], 1), shift_z(from_above[half:], -1)], axis=0
    )
    p_far = jnp.concatenate([shift_z(p_below[:half], 1), shift_z(p_above[half:], -1)], axis=0)
    rel = jnp.stack([block, partner, from_above, p_above, far, p_far, from_below, p_below])
    toks = rel[:, :tok_rows]
    lists = rel[:, tok_rows, : experts * capacity].astype(jnp.int32).reshape(blocks, experts, capacity)

    chip = zi * n_y + yi
    mine_e = chip * 2 + ki
    pair_e = chip * 2 + (1 - ki)
    sel = jnp.stack(
        [
            lax.dynamic_index_in_dim(lists, mine_e, axis=1, keepdims=False),
            lax.dynamic_index_in_dim(lists, pair_e, axis=1, keepdims=False),
        ],
        axis=1,
    )
    token_iota = jnp.arange(tok_rows, dtype=jnp.int32)
    one_hot = (sel[..., None] == token_iota).astype(jnp.bfloat16)
    disp = jnp.einsum(
        "bjct,btd->bjcd", one_hot, toks, preferred_element_type=jnp.float32
    ).astype(jnp.bfloat16)
    got = swap(disp[:, 1], "core")

    pos = jnp.arange(blocks, dtype=jnp.int32)
    inv = ((pos // n_y - zi) % RING) * n_y + (pos % n_y + yi) % n_y
    out_a = expert_block(disp[:, 0], w_first, w_second)
    a_abs = jnp.take(out_a, inv, axis=0)
    ret_a = lax.all_to_all(a_abs, ("z", "yh"), 0, 0, tiled=True)
    a_abs, got = lax.optimization_barrier((a_abs, got))
    out_b = expert_block(got, w_first, w_second)
    ret_a, out_b = lax.optimization_barrier((ret_a, out_b))
    back_b = swap(out_b, "core")
    b_abs = jnp.take(back_b, inv, axis=0)
    ret_b = lax.all_to_all(b_abs, ("z", "yh"), 0, 0, tiled=True)

    matches = (
        expert_ids[:, :, None] == jnp.arange(experts, dtype=jnp.int32)[None, None, :]
    ).astype(jnp.float32)
    gate_of = jnp.einsum("tk,tke->et", gate_weights, matches).astype(jnp.bfloat16)
    rows3 = own_rows.reshape(blocks, 2, capacity)
    gate3 = gate_of.reshape(blocks, 2, tok_rows)
    summed = None
    for which, returned in ((ki, ret_a), (1 - ki, ret_b)):
        rows = lax.dynamic_index_in_dim(rows3, which, axis=1, keepdims=False)
        gates = lax.dynamic_index_in_dim(gate3, which, axis=1, keepdims=False)
        mixing = jnp.where(
            rows[:, :, None] == token_iota[None, None, :],
            gates[:, None, :],
            jnp.zeros((), jnp.bfloat16),
        )
        contrib = jnp.dot(
            mixing.reshape(-1, tok_rows).T,
            returned.reshape(-1, features),
            preferred_element_type=jnp.float32,
        )
        summed = contrib if summed is None else summed + contrib
    return summed.astype(jnp.bfloat16)


def solution(mesh):
    devices = np.asarray(mesh.devices)
    groups = devices.shape[0]
    fine = Mesh(devices.reshape(groups, RING, 2, 2), ("dp",) + AXES)
    rows = ("dp",) + AXES
    in_specs = (
        P(rows, None),
        P(rows, None),
        P(rows, None),
        P(rows, None, None),
        P(AXES, None, None),
        P(AXES, None, None),
    )
    out_specs = P(rows, None)
    return jax.shard_map(shards, mesh=fine, in_specs=in_specs, out_specs=out_specs, check_vma=False)
```

time: 204 us -> 212 us (1.039)
  blocking collectives: 82.4 us -> 0 us
  waiting for transfers between devices: 73.6 us -> 109 us
  starting transfers between devices: 4.77 us -> 28 us
  local copies, waits for them, and re-layouts: 1.45 us -> 13 us
  other arithmetic: 0.37 us -> 11.1 us
  matrix products: 40.9 us -> 49.8 us
    all_to_all x1 -> x0, blocking collectives: 82.4 us -> none  [shards(): lax.all_to_all(part, 'expert', split_axis=0, concat_axis=0, tiled=True)]
    ppermute x0 -> x11, waiting for transfers between devices: none -> 52.2 us  [the longest x8 46.2 us: shift_z(): return lax.ppermute(x, 'z', [(i, (i + step) % RING) for i in range(RING)])]
    ppermute x0 -> x11, starting transfers between devices: none -> 18.3 us  [the longest x8 15.1 us: shift_z(): return lax.ppermute(x, 'z', [(i, (i + step) % RING) for i in range(RING)])]
    all_to_all x1 -> x2, waiting for transfers between devices: 73.6 us -> 56.4 us  [the longest x1 37.7 us: shards(): ret_b = lax.all_to_all(b_abs, ('z', 'yh'), 0, 0, tiled=True)]
    gather x0 -> x2, local copies, waits for them, and re-layouts: none -> 7 us  [the longest x1 4.36 us: shards(): b_abs = jnp.take(back_b, inv, axis=0)]
    select_n x0 -> x2, other arithmetic: none -> 6.07 us  [the longest x1 3.98 us: shards(): b_abs = jnp.take(back_b, inv, axis=0)]
    dot_general x1 -> x2, matrix products: 19 us -> 24.5 us  [expert_block(): projected = jnp.dot(flat, w_first, preferred_element_type=jnp.float32)]
    all_to_all x1 -> x2, starting transfers between devices: 4.77 us -> 9.71 us  [the longest x1 5.13 us: shards(): ret_a = lax.all_to_all(a_abs, ('z', 'yh'), 0, 0, tiled=True)]
  transfers between devices with their start and end apart: 1 -> 13, of which waited for: 1 -> 6; matrix products, arithmetic and copies ran while one was open for 0% -> 23% of each run, Pallas kernels for 0% -> 0%
where the time goes in v4:
time: 212 us; the launch traced here: 211 us
  waiting for transfers between devices  109 us (51%)
  matrix products  49.8 us (23%)
  starting transfers between devices  28 us (13%)
  local copies, waits for them, and re-layouts  13 us (6%)
  other arithmetic  11.1 us (5%)
    ppermute x8, waiting for transfers between devices, shift_z(): return lax.ppermute(x, 'z', [(i, (i + step) % RING) for i in range(RING)])  46.2 us
    all_to_all x1, waiting for transfers between devices, shards(): ret_b = lax.all_to_all(b_abs, ('z', 'yh'), 0, 0, tiled=True)  37.7 us
    dot_general x2, matrix products, expert_block(): projected = jnp.dot(flat, w_first, preferred_element_type=jnp.float32)  24.5 us
    all_to_all x1, waiting for transfers between devices, shards(): ret_a = lax.all_to_all(a_abs, ('z', 'yh'), 0, 0, tiled=True)  18.7 us
    ppermute x8, starting transfers between devices, shift_z(): return lax.ppermute(x, 'z', [(i, (i + step) % RING) for i in range(RING)])  15.1 us
    dot_general x2, matrix products, expert_block(): jnp.dot(intermediate_activation, w_second, preferred_element_type=jnp.flo...  14.9 us
    ppermute x3, waiting for transfers between devices, swap(): return lax.ppermute(x, axis, [(0, 1), (1, 0)])  6 us
    dot_general x2, matrix products, shards(): jnp.dot(mixing.reshape(-1, tok_rows).T, returned.reshape(-1, features), p...  5.79 us
  transfers between devices with their start and end apart: 13, of which 6 were waited for; matrix products, arithmetic and copies ran while one was open for 23% of the time, Pallas kernels for 0%

profile of v4, /device:TPU:0, one launch (start us, length us, event | category | flops | bytes accessed | tf_op | source)
XLA Modules:
  0.0 210.8 jit_solution(17522229742456904849)
XLA Ops:
  0.0 0.6 compare_reduce_fusion
  0.6 1.3 convert_select_fusion
  2.0 0.1 reshape.75
  2.1 1.2 fusion.25
  3.3 4.2 %collective-permute-start.1 = (bf16[129,3072]{1,0:T(8,128)(2,1)S(1)}, bf16[129,3072]{1,0:T(8,128)(2,1)S(1)}, u32[]{:S(2)}, u32[]{:S(2)}) collective-permute-start(bf16[129,3072]{1,0:T(8,128)(2,1)S(1)} %fusion.25), channel_id=1, source_target_pairs={{0,12},{4,0},{8,4},{12,8},{1,13},{5,1},{9,5},{13,9},{2,14},{6,2},{... | collective-permute-start | bytes 2377736 | tf_op jit(solution)/shard_map/ppermute | solution.py:27
  7.5 0.0 collective-permute-start.3
  7.5 3.2 %collective-permute-start = (bf16[129,3072]{1,0:T(8,128)(2,1)S(1)}, bf16[129,3072]{1,0:T(8,128)(2,1)S(1)}, u32[]{:S(2)}, u32[]{:S(2)}) collective-permute-start(bf16[129,3072]{1,0:T(8,128)(2,1)S(1)} %fusion.25), channel_id=1, source_target_pairs={{0,2},{2,0},{1,3},{3,1},{4,6},{6,4},{5,7},{7,5},{8,10},{10,8},{9,1... | collective-permute-start | bytes 2377736 | tf_op jit(solution)/shard_map/ppermute | solution.py:31
  10.7 1.2 bitcast_dynamic-update-slice_fusion.5
  11.9 13.4 %collective-permute-done.1 = bf16[129,3072]{1,0:T(8,128)(2,1)S(1)} collective-permute-done((bf16[129,3072]{1,0:T(8,128)(2,1)S(1)}, bf16[129,3072]{1,0:T(8,128)(2,1)S(1)}, u32[]{:S(2)}, u32[]{:S(2)}) %collective-permute-start.1) | collective-permute-done | bytes 792608 | tf_op jit(solution)/shard_map/ppermute | solution.py:27
  25.4 3.8 %collective-permute-start.5 = (bf16[65,3072]{1,0:T(8,128)(2,1)S(1)}, bf16[65,3072]{1,0:T(8,128)(2,1)S(1)}, u32[]{:S(2)}, u32[]{:S(2)}) collective-permute-start(bf16[65,3072]{1,0:T(8,128)(2,1)S(1)} %slice.69), channel_id=1, source_target_pairs={{0,12},{4,0},{8,4},{12,8},{1,13},{5,1},{9,5},{13,9},{2,14},{6,2},{... | collective-permute-start | bytes 1198088 | tf_op jit(solution)/shard_map/ppermute | solution.py:27
  29.1 0.0 collective-permute-done.3
  29.1 0.1 collective-permute-start.4
  29.2 0.0 collective-permute-done
  29.2 3.2 %collective-permute-start.2 = (bf16[129,3072]{1,0:T(8,128)(2,1)S(1)}, bf16[129,3072]{1,0:T(8,128)(2,1)S(1)}, u32[]{:S(2)}, u32[]{:S(2)}) collective-permute-start(bf16[129,3072]{1,0:T(8,128)(2,1)S(1)} %collective-permute-done), channel_id=1, source_target_pairs={{0,12},{4,0},{8,4},{12,8},{1,13},{5,1},{9,5},{13,9},{2,14},{6,2},{... | collective-permute-start | bytes 2377736 | tf_op jit(solution)/shard_map/ppermute | solution.py:27
  32.5 0.0 collective-permute-start.6
  32.5 0.1 bitcast_dynamic-update-slice_fusion.4
  32.5 0.1 bitcast_dynamic-update-slice_fusion.3
  32.6 23.0 %collective-permute-done.2 = bf16[129,3072]{1,0:T(8,128)(2,1)S(1)} collective-permute-done((bf16[129,3072]{1,0:T(8,128)(2,1)S(1)}, bf16[129,3072]{1,0:T(8,128)(2,1)S(1)}, u32[]{:S(2)}, u32[]{:S(2)}) %collective-permute-start.2) | collective-permute-done | bytes 792608 | tf_op jit(solution)/shard_map/ppermute | solution.py:27
  55.6 3.8 %collective-permute-start.8 = (bf16[65,3072]{1,0:T(8,128)(2,1)S(1)}, bf16[65,3072]{1,0:T(8,128)(2,1)S(1)}, u32[]{:S(2)}, u32[]{:S(2)}) collective-permute-start(bf16[65,3072]{1,0:T(8,128)(2,1)S(1)} %slice.71), channel_id=1, source_target_pairs={{0,12},{4,0},{8,4},{12,8},{1,13},{5,1},{9,5},{13,9},{2,14},{6,2},{... | collective-permute-start | bytes 1198088 | tf_op jit(solution)/shard_map/ppermute | solution.py:27
  59.4 0.0 collective-permute-done.6
  59.4 0.1 collective-permute-start.7
  59.5 0.1 bitcast_dynamic-update-slice_fusion.2
  59.6 0.0 collective-permute-done.4
  59.6 0.0 collective-permute-done.5
  59.6 0.1 fusion.26
  59.6 9.8 %collective-permute-done.7 = bf16[64,3072]{1,0:T(8,128)(2,1)S(1)} collective-permute-done((bf16[64,3072]{1,0:T(8,128)(2,1)S(1)}, bf16[64,3072]{1,0:T(8,128)(2,1)S(1)}, u32[]{:S(2)}, u32[]{:S(2)}) %collective-permute-start.7) | collective-permute-done | bytes 393248 | tf_op jit(solution)/shard_map/ppermute | solution.py:27
  69.5 0.0 collective-permute-done.8
  69.5 0.1 fusion.27
  69.5 0.1 bitcast_dynamic-update-slice_fusion.1
  69.6 0.1 bitcast_dynamic-update-slice_fusion
  69.7 0.0 copy-start
  69.7 2.8 %copy-done = bf16[8,129,3072]{2,1,0:T(8,128)(2,1)} copy-done((bf16[8,129,3072]{2,1,0:T(8,128)(2,1)}, bf16[8,129,3072]{2,1,0:T(8,128)(2,1)S(1)}, u32[]{:S(2)}) %copy-start) | copy-done | bytes 6340632
  72.5 0.1 fusion.39
  72.6 0.1 reshape.79
  72.7 4.6 %fusion.9 = bf16[8,2,64,3072]{3,2,1,0:T(8,128)(2,1)S(1)} fusion(bf16[8,129,3072]{2,1,0:T(8,128)(2,1)} %copy-done, s32[8,2,64]{2,1,0:T(2,128)S(1)} %pad_add_fusion), kind=kOutput, calls=%fused_computation.12 | convolution fusion | flops 808583168 | bytes 12587008 | tf_op jit(solution)/shard_map/bjct,btd->bjcd/dot_general | solution.py:77
  77.3 0.0 slice-start
  77.3 2.2 %slice_bitcast_fusion.4 = (bf16[8,64,3072]{2,1,0:T(8,128)(2,1)}, bf16[8,1,64,3072]{3,2,1,0:T(8,128)(2,1)S(1)}) fusion(bf16[8,2,64,3072]{3,2,1,0:T(8,128)(2,1)S(1)} %fusion.9), kind=kLoop, calls=%fused_computation.19 | loop fusion | bytes 12582912 | tf_op jit(solution)/shard_map/squeeze | solution.py:80
  79.6 0.0 collective-permute-start.9
  79.6 11.9 %fusion.2 = f32[512,2560]{1,0:T(8,128)S(1)} fusion(bf16[512,3072]{1,0:T(8,128)(2,1)S(1)} %bitcast.70, bf16[1,3072,2560]{2,1,0:T(8,128)(2,1)} %param.14), kind=kOutput, calls=%fused_computation.4 | convolution fusion | flops 8053063680 | bytes 24117248 | tf_op jit(solution)/shard_map/dot_general | solution.py:16
  91.5 0.0 slice-done
  91.5 0.0 slice-done.1
  91.5 5.8 %fusion.10 = bf16[512,3072]{1,0:T(8,128)(2,1)} fusion(bf16[1,1280,3072]{2,1,0:T(8,128)(2,1)S(1)} %bitcast.76, f32[512,2560]{1,0:T(8,128)S(1)} %fusion.2), kind=kOutput, calls=%fused_computation.13 | convolution fusion | flops 4032036864 | bytes 16252928 | tf_op jit(solution)/shard_map/dot_general | solution.py:20
  97.3 2.6 %gather_fusion = bf16[8,64,3072]{2,1,0:T(8,128)(2,1)S(1)} fusion(bf16[8,64,3072]{2,1,0:T(8,128)(2,1)} %bitcast.69, s32[1024]{0:T(1024)S(1)} %pad_clamp_fusion), kind=kCustom, calls=%fused_computation.clone | custom fusion | bytes 6291488 | tf_op jit(solution)/shard_map/jit(_take)/gather | solution.py:85
  100.0 2.1 broadcast_select_fusion.1
  102.0 5.1 %all-to-all-start = ((bf16[8,64,3072]{2,1,0:T(8,128)(2,1)}), bf16[8,64,3072]{2,1,0:T(8,128)(2,1)S(1)}, u32[]{:S(2)}, u32[]{:S(2)}) async-start(bf16[8,64,3072]{2,1,0:T(8,128)(2,1)} %broadcast_select_fusion.1), calls=%async_computation | async-start | bytes 6291456 | tf_op jit(solution)/shard_map/all_to_all | solution.py:86
  107.2 0.0 collective-permute-done.9
  107.2 12.6 %fusion = f32[512,2560]{1,0:T(8,128)S(1)} fusion(bf16[512,3072]{1,0:T(8,128)(2,1)} %bitcast.19, bf16[1,3072,2560]{2,1,0:T(8,128)(2,1)} %param.14), kind=kOutput, calls=%fused_computation.2 | convolution fusion | flops 8053063680 | bytes 24117248 | tf_op jit(solution)/shard_map/dot_general | solution.py:16
  119.8 9.1 %fusion.13 = bf16[512,3072]{1,0:T(8,128)(2,1)} fusion(bf16[1,1280,3072]{2,1,0:T(8,128)(2,1)} %param.15, f32[512,2560]{1,0:T(8,128)S(1)} %fusion), kind=kOutput, calls=%fused_computation.14 | convolution fusion | flops 4032036864 | bytes 16252928 | tf_op jit(solution)/shard_map/dot_general | solution.py:20
  128.9 18.7 %all-to-all-done = bf16[8,64,3072]{2,1,0:T(8,128)(2,1)S(1)} async-done(((bf16[8,64,3072]{2,1,0:T(8,128)(2,1)}), bf16[8,64,3072]{2,1,0:T(8,128)(2,1)S(1)}, u32[]{:S(2)}, u32[]{:S(2)}) %all-to-all-start) | async-done | bytes 3145760 | tf_op jit(solution)/shard_map/all_to_all | solution.py:86
  147.6 0.0 collective-permute-start.10
  147.6 6.0 %collective-permute-done.10 = bf16[8,64,3072]{2,1,0:T(8,128)(2,1)} collective-permute-done((bf16[8,64,3072]{2,1,0:T(8,128)(2,1)}, bf16[8,64,3072]{2,1,0:T(8,128)(2,1)}, u32[]{:S(2)}, u32[]{:S(2)}) %collective-permute-start.10) | collective-permute-done | bytes 3145760 | tf_op jit(solution)/shard_map/ppermute | solution.py:31
  153.6 4.4 %gather_fusion.1 = bf16[8,64,3072]{2,1,0:T(8,128)(2,1)} fusion(bf16[8,64,3072]{2,1,0:T(8,128)(2,1)} %collective-permute-done.10, s32[1024]{0:T(1024)S(1)} %pad_clamp_fusion), kind=kCustom, calls=%fused_computation.1.clone | custom fusion | bytes 6291488 | tf_op jit(solution)/shard_map/jit(_take)/gather | solution.py:91
  157.9 4.0 %broadcast_select_fusion = bf16[8,64,3072]{2,1,0:T(8,128)(2,1)} fusion(bf16[8,64,3072]{2,1,0:T(8,128)(2,1)} %gather_fusion.1, pred[8]{0:T(512)(128)(4,1)S(1)} %get-tuple-element.24), kind=kLoop, calls=%fused_computation.20 | loop fusion | flops 1572864 | bytes 6291464 | tf_op jit(solution)/shard_map/jit(_take)/select_n | solution.py:91
  161.9 4.6 %all-to-all-start.1 = ((bf16[8,64,3072]{2,1,0:T(8,128)(2,1)}), bf16[8,64,3072]{2,1,0:T(8,128)(2,1)}, u32[]{:S(2)}, u32[]{:S(2)}) async-start(bf16[8,64,3072]{2,1,0:T(8,128)(2,1)} %broadcast_select_fusion), calls=%async_computation.1 | async-start | bytes 6291456 | tf_op jit(solution)/shard_map/all_to_all | solution.py:92
  166.5 0.0 copy-done.2
  166.5 0.1 copy.17
  166.6 0.0 copy-done.3
  166.6 0.1 copy.9
  166.8 0.4 select_reduce_fusion
  167.1 0.1 copy.13
  167.2 0.0 copy-done.1
  167.3 1.9 convolution_bitcast_fusion.1
  169.1 37.7 %all-to-all-done.1 = bf16[8,64,3072]{2,1,0:T(8,128)(2,1)} async-done(((bf16[8,64,3072]{2,1,0:T(8,128)(2,1)}), bf16[8,64,3072]{2,1,0:T(8,128)(2,1)}, u32[]{:S(2)}, u32[]{:S(2)}) %all-to-all-start.1) | async-done | bytes 3145760 | tf_op jit(solution)/shard_map/all_to_all | solution.py:92
  206.8 3.9 %fusion.17 = bf16[128,3072]{1,0:T(8,128)(2,1)} fusion(f32[128,3072]{1,0:T(8,128)} %convolution_bitcast_fusion.1, bf16[8,64,3072]{2,1,0:T(8,128)(2,1)} %all-to-all-done.1, s32[8,64]{1,0:T(8,128)S(1)} %bitcast.74, bf16[8,128]{1,0:T(8,128)(2,1)S(1)} %get-tuple-element.34), kind=kOutput, calls=%fused_computation.18 | convolution fusion | flops 403570688 | bytes 5509120 | tf_op jit(solution)/shard_map/dot_general | solution.py:109
  (16 shorter events, 0.2 us)
Async XLA Ops:
  3.3 22.0 %collective-permute-start.1 = (bf16[129,3072]{1,0:T(8,128)(2,1)S(1)}, bf16[129,3072]{1,0:T(8,128)(2,1)S(1)}, u32[]{:S(2)}, u32[]{:S(2)}) collective-permute-start(bf16[129,3072]{1,0:T(8,128)(2,1)S(1)} %fusion.25), channel_id=1, source_target_pairs={{0,12},{4,0},{8,4},{12,8},{1,13},{5,1},{9,5},{13,9},{2,14},{6,2},{... | collective-permute-start | bytes 2377736 | tf_op jit(solution)/shard_map/ppermute | solution.py:27
  7.5 21.7 %collective-permute-start.3 = (bf16[129,3072]{1,0:T(8,128)(2,1)S(1)}, bf16[129,3072]{1,0:T(8,128)(2,1)S(1)}, u32[]{:S(2)}, u32[]{:S(2)}) collective-permute-start(bf16[129,3072]{1,0:T(8,128)(2,1)S(1)} %fusion.25), channel_id=1, source_target_pairs={{0,4},{4,8},{8,12},{12,0},{1,5},{5,9},{9,13},{13,1},{2,6},{6,10},{... | collective-permute-start | bytes 2377736 | tf_op jit(solution)/shard_map/ppermute | solution.py:27
  7.5 21.8 %collective-permute-start = (bf16[129,3072]{1,0:T(8,128)(2,1)S(1)}, bf16[129,3072]{1,0:T(8,128)(2,1)S(1)}, u32[]{:S(2)}, u32[]{:S(2)}) collective-permute-start(bf16[129,3072]{1,0:T(8,128)(2,1)S(1)} %fusion.25), channel_id=1, source_target_pairs={{0,2},{2,0},{1,3},{3,1},{4,6},{6,4},{5,7},{7,5},{8,10},{10,8},{9,1... | collective-permute-start | bytes 2377736 | tf_op jit(solution)/shard_map/ppermute | solution.py:31
  25.4 34.2 %collective-permute-start.5 = (bf16[65,3072]{1,0:T(8,128)(2,1)S(1)}, bf16[65,3072]{1,0:T(8,128)(2,1)S(1)}, u32[]{:S(2)}, u32[]{:S(2)}) collective-permute-start(bf16[65,3072]{1,0:T(8,128)(2,1)S(1)} %slice.69), channel_id=1, source_target_pairs={{0,12},{4,0},{8,4},{12,8},{1,13},{5,1},{9,5},{13,9},{2,14},{6,2},{... | collective-permute-start | bytes 1198088 | tf_op jit(solution)/shard_map/ppermute | solution.py:27
  29.1 30.4 %collective-permute-start.4 = (bf16[64,3072]{1,0:T(8,128)(2,1)S(1)}, bf16[64,3072]{1,0:T(8,128)(2,1)S(1)}, u32[]{:S(2)}, u32[]{:S(2)}) collective-permute-start(bf16[64,3072]{1,0:T(8,128)(2,1)S(1)} %slice.68), channel_id=1, source_target_pairs={{0,4},{4,8},{8,12},{12,0},{1,5},{5,9},{9,13},{13,1},{2,6},{6,10},{... | collective-permute-start | bytes 1179656 | tf_op jit(solution)/shard_map/ppermute | solution.py:27
  29.2 26.3 %collective-permute-start.2 = (bf16[129,3072]{1,0:T(8,128)(2,1)S(1)}, bf16[129,3072]{1,0:T(8,128)(2,1)S(1)}, u32[]{:S(2)}, u32[]{:S(2)}) collective-permute-start(bf16[129,3072]{1,0:T(8,128)(2,1)S(1)} %collective-permute-done), channel_id=1, source_target_pairs={{0,12},{4,0},{8,4},{12,8},{1,13},{5,1},{9,5},{13,9},{2,14},{6,2},{... | collective-permute-start | bytes 2377736 | tf_op jit(solution)/shard_map/ppermute | solution.py:27
  32.5 26.9 %collective-permute-start.6 = (bf16[129,3072]{1,0:T(8,128)(2,1)S(1)}, bf16[129,3072]{1,0:T(8,128)(2,1)S(1)}, u32[]{:S(2)}, u32[]{:S(2)}) collective-permute-start(bf16[129,3072]{1,0:T(8,128)(2,1)S(1)} %collective-permute-done), channel_id=1, source_target_pairs={{0,4},{4,8},{8,12},{12,0},{1,5},{5,9},{9,13},{13,1},{2,6},{6,10},{... | collective-permute-start | bytes 2377736 | tf_op jit(solution)/shard_map/ppermute | solution.py:27
  55.6 13.9 %collective-permute-start.8 = (bf16[65,3072]{1,0:T(8,128)(2,1)S(1)}, bf16[65,3072]{1,0:T(8,128)(2,1)S(1)}, u32[]{:S(2)}, u32[]{:S(2)}) collective-permute-start(bf16[65,3072]{1,0:T(8,128)(2,1)S(1)} %slice.71), channel_id=1, source_target_pairs={{0,12},{4,0},{8,4},{12,8},{1,13},{5,1},{9,5},{13,9},{2,14},{6,2},{... | collective-permute-start | bytes 1198088 | tf_op jit(solution)/shard_map/ppermute | solution.py:27
  59.4 10.1 %collective-permute-start.7 = (bf16[64,3072]{1,0:T(8,128)(2,1)S(1)}, bf16[64,3072]{1,0:T(8,128)(2,1)S(1)}, u32[]{:S(2)}, u32[]{:S(2)}) collective-permute-start(bf16[64,3072]{1,0:T(8,128)(2,1)S(1)} %slice.70), channel_id=1, source_target_pairs={{0,4},{4,8},{8,12},{12,0},{1,5},{5,9},{9,13},{13,1},{2,6},{6,10},{... | collective-permute-start | bytes 1179656 | tf_op jit(solution)/shard_map/ppermute | solution.py:27
  69.7 2.8 %copy-start = (bf16[8,129,3072]{2,1,0:T(8,128)(2,1)}, bf16[8,129,3072]{2,1,0:T(8,128)(2,1)S(1)}, u32[]{:S(2)}) copy-start(bf16[8,129,3072]{2,1,0:T(8,128)(2,1)S(1)} %bitcast_dynamic-update-slice_fusion) | copy-start | bytes 19021828
  77.3 14.2 %slice-start = ((s8[7864320]{0:T(1024)(128)(4,1)}), s8[4194304]{0:T(1024)(128)(4,1)S(1)}, s32[]{:S(2)}) async-start(s8[7864320]{0:T(1024)(128)(4,1)} %bitcast.75), calls=%async_computation.2 | async-start | bytes 8388608
  79.6 27.6 %collective-permute-start.9 = (bf16[8,64,3072]{2,1,0:T(8,128)(2,1)}, bf16[8,64,3072]{2,1,0:T(8,128)(2,1)}, u32[]{:S(2)}, u32[]{:S(2)}) collective-permute-start(bf16[8,64,3072]{2,1,0:T(8,128)(2,1)} %get-tuple-element.26), channel_id=1, source_target_pairs={{0,1},{1,0},{2,3},{3,2},{4,5},{5,4},{6,7},{7,6},{8,9},{9,8},{10,11... | collective-permute-start | bytes 9437192 | tf_op jit(solution)/shard_map/ppermute | solution.py:31
  79.6 11.9 %slice-start.1 = ((s8[7864320]{0:T(1024)(128)(4,1)}), s8[3670016]{0:T(1024)(128)(4,1)S(1)}, s32[]{:S(2)}) async-start(s8[7864320]{0:T(1024)(128)(4,1)} %bitcast.75), calls=%async_computation.3 | async-start | bytes 7340032
  102.0 45.5 %all-to-all-start = ((bf16[8,64,3072]{2,1,0:T(8,128)(2,1)}), bf16[8,64,3072]{2,1,0:T(8,128)(2,1)S(1)}, u32[]{:S(2)}, u32[]{:S(2)}) async-start(bf16[8,64,3072]{2,1,0:T(8,128)(2,1)} %broadcast_select_fusion.1), calls=%async_computation | async-start | bytes 6291456 | tf_op jit(solution)/shard_map/all_to_all | solution.py:86
  147.6 6.0 %collective-permute-start.10 = (bf16[8,64,3072]{2,1,0:T(8,128)(2,1)}, bf16[8,64,3072]{2,1,0:T(8,128)(2,1)}, u32[]{:S(2)}, u32[]{:S(2)}) collective-permute-start(bf16[8,64,3072]{2,1,0:T(8,128)(2,1)} %bitcast.77), channel_id=1, source_target_pairs={{0,1},{1,0},{2,3},{3,2},{4,5},{5,4},{6,7},{7,6},{8,9},{9,8},{10,11... | collective-permute-start | bytes 9437192 | tf_op jit(solution)/shard_map/ppermute | solution.py:31
  161.9 4.6 %copy-start.2 = (f32[128,4]{0,1:T(4,128)S(1)}, f32[128,4]{0,1:T(4,128)}, u32[]{:S(2)}) copy-start(f32[128,4]{0,1:T(4,128)} %param.12) | copy-start | bytes 6148
  161.9 4.7 %copy-start.3 = (s32[128,4]{0,1:T(4,128)S(1)}, s32[128,4]{0,1:T(4,128)}, u32[]{:S(2)}) copy-start(s32[128,4]{0,1:T(4,128)} %param.11) | copy-start | bytes 6148
  161.9 5.3 %copy-start.1 = (s32[1,16,64]{2,1,0:T(8,128)S(1)}, s32[1,16,64]{2,1,0:T(8,128)}, u32[]{:S(2)}) copy-start(s32[1,16,64]{2,1,0:T(8,128)} %param.13) | copy-start | bytes 12292
  161.9 44.9 %all-to-all-start.1 = ((bf16[8,64,3072]{2,1,0:T(8,128)(2,1)}), bf16[8,64,3072]{2,1,0:T(8,128)(2,1)}, u32[]{:S(2)}, u32[]{:S(2)}) async-start(bf16[8,64,3072]{2,1,0:T(8,128)(2,1)} %broadcast_select_fusion), calls=%async_computation.1 | async-start | bytes 6291456 | tf_op jit(solution)/shard_map/all_to_all | solution.py:92

commit v5 on v4

--- a/solution.py
+++ b/solution.py
@@ -58,37 +58,53 @@
         [shift_z(from_below[:half], 1), shift_z(from_above[half:], -1)], axis=0
     )
     p_far = jnp.concatenate([shift_z(p_below[:half], 1), shift_z(p_above[half:], -1)], axis=0)
-    rel = jnp.stack([block, partner, from_above, p_above, far, p_far, from_below, p_below])
-    toks = rel[:, :tok_rows]
-    lists = rel[:, tok_rows, : experts * capacity].astype(jnp.int32).reshape(blocks, experts, capacity)
 
     chip = zi * n_y + yi
     mine_e = chip * 2 + ki
     pair_e = chip * 2 + (1 - ki)
-    sel = jnp.stack(
-        [
-            lax.dynamic_index_in_dim(lists, mine_e, axis=1, keepdims=False),
-            lax.dynamic_index_in_dim(lists, pair_e, axis=1, keepdims=False),
-        ],
-        axis=1,
-    )
     token_iota = jnp.arange(tok_rows, dtype=jnp.int32)
-    one_hot = (sel[..., None] == token_iota).astype(jnp.bfloat16)
-    disp = jnp.einsum(
-        "bjct,btd->bjcd", one_hot, toks, preferred_element_type=jnp.float32
-    ).astype(jnp.bfloat16)
-    got = swap(disp[:, 1], "core")
 
-    pos = jnp.arange(blocks, dtype=jnp.int32)
-    inv = ((pos // n_y - zi) % RING) * n_y + (pos % n_y + yi) % n_y
-    out_a = expert_block(disp[:, 0], w_first, w_second)
-    a_abs = jnp.take(out_a, inv, axis=0)
+    def slots_of(pieces):
+        stacked = jnp.stack([arr for _, _, arr in pieces])
+        toks = stacked[:, :tok_rows]
+        lists = stacked[:, tok_rows, : experts * capacity].astype(jnp.int32)
+        lists = lists.reshape(len(pieces), experts, capacity)
+        sel = jnp.stack(
+            [
+                lax.dynamic_index_in_dim(lists, mine_e, axis=1, keepdims=False),
+                lax.dynamic_index_in_dim(lists, pair_e, axis=1, keepdims=False),
+            ],
+            axis=1,
+        )
+        one_hot = (sel[..., None] == token_iota).astype(jnp.bfloat16)
+        disp = jnp.einsum(
+            "bjct,btd->bjcd", one_hot, toks, preferred_element_type=jnp.float32
+        ).astype(jnp.bfloat16)
+        return disp[:, 0], swap(disp[:, 1], "core")
+
+    def place(into, pieces, outs):
+        for i, (r, q, _) in enumerate(pieces):
+            where = ((zi + r) % RING) * n_y + (yi + q) % n_y
+            into = lax.dynamic_update_slice(into, outs[i : i + 1], (where, 0, 0))
+        return into
+
+    early = [(0, 0, block), (0, 1, partner), (1, 0, from_above), (3, 0, from_below)]
+    late = [(2, 0, far), (2, 1, p_far), (1, 1, p_above), (3, 1, p_below)]
+    mine_1, got_1 = slots_of(early)
+    out_m1 = expert_block(mine_1, w_first, w_second)
+    out_g1 = expert_block(got_1, w_first, w_second)
+    late_arrs = [arr for _, _, arr in late]
+    *late_arrs, out_m1, out_g1 = lax.optimization_barrier((*late_arrs, out_m1, out_g1))
+    late = [(r, q, arr) for (r, q, _), arr in zip(late, late_arrs)]
+    mine_2, got_2 = slots_of(late)
+    out_m2 = expert_block(mine_2, w_first, w_second)
+    empty = jnp.zeros((blocks, capacity, features), jnp.bfloat16)
+    a_abs = place(place(empty, early, out_m1), late, out_m2)
     ret_a = lax.all_to_all(a_abs, ("z", "yh"), 0, 0, tiled=True)
-    a_abs, got = lax.optimization_barrier((a_abs, got))
-    out_b = expert_block(got, w_first, w_second)
-    ret_a, out_b = lax.optimization_barrier((ret_a, out_b))
-    back_b = swap(out_b, "core")
-    b_abs = jnp.take(back_b, inv, axis=0)
+    a_abs, got_2 = lax.optimization_barrier((a_abs, got_2))
+    out_g2 = expert_block(got_2, w_first, w_second)
+    b_abs = place(place(empty, early, swap(out_g1, "core")), late, swap(out_g2, "core"))
+    ret_a, b_abs = lax.optimization_barrier((ret_a, b_abs))
     ret_b = lax.all_to_all(b_abs, ("z", "yh"), 0, 0, tiled=True)
 
     matches = (

time: 212 us -> 206 us (0.972)
  local copies, waits for them, and re-layouts: 13 us -> 22.9 us
  waiting for transfers between devices: 109 us -> 100 us
  other arithmetic: 11.1 us -> 4.67 us
  starting transfers between devices: 28 us -> 23.1 us
  matrix products: 49.8 us -> 53.6 us
    dynamic_update_slice x0 -> x16, local copies, waits for them, and re-layouts: none -> 16.5 us  [place(): into = lax.dynamic_update_slice(into, outs[i:i + 1], (where, 0, 0))]
    ppermute x8, waiting for transfers between devices: 46.2 us -> 32.7 us  [shift_z(): return lax.ppermute(x, 'z', [(i, (i + step) % RING) for i in range(RING)])]
    ppermute x3 -> x5, waiting for transfers between devices: 6 us -> 14.7 us  [swap(): return lax.ppermute(x, axis, [(0, 1), (1, 0)])]
    gather x2 -> x0, local copies, waits for them, and re-layouts: 7 us -> none  [the longest x1 4.36 us: shards(): b_abs = jnp.take(back_b, inv, axis=0)]
    select_n x2 -> x0, other arithmetic: 6.07 us -> none  [the longest x1 3.98 us: shards(): b_abs = jnp.take(back_b, inv, axis=0)]
    all_to_all x1, waiting for transfers between devices: 18.7 us -> 14 us  [shards(): ret_a = lax.all_to_all(a_abs, ('z', 'yh'), 0, 0, tiled=True)]
    ppermute x8, starting transfers between devices: 15.1 us -> 10.6 us  [shift_z(): return lax.ppermute(x, 'z', [(i, (i + step) % RING) for i in range(RING)])]
    broadcast_in_dim x0 -> x2, local copies, waits for them, and re-layouts: none -> 4.06 us  [shards(): empty = jnp.zeros((blocks, capacity, features), jnp.bfloat16)]
  transfers between devices with their start and end apart: 13 -> 15, of which waited for: 6 -> 7; matrix products, arithmetic and copies ran while one was open for 23% -> 23% of each run, Pallas kernels for 0% -> 0%
where the time goes in v5:
time: 206 us; the launch traced here: 205 us
  waiting for transfers between devices  100 us (49%)
  matrix products  53.6 us (26%)
  starting transfers between devices  23.1 us (11%)
  local copies, waits for them, and re-layouts  22.9 us (11%)
  other arithmetic  4.67 us (2%)
    all_to_all x1, waiting for transfers between devices, shards(): ret_b = lax.all_to_all(b_abs, ('z', 'yh'), 0, 0, tiled=True)  38.9 us
    ppermute x8, waiting for transfers between devices, shift_z(): return lax.ppermute(x, 'z', [(i, (i + step) % RING) for i in range(RING)])  32.7 us
    dot_general x4, matrix products, expert_block(): projected = jnp.dot(flat, w_first, preferred_element_type=jnp.float32)  27.6 us
    dot_general x4, matrix products, expert_block(): jnp.dot(intermediate_activation, w_second, preferred_element_type=jnp.flo...  16.6 us
    dynamic_update_slice x16, local copies, waits for them, and re-layouts, place(): into = lax.dynamic_update_slice(into, outs[i:i + 1], (where, 0, 0))  16.5 us
    ppermute x5, waiting for transfers between devices, swap(): return lax.ppermute(x, axis, [(0, 1), (1, 0)])  14.7 us
    all_to_all x1, waiting for transfers between devices, shards(): ret_a = lax.all_to_all(a_abs, ('z', 'yh'), 0, 0, tiled=True)  14 us
    ppermute x8, starting transfers between devices, shift_z(): return lax.ppermute(x, 'z', [(i, (i + step) % RING) for i in range(RING)])  10.6 us
  transfers between devices with their start and end apart: 15, of which 7 were waited for; matrix products, arithmetic and copies ran while one was open for 23% of the time, Pallas kernels for 0%

profile of v5, /device:TPU:0, one launch (start us, length us, event | category | flops | bytes accessed | tf_op | source)
XLA Modules:
  0.0 204.8 jit_solution(9999494099853951142)
XLA Ops:
  0.0 0.6 compare_reduce_fusion
  0.6 1.3 convert_select_fusion
  2.0 0.1 reshape.86
  2.1 1.3 fusion.76
  3.4 3.4 %collective-permute-start.4 = (bf16[129,3072]{1,0:T(8,128)(2,1)S(1)}, bf16[129,3072]{1,0:T(8,128)(2,1)}, u32[]{:S(2)}, u32[]{:S(2)}) collective-permute-start(bf16[129,3072]{1,0:T(8,128)(2,1)S(1)} %get-tuple-element.40), channel_id=1, source_target_pairs={{0,2},{2,0},{1,3},{3,1},{4,6},{6,4},{5,7},{7,5},{8,10},{10,8},{9,1... | collective-permute-start | bytes 2377736 | tf_op jit(solution)/shard_map/ppermute | solution.py:31
  6.8 4.0 %collective-permute-start.2 = (bf16[129,3072]{1,0:T(8,128)(2,1)S(1)}, bf16[129,3072]{1,0:T(8,128)(2,1)S(1)}, u32[]{:S(2)}, u32[]{:S(2)}) collective-permute-start(bf16[129,3072]{1,0:T(8,128)(2,1)S(1)} %get-tuple-element.40), channel_id=1, source_target_pairs={{0,12},{4,0},{8,4},{12,8},{1,13},{5,1},{9,5},{13,9},{2,14},{6,2},{... | collective-permute-start | bytes 2377736 | tf_op jit(solution)/shard_map/ppermute | solution.py:27
  10.8 14.7 %collective-permute-done.4 = bf16[129,3072]{1,0:T(8,128)(2,1)} collective-permute-done((bf16[129,3072]{1,0:T(8,128)(2,1)S(1)}, bf16[129,3072]{1,0:T(8,128)(2,1)}, u32[]{:S(2)}, u32[]{:S(2)}) %collective-permute-start.4) | collective-permute-done | bytes 792608 | tf_op jit(solution)/shard_map/ppermute | solution.py:31
  25.5 2.9 %collective-permute-done.2 = bf16[129,3072]{1,0:T(8,128)(2,1)S(1)} collective-permute-done((bf16[129,3072]{1,0:T(8,128)(2,1)S(1)}, bf16[129,3072]{1,0:T(8,128)(2,1)S(1)}, u32[]{:S(2)}, u32[]{:S(2)}) %collective-permute-start.2) | collective-permute-done | bytes 792608 | tf_op jit(solution)/shard_map/ppermute | solution.py:27
  28.4 3.4 %collective-permute-done = bf16[129,3072]{1,0:T(8,128)(2,1)S(1)} collective-permute-done((bf16[129,3072]{1,0:T(8,128)(2,1)S(1)}, bf16[129,3072]{1,0:T(8,128)(2,1)S(1)}, u32[]{:S(2)}, u32[]{:S(2)}) %collective-permute-start) | collective-permute-done | bytes 792608 | tf_op jit(solution)/shard_map/ppermute | solution.py:27
  31.8 0.8 fusion.67
  32.6 0.1 reshape.92
  32.7 2.3 %convolution_convert_fusion.1 = bf16[4,2,64,3072]{3,2,1,0:T(8,128)(2,1)S(1)} fusion(bf16[1,129,3072]{2,1,0:T(8,128)(2,1)S(1)} %bitcast.105, bf16[1,129,3072]{2,1,0:T(8,128)(2,1)S(1)} %bitcast.101, bf16[1,129,3072]{2,1,0:T(8,128)(2,1)} %bitcast.5, bf16[1,129,3072]{2,1,0:T(8,128)(2,1)S(1)} %get-tuple-element.39, s32[4,2,64]{2,1,0:T(2,128)S(1)} %pad_add_fusion), kind=kOutput, calls=%fused_computation.17 | convolution fusion | flops 416874496 | bytes 6318080 | tf_op jit(solution)/shard_map/bjct,btd->bjcd/dot_general | solution.py:80
  35.0 0.2 slice_bitcast_fusion.1
  35.2 0.1 collective-permute-start.9
  35.3 0.3 collective-permute-start.3
  35.7 1.8 collective-permute-start.1
  37.5 1.5 collective-permute-start.7
  39.0 0.5 collective-permute-start.5
  39.6 5.7 %fusion.6 = f32[256,2560]{1,0:T(8,128)} fusion(bf16[256,3072]{1,0:T(8,128)(2,1)S(1)} %bitcast.112, bf16[1,3072,2560]{2,1,0:T(8,128)(2,1)S(1)} %copy-done.4), kind=kOutput, calls=%fused_computation.6 | convolution fusion | flops 4026531840 | bytes 19922944 | tf_op jit(solution)/shard_map/dot_general | solution.py:16
  45.3 20.6 %collective-permute-done.7 = bf16[129,3072]{1,0:T(8,128)(2,1)S(1)} collective-permute-done((bf16[129,3072]{1,0:T(8,128)(2,1)}, bf16[129,3072]{1,0:T(8,128)(2,1)S(1)}, u32[]{:S(2)}, u32[]{:S(2)}) %collective-permute-start.7) | collective-permute-done | bytes 792608 | tf_op jit(solution)/shard_map/ppermute | solution.py:27
  65.9 1.6 collective-permute-start.8
  67.5 0.8 collective-permute-start.6
  68.3 5.2 %fusion.16 = bf16[256,3072]{1,0:T(8,128)(2,1)} fusion(bf16[1,1280,3072]{2,1,0:T(8,128)(2,1)S(1)} %bitcast.119, f32[256,2560]{1,0:T(8,128)} %fusion.6), kind=kOutput, calls=%fused_computation.18 | convolution fusion | flops 2016018432 | bytes 12058624 | tf_op jit(solution)/shard_map/dot_general | solution.py:20
  73.6 0.1 pad_maximum_fusion.10
  73.6 5.8 %collective-permute-done.6 = bf16[64,3072]{1,0:T(8,128)(2,1)S(1)} collective-permute-done((bf16[64,3072]{1,0:T(8,128)(2,1)S(1)}, bf16[64,3072]{1,0:T(8,128)(2,1)S(1)}, u32[]{:S(2)}, u32[]{:S(2)}) %collective-permute-start.6) | collective-permute-done | bytes 393248 | tf_op jit(solution)/shard_map/ppermute | solution.py:27
  79.5 5.6 %fusion.4 = f32[256,2560]{1,0:T(8,128)S(1)} fusion(bf16[256,3072]{1,0:T(8,128)(2,1)} %bitcast.15, bf16[1,3072,2560]{2,1,0:T(8,128)(2,1)S(1)} %copy-done.4), kind=kOutput, calls=%fused_computation.4 | convolution fusion | flops 4026531840 | bytes 19922944 | tf_op jit(solution)/shard_map/dot_general | solution.py:16
  85.1 3.5 %fusion.19 = bf16[256,3072]{1,0:T(8,128)(2,1)} fusion(bf16[1,1280,3072]{2,1,0:T(8,128)(2,1)S(1)} %bitcast.119, f32[256,2560]{1,0:T(8,128)S(1)} %fusion.4), kind=kOutput, calls=%fused_computation.19 | convolution fusion | flops 2016018432 | bytes 12058624 | tf_op jit(solution)/shard_map/dot_general | solution.py:20
  88.7 0.1 reshape.93
  88.8 2.8 %convolution_convert_fusion = bf16[4,2,64,3072]{3,2,1,0:T(8,128)(2,1)S(1)} fusion(bf16[1,129,3072]{2,1,0:T(8,128)(2,1)S(1)} %bitcast.107, bf16[1,129,3072]{2,1,0:T(8,128)(2,1)S(1)} %bitcast.103, bf16[1,129,3072]{2,1,0:T(8,128)(2,1)S(1)} %bitcast.99, bf16[1,129,3072]{2,1,0:T(8,128)(2,1)S(1)} %bitcast.97, s32[4,2,64]{2,1,0:T(2,128)S(1)} %pad_add_fusion.1), kind=kOutput, calls=%fused_computation.16 | convolution fusion | flops 416874496 | bytes 6318080 | tf_op jit(solution)/shard_map/bjct,btd->bjcd/dot_general | solution.py:80
  91.7 1.4 slice_bitcast_fusion
  93.1 8.2 %fusion.2 = f32[256,2560]{1,0:T(8,128)S(1)} fusion(bf16[256,3072]{1,0:T(8,128)(2,1)S(1)} %bitcast.113, bf16[1,3072,2560]{2,1,0:T(8,128)(2,1)} %param.12), kind=kOutput, calls=%fused_computation.2 | convolution fusion | flops 4026531840 | bytes 19922944 | tf_op jit(solution)/shard_map/dot_general | solution.py:16
  101.3 2.3 %fusion.22 = bf16[256,3072]{1,0:T(8,128)(2,1)S(1)} fusion(bf16[1,1280,3072]{2,1,0:T(8,128)(2,1)S(1)} %bitcast.121, f32[256,2560]{1,0:T(8,128)S(1)} %fusion.2), kind=kOutput, calls=%fused_computation.20 | convolution fusion | flops 2016018432 | bytes 12058624 | tf_op jit(solution)/shard_map/dot_general | solution.py:20
  103.6 0.1 collective-permute-start.11
  103.7 0.5 collective-permute-start.10
  104.2 2.0 broadcast_in_dim.41.clone
  106.2 0.8 slice_dynamic-update-slice_fusion.11
  107.0 0.8 slice_dynamic-update-slice_fusion.10
  107.8 0.8 slice_dynamic-update-slice_fusion.9
  108.6 0.8 slice_dynamic-update-slice_fusion.8
  109.4 0.8 fusion.53
  110.2 0.8 fusion.52
  110.9 0.8 fusion.51
  111.7 0.8 fusion.50
  112.5 3.6 %all-to-all-start = ((bf16[8,64,3072]{2,1,0:T(8,128)(2,1)}), bf16[8,64,3072]{2,1,0:T(8,128)(2,1)S(1)}, u32[]{:S(2)}, u32[]{:S(2)}) async-start(bf16[8,64,3072]{2,1,0:T(8,128)(2,1)} %fusion.50), calls=%async_computation | async-start | bytes 6291456 | tf_op jit(solution)/shard_map/all_to_all | solution.py:103
  116.2 8.2 %fusion = f32[256,2560]{1,0:T(8,128)S(1)} fusion(bf16[256,3072]{1,0:T(8,128)(2,1)} %bitcast.29, bf16[1,3072,2560]{2,1,0:T(8,128)(2,1)} %param.12), kind=kOutput, calls=%fused_computation | convolution fusion | flops 4026531840 | bytes 19922944 | tf_op jit(solution)/shard_map/dot_general | solution.py:16
  124.3 5.6 %fusion.25 = bf16[256,3072]{1,0:T(8,128)(2,1)S(1)} fusion(bf16[1,1280,3072]{2,1,0:T(8,128)(2,1)} %param.13, f32[256,2560]{1,0:T(8,128)S(1)} %fusion), kind=kOutput, calls=%fused_computation.21 | convolution fusion | flops 2016018432 | bytes 12058624 | tf_op jit(solution)/shard_map/dot_general | solution.py:20
  129.9 0.4 collective-permute-start.12
  130.3 2.1 %broadcast_in_dim.41.clone.1 = bf16[8,64,3072]{2,1,0:T(8,128)(2,1)} broadcast(bf16[]{:T(256)} %constant.158.clone.1), dimensions={} | broadcast | bytes 3145730 | tf_op jit(solution)/shard_map/broadcast_in_dim | solution.py:101
  132.3 1.8 slice_dynamic-update-slice_fusion.7
  134.1 1.8 slice_dynamic-update-slice_fusion.6
  135.9 1.8 slice_dynamic-update-slice_fusion.5
  137.6 1.8 slice_dynamic-update-slice_fusion.4
  139.4 0.8 slice_dynamic-update-slice_fusion.3
  140.2 0.8 slice_dynamic-update-slice_fusion.2
  141.0 0.8 slice_dynamic-update-slice_fusion.1
  141.8 0.8 slice_dynamic-update-slice_fusion
  142.6 14.0 %all-to-all-done = bf16[8,64,3072]{2,1,0:T(8,128)(2,1)S(1)} async-done(((bf16[8,64,3072]{2,1,0:T(8,128)(2,1)}), bf16[8,64,3072]{2,1,0:T(8,128)(2,1)S(1)}, u32[]{:S(2)}, u32[]{:S(2)}) %all-to-all-start) | async-done | bytes 3145760 | tf_op jit(solution)/shard_map/all_to_all | solution.py:103
  156.6 4.4 %all-to-all-start.1 = ((bf16[8,64,3072]{2,1,0:T(8,128)(2,1)}), bf16[8,64,3072]{2,1,0:T(8,128)(2,1)}, u32[]{:S(2)}, u32[]{:S(2)}) async-start(bf16[8,64,3072]{2,1,0:T(8,128)(2,1)} %slice_dynamic-update-slice_fusion), calls=%async_computation.1 | async-start | bytes 6291456 | tf_op jit(solution)/shard_map/all_to_all | solution.py:108
  161.0 0.1 copy.18
  161.1 0.1 copy.9
  161.3 0.4 select_reduce_fusion
  161.8 38.9 %all-to-all-done.1 = bf16[8,64,3072]{2,1,0:T(8,128)(2,1)} async-done(((bf16[8,64,3072]{2,1,0:T(8,128)(2,1)}), bf16[8,64,3072]{2,1,0:T(8,128)(2,1)}, u32[]{:S(2)}, u32[]{:S(2)}) %all-to-all-start.1) | async-done | bytes 3145760 | tf_op jit(solution)/shard_map/all_to_all | solution.py:108
  200.7 2.6 %convolution_bitcast_fusion = f32[128,3072]{1,0:T(8,128)S(1)} fusion(bf16[8,64,3072]{2,1,0:T(8,128)(2,1)} %all-to-all-done.1, s32[8,64]{1,0:T(8,128)S(1)} %bitcast.116, bf16[8,128]{1,0:T(8,128)(2,1)S(1)} %get-tuple-element.49), kind=kOutput, calls=%fused_computation.22 | convolution fusion | flops 402784256 | bytes 4722688 | tf_op jit(solution)/shard_map/dot_general | solution.py:125
  203.2 1.6 fusion.29
  (43 shorter events, 0.5 us)
Async XLA Ops:
  3.4 22.1 %collective-permute-start.4 = (bf16[129,3072]{1,0:T(8,128)(2,1)S(1)}, bf16[129,3072]{1,0:T(8,128)(2,1)}, u32[]{:S(2)}, u32[]{:S(2)}) collective-permute-start(bf16[129,3072]{1,0:T(8,128)(2,1)S(1)} %get-tuple-element.40), channel_id=1, source_target_pairs={{0,2},{2,0},{1,3},{3,1},{4,6},{6,4},{5,7},{7,5},{8,10},{10,8},{9,1... | collective-permute-start | bytes 2377736 | tf_op jit(solution)/shard_map/ppermute | solution.py:31
  6.8 21.6 %collective-permute-start.2 = (bf16[129,3072]{1,0:T(8,128)(2,1)S(1)}, bf16[129,3072]{1,0:T(8,128)(2,1)S(1)}, u32[]{:S(2)}, u32[]{:S(2)}) collective-permute-start(bf16[129,3072]{1,0:T(8,128)(2,1)S(1)} %get-tuple-element.40), channel_id=1, source_target_pairs={{0,12},{4,0},{8,4},{12,8},{1,13},{5,1},{9,5},{13,9},{2,14},{6,2},{... | collective-permute-start | bytes 2377736 | tf_op jit(solution)/shard_map/ppermute | solution.py:27
  10.8 21.0 %collective-permute-start = (bf16[129,3072]{1,0:T(8,128)(2,1)S(1)}, bf16[129,3072]{1,0:T(8,128)(2,1)S(1)}, u32[]{:S(2)}, u32[]{:S(2)}) collective-permute-start(bf16[129,3072]{1,0:T(8,128)(2,1)S(1)} %get-tuple-element.40), channel_id=1, source_target_pairs={{0,4},{4,8},{8,12},{12,0},{1,5},{5,9},{9,13},{13,1},{2,6},{6,10},{... | collective-permute-start | bytes 2377736 | tf_op jit(solution)/shard_map/ppermute | solution.py:27
  32.7 6.9 %copy-start.4 = (bf16[1,3072,2560]{2,1,0:T(8,128)(2,1)S(1)}, bf16[1,3072,2560]{2,1,0:T(8,128)(2,1)}, u32[]{:S(2)}) copy-start(bf16[1,3072,2560]{2,1,0:T(8,128)(2,1)} %param.12) | copy-start | bytes 47185924
  35.2 44.3 %collective-permute-start.9 = (bf16[4,64,3072]{2,1,0:T(8,128)(2,1)S(1)}, bf16[4,64,3072]{2,1,0:T(8,128)(2,1)}, u32[]{:S(2)}, u32[]{:S(2)}) collective-permute-start(bf16[4,64,3072]{2,1,0:T(8,128)(2,1)S(1)} %get-tuple-element.37), channel_id=1, source_target_pairs={{0,1},{1,0},{2,3},{3,2},{4,5},{5,4},{6,7},{7,6},{8,9},{9,8},{10,11... | collective-permute-start | bytes 4718600 | tf_op jit(solution)/shard_map/ppermute | solution.py:31
  35.3 38.2 %collective-permute-start.3 = (bf16[65,3072]{1,0:T(8,128)(2,1)S(1)}, bf16[65,3072]{1,0:T(8,128)(2,1)S(1)}, u32[]{:S(2)}, u32[]{:S(2)}) collective-permute-start(bf16[65,3072]{1,0:T(8,128)(2,1)S(1)} %slice.177), channel_id=1, source_target_pairs={{0,12},{4,0},{8,4},{12,8},{1,13},{5,1},{9,5},{13,9},{2,14},{6,2},{... | collective-permute-start | bytes 1198088 | tf_op jit(solution)/shard_map/ppermute | solution.py:27
  35.7 32.6 %slice-start = ((s8[7864320]{0:T(1024)(128)(4,1)}), s8[4194304]{0:T(1024)(128)(4,1)S(1)}, s32[]{:S(2)}) async-start(s8[7864320]{0:T(1024)(128)(4,1)} %bitcast.118), calls=%async_computation.2 | async-start | bytes 8388608
  35.7 37.8 %collective-permute-start.1 = (bf16[64,3072]{1,0:T(8,128)(2,1)S(1)}, bf16[64,3072]{1,0:T(8,128)(2,1)S(1)}, u32[]{:S(2)}, u32[]{:S(2)}) collective-permute-start(bf16[64,3072]{1,0:T(8,128)(2,1)S(1)} %slice.176), channel_id=1, source_target_pairs={{0,4},{4,8},{8,12},{12,0},{1,5},{5,9},{9,13},{13,1},{2,6},{6,10},{... | collective-permute-start | bytes 1179656 | tf_op jit(solution)/shard_map/ppermute | solution.py:27
  37.5 28.3 %collective-permute-start.7 = (bf16[129,3072]{1,0:T(8,128)(2,1)}, bf16[129,3072]{1,0:T(8,128)(2,1)S(1)}, u32[]{:S(2)}, u32[]{:S(2)}) collective-permute-start(bf16[129,3072]{1,0:T(8,128)(2,1)} %collective-permute-done.4), channel_id=1, source_target_pairs={{0,12},{4,0},{8,4},{12,8},{1,13},{5,1},{9,5},{13,9},{2,14},{6,2},{... | collective-permute-start | bytes 2377736 | tf_op jit(solution)/shard_map/ppermute | solution.py:27
  39.0 28.5 %collective-permute-start.5 = (bf16[129,3072]{1,0:T(8,128)(2,1)}, bf16[129,3072]{1,0:T(8,128)(2,1)S(1)}, u32[]{:S(2)}, u32[]{:S(2)}) collective-permute-start(bf16[129,3072]{1,0:T(8,128)(2,1)} %collective-permute-done.4), channel_id=1, source_target_pairs={{0,4},{4,8},{8,12},{12,0},{1,5},{5,9},{9,13},{13,1},{2,6},{6,10},{... | collective-permute-start | bytes 2377736 | tf_op jit(solution)/shard_map/ppermute | solution.py:27
  39.6 28.7 %slice-start.1 = ((s8[7864320]{0:T(1024)(128)(4,1)}), s8[3670016]{0:T(1024)(128)(4,1)S(1)}, s32[]{:S(2)}) async-start(s8[7864320]{0:T(1024)(128)(4,1)} %bitcast.118), calls=%async_computation.3 | async-start | bytes 7340032
  65.9 13.5 %collective-permute-start.8 = (bf16[65,3072]{1,0:T(8,128)(2,1)S(1)}, bf16[65,3072]{1,0:T(8,128)(2,1)S(1)}, u32[]{:S(2)}, u32[]{:S(2)}) collective-permute-start(bf16[65,3072]{1,0:T(8,128)(2,1)S(1)} %slice.179), channel_id=1, source_target_pairs={{0,12},{4,0},{8,4},{12,8},{1,13},{5,1},{9,5},{13,9},{2,14},{6,2},{... | collective-permute-start | bytes 1198088 | tf_op jit(solution)/shard_map/ppermute | solution.py:27
  67.5 11.9 %collective-permute-start.6 = (bf16[64,3072]{1,0:T(8,128)(2,1)S(1)}, bf16[64,3072]{1,0:T(8,128)(2,1)S(1)}, u32[]{:S(2)}, u32[]{:S(2)}) collective-permute-start(bf16[64,3072]{1,0:T(8,128)(2,1)S(1)} %slice.178), channel_id=1, source_target_pairs={{0,4},{4,8},{8,12},{12,0},{1,5},{5,9},{9,13},{13,1},{2,6},{6,10},{... | collective-permute-start | bytes 1179656 | tf_op jit(solution)/shard_map/ppermute | solution.py:27
  91.7 9.6 %slice-start.2 = ((s8[7864320]{0:T(1024)(128)(4,1)}), s8[4194304]{0:T(1024)(128)(4,1)S(1)}, s32[]{:S(2)}) async-start(s8[7864320]{0:T(1024)(128)(4,1)} %bitcast.120), calls=%async_computation.4 | async-start | bytes 8388608
  93.1 8.2 %slice-start.3 = ((s8[7864320]{0:T(1024)(128)(4,1)}), s8[3670016]{0:T(1024)(128)(4,1)S(1)}, s32[]{:S(2)}) async-start(s8[7864320]{0:T(1024)(128)(4,1)} %bitcast.120), calls=%async_computation.5 | async-start | bytes 7340032
  103.6 2.6 %copy-start = (bf16[256,3072]{1,0:T(8,128)(2,1)S(1)}, bf16[256,3072]{1,0:T(8,128)(2,1)}, u32[]{:S(2)}) copy-start(bf16[256,3072]{1,0:T(8,128)(2,1)} %fusion.16) | copy-start | bytes 4718596
  103.6 12.5 %collective-permute-start.11 = (bf16[4,64,3072]{2,1,0:T(8,128)(2,1)}, bf16[4,64,3072]{2,1,0:T(8,128)(2,1)}, u32[]{:S(2)}, u32[]{:S(2)}) collective-permute-start(bf16[4,64,3072]{2,1,0:T(8,128)(2,1)} %get-tuple-element.35), channel_id=1, source_target_pairs={{0,1},{1,0},{2,3},{3,2},{4,5},{5,4},{6,7},{7,6},{8,9},{9,8},{10,11... | collective-permute-start | bytes 4718600 | tf_op jit(solution)/shard_map/ppermute | solution.py:31
  103.7 26.5 %collective-permute-start.10 = (bf16[4,64,3072]{2,1,0:T(8,128)(2,1)}, bf16[4,64,3072]{2,1,0:T(8,128)(2,1)}, u32[]{:S(2)}, u32[]{:S(2)}) collective-permute-start(bf16[4,64,3072]{2,1,0:T(8,128)(2,1)} %bitcast.16), channel_id=1, source_target_pairs={{0,1},{1,0},{2,3},{3,2},{4,5},{5,4},{6,7},{7,6},{8,9},{9,8},{10,11... | collective-permute-start | bytes 4718600 | tf_op jit(solution)/shard_map/ppermute | solution.py:31
  112.5 44.1 %all-to-all-start = ((bf16[8,64,3072]{2,1,0:T(8,128)(2,1)}), bf16[8,64,3072]{2,1,0:T(8,128)(2,1)S(1)}, u32[]{:S(2)}, u32[]{:S(2)}) async-start(bf16[8,64,3072]{2,1,0:T(8,128)(2,1)} %fusion.50), calls=%async_computation | async-start | bytes 6291456 | tf_op jit(solution)/shard_map/all_to_all | solution.py:103
  129.9 9.5 %collective-permute-start.12 = (bf16[4,64,3072]{2,1,0:T(8,128)(2,1)S(1)}, bf16[4,64,3072]{2,1,0:T(8,128)(2,1)S(1)}, u32[]{:S(2)}, u32[]{:S(2)}) collective-permute-start(bf16[4,64,3072]{2,1,0:T(8,128)(2,1)S(1)} %bitcast.122), channel_id=1, source_target_pairs={{0,1},{1,0},{2,3},{3,2},{4,5},{5,4},{6,7},{7,6},{8,9},{9,8},{10,11... | collective-permute-start | bytes 4718600 | tf_op jit(solution)/shard_map/ppermute | solution.py:31
  142.6 18.4 %copy-start.2 = (f32[128,4]{0,1:T(4,128)S(1)}, f32[128,4]{0,1:T(4,128)}, u32[]{:S(2)}) copy-start(f32[128,4]{0,1:T(4,128)} %param.10) | copy-start | bytes 6148
  142.6 18.6 %copy-start.3 = (s32[128,4]{0,1:T(4,128)S(1)}, s32[128,4]{0,1:T(4,128)}, u32[]{:S(2)}) copy-start(s32[128,4]{0,1:T(4,128)} %param.9) | copy-start | bytes 6148
  142.6 19.2 %copy-start.1 = (s32[1,16,64]{2,1,0:T(8,128)S(1)}, s32[1,16,64]{2,1,0:T(8,128)}, u32[]{:S(2)}) copy-start(s32[1,16,64]{2,1,0:T(8,128)} %param.11) | copy-start | bytes 12292
  156.6 44.1 %all-to-all-start.1 = ((bf16[8,64,3072]{2,1,0:T(8,128)(2,1)}), bf16[8,64,3072]{2,1,0:T(8,128)(2,1)}, u32[]{:S(2)}, u32[]{:S(2)}) async-start(bf16[8,64,3072]{2,1,0:T(8,128)(2,1)} %slice_dynamic-update-slice_fusion), calls=%async_computation.1 | async-start | bytes 6291456 | tf_op jit(solution)/shard_map/all_to_all | solution.py:108

commit v6 on v5

--- a/solution.py
+++ b/solution.py
@@ -93,13 +93,14 @@
     mine_1, got_1 = slots_of(early)
     out_m1 = expert_block(mine_1, w_first, w_second)
     out_g1 = expert_block(got_1, w_first, w_second)
+    empty = jnp.zeros((blocks, capacity, features), jnp.bfloat16)
+    a_part = place(empty, early, out_m1)
     late_arrs = [arr for _, _, arr in late]
-    *late_arrs, out_m1, out_g1 = lax.optimization_barrier((*late_arrs, out_m1, out_g1))
+    *late_arrs, a_part = lax.optimization_barrier((*late_arrs, a_part))
     late = [(r, q, arr) for (r, q, _), arr in zip(late, late_arrs)]
     mine_2, got_2 = slots_of(late)
     out_m2 = expert_block(mine_2, w_first, w_second)
-    empty = jnp.zeros((blocks, capacity, features), jnp.bfloat16)
-    a_abs = place(place(empty, early, out_m1), late, out_m2)
+    a_abs = place(a_part, late, out_m2)
     ret_a = lax.all_to_all(a_abs, ("z", "yh"), 0, 0, tiled=True)
     a_abs, got_2 = lax.optimization_barrier((a_abs, got_2))
     out_g2 = expert_block(got_2, w_first, w_second)
@@ -113,8 +114,8 @@
     gate_of = jnp.einsum("tk,tke->et", gate_weights, matches).astype(jnp.bfloat16)
     rows3 = own_rows.reshape(blocks, 2, capacity)
     gate3 = gate_of.reshape(blocks, 2, tok_rows)
-    summed = None
-    for which, returned in ((ki, ret_a), (1 - ki, ret_b)):
+
+    def contribution(which, returned):
         rows = lax.dynamic_index_in_dim(rows3, which, axis=1, keepdims=False)
         gates = lax.dynamic_index_in_dim(gate3, which, axis=1, keepdims=False)
         mixing = jnp.where(
@@ -122,12 +123,15 @@
             gates[:, None, :],
             jnp.zeros((), jnp.bfloat16),
         )
-        contrib = jnp.dot(
+        return jnp.dot(
             mixing.reshape(-1, tok_rows).T,
             returned.reshape(-1, features),
             preferred_element_type=jnp.float32,
         )
-        summed = contrib if summed is None else summed + contrib
+
+    first = contribution(ki, ret_a)
+    ret_b, first = lax.optimization_barrier((ret_b, first))
+    summed = first + contribution(1 - ki, ret_b)
     return summed.astype(jnp.bfloat16)
 
 

time: 206 us -> 195 us (0.947)
  waiting for transfers between devices: 100 us -> 92.1 us
  local copies, waits for them, and re-layouts: 22.9 us -> 20.5 us
    all_to_all x1, waiting for transfers between devices: 14 us -> 5.79 us  [shards(): ret_a = lax.all_to_all(a_abs, ('z', 'yh'), 0, 0, tiled=True)]
    dynamic_update_slice x16, local copies, waits for them, and re-layouts: 16.5 us -> 12.4 us  [place(): into = lax.dynamic_update_slice(into, outs[i:i + 1], (where, 0, 0))]
    dot_general x4, matrix products: 16.6 us -> 14.5 us  [expert_block(): jnp.dot(intermediate_activation, w_second, preferred_element_type=jnp.flo...]
  transfers between devices with their start and end apart: 15 -> 15, of which waited for: 7 -> 7; matrix products, arithmetic and copies ran while one was open for 23% -> 34% of each run, Pallas kernels for 0% -> 0%
where the time goes in v6:
time: 195 us
  waiting for transfers between devices  92.1 us (47%)
  matrix products  53.4 us (27%)
  starting transfers between devices  23.7 us (12%)
  local copies, waits for them, and re-layouts  20.5 us (11%)
  other arithmetic  4.67 us (2%)
    all_to_all x1, waiting for transfers between devices, shards(): ret_b = lax.all_to_all(b_abs, ('z', 'yh'), 0, 0, tiled=True)  37.2 us
    ppermute x8, waiting for transfers between devices, shift_z(): return lax.ppermute(x, 'z', [(i, (i + step) % RING) for i in range(RING)])  34.4 us
    dot_general x4, matrix products, expert_block(): projected = jnp.dot(flat, w_first, preferred_element_type=jnp.float32)  27.9 us
    ppermute x5, waiting for transfers between devices, swap(): return lax.ppermute(x, axis, [(0, 1), (1, 0)])  14.7 us
    dot_general x4, matrix products, expert_block(): jnp.dot(intermediate_activation, w_second, preferred_element_type=jnp.flo...  14.5 us
    dynamic_update_slice x16, local copies, waits for them, and re-layouts, place(): into = lax.dynamic_update_slice(into, outs[i:i + 1], (where, 0, 0))  12.4 us
    ppermute x8, starting transfers between devices, shift_z(): return lax.ppermute(x, 'z', [(i, (i + step) % RING) for i in range(RING)])  11.3 us
    dot_general x2, matrix products, contribution(): jnp.dot(mixing.reshape(-1, tok_rows).T, returned.reshape(-1, features), p...  5.79 us
  transfers between devices with their start and end apart: 15, of which 7 were waited for; matrix products, arithmetic and copies ran while one was open for 34% of the time, Pallas kernels for 0%

profile of v6, /device:TPU:0, one launch (start us, length us, event | category | flops | bytes accessed | tf_op | source)
XLA Modules:
  0.0 194.7 jit_solution(5759049166181990929)
XLA Ops:
  0.0 0.6 compare_reduce_fusion
  0.6 1.3 convert_select_fusion
  2.0 0.1 reshape.87
  2.1 1.3 fusion.80
  3.4 3.4 %collective-permute-start.4 = (bf16[129,3072]{1,0:T(8,128)(2,1)S(1)}, bf16[129,3072]{1,0:T(8,128)(2,1)}, u32[]{:S(2)}, u32[]{:S(2)}) collective-permute-start(bf16[129,3072]{1,0:T(8,128)(2,1)S(1)} %get-tuple-element.42), channel_id=1, source_target_pairs={{0,2},{2,0},{1,3},{3,1},{4,6},{6,4},{5,7},{7,5},{8,10},{10,8},{9,1... | collective-permute-start | bytes 2377736 | tf_op jit(solution)/shard_map/ppermute | solution.py:31
  6.8 4.0 %collective-permute-start.2 = (bf16[129,3072]{1,0:T(8,128)(2,1)S(1)}, bf16[129,3072]{1,0:T(8,128)(2,1)S(1)}, u32[]{:S(2)}, u32[]{:S(2)}) collective-permute-start(bf16[129,3072]{1,0:T(8,128)(2,1)S(1)} %get-tuple-element.42), channel_id=1, source_target_pairs={{0,12},{4,0},{8,4},{12,8},{1,13},{5,1},{9,5},{13,9},{2,14},{6,2},{... | collective-permute-start | bytes 2377736 | tf_op jit(solution)/shard_map/ppermute | solution.py:27
  10.8 14.7 %collective-permute-done.4 = bf16[129,3072]{1,0:T(8,128)(2,1)} collective-permute-done((bf16[129,3072]{1,0:T(8,128)(2,1)S(1)}, bf16[129,3072]{1,0:T(8,128)(2,1)}, u32[]{:S(2)}, u32[]{:S(2)}) %collective-permute-start.4) | collective-permute-done | bytes 792608 | tf_op jit(solution)/shard_map/ppermute | solution.py:31
  25.5 2.9 %collective-permute-done.2 = bf16[129,3072]{1,0:T(8,128)(2,1)S(1)} collective-permute-done((bf16[129,3072]{1,0:T(8,128)(2,1)S(1)}, bf16[129,3072]{1,0:T(8,128)(2,1)S(1)}, u32[]{:S(2)}, u32[]{:S(2)}) %collective-permute-start.2) | collective-permute-done | bytes 792608 | tf_op jit(solution)/shard_map/ppermute | solution.py:27
  28.4 3.4 %collective-permute-done = bf16[129,3072]{1,0:T(8,128)(2,1)S(1)} collective-permute-done((bf16[129,3072]{1,0:T(8,128)(2,1)S(1)}, bf16[129,3072]{1,0:T(8,128)(2,1)S(1)}, u32[]{:S(2)}, u32[]{:S(2)}) %collective-permute-start) | collective-permute-done | bytes 792608 | tf_op jit(solution)/shard_map/ppermute | solution.py:27
  31.8 0.8 fusion.71
  32.6 0.1 reshape.93
  32.7 2.3 %convolution_convert_fusion.1 = bf16[4,2,64,3072]{3,2,1,0:T(8,128)(2,1)S(1)} fusion(bf16[1,129,3072]{2,1,0:T(8,128)(2,1)S(1)} %bitcast.120, bf16[1,129,3072]{2,1,0:T(8,128)(2,1)S(1)} %bitcast.116, bf16[1,129,3072]{2,1,0:T(8,128)(2,1)} %bitcast.1, bf16[1,129,3072]{2,1,0:T(8,128)(2,1)S(1)} %get-tuple-element.41, s32[4,2,64]{2,1,0:T(2,128)S(1)} %pad_add_fusion), kind=kOutput, calls=%fused_computation.17 | convolution fusion | flops 416874496 | bytes 6318080 | tf_op jit(solution)/shard_map/bjct,btd->bjcd/dot_general | solution.py:80
  35.0 1.4 slice_bitcast_fusion.1
  36.4 0.3 collective-permute-start.3
  36.8 1.8 collective-permute-start.1
  38.6 0.4 copy-done.3
  39.0 4.2 %fusion.6 = f32[256,2560]{1,0:T(8,128)S(1)} fusion(bf16[256,3072]{1,0:T(8,128)(2,1)S(1)} %bitcast.123, bf16[1,3072,2560]{2,1,0:T(8,128)(2,1)S(1)} %copy-done.3), kind=kOutput, calls=%fused_computation.6 | convolution fusion | flops 4026531840 | bytes 19922944 | tf_op jit(solution)/shard_map/dot_general | solution.py:16
  43.2 2.3 %fusion.16 = bf16[256,3072]{1,0:T(8,128)(2,1)S(1)} fusion(bf16[1,1280,3072]{2,1,0:T(8,128)(2,1)S(1)} %bitcast.132, f32[256,2560]{1,0:T(8,128)S(1)} %fusion.6), kind=kOutput, calls=%fused_computation.18 | convolution fusion | flops 2016018432 | bytes 12058624 | tf_op jit(solution)/shard_map/dot_general | solution.py:20
  45.5 2.0 %broadcast_in_dim.38.clone = bf16[8,64,3072]{2,1,0:T(8,128)(2,1)} broadcast(bf16[]{:T(256)} %constant.158.clone.1), dimensions={} | broadcast | bytes 3145730 | tf_op jit(solution)/shard_map/broadcast_in_dim | solution.py:96
  47.6 0.8 fusion.57
  48.3 1.1 collective-permute-start.7
  49.5 0.9 collective-permute-start.5
  50.4 0.8 fusion.56
  51.1 0.8 fusion.55
  51.9 17.3 %collective-permute-done.7 = bf16[129,3072]{1,0:T(8,128)(2,1)S(1)} collective-permute-done((bf16[129,3072]{1,0:T(8,128)(2,1)}, bf16[129,3072]{1,0:T(8,128)(2,1)S(1)}, u32[]{:S(2)}, u32[]{:S(2)}) %collective-permute-start.7) | collective-permute-done | bytes 792608 | tf_op jit(solution)/shard_map/ppermute | solution.py:27
  69.2 2.8 %collective-permute-start.8 = (bf16[65,3072]{1,0:T(8,128)(2,1)S(1)}, bf16[65,3072]{1,0:T(8,128)(2,1)S(1)}, u32[]{:S(2)}, u32[]{:S(2)}) collective-permute-start(bf16[65,3072]{1,0:T(8,128)(2,1)S(1)} %slice.195), channel_id=1, source_target_pairs={{0,12},{4,0},{8,4},{12,8},{1,13},{5,1},{9,5},{13,9},{2,14},{6,2},{... | collective-permute-start | bytes 1198088 | tf_op jit(solution)/shard_map/ppermute | solution.py:27
  72.0 0.3 collective-permute-start.6
  72.3 0.8 fusion.54
  73.1 0.1 pad_maximum_fusion.10
  73.2 10.8 %collective-permute-done.6 = bf16[64,3072]{1,0:T(8,128)(2,1)S(1)} collective-permute-done((bf16[64,3072]{1,0:T(8,128)(2,1)S(1)}, bf16[64,3072]{1,0:T(8,128)(2,1)S(1)}, u32[]{:S(2)}, u32[]{:S(2)}) %collective-permute-start.6) | collective-permute-done | bytes 393248 | tf_op jit(solution)/shard_map/ppermute | solution.py:27
  84.1 0.1 reshape.94
  84.2 2.8 %convolution_convert_fusion = bf16[4,2,64,3072]{3,2,1,0:T(8,128)(2,1)S(1)} fusion(bf16[1,129,3072]{2,1,0:T(8,128)(2,1)S(1)} %bitcast.122, bf16[1,129,3072]{2,1,0:T(8,128)(2,1)S(1)} %bitcast.118, bf16[1,129,3072]{2,1,0:T(8,128)(2,1)S(1)} %bitcast.114, bf16[1,129,3072]{2,1,0:T(8,128)(2,1)S(1)} %bitcast.112, s32[4,2,64]{2,1,0:T(2,128)S(1)} %pad_add_fusion.1), kind=kOutput, calls=%fused_computation.16 | convolution fusion | flops 416874496 | bytes 6318080 | tf_op jit(solution)/shard_map/bjct,btd->bjcd/dot_general | solution.py:80
  87.1 1.4 slice_bitcast_fusion
  88.5 8.1 %fusion.4 = f32[256,2560]{1,0:T(8,128)S(1)} fusion(bf16[256,3072]{1,0:T(8,128)(2,1)S(1)} %bitcast.124, bf16[1,3072,2560]{2,1,0:T(8,128)(2,1)} %param.12), kind=kOutput, calls=%fused_computation.4 | convolution fusion | flops 4026531840 | bytes 19922944 | tf_op jit(solution)/shard_map/dot_general | solution.py:16
  96.7 2.3 %fusion.19 = bf16[256,3072]{1,0:T(8,128)(2,1)S(1)} fusion(bf16[1,1280,3072]{2,1,0:T(8,128)(2,1)S(1)} %bitcast.134, f32[256,2560]{1,0:T(8,128)S(1)} %fusion.4), kind=kOutput, calls=%fused_computation.19 | convolution fusion | flops 2016018432 | bytes 12058624 | tf_op jit(solution)/shard_map/dot_general | solution.py:20
  99.0 0.1 collective-permute-start.11
  99.1 0.8 fusion.53
  99.9 0.8 fusion.52
  100.7 0.8 fusion.51
  101.4 0.8 fusion.50
  102.2 3.6 %all-to-all-start = ((bf16[8,64,3072]{2,1,0:T(8,128)(2,1)}), bf16[8,64,3072]{2,1,0:T(8,128)(2,1)S(1)}, u32[]{:S(2)}, u32[]{:S(2)}) async-start(bf16[8,64,3072]{2,1,0:T(8,128)(2,1)} %fusion.50), calls=%async_computation | async-start | bytes 6291456 | tf_op jit(solution)/shard_map/all_to_all | solution.py:104
  105.9 8.3 %fusion.2 = f32[256,2560]{1,0:T(8,128)S(1)} fusion(bf16[256,3072]{1,0:T(8,128)(2,1)} %bitcast.25, bf16[1,3072,2560]{2,1,0:T(8,128)(2,1)} %param.12), kind=kOutput, calls=%fused_computation.2 | convolution fusion | flops 4026531840 | bytes 19922944 | tf_op jit(solution)/shard_map/dot_general | solution.py:16
  114.2 5.8 %fusion.22 = bf16[256,3072]{1,0:T(8,128)(2,1)S(1)} fusion(bf16[1,1280,3072]{2,1,0:T(8,128)(2,1)} %param.13, f32[256,2560]{1,0:T(8,128)S(1)} %fusion.2), kind=kOutput, calls=%fused_computation.20 | convolution fusion | flops 2016018432 | bytes 12058624 | tf_op jit(solution)/shard_map/dot_general | solution.py:20
  120.1 0.8 collective-permute-start.10
  120.9 7.3 %fusion = f32[256,2560]{1,0:T(8,128)} fusion(bf16[256,3072]{1,0:T(8,128)(2,1)} %bitcast.28, bf16[1,3072,2560]{2,1,0:T(8,128)(2,1)S(1)} %bitcast.130), kind=kOutput, calls=%fused_computation | convolution fusion | flops 4026531840 | bytes 19922944 | tf_op jit(solution)/shard_map/dot_general | solution.py:16
  128.2 4.1 %fusion.25 = bf16[256,3072]{1,0:T(8,128)(2,1)S(1)} fusion(bf16[1,1280,3072]{2,1,0:T(8,128)(2,1)S(1)} %bitcast.136, f32[256,2560]{1,0:T(8,128)} %fusion), kind=kOutput, calls=%fused_computation.21 | convolution fusion | flops 2016018432 | bytes 12058624 | tf_op jit(solution)/shard_map/dot_general | solution.py:20
  132.2 0.1 collective-permute-start.12
  132.4 2.1 %broadcast_in_dim.38.clone.1 = bf16[8,64,3072]{2,1,0:T(8,128)(2,1)} broadcast(bf16[]{:T(256)} %constant.158.clone.1), dimensions={} | broadcast | bytes 3145730 | tf_op jit(solution)/shard_map/broadcast_in_dim | solution.py:96
  134.4 0.8 slice_dynamic-update-slice_fusion.7
  135.2 0.8 slice_dynamic-update-slice_fusion.6
  136.0 0.8 slice_dynamic-update-slice_fusion.5
  136.8 0.8 slice_dynamic-update-slice_fusion.4
  137.5 0.8 slice_dynamic-update-slice_fusion.3
  138.3 0.8 slice_dynamic-update-slice_fusion.2
  139.1 0.8 slice_dynamic-update-slice_fusion.1
  139.9 0.8 slice_dynamic-update-slice_fusion
  140.7 5.8 %all-to-all-done = bf16[8,64,3072]{2,1,0:T(8,128)(2,1)S(1)} async-done(((bf16[8,64,3072]{2,1,0:T(8,128)(2,1)}), bf16[8,64,3072]{2,1,0:T(8,128)(2,1)S(1)}, u32[]{:S(2)}, u32[]{:S(2)}) %all-to-all-start) | async-done | bytes 3145760 | tf_op jit(solution)/shard_map/all_to_all | solution.py:104
  146.5 4.4 %all-to-all-start.1 = ((bf16[8,64,3072]{2,1,0:T(8,128)(2,1)}), bf16[8,64,3072]{2,1,0:T(8,128)(2,1)}, u32[]{:S(2)}, u32[]{:S(2)}) async-start(bf16[8,64,3072]{2,1,0:T(8,128)(2,1)} %slice_dynamic-update-slice_fusion), calls=%async_computation.1 | async-start | bytes 6291456 | tf_op jit(solution)/shard_map/all_to_all | solution.py:109
  150.9 0.1 copy.18
  151.0 0.1 copy.9
  151.2 0.4 select_reduce_fusion
  151.7 1.9 convolution_bitcast_fusion.1
  153.5 37.2 %all-to-all-done.1 = bf16[8,64,3072]{2,1,0:T(8,128)(2,1)} async-done(((bf16[8,64,3072]{2,1,0:T(8,128)(2,1)}), bf16[8,64,3072]{2,1,0:T(8,128)(2,1)}, u32[]{:S(2)}, u32[]{:S(2)}) %all-to-all-start.1) | async-done | bytes 3145760 | tf_op jit(solution)/shard_map/all_to_all | solution.py:109
  190.8 3.9 %fusion.29 = bf16[128,3072]{1,0:T(8,128)(2,1)} fusion(f32[128,3072]{1,0:T(8,128)} %convolution_bitcast_fusion.1, bf16[8,64,3072]{2,1,0:T(8,128)(2,1)} %all-to-all-done.1, s32[8,64]{1,0:T(8,128)S(1)} %bitcast.128, bf16[8,128]{1,0:T(8,128)(2,1)S(1)} %get-tuple-element.51), kind=kOutput, calls=%fused_computation.25 | convolution fusion | flops 403570688 | bytes 5509120 | tf_op jit(solution)/shard_map/dot_general | solution.py:126
  (55 shorter events, 0.5 us)
Async XLA Ops:
  3.4 22.1 %collective-permute-start.4 = (bf16[129,3072]{1,0:T(8,128)(2,1)S(1)}, bf16[129,3072]{1,0:T(8,128)(2,1)}, u32[]{:S(2)}, u32[]{:S(2)}) collective-permute-start(bf16[129,3072]{1,0:T(8,128)(2,1)S(1)} %get-tuple-element.42), channel_id=1, source_target_pairs={{0,2},{2,0},{1,3},{3,1},{4,6},{6,4},{5,7},{7,5},{8,10},{10,8},{9,1... | collective-permute-start | bytes 2377736 | tf_op jit(solution)/shard_map/ppermute | solution.py:31
  6.8 21.6 %collective-permute-start.2 = (bf16[129,3072]{1,0:T(8,128)(2,1)S(1)}, bf16[129,3072]{1,0:T(8,128)(2,1)S(1)}, u32[]{:S(2)}, u32[]{:S(2)}) collective-permute-start(bf16[129,3072]{1,0:T(8,128)(2,1)S(1)} %get-tuple-element.42), channel_id=1, source_target_pairs={{0,12},{4,0},{8,4},{12,8},{1,13},{5,1},{9,5},{13,9},{2,14},{6,2},{... | collective-permute-start | bytes 2377736 | tf_op jit(solution)/shard_map/ppermute | solution.py:27
  10.8 21.0 %collective-permute-start = (bf16[129,3072]{1,0:T(8,128)(2,1)S(1)}, bf16[129,3072]{1,0:T(8,128)(2,1)S(1)}, u32[]{:S(2)}, u32[]{:S(2)}) collective-permute-start(bf16[129,3072]{1,0:T(8,128)(2,1)S(1)} %get-tuple-element.42), channel_id=1, source_target_pairs={{0,4},{4,8},{8,12},{12,0},{1,5},{5,9},{9,13},{13,1},{2,6},{6,10},{... | collective-permute-start | bytes 2377736 | tf_op jit(solution)/shard_map/ppermute | solution.py:27
  32.7 6.3 %copy-start.3 = (bf16[1,3072,2560]{2,1,0:T(8,128)(2,1)S(1)}, bf16[1,3072,2560]{2,1,0:T(8,128)(2,1)}, u32[]{:S(2)}) copy-start(bf16[1,3072,2560]{2,1,0:T(8,128)(2,1)} %param.12) | copy-start | bytes 47185924
  36.4 36.7 %collective-permute-start.3 = (bf16[65,3072]{1,0:T(8,128)(2,1)S(1)}, bf16[65,3072]{1,0:T(8,128)(2,1)S(1)}, u32[]{:S(2)}, u32[]{:S(2)}) collective-permute-start(bf16[65,3072]{1,0:T(8,128)(2,1)S(1)} %slice.193), channel_id=1, source_target_pairs={{0,12},{4,0},{8,4},{12,8},{1,13},{5,1},{9,5},{13,9},{2,14},{6,2},{... | collective-permute-start | bytes 1198088 | tf_op jit(solution)/shard_map/ppermute | solution.py:27
  36.7 6.4 %slice-start.4 = ((s8[7864320]{0:T(1024)(128)(4,1)}), s8[4194304]{0:T(1024)(128)(4,1)S(1)}, s32[]{:S(2)}) async-start(s8[7864320]{0:T(1024)(128)(4,1)} %bitcast.131), calls=%async_computation.6 | async-start | bytes 8388608
  36.8 36.3 %collective-permute-start.1 = (bf16[64,3072]{1,0:T(8,128)(2,1)S(1)}, bf16[64,3072]{1,0:T(8,128)(2,1)S(1)}, u32[]{:S(2)}, u32[]{:S(2)}) collective-permute-start(bf16[64,3072]{1,0:T(8,128)(2,1)S(1)} %slice.192), channel_id=1, source_target_pairs={{0,4},{4,8},{8,12},{12,0},{1,5},{5,9},{9,13},{13,1},{2,6},{6,10},{... | collective-permute-start | bytes 1179656 | tf_op jit(solution)/shard_map/ppermute | solution.py:27
  38.6 67.3 %collective-permute-start.9 = (bf16[4,64,3072]{2,1,0:T(8,128)(2,1)}, bf16[4,64,3072]{2,1,0:T(8,128)(2,1)}, u32[]{:S(2)}, u32[]{:S(2)}) collective-permute-start(bf16[4,64,3072]{2,1,0:T(8,128)(2,1)} %get-tuple-element.39), channel_id=1, source_target_pairs={{0,1},{1,0},{2,3},{3,2},{4,5},{5,4},{6,7},{7,6},{8,9},{9,8},{10,11... | collective-permute-start | bytes 4718600 | tf_op jit(solution)/shard_map/ppermute | solution.py:31
  39.0 4.2 %slice-start.5 = ((s8[7864320]{0:T(1024)(128)(4,1)}), s8[3670016]{0:T(1024)(128)(4,1)S(1)}, s32[]{:S(2)}) async-start(s8[7864320]{0:T(1024)(128)(4,1)} %bitcast.131), calls=%async_computation.7 | async-start | bytes 7340032
  48.3 20.9 %collective-permute-start.7 = (bf16[129,3072]{1,0:T(8,128)(2,1)}, bf16[129,3072]{1,0:T(8,128)(2,1)S(1)}, u32[]{:S(2)}, u32[]{:S(2)}) collective-permute-start(bf16[129,3072]{1,0:T(8,128)(2,1)} %collective-permute-done.4), channel_id=1, source_target_pairs={{0,12},{4,0},{8,4},{12,8},{1,13},{5,1},{9,5},{13,9},{2,14},{6,2},{... | collective-permute-start | bytes 2377736 | tf_op jit(solution)/shard_map/ppermute | solution.py:27
  49.5 22.5 %collective-permute-start.5 = (bf16[129,3072]{1,0:T(8,128)(2,1)}, bf16[129,3072]{1,0:T(8,128)(2,1)S(1)}, u32[]{:S(2)}, u32[]{:S(2)}) collective-permute-start(bf16[129,3072]{1,0:T(8,128)(2,1)} %collective-permute-done.4), channel_id=1, source_target_pairs={{0,4},{4,8},{8,12},{12,0},{1,5},{5,9},{9,13},{13,1},{2,6},{6,10},{... | collective-permute-start | bytes 2377736 | tf_op jit(solution)/shard_map/ppermute | solution.py:27
  69.2 14.8 %collective-permute-start.8 = (bf16[65,3072]{1,0:T(8,128)(2,1)S(1)}, bf16[65,3072]{1,0:T(8,128)(2,1)S(1)}, u32[]{:S(2)}, u32[]{:S(2)}) collective-permute-start(bf16[65,3072]{1,0:T(8,128)(2,1)S(1)} %slice.195), channel_id=1, source_target_pairs={{0,12},{4,0},{8,4},{12,8},{1,13},{5,1},{9,5},{13,9},{2,14},{6,2},{... | collective-permute-start | bytes 1198088 | tf_op jit(solution)/shard_map/ppermute | solution.py:27
  72.0 11.9 %collective-permute-start.6 = (bf16[64,3072]{1,0:T(8,128)(2,1)S(1)}, bf16[64,3072]{1,0:T(8,128)(2,1)S(1)}, u32[]{:S(2)}, u32[]{:S(2)}) collective-permute-start(bf16[64,3072]{1,0:T(8,128)(2,1)S(1)} %slice.194), channel_id=1, source_target_pairs={{0,4},{4,8},{8,12},{12,0},{1,5},{5,9},{9,13},{13,1},{2,6},{6,10},{... | collective-permute-start | bytes 1179656 | tf_op jit(solution)/shard_map/ppermute | solution.py:27
  87.1 9.6 %slice-start.6 = ((s8[7864320]{0:T(1024)(128)(4,1)}), s8[4194304]{0:T(1024)(128)(4,1)S(1)}, s32[]{:S(2)}) async-start(s8[7864320]{0:T(1024)(128)(4,1)} %bitcast.133), calls=%async_computation.8 | async-start | bytes 8388608
  88.5 8.2 %slice-start.7 = ((s8[7864320]{0:T(1024)(128)(4,1)}), s8[3670016]{0:T(1024)(128)(4,1)S(1)}, s32[]{:S(2)}) async-start(s8[7864320]{0:T(1024)(128)(4,1)} %bitcast.133), calls=%async_computation.9 | async-start | bytes 7340032
  99.0 21.8 %collective-permute-start.11 = (bf16[4,64,3072]{2,1,0:T(8,128)(2,1)}, bf16[4,64,3072]{2,1,0:T(8,128)(2,1)}, u32[]{:S(2)}, u32[]{:S(2)}) collective-permute-start(bf16[4,64,3072]{2,1,0:T(8,128)(2,1)} %get-tuple-element.37), channel_id=1, source_target_pairs={{0,1},{1,0},{2,3},{3,2},{4,5},{5,4},{6,7},{7,6},{8,9},{9,8},{10,11... | collective-permute-start | bytes 4718600 | tf_op jit(solution)/shard_map/ppermute | solution.py:31
  102.2 44.2 %all-to-all-start = ((bf16[8,64,3072]{2,1,0:T(8,128)(2,1)}), bf16[8,64,3072]{2,1,0:T(8,128)(2,1)S(1)}, u32[]{:S(2)}, u32[]{:S(2)}) async-start(bf16[8,64,3072]{2,1,0:T(8,128)(2,1)} %fusion.50), calls=%async_computation | async-start | bytes 6291456 | tf_op jit(solution)/shard_map/all_to_all | solution.py:104
  105.9 15.0 %slice-start = ((s8[15728640]{0:T(1024)(128)(4,1)}), s8[4194304]{0:T(1024)(128)(4,1)S(1)}, s32[]{:S(2)}) async-start(s8[15728640]{0:T(1024)(128)(4,1)} %bitcast.129), calls=%async_computation.2 | async-start | bytes 8388608
  105.9 15.0 %slice-start.1 = ((s8[15728640]{0:T(1024)(128)(4,1)}), s8[4194304]{0:T(1024)(128)(4,1)S(1)}, s32[]{:S(2)}) async-start(s8[15728640]{0:T(1024)(128)(4,1)} %bitcast.129), calls=%async_computation.3 | async-start | bytes 8388608
  105.9 15.0 %slice-start.2 = ((s8[15728640]{0:T(1024)(128)(4,1)}), s8[4194304]{0:T(1024)(128)(4,1)S(1)}, s32[]{:S(2)}) async-start(s8[15728640]{0:T(1024)(128)(4,1)} %bitcast.129), calls=%async_computation.4 | async-start | bytes 8388608
  114.2 6.7 %slice-start.3 = ((s8[15728640]{0:T(1024)(128)(4,1)}), s8[3145728]{0:T(1024)(128)(4,1)S(1)}, s32[]{:S(2)}) async-start(s8[15728640]{0:T(1024)(128)(4,1)} %bitcast.129), calls=%async_computation.5 | async-start | bytes 6291456
  114.2 13.9 %slice-start.8 = ((s8[7864320]{0:T(1024)(128)(4,1)}), s8[4194304]{0:T(1024)(128)(4,1)S(1)}, s32[]{:S(2)}) async-start(s8[7864320]{0:T(1024)(128)(4,1)} %bitcast.135), calls=%async_computation.10 | async-start | bytes 8388608
  120.1 12.3 %collective-permute-start.10 = (bf16[4,64,3072]{2,1,0:T(8,128)(2,1)S(1)}, bf16[4,64,3072]{2,1,0:T(8,128)(2,1)S(1)}, u32[]{:S(2)}, u32[]{:S(2)}) collective-permute-start(bf16[4,64,3072]{2,1,0:T(8,128)(2,1)S(1)} %bitcast.138), channel_id=1, source_target_pairs={{0,1},{1,0},{2,3},{3,2},{4,5},{5,4},{6,7},{7,6},{8,9},{9,8},{10,11... | collective-permute-start | bytes 4718600 | tf_op jit(solution)/shard_map/ppermute | solution.py:31
  120.9 7.3 %slice-start.9 = ((s8[7864320]{0:T(1024)(128)(4,1)}), s8[3670016]{0:T(1024)(128)(4,1)S(1)}, s32[]{:S(2)}) async-start(s8[7864320]{0:T(1024)(128)(4,1)} %bitcast.135), calls=%async_computation.11 | async-start | bytes 7340032
  132.2 5.3 %collective-permute-start.12 = (bf16[4,64,3072]{2,1,0:T(8,128)(2,1)S(1)}, bf16[4,64,3072]{2,1,0:T(8,128)(2,1)S(1)}, u32[]{:S(2)}, u32[]{:S(2)}) collective-permute-start(bf16[4,64,3072]{2,1,0:T(8,128)(2,1)S(1)} %bitcast.137), channel_id=1, source_target_pairs={{0,1},{1,0},{2,3},{3,2},{4,5},{5,4},{6,7},{7,6},{8,9},{9,8},{10,11... | collective-permute-start | bytes 4718600 | tf_op jit(solution)/shard_map/ppermute | solution.py:31
  140.7 10.2 %copy-start.1 = (f32[128,4]{0,1:T(4,128)S(1)}, f32[128,4]{0,1:T(4,128)}, u32[]{:S(2)}) copy-start(f32[128,4]{0,1:T(4,128)} %param.10) | copy-start | bytes 6148
  140.7 10.4 %copy-start.2 = (s32[128,4]{0,1:T(4,128)S(1)}, s32[128,4]{0,1:T(4,128)}, u32[]{:S(2)}) copy-start(s32[128,4]{0,1:T(4,128)} %param.9) | copy-start | bytes 6148
  140.7 11.0 %copy-start = (s32[1,16,64]{2,1,0:T(8,128)S(1)}, s32[1,16,64]{2,1,0:T(8,128)}, u32[]{:S(2)}) copy-start(s32[1,16,64]{2,1,0:T(8,128)} %param.11) | copy-start | bytes 12292
  146.5 44.3 %all-to-all-start.1 = ((bf16[8,64,3072]{2,1,0:T(8,128)(2,1)}), bf16[8,64,3072]{2,1,0:T(8,128)(2,1)}, u32[]{:S(2)}, u32[]{:S(2)}) async-start(bf16[8,64,3072]{2,1,0:T(8,128)(2,1)} %slice_dynamic-update-slice_fusion), calls=%async_computation.1 | async-start | bytes 6291456 | tf_op jit(solution)/shard_map/all_to_all | solution.py:109

commit v7 on v6

--- a/solution.py
+++ b/solution.py
@@ -88,23 +88,27 @@
             into = lax.dynamic_update_slice(into, outs[i : i + 1], (where, 0, 0))
         return into
 
-    early = [(0, 0, block), (0, 1, partner), (1, 0, from_above), (3, 0, from_below)]
-    late = [(2, 0, far), (2, 1, p_far), (1, 1, p_above), (3, 1, p_below)]
-    mine_1, got_1 = slots_of(early)
-    out_m1 = expert_block(mine_1, w_first, w_second)
-    out_g1 = expert_block(got_1, w_first, w_second)
-    empty = jnp.zeros((blocks, capacity, features), jnp.bfloat16)
-    a_part = place(empty, early, out_m1)
-    late_arrs = [arr for _, _, arr in late]
-    *late_arrs, a_part = lax.optimization_barrier((*late_arrs, a_part))
-    late = [(r, q, arr) for (r, q, _), arr in zip(late, late_arrs)]
-    mine_2, got_2 = slots_of(late)
-    out_m2 = expert_block(mine_2, w_first, w_second)
-    a_abs = place(a_part, late, out_m2)
+    stages = [
+        [(0, 0, block), (0, 1, partner), (1, 0, from_above), (3, 0, from_below)],
+        [(2, 0, far), (1, 1, p_above), (3, 1, p_below)],
+        [(2, 1, p_far)],
+    ]
+    a_abs = jnp.zeros((blocks, capacity, features), jnp.bfloat16)
+    got_outs = []
+    for n, pieces in enumerate(stages):
+        if n:
+            arrs = [arr for _, _, arr in pieces]
+            *arrs, a_abs = lax.optimization_barrier((*arrs, a_abs))
+            pieces = [(r, q, arr) for (r, q, _), arr in zip(pieces, arrs)]
+            stages[n] = pieces
+        mine, got = slots_of(pieces)
+        a_abs = place(a_abs, pieces, expert_block(mine, w_first, w_second))
+        got_outs.append(got)
     ret_a = lax.all_to_all(a_abs, ("z", "yh"), 0, 0, tiled=True)
-    a_abs, got_2 = lax.optimization_barrier((a_abs, got_2))
-    out_g2 = expert_block(got_2, w_first, w_second)
-    b_abs = place(place(empty, early, swap(out_g1, "core")), late, swap(out_g2, "core"))
+    a_abs, *got_outs = lax.optimization_barrier((a_abs, *got_outs))
+    b_abs = jnp.zeros((blocks, capacity, features), jnp.bfloat16)
+    for pieces, got in zip(stages, got_outs):
+        b_abs = place(b_abs, pieces, swap(expert_block(got, w_first, w_second), "core"))
     ret_a, b_abs = lax.optimization_barrier((ret_a, b_abs))
     ret_b = lax.all_to_all(b_abs, ("z", "yh"), 0, 0, tiled=True)
 

time: 195 us -> 208 us (1.067)
  matrix products: 53.4 us -> 68.6 us
  waiting for transfers between devices: 92.1 us -> 86.1 us
  starting transfers between devices: 23.7 us -> 27.8 us
    dot_general x4 -> x6, matrix products: 27.9 us -> 41.1 us  [expert_block(): projected = jnp.dot(flat, w_first, preferred_element_type=jnp.float32)]
    all_to_all x1, waiting for transfers between devices: 5.79 us -> 0.01 us  [shards(): ret_a = lax.all_to_all(a_abs, ('z', 'yh'), 0, 0, tiled=True)]
    broadcast_in_dim x2 -> x0, local copies, waits for them, and re-layouts: 4.09 us -> none  [shards(): empty = jnp.zeros((blocks, capacity, features), jnp.bfloat16)]
    another operation x1 -> x3, local copies, waits for them, and re-layouts: 0.09 us -> 4.18 us
    dot_general x4 -> x6, matrix products: 14.5 us -> 17.6 us  [expert_block(): jnp.dot(intermediate_activation, w_second, preferred_element_type=jnp.flo...]
    all_to_all x1, starting transfers between devices: 4.45 us -> 7.05 us  [shards(): ret_b = lax.all_to_all(b_abs, ('z', 'yh'), 0, 0, tiled=True)]
    dot_general x2 -> x3, matrix products: 5.16 us -> 4.09 us  [slots_of(): jnp.einsum('bjct,btd->bjcd', one_hot, toks, preferred_element_type=jnp.fl...]
    dynamic_update_slice x16 -> x15, local copies, waits for them, and re-layouts: 12.4 us -> 11.7 us  [place(): into = lax.dynamic_update_slice(into, outs[i:i + 1], (where, 0, 0))]
  transfers between devices with their start and end apart: 15 -> 17, of which waited for: 7 -> 6; matrix products, arithmetic and copies ran while one was open for 34% -> 39% of each run, Pallas kernels for 0% -> 0%
where the time goes in v7:
time: 208 us
  waiting for transfers between devices  86.1 us (41%)
  matrix products  68.6 us (33%)
  starting transfers between devices  27.8 us (13%)
  local copies, waits for them, and re-layouts  19.9 us (10%)
  other arithmetic  4.89 us (2%)
    dot_general x6, matrix products, expert_block(): projected = jnp.dot(flat, w_first, preferred_element_type=jnp.float32)  41.1 us
    all_to_all x1, waiting for transfers between devices, shards(): ret_b = lax.all_to_all(b_abs, ('z', 'yh'), 0, 0, tiled=True)  37.8 us
    ppermute x8, waiting for transfers between devices, shift_z(): return lax.ppermute(x, 'z', [(i, (i + step) % RING) for i in range(RING)])  33.5 us
    dot_general x6, matrix products, expert_block(): jnp.dot(intermediate_activation, w_second, preferred_element_type=jnp.flo...  17.6 us
    ppermute x7, waiting for transfers between devices, swap(): return lax.ppermute(x, axis, [(0, 1), (1, 0)])  14.8 us
    ppermute x8, starting transfers between devices, shift_z(): return lax.ppermute(x, 'z', [(i, (i + step) % RING) for i in range(RING)])  12.5 us
    dynamic_update_slice x15, local copies, waits for them, and re-layouts, place(): into = lax.dynamic_update_slice(into, outs[i:i + 1], (where, 0, 0))  11.7 us
    all_to_all x1, starting transfers between devices, shards(): ret_b = lax.all_to_all(b_abs, ('z', 'yh'), 0, 0, tiled=True)  7.05 us
  transfers between devices with their start and end apart: 17, of which 6 were waited for; matrix products, arithmetic and copies ran while one was open for 39% of the time, Pallas kernels for 0%

profile of v7, /device:TPU:0, one launch (start us, length us, event | category | flops | bytes accessed | tf_op | source)
XLA Modules:
  0.0 207.7 jit_solution(16292543900699818197)
XLA Ops:
  0.0 0.6 compare_reduce_fusion
  0.6 1.3 convert_select_fusion
  2.0 0.1 reshape.136
  2.1 2.2 %fusion.116 = (bf16[1,129,3072]{2,1,0:T(8,128)(2,1)S(1)}, bf16[129,3072]{1,0:T(8,128)(2,1)}) fusion(bf16[1,1024]{1,0:T(2,128)(2,1)S(1)} %reshape.136, bf16[128,3072]{1,0:T(8,128)(2,1)} %param.8), kind=kLoop, calls=%fused_computation.153 | loop fusion | flops 2377728 | bytes 2373632 | tf_op jit(solution)/shard_map/stack | solution.py:68
  4.3 3.3 %collective-permute-start = (bf16[129,3072]{1,0:T(8,128)(2,1)}, bf16[129,3072]{1,0:T(8,128)(2,1)S(1)}, u32[]{:S(2)}, u32[]{:S(2)}) collective-permute-start(bf16[129,3072]{1,0:T(8,128)(2,1)} %get-tuple-element.48), channel_id=1, source_target_pairs={{0,2},{2,0},{1,3},{3,1},{4,6},{6,4},{5,7},{7,5},{8,10},{10,8},{9,1... | collective-permute-start | bytes 2377736 | tf_op jit(solution)/shard_map/ppermute | solution.py:31
  7.6 4.0 %collective-permute-start.7 = (bf16[129,3072]{1,0:T(8,128)(2,1)}, bf16[129,3072]{1,0:T(8,128)(2,1)S(1)}, u32[]{:S(2)}, u32[]{:S(2)}) collective-permute-start(bf16[129,3072]{1,0:T(8,128)(2,1)} %get-tuple-element.48), channel_id=1, source_target_pairs={{0,12},{4,0},{8,4},{12,8},{1,13},{5,1},{9,5},{13,9},{2,14},{6,2},{... | collective-permute-start | bytes 2377736 | tf_op jit(solution)/shard_map/ppermute | solution.py:27
  11.6 14.8 %collective-permute-done = bf16[129,3072]{1,0:T(8,128)(2,1)S(1)} collective-permute-done((bf16[129,3072]{1,0:T(8,128)(2,1)}, bf16[129,3072]{1,0:T(8,128)(2,1)S(1)}, u32[]{:S(2)}, u32[]{:S(2)}) %collective-permute-start) | collective-permute-done | bytes 792608 | tf_op jit(solution)/shard_map/ppermute | solution.py:31
  26.4 3.1 %collective-permute-done.7 = bf16[129,3072]{1,0:T(8,128)(2,1)S(1)} collective-permute-done((bf16[129,3072]{1,0:T(8,128)(2,1)}, bf16[129,3072]{1,0:T(8,128)(2,1)S(1)}, u32[]{:S(2)}, u32[]{:S(2)}) %collective-permute-start.7) | collective-permute-done | bytes 792608 | tf_op jit(solution)/shard_map/ppermute | solution.py:27
  29.5 3.3 %collective-permute-done.5 = bf16[129,3072]{1,0:T(8,128)(2,1)S(1)} collective-permute-done((bf16[129,3072]{1,0:T(8,128)(2,1)}, bf16[129,3072]{1,0:T(8,128)(2,1)S(1)}, u32[]{:S(2)}, u32[]{:S(2)}) %collective-permute-start.5) | collective-permute-done | bytes 792608 | tf_op jit(solution)/shard_map/ppermute | solution.py:27
  32.9 0.1 reshape.146
  33.0 2.8 %convolution_convert_fusion = bf16[4,2,64,3072]{3,2,1,0:T(8,128)(2,1)S(1)} fusion(bf16[1,129,3072]{2,1,0:T(8,128)(2,1)S(1)} %bitcast.169, bf16[1,129,3072]{2,1,0:T(8,128)(2,1)S(1)} %bitcast.165, bf16[1,129,3072]{2,1,0:T(8,128)(2,1)S(1)} %bitcast.175, bf16[1,129,3072]{2,1,0:T(8,128)(2,1)S(1)} %get-tuple-element.47, s32[4,2,64]{2,1,0:T(2,128)S(1)} %pad_add_fusion), kind=kOutput, calls=%fused_computation.24 | convolution fusion | flops 416874496 | bytes 6318080 | tf_op jit(solution)/shard_map/bjct,btd->bjcd/dot_general | solution.py:80
  35.9 1.3 slice_bitcast_fusion
  37.3 0.3 collective-permute-start.8
  37.6 1.8 collective-permute-start.6
  39.5 4.2 %fusion.10 = f32[256,2560]{1,0:T(8,128)S(1)} fusion(bf16[256,3072]{1,0:T(8,128)(2,1)S(1)} %bitcast.172, bf16[1,3072,2560]{2,1,0:T(8,128)(2,1)S(1)} %copy-done), kind=kOutput, calls=%fused_computation.10 | convolution fusion | flops 4026531840 | bytes 19922944 | tf_op jit(solution)/shard_map/dot_general | solution.py:16
  43.7 2.3 %fusion.24 = bf16[256,3072]{1,0:T(8,128)(2,1)S(1)} fusion(bf16[1,1280,3072]{2,1,0:T(8,128)(2,1)S(1)} %bitcast.153, f32[256,2560]{1,0:T(8,128)S(1)} %fusion.10), kind=kOutput, calls=%fused_computation.26 | convolution fusion | flops 2016018432 | bytes 12058624 | tf_op jit(solution)/shard_map/dot_general | solution.py:20
  46.0 2.0 broadcast.94.clone
  48.0 0.8 fusion.80
  48.8 0.8 fusion.79
  49.6 0.8 fusion.78
  50.4 0.1 collective-permute-start.1
  50.5 3.1 %collective-permute-start.3 = (bf16[129,3072]{1,0:T(8,128)(2,1)S(1)}, bf16[129,3072]{1,0:T(8,128)(2,1)S(1)}, u32[]{:S(2)}, u32[]{:S(2)}) collective-permute-start(bf16[129,3072]{1,0:T(8,128)(2,1)S(1)} %collective-permute-done), channel_id=1, source_target_pairs={{0,12},{4,0},{8,4},{12,8},{1,13},{5,1},{9,5},{13,9},{2,14},{6,2},{... | collective-permute-start | bytes 2377736 | tf_op jit(solution)/shard_map/ppermute | solution.py:27
  53.6 0.8 fusion.77
  54.5 18.1 %collective-permute-done.1 = bf16[129,3072]{1,0:T(8,128)(2,1)S(1)} collective-permute-done((bf16[129,3072]{1,0:T(8,128)(2,1)S(1)}, bf16[129,3072]{1,0:T(8,128)(2,1)S(1)}, u32[]{:S(2)}, u32[]{:S(2)}) %collective-permute-start.1) | collective-permute-done | bytes 792608 | tf_op jit(solution)/shard_map/ppermute | solution.py:27
  72.8 0.8 convolution_convert_fusion.1
  73.6 1.2 slice_bitcast_fusion.1
  74.7 7.7 %fusion.8 = f32[192,2560]{1,0:T(8,128)S(1)} fusion(bf16[192,3072]{1,0:T(8,128)(2,1)S(1)} %bitcast.173, bf16[1,3072,2560]{2,1,0:T(8,128)(2,1)} %param.12), kind=kOutput, calls=%fused_computation.8 | convolution fusion | flops 3019898880 | bytes 18874368 | tf_op jit(solution)/shard_map/dot_general | solution.py:16
  82.5 1.8 fusion.30
  84.4 3.0 %collective-permute-start.4 = (bf16[65,3072]{1,0:T(8,128)(2,1)S(1)}, bf16[65,3072]{1,0:T(8,128)(2,1)S(1)}, u32[]{:S(2)}, u32[]{:S(2)}) collective-permute-start(bf16[65,3072]{1,0:T(8,128)(2,1)S(1)} %slice.213), channel_id=1, source_target_pairs={{0,12},{4,0},{8,4},{12,8},{1,13},{5,1},{9,5},{13,9},{2,14},{6,2},{... | collective-permute-start | bytes 1198088 | tf_op jit(solution)/shard_map/ppermute | solution.py:27
  87.5 0.1 collective-permute-start.10
  87.6 0.8 fusion.76
  88.4 0.8 fusion.75
  89.2 0.8 fusion.74
  89.9 8.9 %collective-permute-done.2 = bf16[64,3072]{1,0:T(8,128)(2,1)S(1)} collective-permute-done((bf16[64,3072]{1,0:T(8,128)(2,1)S(1)}, bf16[64,3072]{1,0:T(8,128)(2,1)S(1)}, u32[]{:S(2)}, u32[]{:S(2)}) %collective-permute-start.2) | collective-permute-done | bytes 393248 | tf_op jit(solution)/shard_map/ppermute | solution.py:27
  99.0 0.4 fusion.38
  99.5 0.8 slice_bitcast_fusion.4
  100.2 8.8 %fusion.6 = f32[64,2560]{1,0:T(8,128)S(1)} fusion(bf16[1,3072,2560]{2,1,0:T(8,128)(2,1)} %param.12, bf16[1,2,64,3072]{3,2,1,0:T(8,128)(2,1)S(1)} %fusion.38), kind=kOutput, calls=%fused_computation.6 | convolution fusion | flops 1006632960 | bytes 16777216 | tf_op jit(solution)/shard_map/dot_general | solution.py:16
  109.1 2.2 %fusion.51 = bf16[8,64,3072]{2,1,0:T(8,128)(2,1)} fusion(bf16[8,64,3072]{2,1,0:T(8,128)(2,1)} %fusion.74, s32[]{:T(128)S(6)} %select_n.156, bf16[1,1280,3072]{2,1,0:T(8,128)(2,1)S(1)} %bitcast.157, f32[64,2560]{1,0:T(8,128)S(1)} %fusion.6), kind=kOutput, calls=%fused_computation.40 | convolution fusion | flops 504004608 | bytes 8912900 | tf_op jit(solution)/shard_map/dot_general | solution.py:20
  111.3 3.9 %all-to-all-start = ((bf16[8,64,3072]{2,1,0:T(8,128)(2,1)}), bf16[8,64,3072]{2,1,0:T(8,128)(2,1)S(1)}, u32[]{:S(2)}, u32[]{:S(2)}) async-start(bf16[8,64,3072]{2,1,0:T(8,128)(2,1)} %fusion.51), calls=%async_computation | async-start | bytes 6291456 | tf_op jit(solution)/shard_map/all_to_all | solution.py:107
  115.2 11.8 %fusion.4 = f32[256,2560]{1,0:T(8,128)} fusion(bf16[256,3072]{1,0:T(8,128)(2,1)} %bitcast.33, bf16[1,3072,2560]{2,1,0:T(8,128)(2,1)} %param.12), kind=kOutput, calls=%fused_computation.4 | convolution fusion | flops 4026531840 | bytes 19922944 | tf_op jit(solution)/shard_map/dot_general | solution.py:16
  127.1 6.4 %fusion.27 = bf16[256,3072]{1,0:T(8,128)(2,1)S(1)} fusion(bf16[1,1280,3072]{2,1,0:T(8,128)(2,1)} %param.13, f32[256,2560]{1,0:T(8,128)} %fusion.4), kind=kOutput, calls=%fused_computation.27 | convolution fusion | flops 2016018432 | bytes 12058624 | tf_op jit(solution)/shard_map/dot_general | solution.py:20
  133.5 0.1 collective-permute-start.12
  133.6 5.8 %fusion.2 = f32[192,2560]{1,0:T(8,128)} fusion(bf16[192,3072]{1,0:T(8,128)(2,1)} %bitcast.35, bf16[1,3072,2560]{2,1,0:T(8,128)(2,1)S(1)} %bitcast.151), kind=kOutput, calls=%fused_computation.2 | convolution fusion | flops 3019898880 | bytes 18874368 | tf_op jit(solution)/shard_map/dot_general | solution.py:16
  139.4 3.3 %fusion.33 = bf16[192,3072]{1,0:T(8,128)(2,1)S(1)} fusion(bf16[1,1280,3072]{2,1,0:T(8,128)(2,1)S(1)} %bitcast.159, f32[192,2560]{1,0:T(8,128)} %fusion.2), kind=kOutput, calls=%fused_computation.29 | convolution fusion | flops 1512013824 | bytes 11010048 | tf_op jit(solution)/shard_map/dot_general | solution.py:20
  142.7 0.6 collective-permute-start.13
  143.3 2.8 %fusion = f32[64,2560]{1,0:T(8,128)S(1)} fusion(bf16[1,3072,2560]{2,1,0:T(8,128)(2,1)S(1)} %bitcast.151, bf16[1,64,3072]{2,1,0:T(8,128)(2,1)S(1)} %collective-permute-done.11), kind=kOutput, calls=%fused_computation | convolution fusion | flops 1006632960 | bytes 16777216 | tf_op jit(solution)/shard_map/dot_general | solution.py:16
  146.1 1.5 fusion.45
  147.6 0.4 collective-permute-start.14
  148.0 2.1 broadcast.94
  150.0 0.8 slice_dynamic-update-slice_fusion.6
  150.8 0.8 slice_dynamic-update-slice_fusion.5
  151.6 0.8 slice_dynamic-update-slice_fusion.4
  152.4 0.8 slice_dynamic-update-slice_fusion.3
  153.1 0.8 slice_dynamic-update-slice_fusion.2
  153.9 0.8 slice_dynamic-update-slice_fusion.1
  154.7 0.8 slice_dynamic-update-slice_fusion
  155.5 0.8 constant_dynamic-update-slice_fusion
  156.3 7.0 %all-to-all-start.1 = ((bf16[8,64,3072]{2,1,0:T(8,128)(2,1)}), bf16[8,64,3072]{2,1,0:T(8,128)(2,1)}, u32[]{:S(2)}, u32[]{:S(2)}) async-start(bf16[8,64,3072]{2,1,0:T(8,128)(2,1)} %constant_dynamic-update-slice_fusion), calls=%async_computation.1 | async-start | bytes 6291456 | tf_op jit(solution)/shard_map/all_to_all | solution.py:113
  163.3 0.1 copy.18
  163.5 0.1 copy.9
  163.6 0.4 select_reduce_fusion
  164.1 1.9 convolution_bitcast_fusion.1
  166.0 37.8 %all-to-all-done.1 = bf16[8,64,3072]{2,1,0:T(8,128)(2,1)} async-done(((bf16[8,64,3072]{2,1,0:T(8,128)(2,1)}), bf16[8,64,3072]{2,1,0:T(8,128)(2,1)}, u32[]{:S(2)}, u32[]{:S(2)}) %all-to-all-start.1) | async-done | bytes 3145760 | tf_op jit(solution)/shard_map/all_to_all | solution.py:113
  203.8 3.9 %fusion.37 = bf16[128,3072]{1,0:T(8,128)(2,1)} fusion(f32[128,3072]{1,0:T(8,128)} %convolution_bitcast_fusion.1, bf16[8,64,3072]{2,1,0:T(8,128)(2,1)} %all-to-all-done.1, s32[8,64]{1,0:T(8,128)S(1)} %bitcast.179, bf16[8,128]{1,0:T(8,128)(2,1)S(1)} %get-tuple-element.59), kind=kOutput, calls=%fused_computation.33 | convolution fusion | flops 403570688 | bytes 5509120 | tf_op jit(solution)/shard_map/dot_general | solution.py:130
  (73 shorter events, 0.9 us)
Async XLA Ops:
  4.3 22.1 %collective-permute-start = (bf16[129,3072]{1,0:T(8,128)(2,1)}, bf16[129,3072]{1,0:T(8,128)(2,1)S(1)}, u32[]{:S(2)}, u32[]{:S(2)}) collective-permute-start(bf16[129,3072]{1,0:T(8,128)(2,1)} %get-tuple-element.48), channel_id=1, source_target_pairs={{0,2},{2,0},{1,3},{3,1},{4,6},{6,4},{5,7},{7,5},{8,10},{10,8},{9,1... | collective-permute-start | bytes 2377736 | tf_op jit(solution)/shard_map/ppermute | solution.py:31
  7.6 21.9 %collective-permute-start.7 = (bf16[129,3072]{1,0:T(8,128)(2,1)}, bf16[129,3072]{1,0:T(8,128)(2,1)S(1)}, u32[]{:S(2)}, u32[]{:S(2)}) collective-permute-start(bf16[129,3072]{1,0:T(8,128)(2,1)} %get-tuple-element.48), channel_id=1, source_target_pairs={{0,12},{4,0},{8,4},{12,8},{1,13},{5,1},{9,5},{13,9},{2,14},{6,2},{... | collective-permute-start | bytes 2377736 | tf_op jit(solution)/shard_map/ppermute | solution.py:27
  11.6 21.2 %collective-permute-start.5 = (bf16[129,3072]{1,0:T(8,128)(2,1)}, bf16[129,3072]{1,0:T(8,128)(2,1)S(1)}, u32[]{:S(2)}, u32[]{:S(2)}) collective-permute-start(bf16[129,3072]{1,0:T(8,128)(2,1)} %get-tuple-element.48), channel_id=1, source_target_pairs={{0,4},{4,8},{8,12},{12,0},{1,5},{5,9},{9,13},{13,1},{2,6},{6,10},{... | collective-permute-start | bytes 2377736 | tf_op jit(solution)/shard_map/ppermute | solution.py:27
  33.0 6.4 %copy-start = (bf16[1,3072,2560]{2,1,0:T(8,128)(2,1)S(1)}, bf16[1,3072,2560]{2,1,0:T(8,128)(2,1)}, u32[]{:S(2)}) copy-start(bf16[1,3072,2560]{2,1,0:T(8,128)(2,1)} %param.12) | copy-start | bytes 47185924
  37.3 17.2 %collective-permute-start.8 = (bf16[65,3072]{1,0:T(8,128)(2,1)S(1)}, bf16[65,3072]{1,0:T(8,128)(2,1)S(1)}, u32[]{:S(2)}, u32[]{:S(2)}) collective-permute-start(bf16[65,3072]{1,0:T(8,128)(2,1)S(1)} %slice.215), channel_id=1, source_target_pairs={{0,12},{4,0},{8,4},{12,8},{1,13},{5,1},{9,5},{13,9},{2,14},{6,2},{... | collective-permute-start | bytes 1198088 | tf_op jit(solution)/shard_map/ppermute | solution.py:27
  37.6 6.1 %slice-start.4 = ((s8[7864320]{0:T(1024)(128)(4,1)}), s8[4194304]{0:T(1024)(128)(4,1)S(1)}, s32[]{:S(2)}) async-start(s8[7864320]{0:T(1024)(128)(4,1)} %bitcast.152), calls=%async_computation.6 | async-start | bytes 8388608
  37.6 16.8 %collective-permute-start.6 = (bf16[64,3072]{1,0:T(8,128)(2,1)S(1)}, bf16[64,3072]{1,0:T(8,128)(2,1)S(1)}, u32[]{:S(2)}, u32[]{:S(2)}) collective-permute-start(bf16[64,3072]{1,0:T(8,128)(2,1)S(1)} %slice.214), channel_id=1, source_target_pairs={{0,4},{4,8},{8,12},{12,0},{1,5},{5,9},{9,13},{13,1},{2,6},{6,10},{... | collective-permute-start | bytes 1179656 | tf_op jit(solution)/shard_map/ppermute | solution.py:27
  39.4 75.7 %collective-permute-start.9 = (bf16[4,64,3072]{2,1,0:T(8,128)(2,1)}, bf16[4,64,3072]{2,1,0:T(8,128)(2,1)}, u32[]{:S(2)}, u32[]{:S(2)}) collective-permute-start(bf16[4,64,3072]{2,1,0:T(8,128)(2,1)} %get-tuple-element.43), channel_id=1, source_target_pairs={{0,1},{1,0},{2,3},{3,2},{4,5},{5,4},{6,7},{7,6},{8,9},{9,8},{10,11... | collective-permute-start | bytes 4718600 | tf_op jit(solution)/shard_map/ppermute | solution.py:31
  39.5 4.2 %slice-start.5 = ((s8[7864320]{0:T(1024)(128)(4,1)}), s8[3670016]{0:T(1024)(128)(4,1)S(1)}, s32[]{:S(2)}) async-start(s8[7864320]{0:T(1024)(128)(4,1)} %bitcast.152), calls=%async_computation.7 | async-start | bytes 7340032
  50.4 22.2 %collective-permute-start.1 = (bf16[129,3072]{1,0:T(8,128)(2,1)S(1)}, bf16[129,3072]{1,0:T(8,128)(2,1)S(1)}, u32[]{:S(2)}, u32[]{:S(2)}) collective-permute-start(bf16[129,3072]{1,0:T(8,128)(2,1)S(1)} %collective-permute-done), channel_id=1, source_target_pairs={{0,4},{4,8},{8,12},{12,0},{1,5},{5,9},{9,13},{13,1},{2,6},{6,10},{... | collective-permute-start | bytes 2377736 | tf_op jit(solution)/shard_map/ppermute | solution.py:27
  50.5 22.1 %collective-permute-start.3 = (bf16[129,3072]{1,0:T(8,128)(2,1)S(1)}, bf16[129,3072]{1,0:T(8,128)(2,1)S(1)}, u32[]{:S(2)}, u32[]{:S(2)}) collective-permute-start(bf16[129,3072]{1,0:T(8,128)(2,1)S(1)} %collective-permute-done), channel_id=1, source_target_pairs={{0,12},{4,0},{8,4},{12,8},{1,13},{5,1},{9,5},{13,9},{2,14},{6,2},{... | collective-permute-start | bytes 2377736 | tf_op jit(solution)/shard_map/ppermute | solution.py:27
  73.6 8.9 %slice-start.6 = ((s8[7864320]{0:T(1024)(128)(4,1)}), s8[4194304]{0:T(1024)(128)(4,1)S(1)}, s32[]{:S(2)}) async-start(s8[7864320]{0:T(1024)(128)(4,1)} %bitcast.154), calls=%async_computation.8 | async-start | bytes 8388608
  74.7 7.8 %slice-start.7 = ((s8[7864320]{0:T(1024)(128)(4,1)}), s8[3670016]{0:T(1024)(128)(4,1)S(1)}, s32[]{:S(2)}) async-start(s8[7864320]{0:T(1024)(128)(4,1)} %bitcast.154), calls=%async_computation.9 | async-start | bytes 7340032
  84.4 14.5 %collective-permute-start.4 = (bf16[65,3072]{1,0:T(8,128)(2,1)S(1)}, bf16[65,3072]{1,0:T(8,128)(2,1)S(1)}, u32[]{:S(2)}, u32[]{:S(2)}) collective-permute-start(bf16[65,3072]{1,0:T(8,128)(2,1)S(1)} %slice.213), channel_id=1, source_target_pairs={{0,12},{4,0},{8,4},{12,8},{1,13},{5,1},{9,5},{13,9},{2,14},{6,2},{... | collective-permute-start | bytes 1198088 | tf_op jit(solution)/shard_map/ppermute | solution.py:27
  87.4 11.4 %collective-permute-start.2 = (bf16[64,3072]{1,0:T(8,128)(2,1)S(1)}, bf16[64,3072]{1,0:T(8,128)(2,1)S(1)}, u32[]{:S(2)}, u32[]{:S(2)}) collective-permute-start(bf16[64,3072]{1,0:T(8,128)(2,1)S(1)} %slice.212), channel_id=1, source_target_pairs={{0,4},{4,8},{8,12},{12,0},{1,5},{5,9},{9,13},{13,1},{2,6},{6,10},{... | collective-permute-start | bytes 1179656 | tf_op jit(solution)/shard_map/ppermute | solution.py:27
  87.5 27.7 %collective-permute-start.10 = (bf16[3,64,3072]{2,1,0:T(8,128)(2,1)}, bf16[3,64,3072]{2,1,0:T(8,128)(2,1)}, u32[]{:S(2)}, u32[]{:S(2)}) collective-permute-start(bf16[3,64,3072]{2,1,0:T(8,128)(2,1)} %get-tuple-element.45), channel_id=1, source_target_pairs={{0,1},{1,0},{2,3},{3,2},{4,5},{5,4},{6,7},{7,6},{8,9},{9,8},{10,11... | collective-permute-start | bytes 3538952 | tf_op jit(solution)/shard_map/ppermute | solution.py:31
  99.5 9.6 %slice-start.8 = ((s8[7864320]{0:T(1024)(128)(4,1)}), s8[4194304]{0:T(1024)(128)(4,1)S(1)}, s32[]{:S(2)}) async-start(s8[7864320]{0:T(1024)(128)(4,1)} %bitcast.156), calls=%async_computation.10 | async-start | bytes 8388608
  100.2 8.8 %slice-start.9 = ((s8[7864320]{0:T(1024)(128)(4,1)}), s8[3670016]{0:T(1024)(128)(4,1)S(1)}, s32[]{:S(2)}) async-start(s8[7864320]{0:T(1024)(128)(4,1)} %bitcast.156), calls=%async_computation.11 | async-start | bytes 7340032
  100.2 14.9 %collective-permute-start.11 = (bf16[1,64,3072]{2,1,0:T(8,128)(2,1)}, bf16[1,64,3072]{2,1,0:T(8,128)(2,1)S(1)}, u32[]{:S(2)}, u32[]{:S(2)}) collective-permute-start(bf16[1,64,3072]{2,1,0:T(8,128)(2,1)} %slice_bitcast_fusion.4), channel_id=1, source_target_pairs={{0,1},{1,0},{2,3},{3,2},{4,5},{5,4},{6,7},{7,6},{8,9},{9,8},{10,11... | collective-permute-start | bytes 1179656 | tf_op jit(solution)/shard_map/ppermute | solution.py:31
  111.3 45.0 %all-to-all-start = ((bf16[8,64,3072]{2,1,0:T(8,128)(2,1)}), bf16[8,64,3072]{2,1,0:T(8,128)(2,1)S(1)}, u32[]{:S(2)}, u32[]{:S(2)}) async-start(bf16[8,64,3072]{2,1,0:T(8,128)(2,1)} %fusion.51), calls=%async_computation | async-start | bytes 6291456 | tf_op jit(solution)/shard_map/all_to_all | solution.py:107
  115.2 18.4 %slice-start = ((s8[15728640]{0:T(1024)(128)(4,1)}), s8[4194304]{0:T(1024)(128)(4,1)S(1)}, s32[]{:S(2)}) async-start(s8[15728640]{0:T(1024)(128)(4,1)} %bitcast.150), calls=%async_computation.2 | async-start | bytes 8388608
  115.2 18.4 %slice-start.1 = ((s8[15728640]{0:T(1024)(128)(4,1)}), s8[4194304]{0:T(1024)(128)(4,1)S(1)}, s32[]{:S(2)}) async-start(s8[15728640]{0:T(1024)(128)(4,1)} %bitcast.150), calls=%async_computation.3 | async-start | bytes 8388608
  115.2 18.4 %slice-start.2 = ((s8[15728640]{0:T(1024)(128)(4,1)}), s8[3145728]{0:T(1024)(128)(4,1)S(1)}, s32[]{:S(2)}) async-start(s8[15728640]{0:T(1024)(128)(4,1)} %bitcast.150), calls=%async_computation.4 | async-start | bytes 6291456
  115.2 24.2 %slice-start.10 = ((s8[7864320]{0:T(1024)(128)(4,1)}), s8[4194304]{0:T(1024)(128)(4,1)S(1)}, s32[]{:S(2)}) async-start(s8[7864320]{0:T(1024)(128)(4,1)} %bitcast.158), calls=%async_computation.12 | async-start | bytes 8388608
  127.1 6.5 %slice-start.3 = ((s8[15728640]{0:T(1024)(128)(4,1)}), s8[4194304]{0:T(1024)(128)(4,1)S(1)}, s32[]{:S(2)}) async-start(s8[15728640]{0:T(1024)(128)(4,1)} %bitcast.150), calls=%async_computation.5 | async-start | bytes 8388608
  127.1 12.3 %slice-start.11 = ((s8[7864320]{0:T(1024)(128)(4,1)}), s8[3670016]{0:T(1024)(128)(4,1)S(1)}, s32[]{:S(2)}) async-start(s8[7864320]{0:T(1024)(128)(4,1)} %bitcast.158), calls=%async_computation.13 | async-start | bytes 7340032
  133.5 14.5 %collective-permute-start.12 = (bf16[4,64,3072]{2,1,0:T(8,128)(2,1)S(1)}, bf16[4,64,3072]{2,1,0:T(8,128)(2,1)S(1)}, u32[]{:S(2)}, u32[]{:S(2)}) collective-permute-start(bf16[4,64,3072]{2,1,0:T(8,128)(2,1)S(1)} %bitcast.180), channel_id=1, source_target_pairs={{0,1},{1,0},{2,3},{3,2},{4,5},{5,4},{6,7},{7,6},{8,9},{9,8},{10,11... | collective-permute-start | bytes 4718600 | tf_op jit(solution)/shard_map/ppermute | solution.py:31
  142.7 10.4 %collective-permute-start.13 = (bf16[3,64,3072]{2,1,0:T(8,128)(2,1)S(1)}, bf16[3,64,3072]{2,1,0:T(8,128)(2,1)S(1)}, u32[]{:S(2)}, u32[]{:S(2)}) collective-permute-start(bf16[3,64,3072]{2,1,0:T(8,128)(2,1)S(1)} %bitcast.181), channel_id=1, source_target_pairs={{0,1},{1,0},{2,3},{3,2},{4,5},{5,4},{6,7},{7,6},{8,9},{9,8},{10,11... | collective-permute-start | bytes 3538952 | tf_op jit(solution)/shard_map/ppermute | solution.py:31
  147.6 7.9 %collective-permute-start.14 = (bf16[1,64,3072]{2,1,0:T(8,128)(2,1)S(1)}, bf16[1,64,3072]{2,1,0:T(8,128)(2,1)S(1)}, u32[]{:S(2)}, u32[]{:S(2)}) collective-permute-start(bf16[1,64,3072]{2,1,0:T(8,128)(2,1)S(1)} %fusion.45), channel_id=1, source_target_pairs={{0,1},{1,0},{2,3},{3,2},{4,5},{5,4},{6,7},{7,6},{8,9},{9,8},{10,11... | collective-permute-start | bytes 1179656 | tf_op jit(solution)/shard_map/ppermute | solution.py:31
  156.3 7.1 %copy-start.2 = (f32[128,4]{0,1:T(4,128)S(1)}, f32[128,4]{0,1:T(4,128)}, u32[]{:S(2)}) copy-start(f32[128,4]{0,1:T(4,128)} %param.10) | copy-start | bytes 6148
  156.3 7.2 %copy-start.3 = (s32[128,4]{0,1:T(4,128)S(1)}, s32[128,4]{0,1:T(4,128)}, u32[]{:S(2)}) copy-start(s32[128,4]{0,1:T(4,128)} %param.9) | copy-start | bytes 6148
  156.3 7.8 %copy-start.1 = (s32[1,16,64]{2,1,0:T(8,128)S(1)}, s32[1,16,64]{2,1,0:T(8,128)}, u32[]{:S(2)}) copy-start(s32[1,16,64]{2,1,0:T(8,128)} %param.11) | copy-start | bytes 12292
  156.3 47.5 %all-to-all-start.1 = ((bf16[8,64,3072]{2,1,0:T(8,128)(2,1)}), bf16[8,64,3072]{2,1,0:T(8,128)(2,1)}, u32[]{:S(2)}, u32[]{:S(2)}) async-start(bf16[8,64,3072]{2,1,0:T(8,128)(2,1)} %constant_dynamic-update-slice_fusion), calls=%async_computation.1 | async-start | bytes 6291456 | tf_op jit(solution)/shard_map/all_to_all | solution.py:113

commit v8 on v3

--- a/solution.py
+++ b/solution.py
@@ -36,6 +36,7 @@
     mixing = jnp.where(picks, gate_of[:, None, :], jnp.zeros((), jnp.bfloat16))
     one_hot = picks.astype(jnp.bfloat16)
     piece = capacity // CHUNKS
+    me = lax.axis_index("expert")
     summed = None
     for k in range(CHUNKS):
         part = jnp.einsum(
@@ -46,11 +47,24 @@
         ).astype(jnp.bfloat16)
         arrived = lax.all_to_all(part, "expert", split_axis=0, concat_axis=0, tiled=True)
         response = expert_block(arrived, w_first, w_second)
-        returned = lax.all_to_all(response, "expert", split_axis=0, concat_axis=0, tiled=True)
-        weights = mixing[:, k * piece:(k + 1) * piece].reshape(-1, tok_rows)
-        contrib = jnp.dot(
-            weights.T, returned.reshape(-1, features), preferred_element_type=jnp.float32
-        )
+        weights = mixing[:, k * piece:(k + 1) * piece]
+        if k == 0:
+            contrib = None
+            for shift in range(experts):
+                sent = lax.dynamic_index_in_dim(response, (me + shift) % experts, 0, keepdims=False)
+                if shift:
+                    perm = [(i, (i + shift) % experts) for i in range(experts)]
+                    sent = lax.ppermute(sent, "expert", perm)
+                w = lax.dynamic_index_in_dim(weights, (me - shift) % experts, 0, keepdims=False)
+                c = jnp.dot(w.T, sent, preferred_element_type=jnp.float32)
+                contrib = c if contrib is None else contrib + c
+        else:
+            returned = lax.all_to_all(response, "expert", split_axis=0, concat_axis=0, tiled=True)
+            contrib = jnp.dot(
+                weights.reshape(-1, tok_rows).T,
+                returned.reshape(-1, features),
+                preferred_element_type=jnp.float32,
+            )
         summed = contrib if summed is None else summed + contrib
     return summed.astype(jnp.bfloat16)
 

time: 192 us -> 244 us (1.27)
  starting transfers between devices: 21.9 us -> 53.9 us
  matrix products: 54.6 us -> 82.8 us
  waiting for transfers between devices: 113 us -> 97.9 us
  local copies, waits for them, and re-layouts: 0.47 us -> 5.9 us
    all_to_all x2 -> x1, waiting for transfers between devices: 55.9 us -> 0.01 us  [shards(): lax.all_to_all(response, 'expert', split_axis=0, concat_axis=0, tiled=True)]
    ppermute x0 -> x15, starting transfers between devices: none -> 36.6 us  [shards(): sent = lax.ppermute(sent, 'expert', perm)]
    ppermute x0 -> x15, waiting for transfers between devices: none -> 35.2 us  [shards(): sent = lax.ppermute(sent, 'expert', perm)]
    dot_general x2 -> x17, matrix products: 5.87 us -> 33.8 us  [the longest x16 31.2 us: shards(): c = jnp.dot(w.T, sent, preferred_element_type=jnp.float32)]
    all_to_all x2, waiting for transfers between devices: 56.8 us -> 62.7 us  [shards(): lax.all_to_all(part, 'expert', split_axis=0, concat_axis=0, tiled=True)]
    all_to_all x2 -> x1, starting transfers between devices: 9.26 us -> 4.48 us  [shards(): lax.all_to_all(response, 'expert', split_axis=0, concat_axis=0, tiled=True)]
    unnamed x10 -> x28, local copies, waits for them, and re-layouts: 0.41 us -> 4.66 us
  transfers between devices with their start and end apart: 4 -> 18, of which waited for: 4 -> 6; matrix products, arithmetic and copies ran while one was open for 26% -> 22% of each run, Pallas kernels for 0% -> 0%
where the time goes in v8:
time: 244 us; the launch traced here: 243 us
  waiting for transfers between devices  97.9 us (40%)
  matrix products  82.8 us (34%)
  starting transfers between devices  53.9 us (22%)
  local copies, waits for them, and re-layouts  5.9 us (2%)
    all_to_all x2, waiting for transfers between devices, shards(): lax.all_to_all(part, 'expert', split_axis=0, concat_axis=0, tiled=True)  62.7 us
    ppermute x15, starting transfers between devices, shards(): sent = lax.ppermute(sent, 'expert', perm)  36.6 us
    ppermute x15, waiting for transfers between devices, shards(): sent = lax.ppermute(sent, 'expert', perm)  35.2 us
    dot_general x16, matrix products, shards(): c = jnp.dot(w.T, sent, preferred_element_type=jnp.float32)  31.2 us
    dot_general x2, matrix products, expert_block(): projected = jnp.dot(flat, w_first, preferred_element_type=jnp.float32)  26.8 us
    dot_general x2, matrix products, expert_block(): jnp.dot(intermediate_activation, w_second, preferred_element_type=jnp.flo...  17 us
    all_to_all x2, starting transfers between devices, shards(): lax.all_to_all(part, 'expert', split_axis=0, concat_axis=0, tiled=True)  12.8 us
    dot_general x2, matrix products, shards(): jnp.einsum('ect,td->ecd', one_hot[:, k * piece:(k + 1) * piece], tokens,...  5.23 us
  transfers between devices with their start and end apart: 18, of which 6 were waited for; matrix products, arithmetic and copies ran while one was open for 22% of the time, Pallas kernels for 0%

profile of v8, /device:TPU:0, one launch (start us, length us, event | category | flops | bytes accessed | tf_op | source)
XLA Modules:
  0.0 242.9 jit_solution(11241914682271005675)
XLA Ops:
  0.0 1.0 iota_compare_fusion
  1.0 0.2 copy-done
  1.2 2.6 %convolution_convert_fusion = bf16[16,32,3072]{2,1,0:T(8,128)(2,1)} fusion(bf16[128,3072]{1,0:T(8,128)(2,1)S(1)} %copy-done, pred[16,64,128]{2,1,0:T(32,128)(4,1)S(1)} %iota_compare_fusion), kind=kOutput, calls=%fused_computation.8 | convolution fusion | flops 404226048 | bytes 3997696 | tf_op jit(solution)/shard_map/ect,td->ecd/dot_general | solution.py:42
  3.8 8.2 %all-to-all-start.1 = ((bf16[16,32,3072]{2,1,0:T(8,128)(2,1)}), bf16[16,32,3072]{2,1,0:T(8,128)(2,1)}, u32[]{:S(2)}, u32[]{:S(2)}) async-start(bf16[16,32,3072]{2,1,0:T(8,128)(2,1)} %convolution_convert_fusion), calls=%async_computation.1 | async-start | bytes 6291456 | tf_op jit(solution)/shard_map/all_to_all | solution.py:48
  11.9 2.6 %convolution_convert_fusion.1 = bf16[16,32,3072]{2,1,0:T(8,128)(2,1)} fusion(bf16[128,3072]{1,0:T(8,128)(2,1)S(1)} %copy-done, pred[16,64,128]{2,1,0:T(32,128)(4,1)S(1)} %iota_compare_fusion), kind=kOutput, calls=%fused_computation.9 | convolution fusion | flops 404226048 | bytes 3997696 | tf_op jit(solution)/shard_map/ect,td->ecd/dot_general | solution.py:42
  14.6 38.0 %all-to-all-done.1 = bf16[16,32,3072]{2,1,0:T(8,128)(2,1)} async-done(((bf16[16,32,3072]{2,1,0:T(8,128)(2,1)}), bf16[16,32,3072]{2,1,0:T(8,128)(2,1)}, u32[]{:S(2)}, u32[]{:S(2)}) %all-to-all-start.1) | async-done | bytes 3145760 | tf_op jit(solution)/shard_map/all_to_all | solution.py:48
  52.6 4.7 %all-to-all-start = ((bf16[16,32,3072]{2,1,0:T(8,128)(2,1)}), bf16[16,32,3072]{2,1,0:T(8,128)(2,1)}, u32[]{:S(2)}, u32[]{:S(2)}) async-start(bf16[16,32,3072]{2,1,0:T(8,128)(2,1)} %convolution_convert_fusion.1), calls=%async_computation | async-start | bytes 6291456 | tf_op jit(solution)/shard_map/all_to_all | solution.py:48
  57.7 0.1 copy.12
  57.8 0.1 copy.7
  58.0 0.4 select_reduce_fusion
  58.3 0.1 copy.11
  58.4 0.2 broadcast_select_fusion
  58.8 14.2 %fusion = f32[512,2560]{1,0:T(8,128)} fusion(bf16[512,3072]{1,0:T(8,128)(2,1)} %bitcast.39, bf16[1,3072,2560]{2,1,0:T(8,128)(2,1)} %param.10), kind=kOutput, calls=%fused_computation | convolution fusion | flops 8053063680 | bytes 24117248 | tf_op jit(solution)/shard_map/dot_general | solution.py:13
  73.0 24.7 %all-to-all-done = bf16[16,32,3072]{2,1,0:T(8,128)(2,1)} async-done(((bf16[16,32,3072]{2,1,0:T(8,128)(2,1)}), bf16[16,32,3072]{2,1,0:T(8,128)(2,1)}, u32[]{:S(2)}, u32[]{:S(2)}) %all-to-all-start) | async-done | bytes 3145760 | tf_op jit(solution)/shard_map/all_to_all | solution.py:48
  97.7 12.6 %fusion.2 = f32[512,2560]{1,0:T(8,128)S(1)} fusion(bf16[512,3072]{1,0:T(8,128)(2,1)} %bitcast.4, bf16[1,3072,2560]{2,1,0:T(8,128)(2,1)} %param.10), kind=kOutput, calls=%fused_computation.2 | convolution fusion | flops 8053063680 | bytes 24117248 | tf_op jit(solution)/shard_map/dot_general | solution.py:13
  110.3 7.9 %fusion.8 = bf16[512,3072]{1,0:T(8,128)(2,1)S(1)} fusion(bf16[1,1280,3072]{2,1,0:T(8,128)(2,1)} %param.11, f32[512,2560]{1,0:T(8,128)S(1)} %fusion.2), kind=kOutput, calls=%fused_computation.10 | convolution fusion | flops 4032036864 | bytes 16252928 | tf_op jit(solution)/shard_map/dot_general | solution.py:17
  118.2 1.2 dynamic-slice_bitcast_fusion.13
  119.4 1.1 copy-done.5
  120.5 0.0 collective-permute-start.14
  120.5 1.8 copy-done.12
  122.3 9.1 %fusion.11 = bf16[512,3072]{1,0:T(8,128)(2,1)} fusion(bf16[1,1280,3072]{2,1,0:T(8,128)(2,1)} %param.11, f32[512,2560]{1,0:T(8,128)S(1)} %copy-done.12), kind=kOutput, calls=%fused_computation.11 | convolution fusion | flops 4032036864 | bytes 16252928 | tf_op jit(solution)/shard_map/dot_general | solution.py:17
  131.4 4.5 %all-to-all-start.2 = ((bf16[16,32,3072]{2,1,0:T(8,128)(2,1)}), bf16[16,32,3072]{2,1,0:T(8,128)(2,1)}, u32[]{:S(2)}, u32[]{:S(2)}) async-start(bf16[16,32,3072]{2,1,0:T(8,128)(2,1)} %bitcast.128), calls=%async_computation.2 | async-start | bytes 6291456 | tf_op jit(solution)/shard_map/all_to_all | solution.py:62
  135.9 5.5 %collective-permute-start.13 = (bf16[32,3072]{1,0:T(8,128)(2,1)}, bf16[32,3072]{1,0:T(8,128)(2,1)S(1)}, u32[]{:S(2)}, u32[]{:S(2)}) collective-permute-start(bf16[32,3072]{1,0:T(8,128)(2,1)} %get-tuple-element.7), channel_id=1, source_target_pairs={{0,14},{1,15},{2,0},{3,1},{4,2},{5,3},{6,4},{7,5},{8,6},{9,7},{10,... | collective-permute-start | bytes 589832 | tf_op jit(solution)/shard_map/ppermute | solution.py:57
  141.4 0.3 collective-permute-start.12
  141.7 0.5 collective-permute-start.11
  142.2 2.9 %collective-permute-start.10 = (bf16[32,3072]{1,0:T(8,128)(2,1)}, bf16[32,3072]{1,0:T(8,128)(2,1)S(1)}, u32[]{:S(2)}, u32[]{:S(2)}) collective-permute-start(bf16[32,3072]{1,0:T(8,128)(2,1)} %get-tuple-element.10), channel_id=1, source_target_pairs={{0,11},{1,12},{2,13},{3,14},{4,15},{5,0},{6,1},{7,2},{8,3},{9,4},{... | collective-permute-start | bytes 589832 | tf_op jit(solution)/shard_map/ppermute | solution.py:57
  145.1 1.3 fusion.39
  146.4 0.0 collective-permute-done.14
  146.5 0.7 copy-done.8
  147.1 2.7 %collective-permute-start.9 = (bf16[32,3072]{1,0:T(8,128)(2,1)}, bf16[32,3072]{1,0:T(8,128)(2,1)S(1)}, u32[]{:S(2)}, u32[]{:S(2)}) collective-permute-start(bf16[32,3072]{1,0:T(8,128)(2,1)} %get-tuple-element.11), channel_id=1, source_target_pairs={{0,10},{1,11},{2,12},{3,13},{4,14},{5,15},{6,0},{7,1},{8,2},{9,3},... | collective-permute-start | bytes 589832 | tf_op jit(solution)/shard_map/ppermute | solution.py:57
  149.9 1.3 fusion.43
  151.2 28.7 %collective-permute-done.13 = bf16[32,3072]{1,0:T(8,128)(2,1)S(1)} collective-permute-done((bf16[32,3072]{1,0:T(8,128)(2,1)}, bf16[32,3072]{1,0:T(8,128)(2,1)S(1)}, u32[]{:S(2)}, u32[]{:S(2)}) %collective-permute-start.13) | collective-permute-done | bytes 196640 | tf_op jit(solution)/shard_map/ppermute | solution.py:57
  179.9 1.4 collective-permute-start.8
  181.3 1.5 fusion.45
  182.9 0.3 collective-permute-done.12
  183.2 2.7 %collective-permute-start.7 = (bf16[32,3072]{1,0:T(8,128)(2,1)S(1)}, bf16[32,3072]{1,0:T(8,128)(2,1)S(1)}, u32[]{:S(2)}, u32[]{:S(2)}) collective-permute-start(bf16[32,3072]{1,0:T(8,128)(2,1)S(1)} %copy-done.6), channel_id=1, source_target_pairs={{0,8},{1,9},{2,10},{3,11},{4,12},{5,13},{6,14},{7,15},{8,0},{9,1},... | collective-permute-start | bytes 589832 | tf_op jit(solution)/shard_map/ppermute | solution.py:57
  185.9 1.6 fusion.47
  187.5 10.6 %collective-permute-start.6 = (bf16[32,3072]{1,0:T(8,128)(2,1)S(1)}, bf16[32,3072]{1,0:T(8,128)(2,1)S(1)}, u32[]{:S(2)}, u32[]{:S(2)}) collective-permute-start(bf16[32,3072]{1,0:T(8,128)(2,1)S(1)} %get-tuple-element.14), channel_id=1, source_target_pairs={{0,7},{1,8},{2,9},{3,10},{4,11},{5,12},{6,13},{7,14},{8,15},{9,0},... | collective-permute-start | bytes 589832 | tf_op jit(solution)/shard_map/ppermute | solution.py:57
  198.1 1.6 fusion.49
  199.7 1.6 collective-permute-start.5
  201.2 1.6 fusion.51
  202.8 0.0 collective-permute-done.9
  202.8 2.0 collective-permute-start.4
  204.8 1.5 fusion.53
  206.4 0.0 collective-permute-done.8
  206.4 1.5 collective-permute-start.3
  207.9 1.6 fusion.55
  209.5 2.0 collective-permute-start.2
  211.5 1.5 fusion.57
  213.0 0.0 collective-permute-done.6
  213.0 0.2 collective-permute-start
  213.2 1.6 fusion.59
  214.8 2.5 %collective-permute-start.1 = (bf16[32,3072]{1,0:T(8,128)(2,1)S(1)}, bf16[32,3072]{1,0:T(8,128)(2,1)S(1)}, u32[]{:S(2)}, u32[]{:S(2)}) collective-permute-start(bf16[32,3072]{1,0:T(8,128)(2,1)S(1)} %get-tuple-element.5), channel_id=1, source_target_pairs={{0,2},{1,3},{2,4},{3,5},{4,6},{5,7},{6,8},{7,9},{8,10},{9,11},{10,... | collective-permute-start | bytes 589832 | tf_op jit(solution)/shard_map/ppermute | solution.py:57
  217.4 1.5 fusion.61
  218.9 1.6 fusion.63
  220.5 6.1 %collective-permute-done.3 = bf16[32,3072]{1,0:T(8,128)(2,1)S(1)} collective-permute-done((bf16[32,3072]{1,0:T(8,128)(2,1)S(1)}, bf16[32,3072]{1,0:T(8,128)(2,1)S(1)}, u32[]{:S(2)}, u32[]{:S(2)}) %collective-permute-start.3) | collective-permute-done | bytes 196640 | tf_op jit(solution)/shard_map/ppermute | solution.py:57
  226.5 1.6 fusion.65
  228.1 0.1 collective-permute-done.2
  228.2 1.6 fusion.67
  229.8 1.6 convolution_add_fusion.1
  231.4 2.6 %convolution_bitcast_fusion = f32[128,3072]{1,0:T(8,128)S(1)} fusion(bf16[16,32,3072]{2,1,0:T(8,128)(2,1)} %all-to-all-done.2, bf16[16,64,128]{2,1,0:T(8,128)(2,1)S(1)} %broadcast_select_fusion), kind=kOutput, calls=%fused_computation.12 | convolution fusion | flops 402653184 | bytes 4849664 | tf_op jit(solution)/shard_map/dot_general | solution.py:63
  234.1 0.1 copy-done.3
  234.3 0.5 copy-done.4
  234.7 8.2 %fusion.28 = bf16[128,3072]{1,0:T(8,128)(2,1)} fusion(f32[128,3072]{1,0:T(8,128)S(1)} %convolution_bitcast_fusion, f32[128,3072]{1,0:T(8,128)S(1)} %fusion.43, f32[128,3072]{1,0:T(8,128)S(1)} %copy-done.2, f32[128,3072]{1,0:T(8,128)S(1)} %copy-done.3, f32[128,3072]{1,0:T(8,128)S(1)} %copy-done.4, f32[128,3072]{1,0:T(8,128)} %fusion.51, ...), kind=kOutput, calls=%fused_computation.29 | convolution fusion | flops 31457280 | bytes 24584196 | tf_op jit(solution)/shard_map/dot_general | solution.py:59
  (29 shorter events, 0.1 us)
Async XLA Ops:
  0.0 1.1 copy-start
  3.8 48.8 %all-to-all-start.1 = ((bf16[16,32,3072]{2,1,0:T(8,128)(2,1)}), bf16[16,32,3072]{2,1,0:T(8,128)(2,1)}, u32[]{:S(2)}, u32[]{:S(2)}) async-start(bf16[16,32,3072]{2,1,0:T(8,128)(2,1)} %convolution_convert_fusion), calls=%async_computation.1 | async-start | bytes 6291456 | tf_op jit(solution)/shard_map/all_to_all | solution.py:48
  14.6 43.1 %copy-start.10 = (f32[128,4]{0,1:T(4,128)S(1)}, f32[128,4]{0,1:T(4,128)}, u32[]{:S(2)}) copy-start(f32[128,4]{0,1:T(4,128)} %param.8) | copy-start | bytes 6148
  14.6 43.3 %copy-start.11 = (s32[128,4]{0,1:T(4,128)S(1)}, s32[128,4]{0,1:T(4,128)}, u32[]{:S(2)}) copy-start(s32[128,4]{0,1:T(4,128)} %param.7) | copy-start | bytes 6148
  14.6 43.8 %copy-start.9 = (s32[1,16,64]{2,1,0:T(8,128)S(1)}, s32[1,16,64]{2,1,0:T(8,128)}, u32[]{:S(2)}) copy-start(s32[1,16,64]{2,1,0:T(8,128)} %param.9) | copy-start | bytes 12292
  52.6 45.1 %all-to-all-start = ((bf16[16,32,3072]{2,1,0:T(8,128)(2,1)}), bf16[16,32,3072]{2,1,0:T(8,128)(2,1)}, u32[]{:S(2)}, u32[]{:S(2)}) async-start(bf16[16,32,3072]{2,1,0:T(8,128)(2,1)} %convolution_convert_fusion.1), calls=%async_computation | async-start | bytes 6291456 | tf_op jit(solution)/shard_map/all_to_all | solution.py:48
  118.2 2.3 copy-start.5
  118.2 4.1 %copy-start.12 = (f32[512,2560]{1,0:T(8,128)S(1)}, f32[512,2560]{1,0:T(8,128)}, u32[]{:S(2)}) copy-start(f32[512,2560]{1,0:T(8,128)} %fusion) | copy-start | bytes 15728644
  120.5 25.9 %collective-permute-start.14 = (bf16[32,3072]{1,0:T(8,128)(2,1)S(1)}, bf16[32,3072]{1,0:T(8,128)(2,1)S(1)}, u32[]{:S(2)}, u32[]{:S(2)}) collective-permute-start(bf16[32,3072]{1,0:T(8,128)(2,1)S(1)} %get-tuple-element.6), channel_id=1, source_target_pairs={{0,15},{1,0},{2,1},{3,2},{4,3},{5,4},{6,5},{7,6},{8,7},{9,8},{10,9... | collective-permute-start | bytes 589832 | tf_op jit(solution)/shard_map/ppermute | solution.py:57
  131.4 100.0 %all-to-all-start.2 = ((bf16[16,32,3072]{2,1,0:T(8,128)(2,1)}), bf16[16,32,3072]{2,1,0:T(8,128)(2,1)}, u32[]{:S(2)}, u32[]{:S(2)}) async-start(bf16[16,32,3072]{2,1,0:T(8,128)(2,1)} %bitcast.128), calls=%async_computation.2 | async-start | bytes 6291456 | tf_op jit(solution)/shard_map/all_to_all | solution.py:62
  135.9 44.0 %collective-permute-start.13 = (bf16[32,3072]{1,0:T(8,128)(2,1)}, bf16[32,3072]{1,0:T(8,128)(2,1)S(1)}, u32[]{:S(2)}, u32[]{:S(2)}) collective-permute-start(bf16[32,3072]{1,0:T(8,128)(2,1)} %get-tuple-element.7), channel_id=1, source_target_pairs={{0,14},{1,15},{2,0},{3,1},{4,2},{5,3},{6,4},{7,5},{8,6},{9,7},{10,... | collective-permute-start | bytes 589832 | tf_op jit(solution)/shard_map/ppermute | solution.py:57
  141.4 41.8 %collective-permute-start.12 = (bf16[32,3072]{1,0:T(8,128)(2,1)}, bf16[32,3072]{1,0:T(8,128)(2,1)S(1)}, u32[]{:S(2)}, u32[]{:S(2)}) collective-permute-start(bf16[32,3072]{1,0:T(8,128)(2,1)} %get-tuple-element.8), channel_id=1, source_target_pairs={{0,13},{1,14},{2,15},{3,0},{4,1},{5,2},{6,3},{7,4},{8,5},{9,6},{10... | collective-permute-start | bytes 589832 | tf_op jit(solution)/shard_map/ppermute | solution.py:57
  141.7 45.8 %collective-permute-start.11 = (bf16[32,3072]{1,0:T(8,128)(2,1)}, bf16[32,3072]{1,0:T(8,128)(2,1)S(1)}, u32[]{:S(2)}, u32[]{:S(2)}) collective-permute-start(bf16[32,3072]{1,0:T(8,128)(2,1)} %get-tuple-element.9), channel_id=1, source_target_pairs={{0,12},{1,13},{2,14},{3,15},{4,0},{5,1},{6,2},{7,3},{8,4},{9,5},{1... | collective-permute-start | bytes 589832 | tf_op jit(solution)/shard_map/ppermute | solution.py:57
  142.2 37.7 %copy-start.7 = (bf16[32,3072]{1,0:T(8,128)(2,1)S(1)}, bf16[32,3072]{1,0:T(8,128)(2,1)}, u32[]{:S(2)}) copy-start(bf16[32,3072]{1,0:T(8,128)(2,1)} %get-tuple-element.12) | copy-start | bytes 589828
  142.2 57.5 %collective-permute-start.10 = (bf16[32,3072]{1,0:T(8,128)(2,1)}, bf16[32,3072]{1,0:T(8,128)(2,1)S(1)}, u32[]{:S(2)}, u32[]{:S(2)}) collective-permute-start(bf16[32,3072]{1,0:T(8,128)(2,1)} %get-tuple-element.10), channel_id=1, source_target_pairs={{0,11},{1,12},{2,13},{3,14},{4,15},{5,0},{6,1},{7,2},{8,3},{9,4},{... | collective-permute-start | bytes 589832 | tf_op jit(solution)/shard_map/ppermute | solution.py:57
  146.4 0.7 copy-start.8
  147.1 36.0 %copy-start.6 = (bf16[32,3072]{1,0:T(8,128)(2,1)S(1)}, bf16[32,3072]{1,0:T(8,128)(2,1)}, u32[]{:S(2)}) copy-start(bf16[32,3072]{1,0:T(8,128)(2,1)} %get-tuple-element.13) | copy-start | bytes 589828
  147.1 55.7 %collective-permute-start.9 = (bf16[32,3072]{1,0:T(8,128)(2,1)}, bf16[32,3072]{1,0:T(8,128)(2,1)S(1)}, u32[]{:S(2)}, u32[]{:S(2)}) collective-permute-start(bf16[32,3072]{1,0:T(8,128)(2,1)} %get-tuple-element.11), channel_id=1, source_target_pairs={{0,10},{1,11},{2,12},{3,13},{4,14},{5,15},{6,0},{7,1},{8,2},{9,3},... | collective-permute-start | bytes 589832 | tf_op jit(solution)/shard_map/ppermute | solution.py:57
  179.9 26.5 %collective-permute-start.8 = (bf16[32,3072]{1,0:T(8,128)(2,1)S(1)}, bf16[32,3072]{1,0:T(8,128)(2,1)S(1)}, u32[]{:S(2)}, u32[]{:S(2)}) collective-permute-start(bf16[32,3072]{1,0:T(8,128)(2,1)S(1)} %copy-done.7), channel_id=1, source_target_pairs={{0,9},{1,10},{2,11},{3,12},{4,13},{5,14},{6,15},{7,0},{8,1},{9,2},... | collective-permute-start | bytes 589832 | tf_op jit(solution)/shard_map/ppermute | solution.py:57
  183.2 26.3 %collective-permute-start.7 = (bf16[32,3072]{1,0:T(8,128)(2,1)S(1)}, bf16[32,3072]{1,0:T(8,128)(2,1)S(1)}, u32[]{:S(2)}, u32[]{:S(2)}) collective-permute-start(bf16[32,3072]{1,0:T(8,128)(2,1)S(1)} %copy-done.6), channel_id=1, source_target_pairs={{0,8},{1,9},{2,10},{3,11},{4,12},{5,13},{6,14},{7,15},{8,0},{9,1},... | collective-permute-start | bytes 589832 | tf_op jit(solution)/shard_map/ppermute | solution.py:57
  187.5 25.5 %collective-permute-start.6 = (bf16[32,3072]{1,0:T(8,128)(2,1)S(1)}, bf16[32,3072]{1,0:T(8,128)(2,1)S(1)}, u32[]{:S(2)}, u32[]{:S(2)}) collective-permute-start(bf16[32,3072]{1,0:T(8,128)(2,1)S(1)} %get-tuple-element.14), channel_id=1, source_target_pairs={{0,7},{1,8},{2,9},{3,10},{4,11},{5,12},{6,13},{7,14},{8,15},{9,0},... | collective-permute-start | bytes 589832 | tf_op jit(solution)/shard_map/ppermute | solution.py:57
  199.7 15.2 %collective-permute-start.5 = (bf16[32,3072]{1,0:T(8,128)(2,1)S(1)}, bf16[32,3072]{1,0:T(8,128)(2,1)S(1)}, u32[]{:S(2)}, u32[]{:S(2)}) collective-permute-start(bf16[32,3072]{1,0:T(8,128)(2,1)S(1)} %get-tuple-element.15), channel_id=1, source_target_pairs={{0,6},{1,7},{2,8},{3,9},{4,10},{5,11},{6,12},{7,13},{8,14},{9,15},... | collective-permute-start | bytes 589832 | tf_op jit(solution)/shard_map/ppermute | solution.py:57
  202.8 16.1 %collective-permute-start.4 = (bf16[32,3072]{1,0:T(8,128)(2,1)S(1)}, bf16[32,3072]{1,0:T(8,128)(2,1)S(1)}, u32[]{:S(2)}, u32[]{:S(2)}) collective-permute-start(bf16[32,3072]{1,0:T(8,128)(2,1)S(1)} %get-tuple-element.16), channel_id=1, source_target_pairs={{0,5},{1,6},{2,7},{3,8},{4,9},{5,10},{6,11},{7,12},{8,13},{9,14},{... | collective-permute-start | bytes 589832 | tf_op jit(solution)/shard_map/ppermute | solution.py:57
  206.4 20.2 %collective-permute-start.3 = (bf16[32,3072]{1,0:T(8,128)(2,1)S(1)}, bf16[32,3072]{1,0:T(8,128)(2,1)S(1)}, u32[]{:S(2)}, u32[]{:S(2)}) collective-permute-start(bf16[32,3072]{1,0:T(8,128)(2,1)S(1)} %get-tuple-element.17), channel_id=1, source_target_pairs={{0,4},{1,5},{2,6},{3,7},{4,8},{5,9},{6,10},{7,11},{8,12},{9,13},{1... | collective-permute-start | bytes 589832 | tf_op jit(solution)/shard_map/ppermute | solution.py:57
  209.5 18.7 %collective-permute-start.2 = (bf16[32,3072]{1,0:T(8,128)(2,1)S(1)}, bf16[32,3072]{1,0:T(8,128)(2,1)S(1)}, u32[]{:S(2)}, u32[]{:S(2)}) collective-permute-start(bf16[32,3072]{1,0:T(8,128)(2,1)S(1)} %get-tuple-element.18), channel_id=1, source_target_pairs={{0,3},{1,4},{2,5},{3,6},{4,7},{5,8},{6,9},{7,10},{8,11},{9,12},{10... | collective-permute-start | bytes 589832 | tf_op jit(solution)/shard_map/ppermute | solution.py:57
  213.0 16.8 %collective-permute-start = (bf16[32,3072]{1,0:T(8,128)(2,1)S(1)}, bf16[32,3072]{1,0:T(8,128)(2,1)S(1)}, u32[]{:S(2)}, u32[]{:S(2)}) collective-permute-start(bf16[32,3072]{1,0:T(8,128)(2,1)S(1)} %get-tuple-element.19), channel_id=1, source_target_pairs={{0,1},{1,2},{2,3},{3,4},{4,5},{5,6},{6,7},{7,8},{8,9},{9,10},{10,1... | collective-permute-start | bytes 589832 | tf_op jit(solution)/shard_map/ppermute | solution.py:57
  214.8 19.2 %collective-permute-start.1 = (bf16[32,3072]{1,0:T(8,128)(2,1)S(1)}, bf16[32,3072]{1,0:T(8,128)(2,1)S(1)}, u32[]{:S(2)}, u32[]{:S(2)}) collective-permute-start(bf16[32,3072]{1,0:T(8,128)(2,1)S(1)} %get-tuple-element.5), channel_id=1, source_target_pairs={{0,2},{1,3},{2,4},{3,5},{4,6},{5,7},{6,8},{7,9},{8,10},{9,11},{10,... | collective-permute-start | bytes 589832 | tf_op jit(solution)/shard_map/ppermute | solution.py:57
  231.4 2.7 %copy-start.2 = (f32[128,3072]{1,0:T(8,128)S(1)}, f32[128,3072]{1,0:T(8,128)}, u32[]{:S(2)}) copy-start(f32[128,3072]{1,0:T(8,128)} %fusion.45) | copy-start | bytes 4718596
  231.4 2.8 %copy-start.3 = (f32[128,3072]{1,0:T(8,128)S(1)}, f32[128,3072]{1,0:T(8,128)}, u32[]{:S(2)}) copy-start(f32[128,3072]{1,0:T(8,128)} %fusion.47) | copy-start | bytes 4718596
  231.4 3.3 %copy-start.4 = (f32[128,3072]{1,0:T(8,128)S(1)}, f32[128,3072]{1,0:T(8,128)}, u32[]{:S(2)}) copy-start(f32[128,3072]{1,0:T(8,128)} %fusion.49) | copy-start | bytes 4718596
  234.7 8.2 %copy-start.1 = (bf16[128,3072]{1,0:T(8,128)(2,1)S(1)}, bf16[128,3072]{1,0:T(8,128)(2,1)}, u32[]{:S(2)}) copy-start(bf16[128,3072]{1,0:T(8,128)(2,1)} %param.6) | copy-start | bytes 2359300

commit v9 on v6

--- a/solution.py
+++ b/solution.py
@@ -52,11 +52,12 @@
     partner = swap(block, "yh")
     from_below = shift_z(block, 1)
     from_above = shift_z(block, -1)
-    p_below = shift_z(partner, 1)
-    p_above = shift_z(partner, -1)
-    far = jnp.concatenate(
-        [shift_z(from_below[:half], 1), shift_z(from_above[half:], -1)], axis=0
-    )
+    rows = tok_rows + 1
+    up = shift_z(jnp.concatenate([partner, from_below[:half]], axis=0), 1)
+    down = shift_z(jnp.concatenate([partner, from_above[half:]], axis=0), -1)
+    p_below = up[:rows]
+    p_above = down[:rows]
+    far = jnp.concatenate([up[rows:], down[rows:]], axis=0)
     p_far = jnp.concatenate([shift_z(p_below[:half], 1), shift_z(p_above[half:], -1)], axis=0)
 
     chip = zi * n_y + yi

time: 195 us -> 192 us (0.985)
  waiting for transfers between devices: 92.1 us -> 84.4 us
  local copies, waits for them, and re-layouts: 20.5 us -> 23.5 us
    ppermute x8 -> x6, waiting for transfers between devices: 34.4 us -> 16.4 us  [shift_z(): return lax.ppermute(x, 'z', [(i, (i + step) % RING) for i in range(RING)])]
    all_to_all x1, waiting for transfers between devices: 5.79 us -> 16.6 us  [shards(): ret_a = lax.all_to_all(a_abs, ('z', 'yh'), 0, 0, tiled=True)]
    dynamic_update_slice x16, local copies, waits for them, and re-layouts: 12.4 us -> 16.7 us  [place(): into = lax.dynamic_update_slice(into, outs[i:i + 1], (where, 0, 0))]
    ppermute x8 -> x6, starting transfers between devices: 11.3 us -> 10.9 us  [shift_z(): return lax.ppermute(x, 'z', [(i, (i + step) % RING) for i in range(RING)])]
  transfers between devices with their start and end apart: 15 -> 13, of which waited for: 7 -> 6; matrix products, arithmetic and copies ran while one was open for 34% -> 37% of each run, Pallas kernels for 0% -> 0%
where the time goes in v9:
time: 192 us; the launch traced here: 191 us
  waiting for transfers between devices  84.4 us (44%)
  matrix products  54.7 us (28%)
  local copies, waits for them, and re-layouts  23.5 us (12%)
  starting transfers between devices  23.2 us (12%)
  other arithmetic  5.18 us (3%)
    all_to_all x1, waiting for transfers between devices, shards(): ret_b = lax.all_to_all(b_abs, ('z', 'yh'), 0, 0, tiled=True)  36.7 us
    dot_general x4, matrix products, expert_block(): projected = jnp.dot(flat, w_first, preferred_element_type=jnp.float32)  27.7 us
    dynamic_update_slice x16, local copies, waits for them, and re-layouts, place(): into = lax.dynamic_update_slice(into, outs[i:i + 1], (where, 0, 0))  16.7 us
    all_to_all x1, waiting for transfers between devices, shards(): ret_a = lax.all_to_all(a_abs, ('z', 'yh'), 0, 0, tiled=True)  16.6 us
    ppermute x6, waiting for transfers between devices, shift_z(): return lax.ppermute(x, 'z', [(i, (i + step) % RING) for i in range(RING)])  16.4 us
    dot_general x4, matrix products, expert_block(): jnp.dot(intermediate_activation, w_second, preferred_element_type=jnp.flo...  15.5 us
    ppermute x5, waiting for transfers between devices, swap(): return lax.ppermute(x, axis, [(0, 1), (1, 0)])  14.8 us
    ppermute x6, starting transfers between devices, shift_z(): return lax.ppermute(x, 'z', [(i, (i + step) % RING) for i in range(RING)])  10.9 us
  transfers between devices with their start and end apart: 13, of which 6 were waited for; matrix products, arithmetic and copies ran while one was open for 37% of the time, Pallas kernels for 0%

profile of v9, /device:TPU:0, one launch (start us, length us, event | category | flops | bytes accessed | tf_op | source)
XLA Modules:
  0.0 191.5 jit_solution(14994161187719160011)
XLA Ops:
  0.0 0.6 compare_reduce_fusion
  0.6 1.3 convert_select_fusion
  2.0 0.1 reshape.87
  2.1 2.3 %fusion.80 = (bf16[1,129,3072]{2,1,0:T(8,128)(2,1)S(1)}, bf16[129,3072]{1,0:T(8,128)(2,1)}) fusion(bf16[1,1024]{1,0:T(2,128)(2,1)S(1)} %reshape.87, bf16[128,3072]{1,0:T(8,128)(2,1)} %param.8), kind=kLoop, calls=%fused_computation.123 | loop fusion | flops 2377728 | bytes 2373632 | tf_op jit(solution)/shard_map/stack | solution.py:69
  4.3 3.3 %collective-permute-start = (bf16[129,3072]{1,0:T(8,128)(2,1)}, bf16[129,3072]{1,0:T(8,128)(2,1)S(1)}, u32[]{:S(2)}, u32[]{:S(2)}) collective-permute-start(bf16[129,3072]{1,0:T(8,128)(2,1)} %get-tuple-element.46), channel_id=1, source_target_pairs={{0,2},{2,0},{1,3},{3,1},{4,6},{6,4},{5,7},{7,5},{8,10},{10,8},{9,1... | collective-permute-start | bytes 2377736 | tf_op jit(solution)/shard_map/ppermute | solution.py:31
  7.6 4.0 %collective-permute-start.3 = (bf16[129,3072]{1,0:T(8,128)(2,1)}, bf16[129,3072]{1,0:T(8,128)(2,1)S(1)}, u32[]{:S(2)}, u32[]{:S(2)}) collective-permute-start(bf16[129,3072]{1,0:T(8,128)(2,1)} %get-tuple-element.46), channel_id=1, source_target_pairs={{0,12},{4,0},{8,4},{12,8},{1,13},{5,1},{9,5},{13,9},{2,14},{6,2},{... | collective-permute-start | bytes 2377736 | tf_op jit(solution)/shard_map/ppermute | solution.py:27
  11.7 14.8 %collective-permute-done = bf16[129,3072]{1,0:T(8,128)(2,1)S(1)} collective-permute-done((bf16[129,3072]{1,0:T(8,128)(2,1)}, bf16[129,3072]{1,0:T(8,128)(2,1)S(1)}, u32[]{:S(2)}, u32[]{:S(2)}) %collective-permute-start) | collective-permute-done | bytes 792608 | tf_op jit(solution)/shard_map/ppermute | solution.py:31
  26.4 3.1 %collective-permute-done.3 = bf16[129,3072]{1,0:T(8,128)(2,1)S(1)} collective-permute-done((bf16[129,3072]{1,0:T(8,128)(2,1)}, bf16[129,3072]{1,0:T(8,128)(2,1)S(1)}, u32[]{:S(2)}, u32[]{:S(2)}) %collective-permute-start.3) | collective-permute-done | bytes 792608 | tf_op jit(solution)/shard_map/ppermute | solution.py:27
  29.5 3.3 %collective-permute-done.1 = bf16[129,3072]{1,0:T(8,128)(2,1)S(1)} collective-permute-done((bf16[129,3072]{1,0:T(8,128)(2,1)}, bf16[129,3072]{1,0:T(8,128)(2,1)S(1)}, u32[]{:S(2)}, u32[]{:S(2)}) %collective-permute-start.1) | collective-permute-done | bytes 792608 | tf_op jit(solution)/shard_map/ppermute | solution.py:27
  32.9 0.1 reshape.93
  33.0 2.8 %convolution_convert_fusion.1 = bf16[4,2,64,3072]{3,2,1,0:T(8,128)(2,1)S(1)} fusion(bf16[1,129,3072]{2,1,0:T(8,128)(2,1)S(1)} %bitcast.124, bf16[1,129,3072]{2,1,0:T(8,128)(2,1)S(1)} %bitcast.122, bf16[1,129,3072]{2,1,0:T(8,128)(2,1)S(1)} %bitcast.112, bf16[1,129,3072]{2,1,0:T(8,128)(2,1)S(1)} %get-tuple-element.45, s32[4,2,64]{2,1,0:T(2,128)S(1)} %pad_add_fusion), kind=kOutput, calls=%fused_computation.17 | convolution fusion | flops 416874496 | bytes 6318080 | tf_op jit(solution)/shard_map/bjct,btd->bjcd/dot_general | solution.py:81
  35.9 0.2 slice_bitcast_fusion.1
  36.1 0.1 pad_maximum_fusion.10
  36.3 0.1 collective-permute-start.2
  36.4 0.2 pad_maximum_fusion.11
  36.6 3.3 %collective-permute-start.4 = (bf16[194,3072]{1,0:T(8,128)(2,1)S(1)}, bf16[194,3072]{1,0:T(8,128)(2,1)S(1)}, u32[]{:S(2)}, u32[]{:S(2)}) collective-permute-start(bf16[194,3072]{1,0:T(8,128)(2,1)S(1)} %pad_maximum_fusion.11), channel_id=1, source_target_pairs={{0,12},{4,0},{8,4},{12,8},{1,13},{5,1},{9,5},{13,9},{2,14},{6,2},{... | collective-permute-start | bytes 3575816 | tf_op jit(solution)/shard_map/ppermute | solution.py:27
  39.9 5.7 %fusion.6 = f32[256,2560]{1,0:T(8,128)} fusion(bf16[256,3072]{1,0:T(8,128)(2,1)S(1)} %bitcast.125, bf16[1,3072,2560]{2,1,0:T(8,128)(2,1)S(1)} %copy-done.3), kind=kOutput, calls=%fused_computation.6 | convolution fusion | flops 4026531840 | bytes 19922944 | tf_op jit(solution)/shard_map/dot_general | solution.py:16
  45.6 4.1 %fusion.16 = bf16[256,3072]{1,0:T(8,128)(2,1)S(1)} fusion(bf16[1,1280,3072]{2,1,0:T(8,128)(2,1)S(1)} %bitcast.132, f32[256,2560]{1,0:T(8,128)} %fusion.6), kind=kOutput, calls=%fused_computation.18 | convolution fusion | flops 2016018432 | bytes 12058624 | tf_op jit(solution)/shard_map/dot_general | solution.py:20
  49.7 2.0 %broadcast_in_dim.38.clone = bf16[8,64,3072]{2,1,0:T(8,128)(2,1)} broadcast(bf16[]{:T(256)} %constant.158.clone.1), dimensions={} | broadcast | bytes 3145730 | tf_op jit(solution)/shard_map/broadcast_in_dim | solution.py:97
  51.7 0.8 fusion.57
  52.5 0.8 fusion.56
  53.3 0.8 fusion.55
  54.1 0.8 fusion.54
  54.9 10.0 %collective-permute-done.2 = bf16[193,3072]{1,0:T(8,128)(2,1)S(1)} collective-permute-done((bf16[193,3072]{1,0:T(8,128)(2,1)S(1)}, bf16[193,3072]{1,0:T(8,128)(2,1)S(1)}, u32[]{:S(2)}, u32[]{:S(2)}) %collective-permute-start.2) | collective-permute-done | bytes 1185824 | tf_op jit(solution)/shard_map/ppermute | solution.py:27
  64.8 0.1 fusion.81
  64.9 0.1 collective-permute-start.5
  65.1 0.1 fusion.82
  65.2 3.5 %collective-permute-start.6 = (bf16[65,3072]{1,0:T(8,128)(2,1)S(1)}, bf16[65,3072]{1,0:T(8,128)(2,1)S(1)}, u32[]{:S(2)}, u32[]{:S(2)}) collective-permute-start(bf16[65,3072]{1,0:T(8,128)(2,1)S(1)} %get-tuple-element.43), channel_id=1, source_target_pairs={{0,12},{4,0},{8,4},{12,8},{1,13},{5,1},{9,5},{13,9},{2,14},{6,2},{... | collective-permute-start | bytes 1198088 | tf_op jit(solution)/shard_map/ppermute | solution.py:27
  68.7 0.1 pad_maximum_fusion.12
  68.8 5.6 %fusion.2 = f32[256,2560]{1,0:T(8,128)S(1)} fusion(bf16[256,3072]{1,0:T(8,128)(2,1)} %bitcast.25, bf16[1,3072,2560]{2,1,0:T(8,128)(2,1)S(1)} %copy-done.3), kind=kOutput, calls=%fused_computation.2 | convolution fusion | flops 4026531840 | bytes 19922944 | tf_op jit(solution)/shard_map/dot_general | solution.py:16
  74.5 6.7 %fusion.22 = bf16[256,3072]{1,0:T(8,128)(2,1)} fusion(bf16[1,1280,3072]{2,1,0:T(8,128)(2,1)} %param.13, f32[256,2560]{1,0:T(8,128)S(1)} %fusion.2), kind=kOutput, calls=%fused_computation.20 | convolution fusion | flops 2016018432 | bytes 12058624 | tf_op jit(solution)/shard_map/dot_general | solution.py:20
  81.2 0.1 pad_maximum_fusion.13
  81.3 0.1 fusion.70
  81.3 0.1 reshape.94
  81.5 2.8 %convolution_convert_fusion = bf16[4,2,64,3072]{3,2,1,0:T(8,128)(2,1)S(1)} fusion(bf16[1,129,3072]{2,1,0:T(8,128)(2,1)S(1)} %bitcast.114, bf16[1,129,3072]{2,1,0:T(8,128)(2,1)S(1)} %bitcast.116, bf16[1,129,3072]{2,1,0:T(8,128)(2,1)S(1)} %bitcast.120, bf16[1,129,3072]{2,1,0:T(8,128)(2,1)S(1)} %bitcast.118, s32[4,2,64]{2,1,0:T(2,128)S(1)} %pad_add_fusion.1), kind=kOutput, calls=%fused_computation.16 | convolution fusion | flops 416874496 | bytes 6318080 | tf_op jit(solution)/shard_map/bjct,btd->bjcd/dot_general | solution.py:81
  84.3 1.5 slice_bitcast_fusion
  85.8 8.1 %fusion.4 = f32[256,2560]{1,0:T(8,128)S(1)} fusion(bf16[256,3072]{1,0:T(8,128)(2,1)S(1)} %bitcast.126, bf16[1,3072,2560]{2,1,0:T(8,128)(2,1)} %param.12), kind=kOutput, calls=%fused_computation.4 | convolution fusion | flops 4026531840 | bytes 19922944 | tf_op jit(solution)/shard_map/dot_general | solution.py:16
  93.9 2.3 %fusion.19 = bf16[256,3072]{1,0:T(8,128)(2,1)S(1)} fusion(bf16[1,1280,3072]{2,1,0:T(8,128)(2,1)S(1)} %bitcast.134, f32[256,2560]{1,0:T(8,128)S(1)} %fusion.4), kind=kOutput, calls=%fused_computation.19 | convolution fusion | flops 2016018432 | bytes 12058624 | tf_op jit(solution)/shard_map/dot_general | solution.py:20
  96.3 0.6 collective-permute-start.9
  96.9 0.8 fusion.53
  97.7 0.8 fusion.52
  98.4 0.8 fusion.51
  99.2 0.8 fusion.50
  100.0 3.9 %all-to-all-start = ((bf16[8,64,3072]{2,1,0:T(8,128)(2,1)}), bf16[8,64,3072]{2,1,0:T(8,128)(2,1)S(1)}, u32[]{:S(2)}, u32[]{:S(2)}) async-start(bf16[8,64,3072]{2,1,0:T(8,128)(2,1)} %fusion.50), calls=%async_computation | async-start | bytes 6291456 | tf_op jit(solution)/shard_map/all_to_all | solution.py:105
  103.9 2.1 %broadcast_in_dim.38.clone.1 = bf16[8,64,3072]{2,1,0:T(8,128)(2,1)} broadcast(bf16[]{:T(256)} %constant.158.clone.1), dimensions={} | broadcast | bytes 3145730 | tf_op jit(solution)/shard_map/broadcast_in_dim | solution.py:97
  105.9 2.1 %slice_dynamic-update-slice_fusion.7 = bf16[8,64,3072]{2,1,0:T(8,128)(2,1)} fusion(bf16[8,64,3072]{2,1,0:T(8,128)(2,1)} %broadcast_in_dim.38.clone.1, s32[]{:T(128)S(6)} %select_n.141, bf16[4,64,3072]{2,1,0:T(8,128)(2,1)} %collective-permute-done.8), kind=kLoop, calls=%fused_computation.64 | loop fusion | bytes 786436 | tf_op jit(solution)/shard_map/dynamic_update_slice | solution.py:89
  108.0 8.3 %fusion = f32[256,2560]{1,0:T(8,128)S(1)} fusion(bf16[256,3072]{1,0:T(8,128)(2,1)} %bitcast.28, bf16[1,3072,2560]{2,1,0:T(8,128)(2,1)} %param.12), kind=kOutput, calls=%fused_computation | convolution fusion | flops 4026531840 | bytes 19922944 | tf_op jit(solution)/shard_map/dot_general | solution.py:16
  116.3 2.3 %fusion.25 = bf16[256,3072]{1,0:T(8,128)(2,1)S(1)} fusion(bf16[1,1280,3072]{2,1,0:T(8,128)(2,1)S(1)} %bitcast.136, f32[256,2560]{1,0:T(8,128)S(1)} %fusion), kind=kOutput, calls=%fused_computation.21 | convolution fusion | flops 2016018432 | bytes 12058624 | tf_op jit(solution)/shard_map/dot_general | solution.py:20
  118.7 0.1 collective-permute-start.10
  118.8 1.8 slice_dynamic-update-slice_fusion.6
  120.5 1.8 slice_dynamic-update-slice_fusion.5
  122.3 1.8 slice_dynamic-update-slice_fusion.4
  124.1 0.8 slice_dynamic-update-slice_fusion.3
  124.9 0.8 slice_dynamic-update-slice_fusion.2
  125.6 0.8 slice_dynamic-update-slice_fusion.1
  126.4 0.8 slice_dynamic-update-slice_fusion
  127.2 16.6 %all-to-all-done = bf16[8,64,3072]{2,1,0:T(8,128)(2,1)S(1)} async-done(((bf16[8,64,3072]{2,1,0:T(8,128)(2,1)}), bf16[8,64,3072]{2,1,0:T(8,128)(2,1)S(1)}, u32[]{:S(2)}, u32[]{:S(2)}) %all-to-all-start) | async-done | bytes 3145760 | tf_op jit(solution)/shard_map/all_to_all | solution.py:105
  143.8 4.5 %all-to-all-start.1 = ((bf16[8,64,3072]{2,1,0:T(8,128)(2,1)}), bf16[8,64,3072]{2,1,0:T(8,128)(2,1)}, u32[]{:S(2)}, u32[]{:S(2)}) async-start(bf16[8,64,3072]{2,1,0:T(8,128)(2,1)} %slice_dynamic-update-slice_fusion), calls=%async_computation.1 | async-start | bytes 6291456 | tf_op jit(solution)/shard_map/all_to_all | solution.py:110
  148.2 0.1 copy.18
  148.3 0.1 copy.9
  148.5 0.4 select_reduce_fusion
  149.0 1.9 convolution_bitcast_fusion.1
  150.8 36.7 %all-to-all-done.1 = bf16[8,64,3072]{2,1,0:T(8,128)(2,1)} async-done(((bf16[8,64,3072]{2,1,0:T(8,128)(2,1)}), bf16[8,64,3072]{2,1,0:T(8,128)(2,1)}, u32[]{:S(2)}, u32[]{:S(2)}) %all-to-all-start.1) | async-done | bytes 3145760 | tf_op jit(solution)/shard_map/all_to_all | solution.py:110
  187.5 3.9 %fusion.29 = bf16[128,3072]{1,0:T(8,128)(2,1)} fusion(f32[128,3072]{1,0:T(8,128)} %convolution_bitcast_fusion.1, bf16[8,64,3072]{2,1,0:T(8,128)(2,1)} %all-to-all-done.1, s32[8,64]{1,0:T(8,128)S(1)} %bitcast.130, bf16[8,128]{1,0:T(8,128)(2,1)S(1)} %get-tuple-element.55), kind=kOutput, calls=%fused_computation.25 | convolution fusion | flops 403570688 | bytes 5509120 | tf_op jit(solution)/shard_map/dot_general | solution.py:127
  (46 shorter events, 0.5 us)
Async XLA Ops:
  4.3 22.1 %collective-permute-start = (bf16[129,3072]{1,0:T(8,128)(2,1)}, bf16[129,3072]{1,0:T(8,128)(2,1)S(1)}, u32[]{:S(2)}, u32[]{:S(2)}) collective-permute-start(bf16[129,3072]{1,0:T(8,128)(2,1)} %get-tuple-element.46), channel_id=1, source_target_pairs={{0,2},{2,0},{1,3},{3,1},{4,6},{6,4},{5,7},{7,5},{8,10},{10,8},{9,1... | collective-permute-start | bytes 2377736 | tf_op jit(solution)/shard_map/ppermute | solution.py:31
  7.6 21.9 %collective-permute-start.3 = (bf16[129,3072]{1,0:T(8,128)(2,1)}, bf16[129,3072]{1,0:T(8,128)(2,1)S(1)}, u32[]{:S(2)}, u32[]{:S(2)}) collective-permute-start(bf16[129,3072]{1,0:T(8,128)(2,1)} %get-tuple-element.46), channel_id=1, source_target_pairs={{0,12},{4,0},{8,4},{12,8},{1,13},{5,1},{9,5},{13,9},{2,14},{6,2},{... | collective-permute-start | bytes 2377736 | tf_op jit(solution)/shard_map/ppermute | solution.py:27
  11.6 21.2 %collective-permute-start.1 = (bf16[129,3072]{1,0:T(8,128)(2,1)}, bf16[129,3072]{1,0:T(8,128)(2,1)S(1)}, u32[]{:S(2)}, u32[]{:S(2)}) collective-permute-start(bf16[129,3072]{1,0:T(8,128)(2,1)} %get-tuple-element.46), channel_id=1, source_target_pairs={{0,4},{4,8},{8,12},{12,0},{1,5},{5,9},{9,13},{13,1},{2,6},{6,10},{... | collective-permute-start | bytes 2377736 | tf_op jit(solution)/shard_map/ppermute | solution.py:27
  33.0 6.8 %copy-start.3 = (bf16[1,3072,2560]{2,1,0:T(8,128)(2,1)S(1)}, bf16[1,3072,2560]{2,1,0:T(8,128)(2,1)}, u32[]{:S(2)}) copy-start(bf16[1,3072,2560]{2,1,0:T(8,128)(2,1)} %param.12) | copy-start | bytes 47185924
  36.3 28.5 %collective-permute-start.2 = (bf16[193,3072]{1,0:T(8,128)(2,1)S(1)}, bf16[193,3072]{1,0:T(8,128)(2,1)S(1)}, u32[]{:S(2)}, u32[]{:S(2)}) collective-permute-start(bf16[193,3072]{1,0:T(8,128)(2,1)S(1)} %pad_maximum_fusion.10), channel_id=1, source_target_pairs={{0,4},{4,8},{8,12},{12,0},{1,5},{5,9},{9,13},{13,1},{2,6},{6,10},{... | collective-permute-start | bytes 3557384 | tf_op jit(solution)/shard_map/ppermute | solution.py:27
  36.4 9.2 %slice-start = ((s8[7864320]{0:T(1024)(128)(4,1)}), s8[4194304]{0:T(1024)(128)(4,1)S(1)}, s32[]{:S(2)}) async-start(s8[7864320]{0:T(1024)(128)(4,1)} %bitcast.131), calls=%async_computation.2 | async-start | bytes 8388608
  36.6 28.5 %collective-permute-start.4 = (bf16[194,3072]{1,0:T(8,128)(2,1)S(1)}, bf16[194,3072]{1,0:T(8,128)(2,1)S(1)}, u32[]{:S(2)}, u32[]{:S(2)}) collective-permute-start(bf16[194,3072]{1,0:T(8,128)(2,1)S(1)} %pad_maximum_fusion.11), channel_id=1, source_target_pairs={{0,12},{4,0},{8,4},{12,8},{1,13},{5,1},{9,5},{13,9},{2,14},{6,2},{... | collective-permute-start | bytes 3575816 | tf_op jit(solution)/shard_map/ppermute | solution.py:27
  39.9 29.0 %collective-permute-start.7 = (bf16[4,64,3072]{2,1,0:T(8,128)(2,1)S(1)}, bf16[4,64,3072]{2,1,0:T(8,128)(2,1)}, u32[]{:S(2)}, u32[]{:S(2)}) collective-permute-start(bf16[4,64,3072]{2,1,0:T(8,128)(2,1)S(1)} %get-tuple-element.39), channel_id=1, source_target_pairs={{0,1},{1,0},{2,3},{3,2},{4,5},{5,4},{6,7},{7,6},{8,9},{9,8},{10,11... | collective-permute-start | bytes 4718600 | tf_op jit(solution)/shard_map/ppermute | solution.py:31
  39.9 5.7 %slice-start.1 = ((s8[7864320]{0:T(1024)(128)(4,1)}), s8[3670016]{0:T(1024)(128)(4,1)S(1)}, s32[]{:S(2)}) async-start(s8[7864320]{0:T(1024)(128)(4,1)} %bitcast.131), calls=%async_computation.3 | async-start | bytes 7340032
  64.9 16.3 %collective-permute-start.5 = (bf16[64,3072]{1,0:T(8,128)(2,1)S(1)}, bf16[64,3072]{1,0:T(8,128)(2,1)S(1)}, u32[]{:S(2)}, u32[]{:S(2)}) collective-permute-start(bf16[64,3072]{1,0:T(8,128)(2,1)S(1)} %get-tuple-element.41), channel_id=1, source_target_pairs={{0,4},{4,8},{8,12},{12,0},{1,5},{5,9},{9,13},{13,1},{2,6},{6,10},{... | collective-permute-start | bytes 1179656 | tf_op jit(solution)/shard_map/ppermute | solution.py:27
  65.2 16.0 %collective-permute-start.6 = (bf16[65,3072]{1,0:T(8,128)(2,1)S(1)}, bf16[65,3072]{1,0:T(8,128)(2,1)S(1)}, u32[]{:S(2)}, u32[]{:S(2)}) collective-permute-start(bf16[65,3072]{1,0:T(8,128)(2,1)S(1)} %get-tuple-element.43), channel_id=1, source_target_pairs={{0,12},{4,0},{8,4},{12,8},{1,13},{5,1},{9,5},{13,9},{2,14},{6,2},{... | collective-permute-start | bytes 1198088 | tf_op jit(solution)/shard_map/ppermute | solution.py:27
  81.2 22.7 %collective-permute-start.8 = (bf16[4,64,3072]{2,1,0:T(8,128)(2,1)}, bf16[4,64,3072]{2,1,0:T(8,128)(2,1)}, u32[]{:S(2)}, u32[]{:S(2)}) collective-permute-start(bf16[4,64,3072]{2,1,0:T(8,128)(2,1)} %bitcast.26), channel_id=1, source_target_pairs={{0,1},{1,0},{2,3},{3,2},{4,5},{5,4},{6,7},{7,6},{8,9},{9,8},{10,11... | collective-permute-start | bytes 4718600 | tf_op jit(solution)/shard_map/ppermute | solution.py:31
  84.3 9.6 %slice-start.2 = ((s8[7864320]{0:T(1024)(128)(4,1)}), s8[4194304]{0:T(1024)(128)(4,1)S(1)}, s32[]{:S(2)}) async-start(s8[7864320]{0:T(1024)(128)(4,1)} %bitcast.133), calls=%async_computation.4 | async-start | bytes 8388608
  85.8 8.1 %slice-start.3 = ((s8[7864320]{0:T(1024)(128)(4,1)}), s8[3670016]{0:T(1024)(128)(4,1)S(1)}, s32[]{:S(2)}) async-start(s8[7864320]{0:T(1024)(128)(4,1)} %bitcast.133), calls=%async_computation.5 | async-start | bytes 7340032
  96.3 11.7 %collective-permute-start.9 = (bf16[4,64,3072]{2,1,0:T(8,128)(2,1)}, bf16[4,64,3072]{2,1,0:T(8,128)(2,1)}, u32[]{:S(2)}, u32[]{:S(2)}) collective-permute-start(bf16[4,64,3072]{2,1,0:T(8,128)(2,1)} %get-tuple-element.37), channel_id=1, source_target_pairs={{0,1},{1,0},{2,3},{3,2},{4,5},{5,4},{6,7},{7,6},{8,9},{9,8},{10,11... | collective-permute-start | bytes 4718600 | tf_op jit(solution)/shard_map/ppermute | solution.py:31
  100.0 43.8 %all-to-all-start = ((bf16[8,64,3072]{2,1,0:T(8,128)(2,1)}), bf16[8,64,3072]{2,1,0:T(8,128)(2,1)S(1)}, u32[]{:S(2)}, u32[]{:S(2)}) async-start(bf16[8,64,3072]{2,1,0:T(8,128)(2,1)} %fusion.50), calls=%async_computation | async-start | bytes 6291456 | tf_op jit(solution)/shard_map/all_to_all | solution.py:105
  103.9 12.4 %slice-start.4 = ((s8[7864320]{0:T(1024)(128)(4,1)}), s8[4194304]{0:T(1024)(128)(4,1)S(1)}, s32[]{:S(2)}) async-start(s8[7864320]{0:T(1024)(128)(4,1)} %bitcast.135), calls=%async_computation.6 | async-start | bytes 8388608
  108.0 8.3 %slice-start.5 = ((s8[7864320]{0:T(1024)(128)(4,1)}), s8[3670016]{0:T(1024)(128)(4,1)S(1)}, s32[]{:S(2)}) async-start(s8[7864320]{0:T(1024)(128)(4,1)} %bitcast.135), calls=%async_computation.7 | async-start | bytes 7340032
  118.7 5.4 %collective-permute-start.10 = (bf16[4,64,3072]{2,1,0:T(8,128)(2,1)S(1)}, bf16[4,64,3072]{2,1,0:T(8,128)(2,1)S(1)}, u32[]{:S(2)}, u32[]{:S(2)}) collective-permute-start(bf16[4,64,3072]{2,1,0:T(8,128)(2,1)S(1)} %bitcast.137), channel_id=1, source_target_pairs={{0,1},{1,0},{2,3},{3,2},{4,5},{5,4},{6,7},{7,6},{8,9},{9,8},{10,11... | collective-permute-start | bytes 4718600 | tf_op jit(solution)/shard_map/ppermute | solution.py:31
  127.2 21.0 %copy-start.1 = (f32[128,4]{0,1:T(4,128)S(1)}, f32[128,4]{0,1:T(4,128)}, u32[]{:S(2)}) copy-start(f32[128,4]{0,1:T(4,128)} %param.10) | copy-start | bytes 6148
  127.2 21.1 %copy-start.2 = (s32[128,4]{0,1:T(4,128)S(1)}, s32[128,4]{0,1:T(4,128)}, u32[]{:S(2)}) copy-start(s32[128,4]{0,1:T(4,128)} %param.9) | copy-start | bytes 6148
  127.2 21.7 %copy-start = (s32[1,16,64]{2,1,0:T(8,128)S(1)}, s32[1,16,64]{2,1,0:T(8,128)}, u32[]{:S(2)}) copy-start(s32[1,16,64]{2,1,0:T(8,128)} %param.11) | copy-start | bytes 12292
  143.8 43.8 %all-to-all-start.1 = ((bf16[8,64,3072]{2,1,0:T(8,128)(2,1)}), bf16[8,64,3072]{2,1,0:T(8,128)(2,1)}, u32[]{:S(2)}, u32[]{:S(2)}) async-start(bf16[8,64,3072]{2,1,0:T(8,128)(2,1)} %slice_dynamic-update-slice_fusion), calls=%async_computation.1 | async-start | bytes 6291456 | tf_op jit(solution)/shard_map/all_to_all | solution.py:110

commit v10 on v9

--- a/solution.py
+++ b/solution.py
@@ -93,7 +93,6 @@
     late = [(2, 0, far), (2, 1, p_far), (1, 1, p_above), (3, 1, p_below)]
     mine_1, got_1 = slots_of(early)
     out_m1 = expert_block(mine_1, w_first, w_second)
-    out_g1 = expert_block(got_1, w_first, w_second)
     empty = jnp.zeros((blocks, capacity, features), jnp.bfloat16)
     a_part = place(empty, early, out_m1)
     late_arrs = [arr for _, _, arr in late]
@@ -103,7 +102,8 @@
     out_m2 = expert_block(mine_2, w_first, w_second)
     a_abs = place(a_part, late, out_m2)
     ret_a = lax.all_to_all(a_abs, ("z", "yh"), 0, 0, tiled=True)
-    a_abs, got_2 = lax.optimization_barrier((a_abs, got_2))
+    a_abs, got_1, got_2 = lax.optimization_barrier((a_abs, got_1, got_2))
+    out_g1 = expert_block(got_1, w_first, w_second)
     out_g2 = expert_block(got_2, w_first, w_second)
     b_abs = place(place(empty, early, swap(out_g1, "core")), late, swap(out_g2, "core"))
     ret_a, b_abs = lax.optimization_barrier((ret_a, b_abs))

time: 192 us -> 188 us (0.979)
  waiting for transfers between devices: 84.4 us -> 80.2 us
  local copies, waits for them, and re-layouts: 23.5 us -> 20.4 us
  matrix products: 54.7 us -> 57.2 us
    all_to_all x1, waiting for transfers between devices: 16.6 us -> 5.59 us  [shards(): ret_a = lax.all_to_all(a_abs, ('z', 'yh'), 0, 0, tiled=True)]
    ppermute x6, waiting for transfers between devices: 16.4 us -> 23 us  [shift_z(): return lax.ppermute(x, 'z', [(i, (i + step) % RING) for i in range(RING)])]
    dynamic_update_slice x16, local copies, waits for them, and re-layouts: 16.7 us -> 12.4 us  [place(): into = lax.dynamic_update_slice(into, outs[i:i + 1], (where, 0, 0))]
  transfers between devices with their start and end apart: 13 -> 13, of which waited for: 6 -> 8; matrix products, arithmetic and copies ran while one was open for 37% -> 37% of each run, Pallas kernels for 0% -> 0%
where the time goes in v10:
time: 188 us
  waiting for transfers between devices  80.2 us (43%)
  matrix products  57.2 us (30%)
  starting transfers between devices  24.6 us (13%)
  local copies, waits for them, and re-layouts  20.4 us (11%)
  other arithmetic  5.17 us (3%)
    all_to_all x1, waiting for transfers between devices, shards(): ret_b = lax.all_to_all(b_abs, ('z', 'yh'), 0, 0, tiled=True)  36.9 us
    dot_general x4, matrix products, expert_block(): projected = jnp.dot(flat, w_first, preferred_element_type=jnp.float32)  29.4 us
    ppermute x6, waiting for transfers between devices, shift_z(): return lax.ppermute(x, 'z', [(i, (i + step) % RING) for i in range(RING)])  23 us
    dot_general x4, matrix products, expert_block(): jnp.dot(intermediate_activation, w_second, preferred_element_type=jnp.flo...  16.3 us
    ppermute x5, waiting for transfers between devices, swap(): return lax.ppermute(x, axis, [(0, 1), (1, 0)])  14.8 us
    dynamic_update_slice x16, local copies, waits for them, and re-layouts, place(): into = lax.dynamic_update_slice(into, outs[i:i + 1], (where, 0, 0))  12.4 us
    ppermute x6, starting transfers between devices, shift_z(): return lax.ppermute(x, 'z', [(i, (i + step) % RING) for i in range(RING)])  10.9 us
    dot_general x2, matrix products, contribution(): jnp.dot(mixing.reshape(-1, tok_rows).T, returned.reshape(-1, features), p...  5.8 us
  transfers between devices with their start and end apart: 13, of which 8 were waited for; matrix products, arithmetic and copies ran while one was open for 37% of the time, Pallas kernels for 0%

profile of v10, /device:TPU:0, one launch (start us, length us, event | category | flops | bytes accessed | tf_op | source)
XLA Modules:
  0.0 188.1 jit_solution(1308815527393200662)
XLA Ops:
  0.0 0.6 compare_reduce_fusion
  0.6 1.3 convert_select_fusion
  2.0 0.1 reshape.87
  2.1 2.3 %fusion.80 = (bf16[1,129,3072]{2,1,0:T(8,128)(2,1)S(1)}, bf16[129,3072]{1,0:T(8,128)(2,1)}) fusion(bf16[1,1024]{1,0:T(2,128)(2,1)S(1)} %reshape.87, bf16[128,3072]{1,0:T(8,128)(2,1)} %param.8), kind=kLoop, calls=%fused_computation.123 | loop fusion | flops 2377728 | bytes 2373632 | tf_op jit(solution)/shard_map/stack | solution.py:69
  4.3 3.3 %collective-permute-start = (bf16[129,3072]{1,0:T(8,128)(2,1)}, bf16[129,3072]{1,0:T(8,128)(2,1)S(1)}, u32[]{:S(2)}, u32[]{:S(2)}) collective-permute-start(bf16[129,3072]{1,0:T(8,128)(2,1)} %get-tuple-element.48), channel_id=1, source_target_pairs={{0,2},{2,0},{1,3},{3,1},{4,6},{6,4},{5,7},{7,5},{8,10},{10,8},{9,1... | collective-permute-start | bytes 2377736 | tf_op jit(solution)/shard_map/ppermute | solution.py:31
  7.6 4.0 %collective-permute-start.3 = (bf16[129,3072]{1,0:T(8,128)(2,1)}, bf16[129,3072]{1,0:T(8,128)(2,1)S(1)}, u32[]{:S(2)}, u32[]{:S(2)}) collective-permute-start(bf16[129,3072]{1,0:T(8,128)(2,1)} %get-tuple-element.48), channel_id=1, source_target_pairs={{0,12},{4,0},{8,4},{12,8},{1,13},{5,1},{9,5},{13,9},{2,14},{6,2},{... | collective-permute-start | bytes 2377736 | tf_op jit(solution)/shard_map/ppermute | solution.py:27
  11.6 14.8 %collective-permute-done = bf16[129,3072]{1,0:T(8,128)(2,1)S(1)} collective-permute-done((bf16[129,3072]{1,0:T(8,128)(2,1)}, bf16[129,3072]{1,0:T(8,128)(2,1)S(1)}, u32[]{:S(2)}, u32[]{:S(2)}) %collective-permute-start) | collective-permute-done | bytes 792608 | tf_op jit(solution)/shard_map/ppermute | solution.py:31
  26.4 3.1 %collective-permute-done.3 = bf16[129,3072]{1,0:T(8,128)(2,1)S(1)} collective-permute-done((bf16[129,3072]{1,0:T(8,128)(2,1)}, bf16[129,3072]{1,0:T(8,128)(2,1)S(1)}, u32[]{:S(2)}, u32[]{:S(2)}) %collective-permute-start.3) | collective-permute-done | bytes 792608 | tf_op jit(solution)/shard_map/ppermute | solution.py:27
  29.5 3.3 %collective-permute-done.1 = bf16[129,3072]{1,0:T(8,128)(2,1)S(1)} collective-permute-done((bf16[129,3072]{1,0:T(8,128)(2,1)}, bf16[129,3072]{1,0:T(8,128)(2,1)S(1)}, u32[]{:S(2)}, u32[]{:S(2)}) %collective-permute-start.1) | collective-permute-done | bytes 792608 | tf_op jit(solution)/shard_map/ppermute | solution.py:27
  32.9 0.1 reshape.93
  33.0 2.8 %convolution_convert_fusion.1 = bf16[4,2,64,3072]{3,2,1,0:T(8,128)(2,1)S(1)} fusion(bf16[1,129,3072]{2,1,0:T(8,128)(2,1)S(1)} %bitcast.124, bf16[1,129,3072]{2,1,0:T(8,128)(2,1)S(1)} %bitcast.122, bf16[1,129,3072]{2,1,0:T(8,128)(2,1)S(1)} %bitcast.112, bf16[1,129,3072]{2,1,0:T(8,128)(2,1)S(1)} %get-tuple-element.47, s32[4,2,64]{2,1,0:T(2,128)S(1)} %pad_add_fusion), kind=kOutput, calls=%fused_computation.17 | convolution fusion | flops 416874496 | bytes 6318080 | tf_op jit(solution)/shard_map/bjct,btd->bjcd/dot_general | solution.py:81
  35.9 1.4 slice_bitcast_fusion.1
  37.3 0.1 pad_maximum_fusion.10
  37.5 0.1 collective-permute-start.2
  37.6 0.2 pad_maximum_fusion.11
  37.8 3.3 %collective-permute-start.4 = (bf16[194,3072]{1,0:T(8,128)(2,1)S(1)}, bf16[194,3072]{1,0:T(8,128)(2,1)S(1)}, u32[]{:S(2)}, u32[]{:S(2)}) collective-permute-start(bf16[194,3072]{1,0:T(8,128)(2,1)S(1)} %pad_maximum_fusion.11), channel_id=1, source_target_pairs={{0,12},{4,0},{8,4},{12,8},{1,13},{5,1},{9,5},{13,9},{2,14},{6,2},{... | collective-permute-start | bytes 3575816 | tf_op jit(solution)/shard_map/ppermute | solution.py:27
  41.1 5.7 %fusion.6 = f32[256,2560]{1,0:T(8,128)} fusion(bf16[256,3072]{1,0:T(8,128)(2,1)S(1)} %bitcast.125, bf16[1,3072,2560]{2,1,0:T(8,128)(2,1)S(1)} %copy-done.3), kind=kOutput, calls=%fused_computation.6 | convolution fusion | flops 4026531840 | bytes 19922944 | tf_op jit(solution)/shard_map/dot_general | solution.py:16
  46.8 4.1 %fusion.16 = bf16[256,3072]{1,0:T(8,128)(2,1)S(1)} fusion(bf16[1,1280,3072]{2,1,0:T(8,128)(2,1)S(1)} %bitcast.134, f32[256,2560]{1,0:T(8,128)} %fusion.6), kind=kOutput, calls=%fused_computation.18 | convolution fusion | flops 2016018432 | bytes 12058624 | tf_op jit(solution)/shard_map/dot_general | solution.py:20
  50.9 2.0 %broadcast_in_dim.38.clone = bf16[8,64,3072]{2,1,0:T(8,128)(2,1)} broadcast(bf16[]{:T(256)} %constant.158.clone.1), dimensions={} | broadcast | bytes 3145730 | tf_op jit(solution)/shard_map/broadcast_in_dim | solution.py:96
  52.9 0.8 fusion.57
  53.7 0.8 fusion.56
  54.4 0.8 fusion.55
  55.2 10.8 %collective-permute-done.2 = bf16[193,3072]{1,0:T(8,128)(2,1)S(1)} collective-permute-done((bf16[193,3072]{1,0:T(8,128)(2,1)S(1)}, bf16[193,3072]{1,0:T(8,128)(2,1)S(1)}, u32[]{:S(2)}, u32[]{:S(2)}) %collective-permute-start.2) | collective-permute-done | bytes 1185824 | tf_op jit(solution)/shard_map/ppermute | solution.py:27
  66.0 0.1 fusion.81
  66.1 0.1 collective-permute-start.5
  66.2 0.1 fusion.82
  66.3 3.5 %collective-permute-start.6 = (bf16[65,3072]{1,0:T(8,128)(2,1)S(1)}, bf16[65,3072]{1,0:T(8,128)(2,1)S(1)}, u32[]{:S(2)}, u32[]{:S(2)}) collective-permute-start(bf16[65,3072]{1,0:T(8,128)(2,1)S(1)} %get-tuple-element.45), channel_id=1, source_target_pairs={{0,12},{4,0},{8,4},{12,8},{1,13},{5,1},{9,5},{13,9},{2,14},{6,2},{... | collective-permute-start | bytes 1198088 | tf_op jit(solution)/shard_map/ppermute | solution.py:27
  69.8 0.8 fusion.54
  70.8 5.1 %collective-permute-done.5 = bf16[64,3072]{1,0:T(8,128)(2,1)S(1)} collective-permute-done((bf16[64,3072]{1,0:T(8,128)(2,1)S(1)}, bf16[64,3072]{1,0:T(8,128)(2,1)S(1)}, u32[]{:S(2)}, u32[]{:S(2)}) %collective-permute-start.5) | collective-permute-done | bytes 393248 | tf_op jit(solution)/shard_map/ppermute | solution.py:27
  75.8 0.7 collective-permute-done.6
  76.7 0.1 reshape.94
  76.8 2.8 %convolution_convert_fusion = bf16[4,2,64,3072]{3,2,1,0:T(8,128)(2,1)S(1)} fusion(bf16[1,129,3072]{2,1,0:T(8,128)(2,1)S(1)} %bitcast.114, bf16[1,129,3072]{2,1,0:T(8,128)(2,1)S(1)} %bitcast.116, bf16[1,129,3072]{2,1,0:T(8,128)(2,1)S(1)} %bitcast.120, bf16[1,129,3072]{2,1,0:T(8,128)(2,1)S(1)} %bitcast.118, s32[4,2,64]{2,1,0:T(2,128)S(1)} %pad_add_fusion.1), kind=kOutput, calls=%fused_computation.16 | convolution fusion | flops 416874496 | bytes 6318080 | tf_op jit(solution)/shard_map/bjct,btd->bjcd/dot_general | solution.py:81
  79.7 1.4 slice_bitcast_fusion
  81.1 8.1 %fusion.4 = f32[256,2560]{1,0:T(8,128)S(1)} fusion(bf16[256,3072]{1,0:T(8,128)(2,1)S(1)} %bitcast.126, bf16[1,3072,2560]{2,1,0:T(8,128)(2,1)} %param.12), kind=kOutput, calls=%fused_computation.4 | convolution fusion | flops 4026531840 | bytes 19922944 | tf_op jit(solution)/shard_map/dot_general | solution.py:16
  89.3 2.3 %fusion.19 = bf16[256,3072]{1,0:T(8,128)(2,1)S(1)} fusion(bf16[1,1280,3072]{2,1,0:T(8,128)(2,1)S(1)} %bitcast.136, f32[256,2560]{1,0:T(8,128)S(1)} %fusion.4), kind=kOutput, calls=%fused_computation.19 | convolution fusion | flops 2016018432 | bytes 12058624 | tf_op jit(solution)/shard_map/dot_general | solution.py:20
  91.6 0.1 collective-permute-start.8
  91.7 0.8 fusion.53
  92.5 0.8 fusion.52
  93.2 0.8 fusion.51
  94.0 0.8 fusion.50
  94.8 5.0 %all-to-all-start = ((bf16[8,64,3072]{2,1,0:T(8,128)(2,1)}), bf16[8,64,3072]{2,1,0:T(8,128)(2,1)S(1)}, u32[]{:S(2)}, u32[]{:S(2)}) async-start(bf16[8,64,3072]{2,1,0:T(8,128)(2,1)} %fusion.50), calls=%async_computation | async-start | bytes 6291456 | tf_op jit(solution)/shard_map/all_to_all | solution.py:104
  99.8 8.3 %fusion.2 = f32[256,2560]{1,0:T(8,128)S(1)} fusion(bf16[256,3072]{1,0:T(8,128)(2,1)} %bitcast.26, bf16[1,3072,2560]{2,1,0:T(8,128)(2,1)} %param.12), kind=kOutput, calls=%fused_computation.2 | convolution fusion | flops 4026531840 | bytes 19922944 | tf_op jit(solution)/shard_map/dot_general | solution.py:16
  108.1 5.8 %fusion.22 = bf16[256,3072]{1,0:T(8,128)(2,1)S(1)} fusion(bf16[1,1280,3072]{2,1,0:T(8,128)(2,1)} %param.13, f32[256,2560]{1,0:T(8,128)S(1)} %fusion.2), kind=kOutput, calls=%fused_computation.20 | convolution fusion | flops 2016018432 | bytes 12058624 | tf_op jit(solution)/shard_map/dot_general | solution.py:20
  114.0 0.5 collective-permute-start.9
  114.5 7.3 %fusion = f32[256,2560]{1,0:T(8,128)} fusion(bf16[256,3072]{1,0:T(8,128)(2,1)} %bitcast.28, bf16[1,3072,2560]{2,1,0:T(8,128)(2,1)S(1)} %bitcast.132), kind=kOutput, calls=%fused_computation | convolution fusion | flops 4026531840 | bytes 19922944 | tf_op jit(solution)/shard_map/dot_general | solution.py:16
  121.8 4.1 %fusion.25 = bf16[256,3072]{1,0:T(8,128)(2,1)S(1)} fusion(bf16[1,1280,3072]{2,1,0:T(8,128)(2,1)S(1)} %bitcast.138, f32[256,2560]{1,0:T(8,128)} %fusion), kind=kOutput, calls=%fused_computation.21 | convolution fusion | flops 2016018432 | bytes 12058624 | tf_op jit(solution)/shard_map/dot_general | solution.py:20
  125.9 0.4 collective-permute-start.10
  126.2 2.1 %broadcast_in_dim.38 = bf16[8,64,3072]{2,1,0:T(8,128)(2,1)} broadcast(bf16[]{:T(256)} %constant.158.clone.1), dimensions={} | broadcast | bytes 3145730 | tf_op jit(solution)/shard_map/broadcast_in_dim | solution.py:96
  128.3 0.8 slice_dynamic-update-slice_fusion.7
  129.1 0.8 slice_dynamic-update-slice_fusion.6
  129.9 0.8 slice_dynamic-update-slice_fusion.5
  130.6 0.8 slice_dynamic-update-slice_fusion.4
  131.4 0.8 slice_dynamic-update-slice_fusion.3
  132.2 0.8 slice_dynamic-update-slice_fusion.2
  133.0 0.8 slice_dynamic-update-slice_fusion.1
  133.8 0.8 slice_dynamic-update-slice_fusion
  134.5 5.6 %all-to-all-done = bf16[8,64,3072]{2,1,0:T(8,128)(2,1)S(1)} async-done(((bf16[8,64,3072]{2,1,0:T(8,128)(2,1)}), bf16[8,64,3072]{2,1,0:T(8,128)(2,1)S(1)}, u32[]{:S(2)}, u32[]{:S(2)}) %all-to-all-start) | async-done | bytes 3145760 | tf_op jit(solution)/shard_map/all_to_all | solution.py:104
  140.1 4.4 %all-to-all-start.1 = ((bf16[8,64,3072]{2,1,0:T(8,128)(2,1)}), bf16[8,64,3072]{2,1,0:T(8,128)(2,1)}, u32[]{:S(2)}, u32[]{:S(2)}) async-start(bf16[8,64,3072]{2,1,0:T(8,128)(2,1)} %slice_dynamic-update-slice_fusion), calls=%async_computation.1 | async-start | bytes 6291456 | tf_op jit(solution)/shard_map/all_to_all | solution.py:110
  144.6 0.1 copy.18
  144.7 0.1 copy.9
  144.8 0.4 select_reduce_fusion
  145.4 1.9 convolution_bitcast_fusion.1
  147.2 36.9 %all-to-all-done.1 = bf16[8,64,3072]{2,1,0:T(8,128)(2,1)} async-done(((bf16[8,64,3072]{2,1,0:T(8,128)(2,1)}), bf16[8,64,3072]{2,1,0:T(8,128)(2,1)}, u32[]{:S(2)}, u32[]{:S(2)}) %all-to-all-start.1) | async-done | bytes 3145760 | tf_op jit(solution)/shard_map/all_to_all | solution.py:110
  184.1 3.9 %fusion.29 = bf16[128,3072]{1,0:T(8,128)(2,1)} fusion(f32[128,3072]{1,0:T(8,128)} %convolution_bitcast_fusion.1, bf16[8,64,3072]{2,1,0:T(8,128)(2,1)} %all-to-all-done.1, s32[8,64]{1,0:T(8,128)S(1)} %bitcast.130, bf16[8,128]{1,0:T(8,128)(2,1)S(1)} %get-tuple-element.57), kind=kOutput, calls=%fused_computation.25 | convolution fusion | flops 403570688 | bytes 5509120 | tf_op jit(solution)/shard_map/dot_general | solution.py:127
  (55 shorter events, 0.7 us)
Async XLA Ops:
  4.3 22.1 %collective-permute-start = (bf16[129,3072]{1,0:T(8,128)(2,1)}, bf16[129,3072]{1,0:T(8,128)(2,1)S(1)}, u32[]{:S(2)}, u32[]{:S(2)}) collective-permute-start(bf16[129,3072]{1,0:T(8,128)(2,1)} %get-tuple-element.48), channel_id=1, source_target_pairs={{0,2},{2,0},{1,3},{3,1},{4,6},{6,4},{5,7},{7,5},{8,10},{10,8},{9,1... | collective-permute-start | bytes 2377736 | tf_op jit(solution)/shard_map/ppermute | solution.py:31
  7.6 21.9 %collective-permute-start.3 = (bf16[129,3072]{1,0:T(8,128)(2,1)}, bf16[129,3072]{1,0:T(8,128)(2,1)S(1)}, u32[]{:S(2)}, u32[]{:S(2)}) collective-permute-start(bf16[129,3072]{1,0:T(8,128)(2,1)} %get-tuple-element.48), channel_id=1, source_target_pairs={{0,12},{4,0},{8,4},{12,8},{1,13},{5,1},{9,5},{13,9},{2,14},{6,2},{... | collective-permute-start | bytes 2377736 | tf_op jit(solution)/shard_map/ppermute | solution.py:27
  11.6 21.2 %collective-permute-start.1 = (bf16[129,3072]{1,0:T(8,128)(2,1)}, bf16[129,3072]{1,0:T(8,128)(2,1)S(1)}, u32[]{:S(2)}, u32[]{:S(2)}) collective-permute-start(bf16[129,3072]{1,0:T(8,128)(2,1)} %get-tuple-element.48), channel_id=1, source_target_pairs={{0,4},{4,8},{8,12},{12,0},{1,5},{5,9},{9,13},{13,1},{2,6},{6,10},{... | collective-permute-start | bytes 2377736 | tf_op jit(solution)/shard_map/ppermute | solution.py:27
  33.0 8.0 %copy-start.3 = (bf16[1,3072,2560]{2,1,0:T(8,128)(2,1)S(1)}, bf16[1,3072,2560]{2,1,0:T(8,128)(2,1)}, u32[]{:S(2)}) copy-start(bf16[1,3072,2560]{2,1,0:T(8,128)(2,1)} %param.12) | copy-start | bytes 47185924
  37.5 28.5 %collective-permute-start.2 = (bf16[193,3072]{1,0:T(8,128)(2,1)S(1)}, bf16[193,3072]{1,0:T(8,128)(2,1)S(1)}, u32[]{:S(2)}, u32[]{:S(2)}) collective-permute-start(bf16[193,3072]{1,0:T(8,128)(2,1)S(1)} %pad_maximum_fusion.10), channel_id=1, source_target_pairs={{0,4},{4,8},{8,12},{12,0},{1,5},{5,9},{9,13},{13,1},{2,6},{6,10},{... | collective-permute-start | bytes 3557384 | tf_op jit(solution)/shard_map/ppermute | solution.py:27
  37.6 9.2 %slice-start.4 = ((s8[7864320]{0:T(1024)(128)(4,1)}), s8[4194304]{0:T(1024)(128)(4,1)S(1)}, s32[]{:S(2)}) async-start(s8[7864320]{0:T(1024)(128)(4,1)} %bitcast.133), calls=%async_computation.6 | async-start | bytes 8388608
  37.8 28.4 %collective-permute-start.4 = (bf16[194,3072]{1,0:T(8,128)(2,1)S(1)}, bf16[194,3072]{1,0:T(8,128)(2,1)S(1)}, u32[]{:S(2)}, u32[]{:S(2)}) collective-permute-start(bf16[194,3072]{1,0:T(8,128)(2,1)S(1)} %pad_maximum_fusion.11), channel_id=1, source_target_pairs={{0,12},{4,0},{8,4},{12,8},{1,13},{5,1},{9,5},{13,9},{2,14},{6,2},{... | collective-permute-start | bytes 3575816 | tf_op jit(solution)/shard_map/ppermute | solution.py:27
  41.1 58.7 %collective-permute-start.7 = (bf16[4,64,3072]{2,1,0:T(8,128)(2,1)}, bf16[4,64,3072]{2,1,0:T(8,128)(2,1)}, u32[]{:S(2)}, u32[]{:S(2)}) collective-permute-start(bf16[4,64,3072]{2,1,0:T(8,128)(2,1)} %get-tuple-element.41), channel_id=1, source_target_pairs={{0,1},{1,0},{2,3},{3,2},{4,5},{5,4},{6,7},{7,6},{8,9},{9,8},{10,11... | collective-permute-start | bytes 4718600 | tf_op jit(solution)/shard_map/ppermute | solution.py:31
  41.1 5.7 %slice-start.5 = ((s8[7864320]{0:T(1024)(128)(4,1)}), s8[3670016]{0:T(1024)(128)(4,1)S(1)}, s32[]{:S(2)}) async-start(s8[7864320]{0:T(1024)(128)(4,1)} %bitcast.133), calls=%async_computation.7 | async-start | bytes 7340032
  66.1 9.7 %collective-permute-start.5 = (bf16[64,3072]{1,0:T(8,128)(2,1)S(1)}, bf16[64,3072]{1,0:T(8,128)(2,1)S(1)}, u32[]{:S(2)}, u32[]{:S(2)}) collective-permute-start(bf16[64,3072]{1,0:T(8,128)(2,1)S(1)} %get-tuple-element.43), channel_id=1, source_target_pairs={{0,4},{4,8},{8,12},{12,0},{1,5},{5,9},{9,13},{13,1},{2,6},{6,10},{... | collective-permute-start | bytes 1179656 | tf_op jit(solution)/shard_map/ppermute | solution.py:27
  66.3 10.2 %collective-permute-start.6 = (bf16[65,3072]{1,0:T(8,128)(2,1)S(1)}, bf16[65,3072]{1,0:T(8,128)(2,1)S(1)}, u32[]{:S(2)}, u32[]{:S(2)}) collective-permute-start(bf16[65,3072]{1,0:T(8,128)(2,1)S(1)} %get-tuple-element.45), channel_id=1, source_target_pairs={{0,12},{4,0},{8,4},{12,8},{1,13},{5,1},{9,5},{13,9},{2,14},{6,2},{... | collective-permute-start | bytes 1198088 | tf_op jit(solution)/shard_map/ppermute | solution.py:27
  79.6 9.6 %slice-start.6 = ((s8[7864320]{0:T(1024)(128)(4,1)}), s8[4194304]{0:T(1024)(128)(4,1)S(1)}, s32[]{:S(2)}) async-start(s8[7864320]{0:T(1024)(128)(4,1)} %bitcast.135), calls=%async_computation.8 | async-start | bytes 8388608
  81.1 8.2 %slice-start.7 = ((s8[7864320]{0:T(1024)(128)(4,1)}), s8[3670016]{0:T(1024)(128)(4,1)S(1)}, s32[]{:S(2)}) async-start(s8[7864320]{0:T(1024)(128)(4,1)} %bitcast.135), calls=%async_computation.9 | async-start | bytes 7340032
  91.6 8.2 %collective-permute-start.8 = (bf16[4,64,3072]{2,1,0:T(8,128)(2,1)}, bf16[4,64,3072]{2,1,0:T(8,128)(2,1)}, u32[]{:S(2)}, u32[]{:S(2)}) collective-permute-start(bf16[4,64,3072]{2,1,0:T(8,128)(2,1)} %get-tuple-element.39), channel_id=1, source_target_pairs={{0,1},{1,0},{2,3},{3,2},{4,5},{5,4},{6,7},{7,6},{8,9},{9,8},{10,11... | collective-permute-start | bytes 4718600 | tf_op jit(solution)/shard_map/ppermute | solution.py:31
  94.8 45.4 %all-to-all-start = ((bf16[8,64,3072]{2,1,0:T(8,128)(2,1)}), bf16[8,64,3072]{2,1,0:T(8,128)(2,1)S(1)}, u32[]{:S(2)}, u32[]{:S(2)}) async-start(bf16[8,64,3072]{2,1,0:T(8,128)(2,1)} %fusion.50), calls=%async_computation | async-start | bytes 6291456 | tf_op jit(solution)/shard_map/all_to_all | solution.py:104
  99.8 14.7 %slice-start = ((s8[15728640]{0:T(1024)(128)(4,1)}), s8[4194304]{0:T(1024)(128)(4,1)S(1)}, s32[]{:S(2)}) async-start(s8[15728640]{0:T(1024)(128)(4,1)} %bitcast.131), calls=%async_computation.2 | async-start | bytes 8388608
  99.8 14.7 %slice-start.1 = ((s8[15728640]{0:T(1024)(128)(4,1)}), s8[4194304]{0:T(1024)(128)(4,1)S(1)}, s32[]{:S(2)}) async-start(s8[15728640]{0:T(1024)(128)(4,1)} %bitcast.131), calls=%async_computation.3 | async-start | bytes 8388608
  99.8 14.7 %slice-start.2 = ((s8[15728640]{0:T(1024)(128)(4,1)}), s8[4194304]{0:T(1024)(128)(4,1)S(1)}, s32[]{:S(2)}) async-start(s8[15728640]{0:T(1024)(128)(4,1)} %bitcast.131), calls=%async_computation.4 | async-start | bytes 8388608
  108.1 6.4 %slice-start.3 = ((s8[15728640]{0:T(1024)(128)(4,1)}), s8[3145728]{0:T(1024)(128)(4,1)S(1)}, s32[]{:S(2)}) async-start(s8[15728640]{0:T(1024)(128)(4,1)} %bitcast.131), calls=%async_computation.5 | async-start | bytes 6291456
  108.1 13.6 %slice-start.8 = ((s8[7864320]{0:T(1024)(128)(4,1)}), s8[4194304]{0:T(1024)(128)(4,1)S(1)}, s32[]{:S(2)}) async-start(s8[7864320]{0:T(1024)(128)(4,1)} %bitcast.137), calls=%async_computation.10 | async-start | bytes 8388608
  114.0 12.3 %collective-permute-start.9 = (bf16[4,64,3072]{2,1,0:T(8,128)(2,1)S(1)}, bf16[4,64,3072]{2,1,0:T(8,128)(2,1)S(1)}, u32[]{:S(2)}, u32[]{:S(2)}) collective-permute-start(bf16[4,64,3072]{2,1,0:T(8,128)(2,1)S(1)} %bitcast.140), channel_id=1, source_target_pairs={{0,1},{1,0},{2,3},{3,2},{4,5},{5,4},{6,7},{7,6},{8,9},{9,8},{10,11... | collective-permute-start | bytes 4718600 | tf_op jit(solution)/shard_map/ppermute | solution.py:31
  114.5 7.3 %slice-start.9 = ((s8[7864320]{0:T(1024)(128)(4,1)}), s8[3670016]{0:T(1024)(128)(4,1)S(1)}, s32[]{:S(2)}) async-start(s8[7864320]{0:T(1024)(128)(4,1)} %bitcast.137), calls=%async_computation.11 | async-start | bytes 7340032
  125.9 5.6 %collective-permute-start.10 = (bf16[4,64,3072]{2,1,0:T(8,128)(2,1)S(1)}, bf16[4,64,3072]{2,1,0:T(8,128)(2,1)S(1)}, u32[]{:S(2)}, u32[]{:S(2)}) collective-permute-start(bf16[4,64,3072]{2,1,0:T(8,128)(2,1)S(1)} %bitcast.139), channel_id=1, source_target_pairs={{0,1},{1,0},{2,3},{3,2},{4,5},{5,4},{6,7},{7,6},{8,9},{9,8},{10,11... | collective-permute-start | bytes 4718600 | tf_op jit(solution)/shard_map/ppermute | solution.py:31
  134.5 10.1 %copy-start.1 = (f32[128,4]{0,1:T(4,128)S(1)}, f32[128,4]{0,1:T(4,128)}, u32[]{:S(2)}) copy-start(f32[128,4]{0,1:T(4,128)} %param.10) | copy-start | bytes 6148
  134.5 10.2 %copy-start.2 = (s32[128,4]{0,1:T(4,128)S(1)}, s32[128,4]{0,1:T(4,128)}, u32[]{:S(2)}) copy-start(s32[128,4]{0,1:T(4,128)} %param.9) | copy-start | bytes 6148
  134.5 10.8 %copy-start = (s32[1,16,64]{2,1,0:T(8,128)S(1)}, s32[1,16,64]{2,1,0:T(8,128)}, u32[]{:S(2)}) copy-start(s32[1,16,64]{2,1,0:T(8,128)} %param.11) | copy-start | bytes 12292
  140.1 44.0 %all-to-all-start.1 = ((bf16[8,64,3072]{2,1,0:T(8,128)(2,1)}), bf16[8,64,3072]{2,1,0:T(8,128)(2,1)}, u32[]{:S(2)}, u32[]{:S(2)}) async-start(bf16[8,64,3072]{2,1,0:T(8,128)(2,1)} %slice_dynamic-update-slice_fusion), calls=%async_computation.1 | async-start | bytes 6291456 | tf_op jit(solution)/shard_map/all_to_all | solution.py:110

commit v11 on v7

--- a/solution.py
+++ b/solution.py
@@ -52,12 +52,13 @@
     partner = swap(block, "yh")
     from_below = shift_z(block, 1)
     from_above = shift_z(block, -1)
-    p_below = shift_z(partner, 1)
-    p_above = shift_z(partner, -1)
-    far = jnp.concatenate(
-        [shift_z(from_below[:half], 1), shift_z(from_above[half:], -1)], axis=0
-    )
-    p_far = jnp.concatenate([shift_z(p_below[:half], 1), shift_z(p_above[half:], -1)], axis=0)
+    rows = tok_rows + 1
+    up = shift_z(jnp.concatenate([partner, from_below[:half]], axis=0), 1)
+    down = shift_z(jnp.concatenate([partner, from_above[half:]], axis=0), -1)
+    p_below = up[:rows]
+    p_above = down[:rows]
+    far = jnp.concatenate([up[rows:], down[rows:]], axis=0)
+    p_far = swap(far, "yh")
 
     chip = zi * n_y + yi
     mine_e = chip * 2 + ki
@@ -80,7 +81,7 @@
         disp = jnp.einsum(
             "bjct,btd->bjcd", one_hot, toks, preferred_element_type=jnp.float32
         ).astype(jnp.bfloat16)
-        return disp[:, 0], swap(disp[:, 1], "core")
+        return disp[:, 0], disp[:, 1]
 
     def place(into, pieces, outs):
         for i, (r, q, _) in enumerate(pieces):
@@ -94,7 +95,8 @@
         [(2, 1, p_far)],
     ]
     a_abs = jnp.zeros((blocks, capacity, features), jnp.bfloat16)
-    got_outs = []
+    empty = a_abs
+    gots = []
     for n, pieces in enumerate(stages):
         if n:
             arrs = [arr for _, _, arr in pieces]
@@ -103,11 +105,12 @@
             stages[n] = pieces
         mine, got = slots_of(pieces)
         a_abs = place(a_abs, pieces, expert_block(mine, w_first, w_second))
-        got_outs.append(got)
+        gots.append(got)
     ret_a = lax.all_to_all(a_abs, ("z", "yh"), 0, 0, tiled=True)
-    a_abs, *got_outs = lax.optimization_barrier((a_abs, *got_outs))
-    b_abs = jnp.zeros((blocks, capacity, features), jnp.bfloat16)
-    for pieces, got in zip(stages, got_outs):
+    a_abs, *gots = lax.optimization_barrier((a_abs, *gots))
+    b_abs = empty
+    for pieces, theirs in zip(stages, gots):
+        got = swap(theirs, "core")
         b_abs = place(b_abs, pieces, swap(expert_block(got, w_first, w_second), "core"))
     ret_a, b_abs = lax.optimization_barrier((ret_a, b_abs))
     ret_b = lax.all_to_all(b_abs, ("z", "yh"), 0, 0, tiled=True)

time: 208 us -> 207 us (level)
  waiting for transfers between devices: 86.1 us -> 72.8 us
  matrix products: 68.6 us -> 75.5 us
  other arithmetic: 4.89 us -> 8.77 us
  local copies, waits for them, and re-layouts: 19.9 us -> 23.1 us
  starting transfers between devices: 27.8 us -> 25.5 us
    ppermute x8 -> x4, waiting for transfers between devices: 33.5 us -> 15.8 us  [shift_z(): return lax.ppermute(x, 'z', [(i, (i + step) % RING) for i in range(RING)])]
    dot_general x6, matrix products: 17.6 us -> 23.6 us  [expert_block(): jnp.dot(intermediate_activation, w_second, preferred_element_type=jnp.flo...]
    ppermute x8 -> x4, starting transfers between devices: 12.5 us -> 7.4 us  [shift_z(): return lax.ppermute(x, 'z', [(i, (i + step) % RING) for i in range(RING)])]
    ppermute x7 -> x8, waiting for transfers between devices: 14.8 us -> 19.6 us  [swap(): return lax.ppermute(x, axis, [(0, 1), (1, 0)])]
    another operation x3 -> x1, local copies, waits for them, and re-layouts: 4.18 us -> 0.09 us
    broadcast_in_dim x0 -> x2, local copies, waits for them, and re-layouts: none -> 4.09 us  [shards(): a_abs = jnp.zeros((blocks, capacity, features), jnp.bfloat16)]
    slice x4 -> x6, local copies, waits for them, and re-layouts: 0.11 us -> 3.13 us  [the longest x1 1.77 us: shards(): up = shift_z(jnp.concatenate([partner, from_below[:half]], axis=0), 1)]
    concatenate x2 -> x3, other arithmetic: 0.13 us -> 2.83 us  [the longest x1 1.45 us: shards(): down = shift_z(jnp.concatenate([partner, from_above[half:]], axis=0), -1)]
  transfers between devices with their start and end apart: 17 -> 14, of which waited for: 6 -> 7; matrix products, arithmetic and copies ran while one was open for 39% -> 36% of each run, Pallas kernels for 0% -> 0%
where the time goes in v11:
time: 207 us; the launch traced here: 206 us
  matrix products  75.5 us (36%)
  waiting for transfers between devices  72.8 us (35%)
  starting transfers between devices  25.5 us (12%)
  local copies, waits for them, and re-layouts  23.1 us (11%)
  other arithmetic  8.77 us (4%)
    dot_general x6, matrix products, expert_block(): projected = jnp.dot(flat, w_first, preferred_element_type=jnp.float32)  41.8 us
    all_to_all x1, waiting for transfers between devices, shards(): ret_b = lax.all_to_all(b_abs, ('z', 'yh'), 0, 0, tiled=True)  37.4 us
    dot_general x6, matrix products, expert_block(): jnp.dot(intermediate_activation, w_second, preferred_element_type=jnp.flo...  23.6 us
    ppermute x8, waiting for transfers between devices, swap(): return lax.ppermute(x, axis, [(0, 1), (1, 0)])  19.6 us
    ppermute x4, waiting for transfers between devices, shift_z(): return lax.ppermute(x, 'z', [(i, (i + step) % RING) for i in range(RING)])  15.8 us
    dynamic_update_slice x15, local copies, waits for them, and re-layouts, place(): into = lax.dynamic_update_slice(into, outs[i:i + 1], (where, 0, 0))  11.7 us
    ppermute x4, starting transfers between devices, shift_z(): return lax.ppermute(x, 'z', [(i, (i + step) % RING) for i in range(RING)])  7.4 us
    all_to_all x1, starting transfers between devices, shards(): ret_b = lax.all_to_all(b_abs, ('z', 'yh'), 0, 0, tiled=True)  7.35 us
  transfers between devices with their start and end apart: 14, of which 7 were waited for; matrix products, arithmetic and copies ran while one was open for 36% of the time, Pallas kernels for 0%

profile of v11, /device:TPU:0, one launch (start us, length us, event | category | flops | bytes accessed | tf_op | source)
XLA Modules:
  0.0 206.0 jit_solution(13303980238905846376)
XLA Ops:
  0.0 0.6 compare_reduce_fusion
  0.6 1.3 convert_select_fusion
  2.1 2.7 %fusion.116 = (bf16[1,129,3072]{2,1,0:T(8,128)(2,1)}, bf16[129,3072]{1,0:T(8,128)(2,1)}) fusion(bf16[1,1024]{1,0:T(2,128)(2,1)S(1)} %reshape.136, bf16[128,3072]{1,0:T(8,128)(2,1)} %param.8), kind=kLoop, calls=%fused_computation.154 | loop fusion | flops 2377728 | bytes 2373632 | tf_op jit(solution)/shard_map/stack | solution.py:69
  4.7 3.3 %collective-permute-start = (bf16[129,3072]{1,0:T(8,128)(2,1)}, bf16[129,3072]{1,0:T(8,128)(2,1)}, u32[]{:S(2)}, u32[]{:S(2)}) collective-permute-start(bf16[129,3072]{1,0:T(8,128)(2,1)} %get-tuple-element.48), channel_id=1, source_target_pairs={{0,2},{2,0},{1,3},{3,1},{4,6},{6,4},{5,7},{7,5},{8,10},{10,8},{9,1... | collective-permute-start | bytes 2377736 | tf_op jit(solution)/shard_map/ppermute | solution.py:31
  8.0 4.0 %collective-permute-start.3 = (bf16[129,3072]{1,0:T(8,128)(2,1)}, bf16[129,3072]{1,0:T(8,128)(2,1)}, u32[]{:S(2)}, u32[]{:S(2)}) collective-permute-start(bf16[129,3072]{1,0:T(8,128)(2,1)} %get-tuple-element.48), channel_id=1, source_target_pairs={{0,12},{4,0},{8,4},{12,8},{1,13},{5,1},{9,5},{13,9},{2,14},{6,2},{... | collective-permute-start | bytes 2377736 | tf_op jit(solution)/shard_map/ppermute | solution.py:27
  12.1 14.9 %collective-permute-done = bf16[129,3072]{1,0:T(8,128)(2,1)} collective-permute-done((bf16[129,3072]{1,0:T(8,128)(2,1)}, bf16[129,3072]{1,0:T(8,128)(2,1)}, u32[]{:S(2)}, u32[]{:S(2)}) %collective-permute-start) | collective-permute-done | bytes 792608 | tf_op jit(solution)/shard_map/ppermute | solution.py:31
  26.9 3.0 %collective-permute-done.3 = bf16[129,3072]{1,0:T(8,128)(2,1)} collective-permute-done((bf16[129,3072]{1,0:T(8,128)(2,1)}, bf16[129,3072]{1,0:T(8,128)(2,1)}, u32[]{:S(2)}, u32[]{:S(2)}) %collective-permute-start.3) | collective-permute-done | bytes 792608 | tf_op jit(solution)/shard_map/ppermute | solution.py:27
  29.9 3.4 %collective-permute-done.1 = bf16[129,3072]{1,0:T(8,128)(2,1)} collective-permute-done((bf16[129,3072]{1,0:T(8,128)(2,1)}, bf16[129,3072]{1,0:T(8,128)(2,1)}, u32[]{:S(2)}, u32[]{:S(2)}) %collective-permute-start.1) | collective-permute-done | bytes 792608 | tf_op jit(solution)/shard_map/ppermute | solution.py:27
  33.4 0.8 fusion.103
  34.3 3.0 %convolution_convert_fusion = bf16[4,2,64,3072]{3,2,1,0:T(8,128)(2,1)S(1)} fusion(bf16[1,129,3072]{2,1,0:T(8,128)(2,1)} %bitcast.3, bf16[1,129,3072]{2,1,0:T(8,128)(2,1)} %bitcast.2, bf16[1,129,3072]{2,1,0:T(8,128)(2,1)} %bitcast.1, bf16[1,129,3072]{2,1,0:T(8,128)(2,1)} %get-tuple-element.47, s32[4,2,64]{2,1,0:T(2,128)S(1)} %pad_add_fusion), kind=kOutput, calls=%fused_computation.24 | convolution fusion | flops 416874496 | bytes 6318080 | tf_op jit(solution)/shard_map/bjct,btd->bjcd/dot_general | solution.py:81
  37.4 1.3 slice_bitcast_fusion
  38.7 1.8 slice.220
  40.5 1.3 pad_maximum_fusion.8
  41.9 1.0 slice.222
  42.9 1.4 pad_maximum_fusion.9
  44.4 3.3 %collective-permute-start.4 = (bf16[194,3072]{1,0:T(8,128)(2,1)S(1)}, bf16[194,3072]{1,0:T(8,128)(2,1)S(1)}, u32[]{:S(2)}, u32[]{:S(2)}) collective-permute-start(bf16[194,3072]{1,0:T(8,128)(2,1)S(1)} %pad_maximum_fusion.9), channel_id=1, source_target_pairs={{0,12},{4,0},{8,4},{12,8},{1,13},{5,1},{9,5},{13,9},{2,14},{6,2},{... | collective-permute-start | bytes 3575816 | tf_op jit(solution)/shard_map/ppermute | solution.py:27
  47.7 5.7 %fusion.10 = f32[256,2560]{1,0:T(8,128)} fusion(bf16[256,3072]{1,0:T(8,128)(2,1)S(1)} %bitcast.166, bf16[1,3072,2560]{2,1,0:T(8,128)(2,1)S(1)} %bitcast.151), kind=kOutput, calls=%fused_computation.10 | convolution fusion | flops 4026531840 | bytes 19922944 | tf_op jit(solution)/shard_map/dot_general | solution.py:16
  53.4 4.1 %fusion.24 = bf16[256,3072]{1,0:T(8,128)(2,1)S(1)} fusion(bf16[1,1280,3072]{2,1,0:T(8,128)(2,1)S(1)} %bitcast.155, f32[256,2560]{1,0:T(8,128)} %fusion.10), kind=kOutput, calls=%fused_computation.26 | convolution fusion | flops 2016018432 | bytes 12058624 | tf_op jit(solution)/shard_map/dot_general | solution.py:20
  57.5 2.0 broadcast_in_dim.40.clone
  59.5 0.8 fusion.80
  60.3 0.8 fusion.79
  61.1 0.8 fusion.78
  61.9 0.8 fusion.77
  62.6 7.7 %collective-permute-done.2 = bf16[193,3072]{1,0:T(8,128)(2,1)S(1)} collective-permute-done((bf16[193,3072]{1,0:T(8,128)(2,1)S(1)}, bf16[193,3072]{1,0:T(8,128)(2,1)S(1)}, u32[]{:S(2)}, u32[]{:S(2)}) %collective-permute-start.2) | collective-permute-done | bytes 1185824 | tf_op jit(solution)/shard_map/ppermute | solution.py:27
  70.5 1.7 collective-permute-done.4
  72.4 0.6 collective-permute-start.5
  73.2 0.8 convolution_convert_fusion.1
  74.0 1.3 slice_bitcast_fusion.1
  75.3 7.6 %fusion.8 = f32[192,2560]{1,0:T(8,128)S(1)} fusion(bf16[192,3072]{1,0:T(8,128)(2,1)S(1)} %bitcast.167, bf16[1,3072,2560]{2,1,0:T(8,128)(2,1)} %param.12), kind=kOutput, calls=%fused_computation.8 | convolution fusion | flops 3019898880 | bytes 18874368 | tf_op jit(solution)/shard_map/dot_general | solution.py:16
  83.0 1.8 fusion.30
  84.8 0.8 fusion.76
  85.6 0.8 fusion.75
  86.3 0.8 fusion.74
  87.1 4.7 %collective-permute-done.5 = bf16[129,3072]{1,0:T(8,128)(2,1)S(1)} collective-permute-done((bf16[129,3072]{1,0:T(8,128)(2,1)S(1)}, bf16[129,3072]{1,0:T(8,128)(2,1)S(1)}, u32[]{:S(2)}, u32[]{:S(2)}) %collective-permute-start.5) | collective-permute-done | bytes 792608 | tf_op jit(solution)/shard_map/ppermute | solution.py:31
  91.9 0.4 fusion.38
  92.3 8.3 %fusion.6 = f32[64,2560]{1,0:T(8,128)S(1)} fusion(bf16[1,3072,2560]{2,1,0:T(8,128)(2,1)} %param.12, bf16[1,2,64,3072]{3,2,1,0:T(8,128)(2,1)S(1)} %fusion.38), kind=kOutput, calls=%fused_computation.6 | convolution fusion | flops 1006632960 | bytes 16777216 | tf_op jit(solution)/shard_map/dot_general | solution.py:16
  100.6 0.8 slice_bitcast_fusion.4
  101.4 5.5 %fusion.51 = bf16[8,64,3072]{2,1,0:T(8,128)(2,1)} fusion(bf16[8,64,3072]{2,1,0:T(8,128)(2,1)} %fusion.74, s32[]{:T(128)S(6)} %select_n.156, bf16[1,1280,3072]{2,1,0:T(8,128)(2,1)} %param.13, f32[64,2560]{1,0:T(8,128)S(1)} %fusion.6), kind=kOutput, calls=%fused_computation.40 | convolution fusion | flops 504004608 | bytes 8912900 | tf_op jit(solution)/shard_map/dot_general | solution.py:20
  106.9 0.5 collective-permute-start.6
  107.4 5.0 %all-to-all-start = ((bf16[8,64,3072]{2,1,0:T(8,128)(2,1)}), bf16[8,64,3072]{2,1,0:T(8,128)(2,1)S(1)}, u32[]{:S(2)}, u32[]{:S(2)}) async-start(bf16[8,64,3072]{2,1,0:T(8,128)(2,1)} %fusion.51), calls=%async_computation | async-start | bytes 6291456 | tf_op jit(solution)/shard_map/all_to_all | solution.py:109
  112.4 8.4 %fusion = f32[64,2560]{1,0:T(8,128)S(1)} fusion(bf16[1,3072,2560]{2,1,0:T(8,128)(2,1)} %param.12, bf16[1,64,3072]{2,1,0:T(8,128)(2,1)S(1)} %collective-permute-done.10), kind=kOutput, calls=%fused_computation | convolution fusion | flops 1006632960 | bytes 16777216 | tf_op jit(solution)/shard_map/dot_general | solution.py:16
  120.8 4.9 %fusion.45 = bf16[1,64,3072]{2,1,0:T(8,128)(2,1)S(1)} fusion(bf16[1,1280,3072]{2,1,0:T(8,128)(2,1)} %param.13, f32[64,2560]{1,0:T(8,128)S(1)} %fusion), kind=kOutput, calls=%fused_computation.38 | convolution fusion | flops 504004608 | bytes 8912896 | tf_op jit(solution)/shard_map/dot_general | solution.py:20
  125.7 0.8 collective-permute-start.11
  126.5 7.3 %fusion.4 = f32[256,2560]{1,0:T(8,128)} fusion(bf16[256,3072]{1,0:T(8,128)(2,1)} %bitcast.33, bf16[1,3072,2560]{2,1,0:T(8,128)(2,1)S(1)} %bitcast.153), kind=kOutput, calls=%fused_computation.4 | convolution fusion | flops 4026531840 | bytes 19922944 | tf_op jit(solution)/shard_map/dot_general | solution.py:16
  133.8 4.1 %fusion.27 = bf16[256,3072]{1,0:T(8,128)(2,1)S(1)} fusion(bf16[1,1280,3072]{2,1,0:T(8,128)(2,1)S(1)} %bitcast.159, f32[256,2560]{1,0:T(8,128)} %fusion.4), kind=kOutput, calls=%fused_computation.27 | convolution fusion | flops 2016018432 | bytes 12058624 | tf_op jit(solution)/shard_map/dot_general | solution.py:20
  137.9 0.1 collective-permute-start.7
  138.0 4.5 %fusion.2 = f32[192,2560]{1,0:T(8,128)} fusion(bf16[192,3072]{1,0:T(8,128)(2,1)S(1)} %bitcast.175, bf16[1,3072,2560]{2,1,0:T(8,128)(2,1)S(1)} %bitcast.153), kind=kOutput, calls=%fused_computation.2 | convolution fusion | flops 3019898880 | bytes 18874368 | tf_op jit(solution)/shard_map/dot_general | solution.py:16
  142.5 3.3 %fusion.33 = bf16[192,3072]{1,0:T(8,128)(2,1)S(1)} fusion(bf16[1,1280,3072]{2,1,0:T(8,128)(2,1)S(1)} %bitcast.159, f32[192,2560]{1,0:T(8,128)} %fusion.2), kind=kOutput, calls=%fused_computation.29 | convolution fusion | flops 1512013824 | bytes 11010048 | tf_op jit(solution)/shard_map/dot_general | solution.py:20
  145.8 0.5 collective-permute-start.9
  146.4 2.1 %broadcast_in_dim.40 = bf16[8,64,3072]{2,1,0:T(8,128)(2,1)} broadcast(bf16[]{:T(256)} %constant.170.clone.1), dimensions={} | broadcast | bytes 3145730 | tf_op jit(solution)/shard_map/broadcast_in_dim | solution.py:97
  148.5 0.8 slice_dynamic-update-slice_fusion.6
  149.2 0.8 slice_dynamic-update-slice_fusion.5
  150.0 0.8 slice_dynamic-update-slice_fusion.4
  150.8 0.8 slice_dynamic-update-slice_fusion.3
  151.6 0.8 slice_dynamic-update-slice_fusion.2
  152.4 0.8 slice_dynamic-update-slice_fusion.1
  153.1 0.8 slice_dynamic-update-slice_fusion
  153.9 0.8 constant_dynamic-update-slice_fusion
  154.7 7.4 %all-to-all-start.1 = ((bf16[8,64,3072]{2,1,0:T(8,128)(2,1)}), bf16[8,64,3072]{2,1,0:T(8,128)(2,1)}, u32[]{:S(2)}, u32[]{:S(2)}) async-start(bf16[8,64,3072]{2,1,0:T(8,128)(2,1)} %constant_dynamic-update-slice_fusion), calls=%async_computation.1 | async-start | bytes 6291456 | tf_op jit(solution)/shard_map/all_to_all | solution.py:116
  162.1 0.1 copy.18
  162.3 0.4 select_reduce_fusion
  162.8 1.9 convolution_bitcast_fusion.1
  164.7 37.4 %all-to-all-done.1 = bf16[8,64,3072]{2,1,0:T(8,128)(2,1)} async-done(((bf16[8,64,3072]{2,1,0:T(8,128)(2,1)}), bf16[8,64,3072]{2,1,0:T(8,128)(2,1)}, u32[]{:S(2)}, u32[]{:S(2)}) %all-to-all-start.1) | async-done | bytes 3145760 | tf_op jit(solution)/shard_map/all_to_all | solution.py:116
  202.1 3.9 %fusion.37 = bf16[128,3072]{1,0:T(8,128)(2,1)} fusion(f32[128,3072]{1,0:T(8,128)} %convolution_bitcast_fusion.1, bf16[8,64,3072]{2,1,0:T(8,128)(2,1)} %all-to-all-done.1, s32[8,64]{1,0:T(8,128)S(1)} %bitcast.173, bf16[8,128]{1,0:T(8,128)(2,1)S(1)} %get-tuple-element.59), kind=kOutput, calls=%fused_computation.33 | convolution fusion | flops 403570688 | bytes 5509120 | tf_op jit(solution)/shard_map/dot_general | solution.py:133
  (72 shorter events, 1.3 us)
Async XLA Ops:
  2.1 45.6 %slice-start = ((s8[15728640]{0:T(1024)(128)(4,1)}), s8[3145728]{0:T(1024)(128)(4,1)S(1)}, s32[]{:S(2)}) async-start(s8[15728640]{0:T(1024)(128)(4,1)} %bitcast.150), calls=%async_computation.2 | async-start | bytes 6291456
  4.7 22.2 %collective-permute-start = (bf16[129,3072]{1,0:T(8,128)(2,1)}, bf16[129,3072]{1,0:T(8,128)(2,1)}, u32[]{:S(2)}, u32[]{:S(2)}) collective-permute-start(bf16[129,3072]{1,0:T(8,128)(2,1)} %get-tuple-element.48), channel_id=1, source_target_pairs={{0,2},{2,0},{1,3},{3,1},{4,6},{6,4},{5,7},{7,5},{8,10},{10,8},{9,1... | collective-permute-start | bytes 2377736 | tf_op jit(solution)/shard_map/ppermute | solution.py:31
  8.0 21.9 %collective-permute-start.3 = (bf16[129,3072]{1,0:T(8,128)(2,1)}, bf16[129,3072]{1,0:T(8,128)(2,1)}, u32[]{:S(2)}, u32[]{:S(2)}) collective-permute-start(bf16[129,3072]{1,0:T(8,128)(2,1)} %get-tuple-element.48), channel_id=1, source_target_pairs={{0,12},{4,0},{8,4},{12,8},{1,13},{5,1},{9,5},{13,9},{2,14},{6,2},{... | collective-permute-start | bytes 2377736 | tf_op jit(solution)/shard_map/ppermute | solution.py:27
  12.1 21.3 %collective-permute-start.1 = (bf16[129,3072]{1,0:T(8,128)(2,1)}, bf16[129,3072]{1,0:T(8,128)(2,1)}, u32[]{:S(2)}, u32[]{:S(2)}) collective-permute-start(bf16[129,3072]{1,0:T(8,128)(2,1)} %get-tuple-element.48), channel_id=1, source_target_pairs={{0,4},{4,8},{8,12},{12,0},{1,5},{5,9},{9,13},{13,1},{2,6},{6,10},{... | collective-permute-start | bytes 2377736 | tf_op jit(solution)/shard_map/ppermute | solution.py:27
  34.3 13.4 %slice-start.1 = ((s8[15728640]{0:T(1024)(128)(4,1)}), s8[4194304]{0:T(1024)(128)(4,1)S(1)}, s32[]{:S(2)}) async-start(s8[15728640]{0:T(1024)(128)(4,1)} %bitcast.150), calls=%async_computation.3 | async-start | bytes 8388608
  34.3 13.4 %slice-start.2 = ((s8[15728640]{0:T(1024)(128)(4,1)}), s8[4194304]{0:T(1024)(128)(4,1)S(1)}, s32[]{:S(2)}) async-start(s8[15728640]{0:T(1024)(128)(4,1)} %bitcast.150), calls=%async_computation.4 | async-start | bytes 8388608
  37.3 10.3 %slice-start.3 = ((s8[15728640]{0:T(1024)(128)(4,1)}), s8[4194304]{0:T(1024)(128)(4,1)S(1)}, s32[]{:S(2)}) async-start(s8[15728640]{0:T(1024)(128)(4,1)} %bitcast.150), calls=%async_computation.5 | async-start | bytes 8388608
  41.8 28.6 %collective-permute-start.2 = (bf16[193,3072]{1,0:T(8,128)(2,1)S(1)}, bf16[193,3072]{1,0:T(8,128)(2,1)S(1)}, u32[]{:S(2)}, u32[]{:S(2)}) collective-permute-start(bf16[193,3072]{1,0:T(8,128)(2,1)S(1)} %pad_maximum_fusion.8), channel_id=1, source_target_pairs={{0,4},{4,8},{8,12},{12,0},{1,5},{5,9},{9,13},{13,1},{2,6},{6,10},{... | collective-permute-start | bytes 3557384 | tf_op jit(solution)/shard_map/ppermute | solution.py:27
  42.9 10.5 %slice-start.8 = ((s8[7864320]{0:T(1024)(128)(4,1)}), s8[4194304]{0:T(1024)(128)(4,1)S(1)}, s32[]{:S(2)}) async-start(s8[7864320]{0:T(1024)(128)(4,1)} %bitcast.154), calls=%async_computation.10 | async-start | bytes 8388608
  44.4 27.8 %collective-permute-start.4 = (bf16[194,3072]{1,0:T(8,128)(2,1)S(1)}, bf16[194,3072]{1,0:T(8,128)(2,1)S(1)}, u32[]{:S(2)}, u32[]{:S(2)}) collective-permute-start(bf16[194,3072]{1,0:T(8,128)(2,1)S(1)} %pad_maximum_fusion.9), channel_id=1, source_target_pairs={{0,12},{4,0},{8,4},{12,8},{1,13},{5,1},{9,5},{13,9},{2,14},{6,2},{... | collective-permute-start | bytes 3575816 | tf_op jit(solution)/shard_map/ppermute | solution.py:27
  47.7 5.7 %slice-start.9 = ((s8[7864320]{0:T(1024)(128)(4,1)}), s8[3670016]{0:T(1024)(128)(4,1)S(1)}, s32[]{:S(2)}) async-start(s8[7864320]{0:T(1024)(128)(4,1)} %bitcast.154), calls=%async_computation.11 | async-start | bytes 7340032
  72.4 19.4 %collective-permute-start.5 = (bf16[129,3072]{1,0:T(8,128)(2,1)S(1)}, bf16[129,3072]{1,0:T(8,128)(2,1)S(1)}, u32[]{:S(2)}, u32[]{:S(2)}) collective-permute-start(bf16[129,3072]{1,0:T(8,128)(2,1)S(1)} %pad_maximum_fusion.10), channel_id=1, source_target_pairs={{0,2},{2,0},{1,3},{3,1},{4,6},{6,4},{5,7},{7,5},{8,10},{10,8},{9,1... | collective-permute-start | bytes 2377736 | tf_op jit(solution)/shard_map/ppermute | solution.py:31
  74.0 8.9 %slice-start.10 = ((s8[7864320]{0:T(1024)(128)(4,1)}), s8[4194304]{0:T(1024)(128)(4,1)S(1)}, s32[]{:S(2)}) async-start(s8[7864320]{0:T(1024)(128)(4,1)} %bitcast.156), calls=%async_computation.12 | async-start | bytes 8388608
  75.3 7.7 %slice-start.11 = ((s8[7864320]{0:T(1024)(128)(4,1)}), s8[3670016]{0:T(1024)(128)(4,1)S(1)}, s32[]{:S(2)}) async-start(s8[7864320]{0:T(1024)(128)(4,1)} %bitcast.156), calls=%async_computation.13 | async-start | bytes 7340032
  106.8 5.5 %collective-permute-start.10 = (bf16[1,64,3072]{2,1,0:T(8,128)(2,1)}, bf16[1,64,3072]{2,1,0:T(8,128)(2,1)S(1)}, u32[]{:S(2)}, u32[]{:S(2)}) collective-permute-start(bf16[1,64,3072]{2,1,0:T(8,128)(2,1)} %slice_bitcast_fusion.4), channel_id=1, source_target_pairs={{0,1},{1,0},{2,3},{3,2},{4,5},{5,4},{6,7},{7,6},{8,9},{9,8},{10,11... | collective-permute-start | bytes 1179656 | tf_op jit(solution)/shard_map/ppermute | solution.py:31
  106.9 19.6 %collective-permute-start.6 = (bf16[4,64,3072]{2,1,0:T(8,128)(2,1)}, bf16[4,64,3072]{2,1,0:T(8,128)(2,1)}, u32[]{:S(2)}, u32[]{:S(2)}) collective-permute-start(bf16[4,64,3072]{2,1,0:T(8,128)(2,1)} %get-tuple-element.36), channel_id=1, source_target_pairs={{0,1},{1,0},{2,3},{3,2},{4,5},{5,4},{6,7},{7,6},{8,9},{9,8},{10,11... | collective-permute-start | bytes 4718600 | tf_op jit(solution)/shard_map/ppermute | solution.py:31
  107.4 47.4 %all-to-all-start = ((bf16[8,64,3072]{2,1,0:T(8,128)(2,1)}), bf16[8,64,3072]{2,1,0:T(8,128)(2,1)S(1)}, u32[]{:S(2)}, u32[]{:S(2)}) async-start(bf16[8,64,3072]{2,1,0:T(8,128)(2,1)} %fusion.51), calls=%async_computation | async-start | bytes 6291456 | tf_op jit(solution)/shard_map/all_to_all | solution.py:109
  112.3 25.7 %collective-permute-start.8 = (bf16[3,64,3072]{2,1,0:T(8,128)(2,1)}, bf16[3,64,3072]{2,1,0:T(8,128)(2,1)S(1)}, u32[]{:S(2)}, u32[]{:S(2)}) collective-permute-start(bf16[3,64,3072]{2,1,0:T(8,128)(2,1)} %get-tuple-element.37), channel_id=1, source_target_pairs={{0,1},{1,0},{2,3},{3,2},{4,5},{5,4},{6,7},{7,6},{8,9},{9,8},{10,11... | collective-permute-start | bytes 3538952 | tf_op jit(solution)/shard_map/ppermute | solution.py:31
  112.3 14.1 %slice-start.4 = ((s8[15728640]{0:T(1024)(128)(4,1)}), s8[4194304]{0:T(1024)(128)(4,1)S(1)}, s32[]{:S(2)}) async-start(s8[15728640]{0:T(1024)(128)(4,1)} %bitcast.152), calls=%async_computation.6 | async-start | bytes 8388608
  112.4 14.1 %slice-start.5 = ((s8[15728640]{0:T(1024)(128)(4,1)}), s8[4194304]{0:T(1024)(128)(4,1)S(1)}, s32[]{:S(2)}) async-start(s8[15728640]{0:T(1024)(128)(4,1)} %bitcast.152), calls=%async_computation.7 | async-start | bytes 8388608
  112.4 14.1 %slice-start.6 = ((s8[15728640]{0:T(1024)(128)(4,1)}), s8[4194304]{0:T(1024)(128)(4,1)S(1)}, s32[]{:S(2)}) async-start(s8[15728640]{0:T(1024)(128)(4,1)} %bitcast.152), calls=%async_computation.8 | async-start | bytes 8388608
  120.8 5.7 %slice-start.7 = ((s8[15728640]{0:T(1024)(128)(4,1)}), s8[3145728]{0:T(1024)(128)(4,1)S(1)}, s32[]{:S(2)}) async-start(s8[15728640]{0:T(1024)(128)(4,1)} %bitcast.152), calls=%async_computation.9 | async-start | bytes 6291456
  120.8 13.0 %slice-start.12 = ((s8[7864320]{0:T(1024)(128)(4,1)}), s8[4194304]{0:T(1024)(128)(4,1)S(1)}, s32[]{:S(2)}) async-start(s8[7864320]{0:T(1024)(128)(4,1)} %bitcast.158), calls=%async_computation.14 | async-start | bytes 8388608
  125.7 28.3 %collective-permute-start.11 = (bf16[1,64,3072]{2,1,0:T(8,128)(2,1)S(1)}, bf16[1,64,3072]{2,1,0:T(8,128)(2,1)S(1)}, u32[]{:S(2)}, u32[]{:S(2)}) collective-permute-start(bf16[1,64,3072]{2,1,0:T(8,128)(2,1)S(1)} %fusion.45), channel_id=1, source_target_pairs={{0,1},{1,0},{2,3},{3,2},{4,5},{5,4},{6,7},{7,6},{8,9},{9,8},{10,11... | collective-permute-start | bytes 1179656 | tf_op jit(solution)/shard_map/ppermute | solution.py:31
  126.5 7.3 %slice-start.13 = ((s8[7864320]{0:T(1024)(128)(4,1)}), s8[3670016]{0:T(1024)(128)(4,1)S(1)}, s32[]{:S(2)}) async-start(s8[7864320]{0:T(1024)(128)(4,1)} %bitcast.158), calls=%async_computation.15 | async-start | bytes 7340032
  137.9 8.5 %collective-permute-start.7 = (bf16[4,64,3072]{2,1,0:T(8,128)(2,1)S(1)}, bf16[4,64,3072]{2,1,0:T(8,128)(2,1)S(1)}, u32[]{:S(2)}, u32[]{:S(2)}) collective-permute-start(bf16[4,64,3072]{2,1,0:T(8,128)(2,1)S(1)} %bitcast.174), channel_id=1, source_target_pairs={{0,1},{1,0},{2,3},{3,2},{4,5},{5,4},{6,7},{7,6},{8,9},{9,8},{10,11... | collective-permute-start | bytes 4718600 | tf_op jit(solution)/shard_map/ppermute | solution.py:31
  145.8 5.7 %collective-permute-start.9 = (bf16[3,64,3072]{2,1,0:T(8,128)(2,1)S(1)}, bf16[3,64,3072]{2,1,0:T(8,128)(2,1)S(1)}, u32[]{:S(2)}, u32[]{:S(2)}) collective-permute-start(bf16[3,64,3072]{2,1,0:T(8,128)(2,1)S(1)} %bitcast.176), channel_id=1, source_target_pairs={{0,1},{1,0},{2,3},{3,2},{4,5},{5,4},{6,7},{7,6},{8,9},{9,8},{10,11... | collective-permute-start | bytes 3538952 | tf_op jit(solution)/shard_map/ppermute | solution.py:31
  154.7 7.4 %copy-start.1 = (f32[128,4]{0,1:T(4,128)S(1)}, f32[128,4]{0,1:T(4,128)}, u32[]{:S(2)}) copy-start(f32[128,4]{0,1:T(4,128)} %param.10) | copy-start | bytes 6148
  154.7 7.5 %copy-start.2 = (s32[128,4]{0,1:T(4,128)S(1)}, s32[128,4]{0,1:T(4,128)}, u32[]{:S(2)}) copy-start(s32[128,4]{0,1:T(4,128)} %param.9) | copy-start | bytes 6148
  154.7 8.1 %copy-start = (s32[1,16,64]{2,1,0:T(8,128)S(1)}, s32[1,16,64]{2,1,0:T(8,128)}, u32[]{:S(2)}) copy-start(s32[1,16,64]{2,1,0:T(8,128)} %param.11) | copy-start | bytes 12292
  154.7 47.4 %all-to-all-start.1 = ((bf16[8,64,3072]{2,1,0:T(8,128)(2,1)}), bf16[8,64,3072]{2,1,0:T(8,128)(2,1)}, u32[]{:S(2)}, u32[]{:S(2)}) async-start(bf16[8,64,3072]{2,1,0:T(8,128)(2,1)} %constant_dynamic-update-slice_fusion), calls=%async_computation.1 | async-start | bytes 6291456 | tf_op jit(solution)/shard_map/all_to_all | solution.py:116

commit v12 on v10

--- a/solution.py
+++ b/solution.py
@@ -78,10 +78,13 @@
             axis=1,
         )
         one_hot = (sel[..., None] == token_iota).astype(jnp.bfloat16)
-        disp = jnp.einsum(
-            "bjct,btd->bjcd", one_hot, toks, preferred_element_type=jnp.float32
-        ).astype(jnp.bfloat16)
-        return disp[:, 0], swap(disp[:, 1], "core")
+        disp = [
+            jnp.einsum(
+                "bct,btd->bcd", one_hot[:, j], toks, preferred_element_type=jnp.float32
+            ).astype(jnp.bfloat16)
+            for j in range(2)
+        ]
+        return disp[0], swap(disp[1], "core")
 
     def place(into, pieces, outs):
         for i, (r, q, _) in enumerate(pieces):

time: 188 us -> 187 us (level)
  waiting for transfers between devices: 80.2 us -> 76.6 us
  local copies, waits for them, and re-layouts: 20.4 us -> 17.7 us
  starting transfers between devices: 24.6 us -> 27.2 us
    ppermute x5, waiting for transfers between devices: 14.8 us -> 0.32 us  [swap(): return lax.ppermute(x, axis, [(0, 1), (1, 0)])]
    ppermute x6, waiting for transfers between devices: 23 us -> 33.9 us  [shift_z(): return lax.ppermute(x, 'z', [(i, (i + step) % RING) for i in range(RING)])]
    squeeze x2 -> x0, local copies, waits for them, and re-layouts: 2.84 us -> none  [slots_of(): return (disp[:, 0], swap(disp[:, 1], 'core'))]
    all_to_all x1, starting transfers between devices: 4.99 us -> 7.52 us  [shards(): ret_a = lax.all_to_all(a_abs, ('z', 'yh'), 0, 0, tiled=True)]
    dot_general x2 -> x4, matrix products: 5.69 us -> 5.92 us  [slots_of(): jnp.einsum('bct,btd->bcd', one_hot[:, j], toks, preferred_element_type=jn...]
where the time goes in v12:
time: 187 us; the launch traced here: 186 us
  waiting for transfers between devices  76.6 us (41%)
  matrix products  59 us (32%)
  starting transfers between devices  27.2 us (15%)
  local copies, waits for them, and re-layouts  17.7 us (9%)
  other arithmetic  5.45 us (3%)
    all_to_all x1, waiting for transfers between devices, shards(): ret_b = lax.all_to_all(b_abs, ('z', 'yh'), 0, 0, tiled=True)  36.9 us
    ppermute x6, waiting for transfers between devices, shift_z(): return lax.ppermute(x, 'z', [(i, (i + step) % RING) for i in range(RING)])  33.9 us
    dot_general x4, matrix products, expert_block(): projected = jnp.dot(flat, w_first, preferred_element_type=jnp.float32)  31 us
    dot_general x4, matrix products, expert_block(): jnp.dot(intermediate_activation, w_second, preferred_element_type=jnp.flo...  16.3 us
    dynamic_update_slice x16, local copies, waits for them, and re-layouts, place(): into = lax.dynamic_update_slice(into, outs[i:i + 1], (where, 0, 0))  12.5 us
    ppermute x6, starting transfers between devices, shift_z(): return lax.ppermute(x, 'z', [(i, (i + step) % RING) for i in range(RING)])  11 us
    all_to_all x1, starting transfers between devices, shards(): ret_a = lax.all_to_all(a_abs, ('z', 'yh'), 0, 0, tiled=True)  7.52 us
    dot_general x4, matrix products, slots_of(): jnp.einsum('bct,btd->bcd', one_hot[:, j], toks, preferred_element_type=jn...  5.92 us
  transfers between devices with their start and end apart: 13, of which 8 were waited for; matrix products, arithmetic and copies ran while one was open for 37% of the time, Pallas kernels for 0%

profile of v12, /device:TPU:0, one launch (start us, length us, event | category | flops | bytes accessed | tf_op | source)
XLA Modules:
  0.0 186.4 jit_solution(2546094758615112627)
XLA Ops:
  0.0 0.6 compare_reduce_fusion
  0.6 1.3 convert_select_fusion
  2.0 0.1 reshape.93
  2.1 2.3 %fusion.74 = (bf16[1,129,3072]{2,1,0:T(8,128)(2,1)S(1)}, bf16[129,3072]{1,0:T(8,128)(2,1)}) fusion(bf16[1,1024]{1,0:T(2,128)(2,1)S(1)} %reshape.93, bf16[128,3072]{1,0:T(8,128)(2,1)} %param.8), kind=kLoop, calls=%fused_computation.123 | loop fusion | flops 2377728 | bytes 2373632 | tf_op jit(solution)/shard_map/stack | solution.py:69
  4.3 4.1 %collective-permute-start.3 = (bf16[129,3072]{1,0:T(8,128)(2,1)}, bf16[129,3072]{1,0:T(8,128)(2,1)S(1)}, u32[]{:S(2)}, u32[]{:S(2)}) collective-permute-start(bf16[129,3072]{1,0:T(8,128)(2,1)} %get-tuple-element.44), channel_id=1, source_target_pairs={{0,12},{4,0},{8,4},{12,8},{1,13},{5,1},{9,5},{13,9},{2,14},{6,2},{... | collective-permute-start | bytes 2377736 | tf_op jit(solution)/shard_map/ppermute | solution.py:27
  8.5 3.2 %collective-permute-start = (bf16[129,3072]{1,0:T(8,128)(2,1)}, bf16[129,3072]{1,0:T(8,128)(2,1)S(1)}, u32[]{:S(2)}, u32[]{:S(2)}) collective-permute-start(bf16[129,3072]{1,0:T(8,128)(2,1)} %get-tuple-element.44), channel_id=1, source_target_pairs={{0,2},{2,0},{1,3},{3,1},{4,6},{6,4},{5,7},{7,5},{8,10},{10,8},{9,1... | collective-permute-start | bytes 2377736 | tf_op jit(solution)/shard_map/ppermute | solution.py:31
  11.7 15.0 %collective-permute-done.3 = bf16[129,3072]{1,0:T(8,128)(2,1)S(1)} collective-permute-done((bf16[129,3072]{1,0:T(8,128)(2,1)}, bf16[129,3072]{1,0:T(8,128)(2,1)S(1)}, u32[]{:S(2)}, u32[]{:S(2)}) %collective-permute-start.3) | collective-permute-done | bytes 792608 | tf_op jit(solution)/shard_map/ppermute | solution.py:27
  26.6 3.3 %collective-permute-done.1 = bf16[129,3072]{1,0:T(8,128)(2,1)S(1)} collective-permute-done((bf16[129,3072]{1,0:T(8,128)(2,1)}, bf16[129,3072]{1,0:T(8,128)(2,1)S(1)}, u32[]{:S(2)}, u32[]{:S(2)}) %collective-permute-start.1) | collective-permute-done | bytes 792608 | tf_op jit(solution)/shard_map/ppermute | solution.py:27
  29.9 0.3 collective-permute-done
  30.3 0.1 reshape.101
  30.4 0.1 iota_compare_fusion.5
  30.6 1.8 convolution_convert_fusion.1
  32.4 1.7 convolution_convert_fusion.3
  34.1 0.1 pad_maximum_fusion.6
  34.4 0.2 pad_maximum_fusion.7
  34.5 3.3 %collective-permute-start.4 = (bf16[194,3072]{1,0:T(8,128)(2,1)S(1)}, bf16[194,3072]{1,0:T(8,128)(2,1)S(1)}, u32[]{:S(2)}, u32[]{:S(2)}) collective-permute-start(bf16[194,3072]{1,0:T(8,128)(2,1)S(1)} %pad_maximum_fusion.7), channel_id=1, source_target_pairs={{0,12},{4,0},{8,4},{12,8},{1,13},{5,1},{9,5},{13,9},{2,14},{6,2},{... | collective-permute-start | bytes 3575816 | tf_op jit(solution)/shard_map/ppermute | solution.py:27
  37.9 7.2 %fusion.6 = f32[256,2560]{1,0:T(8,128)} fusion(bf16[256,3072]{1,0:T(8,128)(2,1)} %bitcast.146, bf16[1,3072,2560]{2,1,0:T(8,128)(2,1)S(1)} %bitcast.135), kind=kOutput, calls=%fused_computation.6 | convolution fusion | flops 4026531840 | bytes 19922944 | tf_op jit(solution)/shard_map/dot_general | solution.py:16
  45.1 4.1 %fusion.16 = bf16[256,3072]{1,0:T(8,128)(2,1)S(1)} fusion(bf16[1,1280,3072]{2,1,0:T(8,128)(2,1)S(1)} %bitcast.139, f32[256,2560]{1,0:T(8,128)} %fusion.6), kind=kOutput, calls=%fused_computation.16 | convolution fusion | flops 2016018432 | bytes 12058624 | tf_op jit(solution)/shard_map/dot_general | solution.py:20
  49.2 2.0 %broadcast_in_dim.38.clone = bf16[8,64,3072]{2,1,0:T(8,128)(2,1)} broadcast(bf16[]{:T(256)} %constant.158.clone.1), dimensions={} | broadcast | bytes 3145730 | tf_op jit(solution)/shard_map/broadcast_in_dim | solution.py:99
  51.3 0.8 fusion.51
  52.0 0.8 fusion.50
  52.8 0.8 fusion.49
  53.6 9.5 %collective-permute-done.2 = bf16[193,3072]{1,0:T(8,128)(2,1)S(1)} collective-permute-done((bf16[193,3072]{1,0:T(8,128)(2,1)S(1)}, bf16[193,3072]{1,0:T(8,128)(2,1)S(1)}, u32[]{:S(2)}, u32[]{:S(2)}) %collective-permute-start.2) | collective-permute-done | bytes 1185824 | tf_op jit(solution)/shard_map/ppermute | solution.py:27
  63.1 0.1 fusion.75
  63.3 0.1 fusion.76
  63.4 3.5 %collective-permute-start.6 = (bf16[65,3072]{1,0:T(8,128)(2,1)S(1)}, bf16[65,3072]{1,0:T(8,128)(2,1)S(1)}, u32[]{:S(2)}, u32[]{:S(2)}) collective-permute-start(bf16[65,3072]{1,0:T(8,128)(2,1)S(1)} %get-tuple-element.41), channel_id=1, source_target_pairs={{0,12},{4,0},{8,4},{12,8},{1,13},{5,1},{9,5},{13,9},{2,14},{6,2},{... | collective-permute-start | bytes 1198088 | tf_op jit(solution)/shard_map/ppermute | solution.py:27
  66.9 0.8 fusion.48
  67.9 5.4 %collective-permute-done.5 = bf16[64,3072]{1,0:T(8,128)(2,1)S(1)} collective-permute-done((bf16[64,3072]{1,0:T(8,128)(2,1)S(1)}, bf16[64,3072]{1,0:T(8,128)(2,1)S(1)}, u32[]{:S(2)}, u32[]{:S(2)}) %collective-permute-start.5) | collective-permute-done | bytes 393248 | tf_op jit(solution)/shard_map/ppermute | solution.py:27
  73.2 0.7 collective-permute-done.6
  74.1 0.1 reshape.102
  74.2 0.1 iota_compare_fusion.4
  74.3 1.7 convolution_convert_fusion
  76.0 0.8 convolution_convert_fusion.2
  76.8 8.1 %fusion.4 = f32[256,2560]{1,0:T(8,128)S(1)} fusion(bf16[256,3072]{1,0:T(8,128)(2,1)S(1)} %bitcast.147, bf16[1,3072,2560]{2,1,0:T(8,128)(2,1)} %param.12), kind=kOutput, calls=%fused_computation.4 | convolution fusion | flops 4026531840 | bytes 19922944 | tf_op jit(solution)/shard_map/dot_general | solution.py:16
  85.0 2.3 %fusion.19 = bf16[256,3072]{1,0:T(8,128)(2,1)S(1)} fusion(bf16[1,1280,3072]{2,1,0:T(8,128)(2,1)S(1)} %bitcast.141, f32[256,2560]{1,0:T(8,128)S(1)} %fusion.4), kind=kOutput, calls=%fused_computation.17 | convolution fusion | flops 2016018432 | bytes 12058624 | tf_op jit(solution)/shard_map/dot_general | solution.py:20
  87.3 0.1 collective-permute-start.8
  87.4 0.8 fusion.47
  88.2 0.8 fusion.46
  89.0 0.8 fusion.45
  89.8 0.8 fusion.44
  90.6 7.5 %all-to-all-start = ((bf16[8,64,3072]{2,1,0:T(8,128)(2,1)}), bf16[8,64,3072]{2,1,0:T(8,128)(2,1)S(1)}, u32[]{:S(2)}, u32[]{:S(2)}) async-start(bf16[8,64,3072]{2,1,0:T(8,128)(2,1)} %fusion.44), calls=%async_computation | async-start | bytes 6291456 | tf_op jit(solution)/shard_map/all_to_all | solution.py:107
  98.1 8.3 %fusion.2 = f32[256,2560]{1,0:T(8,128)S(1)} fusion(bf16[256,3072]{1,0:T(8,128)(2,1)} %bitcast.24, bf16[1,3072,2560]{2,1,0:T(8,128)(2,1)} %param.12), kind=kOutput, calls=%fused_computation.2 | convolution fusion | flops 4026531840 | bytes 19922944 | tf_op jit(solution)/shard_map/dot_general | solution.py:16
  106.5 5.8 %fusion.22 = bf16[256,3072]{1,0:T(8,128)(2,1)S(1)} fusion(bf16[1,1280,3072]{2,1,0:T(8,128)(2,1)} %param.13, f32[256,2560]{1,0:T(8,128)S(1)} %fusion.2), kind=kOutput, calls=%fused_computation.18 | convolution fusion | flops 2016018432 | bytes 12058624 | tf_op jit(solution)/shard_map/dot_general | solution.py:20
  112.3 0.5 collective-permute-start.9
  112.8 7.3 %fusion = f32[256,2560]{1,0:T(8,128)} fusion(bf16[256,3072]{1,0:T(8,128)(2,1)} %bitcast.26, bf16[1,3072,2560]{2,1,0:T(8,128)(2,1)S(1)} %bitcast.137), kind=kOutput, calls=%fused_computation | convolution fusion | flops 4026531840 | bytes 19922944 | tf_op jit(solution)/shard_map/dot_general | solution.py:16
  120.1 4.1 %fusion.25 = bf16[256,3072]{1,0:T(8,128)(2,1)S(1)} fusion(bf16[1,1280,3072]{2,1,0:T(8,128)(2,1)S(1)} %bitcast.143, f32[256,2560]{1,0:T(8,128)} %fusion), kind=kOutput, calls=%fused_computation.19 | convolution fusion | flops 2016018432 | bytes 12058624 | tf_op jit(solution)/shard_map/dot_general | solution.py:20
  124.2 0.4 collective-permute-start.10
  124.6 2.1 %broadcast_in_dim.38 = bf16[8,64,3072]{2,1,0:T(8,128)(2,1)} broadcast(bf16[]{:T(256)} %constant.158.clone.1), dimensions={} | broadcast | bytes 3145730 | tf_op jit(solution)/shard_map/broadcast_in_dim | solution.py:99
  126.6 0.8 slice_dynamic-update-slice_fusion.7
  127.4 0.8 slice_dynamic-update-slice_fusion.6
  128.2 0.8 slice_dynamic-update-slice_fusion.5
  128.9 0.8 slice_dynamic-update-slice_fusion.4
  129.7 0.8 slice_dynamic-update-slice_fusion.3
  130.6 0.8 slice_dynamic-update-slice_fusion.2
  131.3 0.8 slice_dynamic-update-slice_fusion.1
  132.1 0.8 slice_dynamic-update-slice_fusion
  132.9 5.5 %all-to-all-done = bf16[8,64,3072]{2,1,0:T(8,128)(2,1)S(1)} async-done(((bf16[8,64,3072]{2,1,0:T(8,128)(2,1)}), bf16[8,64,3072]{2,1,0:T(8,128)(2,1)S(1)}, u32[]{:S(2)}, u32[]{:S(2)}) %all-to-all-start) | async-done | bytes 3145760 | tf_op jit(solution)/shard_map/all_to_all | solution.py:107
  138.5 4.4 %all-to-all-start.1 = ((bf16[8,64,3072]{2,1,0:T(8,128)(2,1)}), bf16[8,64,3072]{2,1,0:T(8,128)(2,1)}, u32[]{:S(2)}, u32[]{:S(2)}) async-start(bf16[8,64,3072]{2,1,0:T(8,128)(2,1)} %slice_dynamic-update-slice_fusion), calls=%async_computation.1 | async-start | bytes 6291456 | tf_op jit(solution)/shard_map/all_to_all | solution.py:113
  142.9 0.1 copy.15
  143.0 0.1 copy.22
  143.1 0.4 select_reduce_fusion
  143.7 1.9 %convolution_bitcast_fusion.1 = f32[128,3072]{1,0:T(8,128)} fusion(bf16[8,64,3072]{2,1,0:T(8,128)(2,1)S(1)} %all-to-all-done, s32[8,64]{1,0:T(8,128)S(1)} %bitcast.132, bf16[8,128]{1,0:T(8,128)(2,1)S(1)} %get-tuple-element.54), kind=kOutput, calls=%fused_computation.25 | convolution fusion | flops 402784256 | bytes 4722688 | tf_op jit(solution)/shard_map/dot_general | solution.py:130
  145.5 36.9 %all-to-all-done.1 = bf16[8,64,3072]{2,1,0:T(8,128)(2,1)} async-done(((bf16[8,64,3072]{2,1,0:T(8,128)(2,1)}), bf16[8,64,3072]{2,1,0:T(8,128)(2,1)}, u32[]{:S(2)}, u32[]{:S(2)}) %all-to-all-start.1) | async-done | bytes 3145760 | tf_op jit(solution)/shard_map/all_to_all | solution.py:113
  182.4 3.9 %fusion.29 = bf16[128,3072]{1,0:T(8,128)(2,1)} fusion(f32[128,3072]{1,0:T(8,128)} %convolution_bitcast_fusion.1, bf16[8,64,3072]{2,1,0:T(8,128)(2,1)} %all-to-all-done.1, s32[8,64]{1,0:T(8,128)S(1)} %bitcast.133, bf16[8,128]{1,0:T(8,128)(2,1)S(1)} %get-tuple-element.53), kind=kOutput, calls=%fused_computation.27 | convolution fusion | flops 403570688 | bytes 5509120 | tf_op jit(solution)/shard_map/dot_general | solution.py:130
  (66 shorter events, 0.9 us)
Async XLA Ops:
  4.3 22.3 %collective-permute-start.3 = (bf16[129,3072]{1,0:T(8,128)(2,1)}, bf16[129,3072]{1,0:T(8,128)(2,1)S(1)}, u32[]{:S(2)}, u32[]{:S(2)}) collective-permute-start(bf16[129,3072]{1,0:T(8,128)(2,1)} %get-tuple-element.44), channel_id=1, source_target_pairs={{0,12},{4,0},{8,4},{12,8},{1,13},{5,1},{9,5},{13,9},{2,14},{6,2},{... | collective-permute-start | bytes 2377736 | tf_op jit(solution)/shard_map/ppermute | solution.py:27
  8.5 21.5 %collective-permute-start.1 = (bf16[129,3072]{1,0:T(8,128)(2,1)}, bf16[129,3072]{1,0:T(8,128)(2,1)S(1)}, u32[]{:S(2)}, u32[]{:S(2)}) collective-permute-start(bf16[129,3072]{1,0:T(8,128)(2,1)} %get-tuple-element.44), channel_id=1, source_target_pairs={{0,4},{4,8},{8,12},{12,0},{1,5},{5,9},{9,13},{13,1},{2,6},{6,10},{... | collective-permute-start | bytes 2377736 | tf_op jit(solution)/shard_map/ppermute | solution.py:27
  8.5 21.8 %collective-permute-start = (bf16[129,3072]{1,0:T(8,128)(2,1)}, bf16[129,3072]{1,0:T(8,128)(2,1)S(1)}, u32[]{:S(2)}, u32[]{:S(2)}) collective-permute-start(bf16[129,3072]{1,0:T(8,128)(2,1)} %get-tuple-element.44), channel_id=1, source_target_pairs={{0,2},{2,0},{1,3},{3,1},{4,6},{6,4},{5,7},{7,5},{8,10},{10,8},{9,1... | collective-permute-start | bytes 2377736 | tf_op jit(solution)/shard_map/ppermute | solution.py:31
  30.6 7.3 %slice-start = ((s8[15728640]{0:T(1024)(128)(4,1)}), s8[4194304]{0:T(1024)(128)(4,1)S(1)}, s32[]{:S(2)}) async-start(s8[15728640]{0:T(1024)(128)(4,1)} %bitcast.134), calls=%async_computation.2 | async-start | bytes 8388608
  30.6 7.2 %slice-start.1 = ((s8[15728640]{0:T(1024)(128)(4,1)}), s8[4194304]{0:T(1024)(128)(4,1)S(1)}, s32[]{:S(2)}) async-start(s8[15728640]{0:T(1024)(128)(4,1)} %bitcast.134), calls=%async_computation.3 | async-start | bytes 8388608
  32.4 5.5 %slice-start.2 = ((s8[15728640]{0:T(1024)(128)(4,1)}), s8[4194304]{0:T(1024)(128)(4,1)S(1)}, s32[]{:S(2)}) async-start(s8[15728640]{0:T(1024)(128)(4,1)} %bitcast.134), calls=%async_computation.4 | async-start | bytes 8388608
  32.4 5.5 %slice-start.3 = ((s8[15728640]{0:T(1024)(128)(4,1)}), s8[3145728]{0:T(1024)(128)(4,1)S(1)}, s32[]{:S(2)}) async-start(s8[15728640]{0:T(1024)(128)(4,1)} %bitcast.134), calls=%async_computation.5 | async-start | bytes 6291456
  34.2 28.9 %collective-permute-start.2 = (bf16[193,3072]{1,0:T(8,128)(2,1)S(1)}, bf16[193,3072]{1,0:T(8,128)(2,1)S(1)}, u32[]{:S(2)}, u32[]{:S(2)}) collective-permute-start(bf16[193,3072]{1,0:T(8,128)(2,1)S(1)} %pad_maximum_fusion.6), channel_id=1, source_target_pairs={{0,4},{4,8},{8,12},{12,0},{1,5},{5,9},{9,13},{13,1},{2,6},{6,10},{... | collective-permute-start | bytes 3557384 | tf_op jit(solution)/shard_map/ppermute | solution.py:27
  34.4 10.8 %slice-start.8 = ((s8[7864320]{0:T(1024)(128)(4,1)}), s8[4194304]{0:T(1024)(128)(4,1)S(1)}, s32[]{:S(2)}) async-start(s8[7864320]{0:T(1024)(128)(4,1)} %bitcast.138), calls=%async_computation.10 | async-start | bytes 8388608
  34.5 28.8 %collective-permute-start.4 = (bf16[194,3072]{1,0:T(8,128)(2,1)S(1)}, bf16[194,3072]{1,0:T(8,128)(2,1)S(1)}, u32[]{:S(2)}, u32[]{:S(2)}) collective-permute-start(bf16[194,3072]{1,0:T(8,128)(2,1)S(1)} %pad_maximum_fusion.7), channel_id=1, source_target_pairs={{0,12},{4,0},{8,4},{12,8},{1,13},{5,1},{9,5},{13,9},{2,14},{6,2},{... | collective-permute-start | bytes 3575816 | tf_op jit(solution)/shard_map/ppermute | solution.py:27
  37.8 60.3 %collective-permute-start.7 = (bf16[4,64,3072]{2,1,0:T(8,128)(2,1)}, bf16[4,64,3072]{2,1,0:T(8,128)(2,1)}, u32[]{:S(2)}, u32[]{:S(2)}) collective-permute-start(bf16[4,64,3072]{2,1,0:T(8,128)(2,1)} %convolution_convert_fusion.1), channel_id=1, source_target_pairs={{0,1},{1,0},{2,3},{3,2},{4,5},{5,4},{6,7},{7,6},{8,9},{9,8},{10,11... | collective-permute-start | bytes 4718600 | tf_op jit(solution)/shard_map/ppermute | solution.py:31
  37.9 7.3 %slice-start.9 = ((s8[7864320]{0:T(1024)(128)(4,1)}), s8[3670016]{0:T(1024)(128)(4,1)S(1)}, s32[]{:S(2)}) async-start(s8[7864320]{0:T(1024)(128)(4,1)} %bitcast.138), calls=%async_computation.11 | async-start | bytes 7340032
  63.2 10.0 %collective-permute-start.5 = (bf16[64,3072]{1,0:T(8,128)(2,1)S(1)}, bf16[64,3072]{1,0:T(8,128)(2,1)S(1)}, u32[]{:S(2)}, u32[]{:S(2)}) collective-permute-start(bf16[64,3072]{1,0:T(8,128)(2,1)S(1)} %get-tuple-element.39), channel_id=1, source_target_pairs={{0,4},{4,8},{8,12},{12,0},{1,5},{5,9},{9,13},{13,1},{2,6},{6,10},{... | collective-permute-start | bytes 1179656 | tf_op jit(solution)/shard_map/ppermute | solution.py:27
  63.4 10.5 %collective-permute-start.6 = (bf16[65,3072]{1,0:T(8,128)(2,1)S(1)}, bf16[65,3072]{1,0:T(8,128)(2,1)S(1)}, u32[]{:S(2)}, u32[]{:S(2)}) collective-permute-start(bf16[65,3072]{1,0:T(8,128)(2,1)S(1)} %get-tuple-element.41), channel_id=1, source_target_pairs={{0,12},{4,0},{8,4},{12,8},{1,13},{5,1},{9,5},{13,9},{2,14},{6,2},{... | collective-permute-start | bytes 1198088 | tf_op jit(solution)/shard_map/ppermute | solution.py:27
  76.0 8.9 %slice-start.10 = ((s8[7864320]{0:T(1024)(128)(4,1)}), s8[4194304]{0:T(1024)(128)(4,1)S(1)}, s32[]{:S(2)}) async-start(s8[7864320]{0:T(1024)(128)(4,1)} %bitcast.140), calls=%async_computation.12 | async-start | bytes 8388608
  76.8 8.2 %slice-start.11 = ((s8[7864320]{0:T(1024)(128)(4,1)}), s8[3670016]{0:T(1024)(128)(4,1)S(1)}, s32[]{:S(2)}) async-start(s8[7864320]{0:T(1024)(128)(4,1)} %bitcast.140), calls=%async_computation.13 | async-start | bytes 7340032
  87.3 10.8 %collective-permute-start.8 = (bf16[4,64,3072]{2,1,0:T(8,128)(2,1)}, bf16[4,64,3072]{2,1,0:T(8,128)(2,1)}, u32[]{:S(2)}, u32[]{:S(2)}) collective-permute-start(bf16[4,64,3072]{2,1,0:T(8,128)(2,1)} %convolution_convert_fusion), channel_id=1, source_target_pairs={{0,1},{1,0},{2,3},{3,2},{4,5},{5,4},{6,7},{7,6},{8,9},{9,8},{10,11... | collective-permute-start | bytes 4718600 | tf_op jit(solution)/shard_map/ppermute | solution.py:31
  90.6 47.9 %all-to-all-start = ((bf16[8,64,3072]{2,1,0:T(8,128)(2,1)}), bf16[8,64,3072]{2,1,0:T(8,128)(2,1)S(1)}, u32[]{:S(2)}, u32[]{:S(2)}) async-start(bf16[8,64,3072]{2,1,0:T(8,128)(2,1)} %fusion.44), calls=%async_computation | async-start | bytes 6291456 | tf_op jit(solution)/shard_map/all_to_all | solution.py:107
  98.1 14.7 %slice-start.4 = ((s8[15728640]{0:T(1024)(128)(4,1)}), s8[4194304]{0:T(1024)(128)(4,1)S(1)}, s32[]{:S(2)}) async-start(s8[15728640]{0:T(1024)(128)(4,1)} %bitcast.136), calls=%async_computation.6 | async-start | bytes 8388608
  98.1 14.7 %slice-start.5 = ((s8[15728640]{0:T(1024)(128)(4,1)}), s8[4194304]{0:T(1024)(128)(4,1)S(1)}, s32[]{:S(2)}) async-start(s8[15728640]{0:T(1024)(128)(4,1)} %bitcast.136), calls=%async_computation.7 | async-start | bytes 8388608
  98.1 14.7 %slice-start.6 = ((s8[15728640]{0:T(1024)(128)(4,1)}), s8[4194304]{0:T(1024)(128)(4,1)S(1)}, s32[]{:S(2)}) async-start(s8[15728640]{0:T(1024)(128)(4,1)} %bitcast.136), calls=%async_computation.8 | async-start | bytes 8388608
  106.4 6.4 %slice-start.7 = ((s8[15728640]{0:T(1024)(128)(4,1)}), s8[3145728]{0:T(1024)(128)(4,1)S(1)}, s32[]{:S(2)}) async-start(s8[15728640]{0:T(1024)(128)(4,1)} %bitcast.136), calls=%async_computation.9 | async-start | bytes 6291456
  106.4 13.6 %slice-start.12 = ((s8[7864320]{0:T(1024)(128)(4,1)}), s8[4194304]{0:T(1024)(128)(4,1)S(1)}, s32[]{:S(2)}) async-start(s8[7864320]{0:T(1024)(128)(4,1)} %bitcast.142), calls=%async_computation.14 | async-start | bytes 8388608
  112.3 12.3 %collective-permute-start.9 = (bf16[4,64,3072]{2,1,0:T(8,128)(2,1)S(1)}, bf16[4,64,3072]{2,1,0:T(8,128)(2,1)S(1)}, u32[]{:S(2)}, u32[]{:S(2)}) collective-permute-start(bf16[4,64,3072]{2,1,0:T(8,128)(2,1)S(1)} %bitcast.145), channel_id=1, source_target_pairs={{0,1},{1,0},{2,3},{3,2},{4,5},{5,4},{6,7},{7,6},{8,9},{9,8},{10,11... | collective-permute-start | bytes 4718600 | tf_op jit(solution)/shard_map/ppermute | solution.py:31
  112.8 7.3 %slice-start.13 = ((s8[7864320]{0:T(1024)(128)(4,1)}), s8[3670016]{0:T(1024)(128)(4,1)S(1)}, s32[]{:S(2)}) async-start(s8[7864320]{0:T(1024)(128)(4,1)} %bitcast.142), calls=%async_computation.15 | async-start | bytes 7340032
  124.2 5.6 %collective-permute-start.10 = (bf16[4,64,3072]{2,1,0:T(8,128)(2,1)S(1)}, bf16[4,64,3072]{2,1,0:T(8,128)(2,1)S(1)}, u32[]{:S(2)}, u32[]{:S(2)}) collective-permute-start(bf16[4,64,3072]{2,1,0:T(8,128)(2,1)S(1)} %bitcast.144), channel_id=1, source_target_pairs={{0,1},{1,0},{2,3},{3,2},{4,5},{5,4},{6,7},{7,6},{8,9},{9,8},{10,11... | collective-permute-start | bytes 4718600 | tf_op jit(solution)/shard_map/ppermute | solution.py:31
  132.9 10.0 %copy-start.1 = (s32[128,4]{0,1:T(4,128)S(1)}, s32[128,4]{0,1:T(4,128)}, u32[]{:S(2)}) copy-start(s32[128,4]{0,1:T(4,128)} %param.9) | copy-start | bytes 6148
  132.9 10.1 %copy-start.2 = (f32[128,4]{0,1:T(4,128)S(1)}, f32[128,4]{0,1:T(4,128)}, u32[]{:S(2)}) copy-start(f32[128,4]{0,1:T(4,128)} %param.10) | copy-start | bytes 6148
  132.9 10.7 %copy-start = (s32[1,16,64]{2,1,0:T(8,128)S(1)}, s32[1,16,64]{2,1,0:T(8,128)}, u32[]{:S(2)}) copy-start(s32[1,16,64]{2,1,0:T(8,128)} %param.11) | copy-start | bytes 12292
  138.5 44.0 %all-to-all-start.1 = ((bf16[8,64,3072]{2,1,0:T(8,128)(2,1)}), bf16[8,64,3072]{2,1,0:T(8,128)(2,1)}, u32[]{:S(2)}, u32[]{:S(2)}) async-start(bf16[8,64,3072]{2,1,0:T(8,128)(2,1)} %slice_dynamic-update-slice_fusion), calls=%async_computation.1 | async-start | bytes 6291456 | tf_op jit(solution)/shard_map/all_to_all | solution.py:113

commit v13 on v12

--- a/solution.py
+++ b/solution.py
@@ -44,8 +44,13 @@
     n_y = 2
     blocks = RING * n_y
 
-    meta = jnp.zeros((1, features), jnp.bfloat16)
-    meta = meta.at[0, : experts * capacity].set(own_rows.reshape(-1).astype(jnp.bfloat16))
+    meta = jnp.concatenate(
+        [
+            own_rows.reshape(1, -1).astype(jnp.bfloat16),
+            jnp.zeros((1, features - experts * capacity), jnp.bfloat16),
+        ],
+        axis=1,
+    )
     block = jnp.concatenate([tokens, meta], axis=0)
 
     half = (tok_rows + 1) // 2

time: 187 us -> 185 us (0.989)
    another operation x2 -> x0, other arithmetic: 1.98 us -> none
  transfers between devices with their start and end apart: 13 -> 13, of which waited for: 8 -> 8; matrix products, arithmetic and copies ran while one was open for 37% -> 38% of each run, Pallas kernels for 0% -> 0%
where the time goes in v13:
time: 185 us
  waiting for transfers between devices  76.7 us (41%)
  matrix products  59 us (32%)
  starting transfers between devices  27.1 us (15%)
  local copies, waits for them, and re-layouts  17.7 us (10%)
  other arithmetic  4.17 us (2%)
    all_to_all x1, waiting for transfers between devices, shards(): ret_b = lax.all_to_all(b_abs, ('z', 'yh'), 0, 0, tiled=True)  36.9 us
    ppermute x6, waiting for transfers between devices, shift_z(): return lax.ppermute(x, 'z', [(i, (i + step) % RING) for i in range(RING)])  33.9 us
    dot_general x4, matrix products, expert_block(): projected = jnp.dot(flat, w_first, preferred_element_type=jnp.float32)  31 us
    dot_general x4, matrix products, expert_block(): jnp.dot(intermediate_activation, w_second, preferred_element_type=jnp.flo...  16.3 us
    dynamic_update_slice x16, local copies, waits for them, and re-layouts, place(): into = lax.dynamic_update_slice(into, outs[i:i + 1], (where, 0, 0))  12.5 us
    ppermute x6, starting transfers between devices, shift_z(): return lax.ppermute(x, 'z', [(i, (i + step) % RING) for i in range(RING)])  11 us
    all_to_all x1, starting transfers between devices, shards(): ret_a = lax.all_to_all(a_abs, ('z', 'yh'), 0, 0, tiled=True)  7.5 us
    dot_general x4, matrix products, slots_of(): jnp.einsum('bct,btd->bcd', one_hot[:, j], toks, preferred_element_type=jn...  5.91 us
  transfers between devices with their start and end apart: 13, of which 8 were waited for; matrix products, arithmetic and copies ran while one was open for 38% of the time, Pallas kernels for 0%

profile of v13, /device:TPU:0, one launch (start us, length us, event | category | flops | bytes accessed | tf_op | source)
XLA Modules:
  0.0 185.1 jit_solution(13775811949365879361)
XLA Ops:
  0.0 0.7 convert_element_type.76
  0.7 0.1 convert_element_type.77
  0.8 2.3 %fusion.74 = (bf16[1,129,3072]{2,1,0:T(8,128)(2,1)S(1)}, bf16[129,3072]{1,0:T(8,128)(2,1)}) fusion(bf16[1,1024]{1,0:T(2,128)(2,1)S(1)} %convert_element_type.77, bf16[128,3072]{1,0:T(8,128)(2,1)} %param.6), kind=kLoop, calls=%fused_computation.121 | loop fusion | flops 2377728 | bytes 2373632 | tf_op jit(solution)/shard_map/stack | solution.py:74
  3.1 4.1 %collective-permute-start.3 = (bf16[129,3072]{1,0:T(8,128)(2,1)}, bf16[129,3072]{1,0:T(8,128)(2,1)S(1)}, u32[]{:S(2)}, u32[]{:S(2)}) collective-permute-start(bf16[129,3072]{1,0:T(8,128)(2,1)} %get-tuple-element.32), channel_id=1, source_target_pairs={{0,12},{4,0},{8,4},{12,8},{1,13},{5,1},{9,5},{13,9},{2,14},{6,2},{... | collective-permute-start | bytes 2377736 | tf_op jit(solution)/shard_map/ppermute | solution.py:27
  7.2 3.2 %collective-permute-start = (bf16[129,3072]{1,0:T(8,128)(2,1)}, bf16[129,3072]{1,0:T(8,128)(2,1)S(1)}, u32[]{:S(2)}, u32[]{:S(2)}) collective-permute-start(bf16[129,3072]{1,0:T(8,128)(2,1)} %get-tuple-element.32), channel_id=1, source_target_pairs={{0,2},{2,0},{1,3},{3,1},{4,6},{6,4},{5,7},{7,5},{8,10},{10,8},{9,1... | collective-permute-start | bytes 2377736 | tf_op jit(solution)/shard_map/ppermute | solution.py:31
  10.4 15.0 %collective-permute-done.3 = bf16[129,3072]{1,0:T(8,128)(2,1)S(1)} collective-permute-done((bf16[129,3072]{1,0:T(8,128)(2,1)}, bf16[129,3072]{1,0:T(8,128)(2,1)S(1)}, u32[]{:S(2)}, u32[]{:S(2)}) %collective-permute-start.3) | collective-permute-done | bytes 792608 | tf_op jit(solution)/shard_map/ppermute | solution.py:27
  25.3 3.3 %collective-permute-done.1 = bf16[129,3072]{1,0:T(8,128)(2,1)S(1)} collective-permute-done((bf16[129,3072]{1,0:T(8,128)(2,1)}, bf16[129,3072]{1,0:T(8,128)(2,1)S(1)}, u32[]{:S(2)}, u32[]{:S(2)}) %collective-permute-start.1) | collective-permute-done | bytes 792608 | tf_op jit(solution)/shard_map/ppermute | solution.py:27
  28.6 0.3 collective-permute-done
  29.0 0.1 reshape.70
  29.1 0.1 iota_compare_fusion.5
  29.3 1.8 convolution_convert_fusion.1
  31.1 1.7 convolution_convert_fusion.3
  32.8 0.1 pad_maximum_fusion.6
  33.0 0.1 collective-permute-start.2
  33.1 0.2 pad_maximum_fusion.7
  33.2 3.3 %collective-permute-start.4 = (bf16[194,3072]{1,0:T(8,128)(2,1)S(1)}, bf16[194,3072]{1,0:T(8,128)(2,1)S(1)}, u32[]{:S(2)}, u32[]{:S(2)}) collective-permute-start(bf16[194,3072]{1,0:T(8,128)(2,1)S(1)} %pad_maximum_fusion.7), channel_id=1, source_target_pairs={{0,12},{4,0},{8,4},{12,8},{1,13},{5,1},{9,5},{13,9},{2,14},{6,2},{... | collective-permute-start | bytes 3575816 | tf_op jit(solution)/shard_map/ppermute | solution.py:27
  36.6 7.3 %fusion.6 = f32[256,2560]{1,0:T(8,128)} fusion(bf16[256,3072]{1,0:T(8,128)(2,1)} %bitcast.146, bf16[1,3072,2560]{2,1,0:T(8,128)(2,1)S(1)} %bitcast.135), kind=kOutput, calls=%fused_computation.6 | convolution fusion | flops 4026531840 | bytes 19922944 | tf_op jit(solution)/shard_map/dot_general | solution.py:16
  43.8 4.1 %fusion.16 = bf16[256,3072]{1,0:T(8,128)(2,1)S(1)} fusion(bf16[1,1280,3072]{2,1,0:T(8,128)(2,1)S(1)} %bitcast.139, f32[256,2560]{1,0:T(8,128)} %fusion.6), kind=kOutput, calls=%fused_computation.16 | convolution fusion | flops 2016018432 | bytes 12058624 | tf_op jit(solution)/shard_map/dot_general | solution.py:20
  47.9 2.0 %broadcast_in_dim.38.clone = bf16[8,64,3072]{2,1,0:T(8,128)(2,1)} broadcast(bf16[]{:T(256)} %constant.129.clone.1), dimensions={} | broadcast | bytes 3145730 | tf_op jit(solution)/shard_map/broadcast_in_dim | solution.py:104
  50.0 0.8 fusion.51
  50.7 0.8 fusion.50
  51.5 0.8 fusion.49
  52.3 9.5 %collective-permute-done.2 = bf16[193,3072]{1,0:T(8,128)(2,1)S(1)} collective-permute-done((bf16[193,3072]{1,0:T(8,128)(2,1)S(1)}, bf16[193,3072]{1,0:T(8,128)(2,1)S(1)}, u32[]{:S(2)}, u32[]{:S(2)}) %collective-permute-start.2) | collective-permute-done | bytes 1185824 | tf_op jit(solution)/shard_map/ppermute | solution.py:27
  61.8 0.1 fusion.75
  62.0 0.1 fusion.76
  62.1 3.5 %collective-permute-start.6 = (bf16[65,3072]{1,0:T(8,128)(2,1)S(1)}, bf16[65,3072]{1,0:T(8,128)(2,1)S(1)}, u32[]{:S(2)}, u32[]{:S(2)}) collective-permute-start(bf16[65,3072]{1,0:T(8,128)(2,1)S(1)} %get-tuple-element.29), channel_id=1, source_target_pairs={{0,12},{4,0},{8,4},{12,8},{1,13},{5,1},{9,5},{13,9},{2,14},{6,2},{... | collective-permute-start | bytes 1198088 | tf_op jit(solution)/shard_map/ppermute | solution.py:27
  65.6 0.8 fusion.48
  66.6 5.4 %collective-permute-done.5 = bf16[64,3072]{1,0:T(8,128)(2,1)S(1)} collective-permute-done((bf16[64,3072]{1,0:T(8,128)(2,1)S(1)}, bf16[64,3072]{1,0:T(8,128)(2,1)S(1)}, u32[]{:S(2)}, u32[]{:S(2)}) %collective-permute-start.5) | collective-permute-done | bytes 393248 | tf_op jit(solution)/shard_map/ppermute | solution.py:27
  72.0 0.7 collective-permute-done.6
  72.8 0.1 reshape.71
  72.9 0.1 iota_compare_fusion.4
  73.0 1.7 convolution_convert_fusion
  74.7 0.8 convolution_convert_fusion.2
  75.5 8.2 %fusion.4 = f32[256,2560]{1,0:T(8,128)S(1)} fusion(bf16[256,3072]{1,0:T(8,128)(2,1)S(1)} %bitcast.147, bf16[1,3072,2560]{2,1,0:T(8,128)(2,1)} %param.10), kind=kOutput, calls=%fused_computation.4 | convolution fusion | flops 4026531840 | bytes 19922944 | tf_op jit(solution)/shard_map/dot_general | solution.py:16
  83.7 2.3 %fusion.19 = bf16[256,3072]{1,0:T(8,128)(2,1)S(1)} fusion(bf16[1,1280,3072]{2,1,0:T(8,128)(2,1)S(1)} %bitcast.141, f32[256,2560]{1,0:T(8,128)S(1)} %fusion.4), kind=kOutput, calls=%fused_computation.17 | convolution fusion | flops 2016018432 | bytes 12058624 | tf_op jit(solution)/shard_map/dot_general | solution.py:20
  86.0 0.1 collective-permute-start.8
  86.1 0.8 fusion.47
  86.9 0.8 fusion.46
  87.7 0.8 fusion.45
  88.5 0.8 fusion.44
  89.3 7.5 %all-to-all-start = ((bf16[8,64,3072]{2,1,0:T(8,128)(2,1)}), bf16[8,64,3072]{2,1,0:T(8,128)(2,1)S(1)}, u32[]{:S(2)}, u32[]{:S(2)}) async-start(bf16[8,64,3072]{2,1,0:T(8,128)(2,1)} %fusion.44), calls=%async_computation | async-start | bytes 6291456 | tf_op jit(solution)/shard_map/all_to_all | solution.py:112
  96.8 8.3 %fusion.2 = f32[256,2560]{1,0:T(8,128)S(1)} fusion(bf16[256,3072]{1,0:T(8,128)(2,1)} %bitcast.24, bf16[1,3072,2560]{2,1,0:T(8,128)(2,1)} %param.10), kind=kOutput, calls=%fused_computation.2 | convolution fusion | flops 4026531840 | bytes 19922944 | tf_op jit(solution)/shard_map/dot_general | solution.py:16
  105.1 5.8 %fusion.22 = bf16[256,3072]{1,0:T(8,128)(2,1)S(1)} fusion(bf16[1,1280,3072]{2,1,0:T(8,128)(2,1)} %param.11, f32[256,2560]{1,0:T(8,128)S(1)} %fusion.2), kind=kOutput, calls=%fused_computation.18 | convolution fusion | flops 2016018432 | bytes 12058624 | tf_op jit(solution)/shard_map/dot_general | solution.py:20
  111.0 0.5 collective-permute-start.9
  111.5 7.3 %fusion = f32[256,2560]{1,0:T(8,128)} fusion(bf16[256,3072]{1,0:T(8,128)(2,1)} %bitcast.26, bf16[1,3072,2560]{2,1,0:T(8,128)(2,1)S(1)} %bitcast.137), kind=kOutput, calls=%fused_computation | convolution fusion | flops 4026531840 | bytes 19922944 | tf_op jit(solution)/shard_map/dot_general | solution.py:16
  118.8 4.1 %fusion.25 = bf16[256,3072]{1,0:T(8,128)(2,1)S(1)} fusion(bf16[1,1280,3072]{2,1,0:T(8,128)(2,1)S(1)} %bitcast.143, f32[256,2560]{1,0:T(8,128)} %fusion), kind=kOutput, calls=%fused_computation.19 | convolution fusion | flops 2016018432 | bytes 12058624 | tf_op jit(solution)/shard_map/dot_general | solution.py:20
  122.9 0.4 collective-permute-start.10
  123.3 2.1 %broadcast_in_dim.38 = bf16[8,64,3072]{2,1,0:T(8,128)(2,1)} broadcast(bf16[]{:T(256)} %constant.129.clone.1), dimensions={} | broadcast | bytes 3145730 | tf_op jit(solution)/shard_map/broadcast_in_dim | solution.py:104
  125.3 0.8 slice_dynamic-update-slice_fusion.7
  126.1 0.8 slice_dynamic-update-slice_fusion.6
  126.9 0.8 slice_dynamic-update-slice_fusion.5
  127.7 0.8 slice_dynamic-update-slice_fusion.4
  128.4 0.8 slice_dynamic-update-slice_fusion.3
  129.2 0.8 slice_dynamic-update-slice_fusion.2
  130.0 0.8 slice_dynamic-update-slice_fusion.1
  130.8 0.8 slice_dynamic-update-slice_fusion
  131.6 5.6 %all-to-all-done = bf16[8,64,3072]{2,1,0:T(8,128)(2,1)S(1)} async-done(((bf16[8,64,3072]{2,1,0:T(8,128)(2,1)}), bf16[8,64,3072]{2,1,0:T(8,128)(2,1)S(1)}, u32[]{:S(2)}, u32[]{:S(2)}) %all-to-all-start) | async-done | bytes 3145760 | tf_op jit(solution)/shard_map/all_to_all | solution.py:112
  137.1 4.4 %all-to-all-start.1 = ((bf16[8,64,3072]{2,1,0:T(8,128)(2,1)}), bf16[8,64,3072]{2,1,0:T(8,128)(2,1)}, u32[]{:S(2)}, u32[]{:S(2)}) async-start(bf16[8,64,3072]{2,1,0:T(8,128)(2,1)} %slice_dynamic-update-slice_fusion), calls=%async_computation.1 | async-start | bytes 6291456 | tf_op jit(solution)/shard_map/all_to_all | solution.py:118
  141.6 0.1 copy.15
  141.7 0.1 copy.22
  141.8 0.4 select_reduce_fusion
  142.3 1.9 %convolution_bitcast_fusion.1 = f32[128,3072]{1,0:T(8,128)} fusion(bf16[8,64,3072]{2,1,0:T(8,128)(2,1)S(1)} %all-to-all-done, s32[8,64]{1,0:T(8,128)S(1)} %bitcast.132, bf16[8,128]{1,0:T(8,128)(2,1)S(1)} %get-tuple-element.42), kind=kOutput, calls=%fused_computation.25 | convolution fusion | flops 402784256 | bytes 4722688 | tf_op jit(solution)/shard_map/dot_general | solution.py:135
  144.2 36.9 %all-to-all-done.1 = bf16[8,64,3072]{2,1,0:T(8,128)(2,1)} async-done(((bf16[8,64,3072]{2,1,0:T(8,128)(2,1)}), bf16[8,64,3072]{2,1,0:T(8,128)(2,1)}, u32[]{:S(2)}, u32[]{:S(2)}) %all-to-all-start.1) | async-done | bytes 3145760 | tf_op jit(solution)/shard_map/all_to_all | solution.py:118
  181.1 3.9 %fusion.29 = bf16[128,3072]{1,0:T(8,128)(2,1)} fusion(f32[128,3072]{1,0:T(8,128)} %convolution_bitcast_fusion.1, bf16[8,64,3072]{2,1,0:T(8,128)(2,1)} %all-to-all-done.1, s32[8,64]{1,0:T(8,128)S(1)} %bitcast.133, bf16[8,128]{1,0:T(8,128)(2,1)S(1)} %get-tuple-element.41), kind=kOutput, calls=%fused_computation.27 | convolution fusion | flops 403570688 | bytes 5509120 | tf_op jit(solution)/shard_map/dot_general | solution.py:135
  (65 shorter events, 0.8 us)
Async XLA Ops:
  3.1 22.3 %collective-permute-start.3 = (bf16[129,3072]{1,0:T(8,128)(2,1)}, bf16[129,3072]{1,0:T(8,128)(2,1)S(1)}, u32[]{:S(2)}, u32[]{:S(2)}) collective-permute-start(bf16[129,3072]{1,0:T(8,128)(2,1)} %get-tuple-element.32), channel_id=1, source_target_pairs={{0,12},{4,0},{8,4},{12,8},{1,13},{5,1},{9,5},{13,9},{2,14},{6,2},{... | collective-permute-start | bytes 2377736 | tf_op jit(solution)/shard_map/ppermute | solution.py:27
  7.2 21.5 %collective-permute-start.1 = (bf16[129,3072]{1,0:T(8,128)(2,1)}, bf16[129,3072]{1,0:T(8,128)(2,1)S(1)}, u32[]{:S(2)}, u32[]{:S(2)}) collective-permute-start(bf16[129,3072]{1,0:T(8,128)(2,1)} %get-tuple-element.32), channel_id=1, source_target_pairs={{0,4},{4,8},{8,12},{12,0},{1,5},{5,9},{9,13},{13,1},{2,6},{6,10},{... | collective-permute-start | bytes 2377736 | tf_op jit(solution)/shard_map/ppermute | solution.py:27
  7.2 21.8 %collective-permute-start = (bf16[129,3072]{1,0:T(8,128)(2,1)}, bf16[129,3072]{1,0:T(8,128)(2,1)S(1)}, u32[]{:S(2)}, u32[]{:S(2)}) collective-permute-start(bf16[129,3072]{1,0:T(8,128)(2,1)} %get-tuple-element.32), channel_id=1, source_target_pairs={{0,2},{2,0},{1,3},{3,1},{4,6},{6,4},{5,7},{7,5},{8,10},{10,8},{9,1... | collective-permute-start | bytes 2377736 | tf_op jit(solution)/shard_map/ppermute | solution.py:31
  29.3 7.3 %slice-start = ((s8[15728640]{0:T(1024)(128)(4,1)}), s8[4194304]{0:T(1024)(128)(4,1)S(1)}, s32[]{:S(2)}) async-start(s8[15728640]{0:T(1024)(128)(4,1)} %bitcast.134), calls=%async_computation.2 | async-start | bytes 8388608
  29.3 7.2 %slice-start.1 = ((s8[15728640]{0:T(1024)(128)(4,1)}), s8[4194304]{0:T(1024)(128)(4,1)S(1)}, s32[]{:S(2)}) async-start(s8[15728640]{0:T(1024)(128)(4,1)} %bitcast.134), calls=%async_computation.3 | async-start | bytes 8388608
  31.1 5.5 %slice-start.2 = ((s8[15728640]{0:T(1024)(128)(4,1)}), s8[4194304]{0:T(1024)(128)(4,1)S(1)}, s32[]{:S(2)}) async-start(s8[15728640]{0:T(1024)(128)(4,1)} %bitcast.134), calls=%async_computation.4 | async-start | bytes 8388608
  31.1 5.5 %slice-start.3 = ((s8[15728640]{0:T(1024)(128)(4,1)}), s8[3145728]{0:T(1024)(128)(4,1)S(1)}, s32[]{:S(2)}) async-start(s8[15728640]{0:T(1024)(128)(4,1)} %bitcast.134), calls=%async_computation.5 | async-start | bytes 6291456
  33.0 28.9 %collective-permute-start.2 = (bf16[193,3072]{1,0:T(8,128)(2,1)S(1)}, bf16[193,3072]{1,0:T(8,128)(2,1)S(1)}, u32[]{:S(2)}, u32[]{:S(2)}) collective-permute-start(bf16[193,3072]{1,0:T(8,128)(2,1)S(1)} %pad_maximum_fusion.6), channel_id=1, source_target_pairs={{0,4},{4,8},{8,12},{12,0},{1,5},{5,9},{9,13},{13,1},{2,6},{6,10},{... | collective-permute-start | bytes 3557384 | tf_op jit(solution)/shard_map/ppermute | solution.py:27
  33.1 10.8 %slice-start.8 = ((s8[7864320]{0:T(1024)(128)(4,1)}), s8[4194304]{0:T(1024)(128)(4,1)S(1)}, s32[]{:S(2)}) async-start(s8[7864320]{0:T(1024)(128)(4,1)} %bitcast.138), calls=%async_computation.10 | async-start | bytes 8388608
  33.2 28.8 %collective-permute-start.4 = (bf16[194,3072]{1,0:T(8,128)(2,1)S(1)}, bf16[194,3072]{1,0:T(8,128)(2,1)S(1)}, u32[]{:S(2)}, u32[]{:S(2)}) collective-permute-start(bf16[194,3072]{1,0:T(8,128)(2,1)S(1)} %pad_maximum_fusion.7), channel_id=1, source_target_pairs={{0,12},{4,0},{8,4},{12,8},{1,13},{5,1},{9,5},{13,9},{2,14},{6,2},{... | collective-permute-start | bytes 3575816 | tf_op jit(solution)/shard_map/ppermute | solution.py:27
  36.5 60.2 %collective-permute-start.7 = (bf16[4,64,3072]{2,1,0:T(8,128)(2,1)}, bf16[4,64,3072]{2,1,0:T(8,128)(2,1)}, u32[]{:S(2)}, u32[]{:S(2)}) collective-permute-start(bf16[4,64,3072]{2,1,0:T(8,128)(2,1)} %convolution_convert_fusion.1), channel_id=1, source_target_pairs={{0,1},{1,0},{2,3},{3,2},{4,5},{5,4},{6,7},{7,6},{8,9},{9,8},{10,11... | collective-permute-start | bytes 4718600 | tf_op jit(solution)/shard_map/ppermute | solution.py:31
  36.6 7.3 %slice-start.9 = ((s8[7864320]{0:T(1024)(128)(4,1)}), s8[3670016]{0:T(1024)(128)(4,1)S(1)}, s32[]{:S(2)}) async-start(s8[7864320]{0:T(1024)(128)(4,1)} %bitcast.138), calls=%async_computation.11 | async-start | bytes 7340032
  61.9 10.0 %collective-permute-start.5 = (bf16[64,3072]{1,0:T(8,128)(2,1)S(1)}, bf16[64,3072]{1,0:T(8,128)(2,1)S(1)}, u32[]{:S(2)}, u32[]{:S(2)}) collective-permute-start(bf16[64,3072]{1,0:T(8,128)(2,1)S(1)} %get-tuple-element.27), channel_id=1, source_target_pairs={{0,4},{4,8},{8,12},{12,0},{1,5},{5,9},{9,13},{13,1},{2,6},{6,10},{... | collective-permute-start | bytes 1179656 | tf_op jit(solution)/shard_map/ppermute | solution.py:27
  62.1 10.5 %collective-permute-start.6 = (bf16[65,3072]{1,0:T(8,128)(2,1)S(1)}, bf16[65,3072]{1,0:T(8,128)(2,1)S(1)}, u32[]{:S(2)}, u32[]{:S(2)}) collective-permute-start(bf16[65,3072]{1,0:T(8,128)(2,1)S(1)} %get-tuple-element.29), channel_id=1, source_target_pairs={{0,12},{4,0},{8,4},{12,8},{1,13},{5,1},{9,5},{13,9},{2,14},{6,2},{... | collective-permute-start | bytes 1198088 | tf_op jit(solution)/shard_map/ppermute | solution.py:27
  74.7 8.9 %slice-start.10 = ((s8[7864320]{0:T(1024)(128)(4,1)}), s8[4194304]{0:T(1024)(128)(4,1)S(1)}, s32[]{:S(2)}) async-start(s8[7864320]{0:T(1024)(128)(4,1)} %bitcast.140), calls=%async_computation.12 | async-start | bytes 8388608
  75.5 8.2 %slice-start.11 = ((s8[7864320]{0:T(1024)(128)(4,1)}), s8[3670016]{0:T(1024)(128)(4,1)S(1)}, s32[]{:S(2)}) async-start(s8[7864320]{0:T(1024)(128)(4,1)} %bitcast.140), calls=%async_computation.13 | async-start | bytes 7340032
  86.0 10.7 %collective-permute-start.8 = (bf16[4,64,3072]{2,1,0:T(8,128)(2,1)}, bf16[4,64,3072]{2,1,0:T(8,128)(2,1)}, u32[]{:S(2)}, u32[]{:S(2)}) collective-permute-start(bf16[4,64,3072]{2,1,0:T(8,128)(2,1)} %convolution_convert_fusion), channel_id=1, source_target_pairs={{0,1},{1,0},{2,3},{3,2},{4,5},{5,4},{6,7},{7,6},{8,9},{9,8},{10,11... | collective-permute-start | bytes 4718600 | tf_op jit(solution)/shard_map/ppermute | solution.py:31
  89.3 47.9 %all-to-all-start = ((bf16[8,64,3072]{2,1,0:T(8,128)(2,1)}), bf16[8,64,3072]{2,1,0:T(8,128)(2,1)S(1)}, u32[]{:S(2)}, u32[]{:S(2)}) async-start(bf16[8,64,3072]{2,1,0:T(8,128)(2,1)} %fusion.44), calls=%async_computation | async-start | bytes 6291456 | tf_op jit(solution)/shard_map/all_to_all | solution.py:112
  96.8 14.7 %slice-start.4 = ((s8[15728640]{0:T(1024)(128)(4,1)}), s8[4194304]{0:T(1024)(128)(4,1)S(1)}, s32[]{:S(2)}) async-start(s8[15728640]{0:T(1024)(128)(4,1)} %bitcast.136), calls=%async_computation.6 | async-start | bytes 8388608
  96.8 14.7 %slice-start.5 = ((s8[15728640]{0:T(1024)(128)(4,1)}), s8[4194304]{0:T(1024)(128)(4,1)S(1)}, s32[]{:S(2)}) async-start(s8[15728640]{0:T(1024)(128)(4,1)} %bitcast.136), calls=%async_computation.7 | async-start | bytes 8388608
  96.8 14.7 %slice-start.6 = ((s8[15728640]{0:T(1024)(128)(4,1)}), s8[4194304]{0:T(1024)(128)(4,1)S(1)}, s32[]{:S(2)}) async-start(s8[15728640]{0:T(1024)(128)(4,1)} %bitcast.136), calls=%async_computation.8 | async-start | bytes 8388608
  105.1 6.4 %slice-start.7 = ((s8[15728640]{0:T(1024)(128)(4,1)}), s8[3145728]{0:T(1024)(128)(4,1)S(1)}, s32[]{:S(2)}) async-start(s8[15728640]{0:T(1024)(128)(4,1)} %bitcast.136), calls=%async_computation.9 | async-start | bytes 6291456
  105.1 13.6 %slice-start.12 = ((s8[7864320]{0:T(1024)(128)(4,1)}), s8[4194304]{0:T(1024)(128)(4,1)S(1)}, s32[]{:S(2)}) async-start(s8[7864320]{0:T(1024)(128)(4,1)} %bitcast.142), calls=%async_computation.14 | async-start | bytes 8388608
  111.0 12.3 %collective-permute-start.9 = (bf16[4,64,3072]{2,1,0:T(8,128)(2,1)S(1)}, bf16[4,64,3072]{2,1,0:T(8,128)(2,1)S(1)}, u32[]{:S(2)}, u32[]{:S(2)}) collective-permute-start(bf16[4,64,3072]{2,1,0:T(8,128)(2,1)S(1)} %bitcast.145), channel_id=1, source_target_pairs={{0,1},{1,0},{2,3},{3,2},{4,5},{5,4},{6,7},{7,6},{8,9},{9,8},{10,11... | collective-permute-start | bytes 4718600 | tf_op jit(solution)/shard_map/ppermute | solution.py:31
  111.5 7.3 %slice-start.13 = ((s8[7864320]{0:T(1024)(128)(4,1)}), s8[3670016]{0:T(1024)(128)(4,1)S(1)}, s32[]{:S(2)}) async-start(s8[7864320]{0:T(1024)(128)(4,1)} %bitcast.142), calls=%async_computation.15 | async-start | bytes 7340032
  122.9 5.6 %collective-permute-start.10 = (bf16[4,64,3072]{2,1,0:T(8,128)(2,1)S(1)}, bf16[4,64,3072]{2,1,0:T(8,128)(2,1)S(1)}, u32[]{:S(2)}, u32[]{:S(2)}) collective-permute-start(bf16[4,64,3072]{2,1,0:T(8,128)(2,1)S(1)} %bitcast.144), channel_id=1, source_target_pairs={{0,1},{1,0},{2,3},{3,2},{4,5},{5,4},{6,7},{7,6},{8,9},{9,8},{10,11... | collective-permute-start | bytes 4718600 | tf_op jit(solution)/shard_map/ppermute | solution.py:31
  131.6 10.0 %copy-start.1 = (s32[128,4]{0,1:T(4,128)S(1)}, s32[128,4]{0,1:T(4,128)}, u32[]{:S(2)}) copy-start(s32[128,4]{0,1:T(4,128)} %param.7) | copy-start | bytes 6148
  131.6 10.1 %copy-start.2 = (f32[128,4]{0,1:T(4,128)S(1)}, f32[128,4]{0,1:T(4,128)}, u32[]{:S(2)}) copy-start(f32[128,4]{0,1:T(4,128)} %param.8) | copy-start | bytes 6148
  131.6 10.7 %copy-start = (s32[1,16,64]{2,1,0:T(8,128)S(1)}, s32[1,16,64]{2,1,0:T(8,128)}, u32[]{:S(2)}) copy-start(s32[1,16,64]{2,1,0:T(8,128)} %param.9) | copy-start | bytes 12292
  137.1 44.0 %all-to-all-start.1 = ((bf16[8,64,3072]{2,1,0:T(8,128)(2,1)}), bf16[8,64,3072]{2,1,0:T(8,128)(2,1)}, u32[]{:S(2)}, u32[]{:S(2)}) async-start(bf16[8,64,3072]{2,1,0:T(8,128)(2,1)} %slice_dynamic-update-slice_fusion), calls=%async_computation.1 | async-start | bytes 6291456 | tf_op jit(solution)/shard_map/all_to_all | solution.py:118

commit v14 on v13

--- a/solution.py
+++ b/solution.py
@@ -97,7 +97,8 @@
             into = lax.dynamic_update_slice(into, outs[i : i + 1], (where, 0, 0))
         return into
 
-    early = [(0, 0, block), (0, 1, partner), (1, 0, from_above), (3, 0, from_below)]
+    own, partner = lax.optimization_barrier((block, partner))
+    early = [(0, 0, own), (0, 1, partner), (1, 0, from_above), (3, 0, from_below)]
     late = [(2, 0, far), (2, 1, p_far), (1, 1, p_above), (3, 1, p_below)]
     mine_1, got_1 = slots_of(early)
     out_m1 = expert_block(mine_1, w_first, w_second)

time: 185 us -> 184 us (level)
  starting transfers between devices: 27.1 us -> 24.7 us
    ppermute x5, waiting for transfers between devices: 0.32 us -> 14.6 us  [swap(): return lax.ppermute(x, axis, [(0, 1), (1, 0)])]
    ppermute x6, waiting for transfers between devices: 33.9 us -> 21.4 us  [shift_z(): return lax.ppermute(x, 'z', [(i, (i + step) % RING) for i in range(RING)])]
    all_to_all x1, starting transfers between devices: 7.5 us -> 4.97 us  [shards(): ret_a = lax.all_to_all(a_abs, ('z', 'yh'), 0, 0, tiled=True)]
    another operation x1 -> x0, other arithmetic: 2.27 us -> none  [slots_of(): stacked = jnp.stack([arr for _, _, arr in pieces])]
where the time goes in v14:
time: 184 us; the launch traced here: 183 us
  waiting for transfers between devices  78.4 us (43%)
  matrix products  58.9 us (32%)
  starting transfers between devices  24.7 us (13%)
  local copies, waits for them, and re-layouts  17.7 us (10%)
  other arithmetic  3.1 us (2%)
    all_to_all x1, waiting for transfers between devices, shards(): ret_b = lax.all_to_all(b_abs, ('z', 'yh'), 0, 0, tiled=True)  36.9 us
    dot_general x4, matrix products, expert_block(): projected = jnp.dot(flat, w_first, preferred_element_type=jnp.float32)  30.9 us
    ppermute x6, waiting for transfers between devices, shift_z(): return lax.ppermute(x, 'z', [(i, (i + step) % RING) for i in range(RING)])  21.4 us
    dot_general x4, matrix products, expert_block(): jnp.dot(intermediate_activation, w_second, preferred_element_type=jnp.flo...  16.3 us
    ppermute x5, waiting for transfers between devices, swap(): return lax.ppermute(x, axis, [(0, 1), (1, 0)])  14.6 us
    dynamic_update_slice x16, local copies, waits for them, and re-layouts, place(): into = lax.dynamic_update_slice(into, outs[i:i + 1], (where, 0, 0))  12.5 us
    ppermute x6, starting transfers between devices, shift_z(): return lax.ppermute(x, 'z', [(i, (i + step) % RING) for i in range(RING)])  10.9 us
    dot_general x4, matrix products, slots_of(): jnp.einsum('bct,btd->bcd', one_hot[:, j], toks, preferred_element_type=jn...  5.89 us
  transfers between devices with their start and end apart: 13, of which 8 were waited for; matrix products, arithmetic and copies ran while one was open for 38% of the time, Pallas kernels for 0%

profile of v14, /device:TPU:0, one launch (start us, length us, event | category | flops | bytes accessed | tf_op | source)
XLA Modules:
  0.0 183.3 jit_solution(3738427295660998283)
XLA Ops:
  0.0 0.7 convert_element_type.76
  0.7 0.1 convert_element_type.77
  0.8 1.2 fusion.35
  2.0 3.4 %collective-permute-start = (bf16[129,3072]{1,0:T(8,128)(2,1)S(1)}, bf16[129,3072]{1,0:T(8,128)(2,1)S(1)}, u32[]{:S(2)}, u32[]{:S(2)}) collective-permute-start(bf16[129,3072]{1,0:T(8,128)(2,1)S(1)} %fusion.35), channel_id=1, source_target_pairs={{0,2},{2,0},{1,3},{3,1},{4,6},{6,4},{5,7},{7,5},{8,10},{10,8},{9,1... | collective-permute-start | bytes 2377736 | tf_op jit(solution)/shard_map/ppermute | solution.py:31
  5.3 4.0 %collective-permute-start.3 = (bf16[129,3072]{1,0:T(8,128)(2,1)S(1)}, bf16[129,3072]{1,0:T(8,128)(2,1)S(1)}, u32[]{:S(2)}, u32[]{:S(2)}) collective-permute-start(bf16[129,3072]{1,0:T(8,128)(2,1)S(1)} %fusion.35), channel_id=1, source_target_pairs={{0,12},{4,0},{8,4},{12,8},{1,13},{5,1},{9,5},{13,9},{2,14},{6,2},{... | collective-permute-start | bytes 2377736 | tf_op jit(solution)/shard_map/ppermute | solution.py:27
  9.4 14.6 %collective-permute-done = bf16[129,3072]{1,0:T(8,128)(2,1)S(1)} collective-permute-done((bf16[129,3072]{1,0:T(8,128)(2,1)S(1)}, bf16[129,3072]{1,0:T(8,128)(2,1)S(1)}, u32[]{:S(2)}, u32[]{:S(2)}) %collective-permute-start) | collective-permute-done | bytes 792608 | tf_op jit(solution)/shard_map/ppermute | solution.py:31
  23.9 3.0 %collective-permute-done.3 = bf16[129,3072]{1,0:T(8,128)(2,1)S(1)} collective-permute-done((bf16[129,3072]{1,0:T(8,128)(2,1)S(1)}, bf16[129,3072]{1,0:T(8,128)(2,1)S(1)}, u32[]{:S(2)}, u32[]{:S(2)}) %collective-permute-start.3) | collective-permute-done | bytes 792608 | tf_op jit(solution)/shard_map/ppermute | solution.py:27
  27.0 3.4 %collective-permute-done.1 = bf16[129,3072]{1,0:T(8,128)(2,1)S(1)} collective-permute-done((bf16[129,3072]{1,0:T(8,128)(2,1)S(1)}, bf16[129,3072]{1,0:T(8,128)(2,1)S(1)}, u32[]{:S(2)}, u32[]{:S(2)}) %collective-permute-start.1) | collective-permute-done | bytes 792608 | tf_op jit(solution)/shard_map/ppermute | solution.py:27
  30.4 0.1 reshape.70
  30.6 0.1 iota_compare_fusion.5
  30.7 1.7 convolution_convert_fusion.1
  32.4 1.8 convolution_convert_fusion.3
  34.2 0.1 pad_maximum_fusion.6
  34.4 0.1 collective-permute-start.2
  34.5 0.2 pad_maximum_fusion.7
  34.7 3.3 %collective-permute-start.4 = (bf16[194,3072]{1,0:T(8,128)(2,1)S(1)}, bf16[194,3072]{1,0:T(8,128)(2,1)S(1)}, u32[]{:S(2)}, u32[]{:S(2)}) collective-permute-start(bf16[194,3072]{1,0:T(8,128)(2,1)S(1)} %pad_maximum_fusion.7), channel_id=1, source_target_pairs={{0,12},{4,0},{8,4},{12,8},{1,13},{5,1},{9,5},{13,9},{2,14},{6,2},{... | collective-permute-start | bytes 3575816 | tf_op jit(solution)/shard_map/ppermute | solution.py:27
  38.0 7.2 %fusion.6 = f32[256,2560]{1,0:T(8,128)} fusion(bf16[256,3072]{1,0:T(8,128)(2,1)} %bitcast.148, bf16[1,3072,2560]{2,1,0:T(8,128)(2,1)S(1)} %bitcast.137), kind=kOutput, calls=%fused_computation.6 | convolution fusion | flops 4026531840 | bytes 19922944 | tf_op jit(solution)/shard_map/dot_general | solution.py:16
  45.2 4.1 %fusion.16 = bf16[256,3072]{1,0:T(8,128)(2,1)S(1)} fusion(bf16[1,1280,3072]{2,1,0:T(8,128)(2,1)S(1)} %bitcast.141, f32[256,2560]{1,0:T(8,128)} %fusion.6), kind=kOutput, calls=%fused_computation.16 | convolution fusion | flops 2016018432 | bytes 12058624 | tf_op jit(solution)/shard_map/dot_general | solution.py:20
  49.3 2.0 %broadcast_in_dim.38.clone = bf16[8,64,3072]{2,1,0:T(8,128)(2,1)} broadcast(bf16[]{:T(256)} %constant.129.clone.1), dimensions={} | broadcast | bytes 3145730 | tf_op jit(solution)/shard_map/broadcast_in_dim | solution.py:105
  51.4 0.8 fusion.51
  52.1 0.8 fusion.50
  52.9 0.8 fusion.49
  53.7 9.2 %collective-permute-done.2 = bf16[193,3072]{1,0:T(8,128)(2,1)S(1)} collective-permute-done((bf16[193,3072]{1,0:T(8,128)(2,1)S(1)}, bf16[193,3072]{1,0:T(8,128)(2,1)S(1)}, u32[]{:S(2)}, u32[]{:S(2)}) %collective-permute-start.2) | collective-permute-done | bytes 1185824 | tf_op jit(solution)/shard_map/ppermute | solution.py:27
  62.9 0.1 fusion.74
  63.1 0.1 fusion.75
  63.2 3.5 %collective-permute-start.6 = (bf16[65,3072]{1,0:T(8,128)(2,1)S(1)}, bf16[65,3072]{1,0:T(8,128)(2,1)S(1)}, u32[]{:S(2)}, u32[]{:S(2)}) collective-permute-start(bf16[65,3072]{1,0:T(8,128)(2,1)S(1)} %get-tuple-element.33), channel_id=1, source_target_pairs={{0,12},{4,0},{8,4},{12,8},{1,13},{5,1},{9,5},{13,9},{2,14},{6,2},{... | collective-permute-start | bytes 1198088 | tf_op jit(solution)/shard_map/ppermute | solution.py:27
  66.7 0.8 fusion.48
  67.7 5.1 %collective-permute-done.5 = bf16[64,3072]{1,0:T(8,128)(2,1)S(1)} collective-permute-done((bf16[64,3072]{1,0:T(8,128)(2,1)S(1)}, bf16[64,3072]{1,0:T(8,128)(2,1)S(1)}, u32[]{:S(2)}, u32[]{:S(2)}) %collective-permute-start.5) | collective-permute-done | bytes 393248 | tf_op jit(solution)/shard_map/ppermute | solution.py:27
  72.7 0.7 collective-permute-done.6
  73.6 0.1 reshape.71
  73.7 0.1 iota_compare_fusion.4
  73.8 1.7 convolution_convert_fusion
  75.5 0.8 convolution_convert_fusion.2
  76.3 8.2 %fusion.4 = f32[256,2560]{1,0:T(8,128)S(1)} fusion(bf16[256,3072]{1,0:T(8,128)(2,1)S(1)} %bitcast.149, bf16[1,3072,2560]{2,1,0:T(8,128)(2,1)} %param.10), kind=kOutput, calls=%fused_computation.4 | convolution fusion | flops 4026531840 | bytes 19922944 | tf_op jit(solution)/shard_map/dot_general | solution.py:16
  84.5 2.3 %fusion.19 = bf16[256,3072]{1,0:T(8,128)(2,1)S(1)} fusion(bf16[1,1280,3072]{2,1,0:T(8,128)(2,1)S(1)} %bitcast.143, f32[256,2560]{1,0:T(8,128)S(1)} %fusion.4), kind=kOutput, calls=%fused_computation.17 | convolution fusion | flops 2016018432 | bytes 12058624 | tf_op jit(solution)/shard_map/dot_general | solution.py:20
  86.8 0.1 collective-permute-start.8
  86.9 0.8 fusion.47
  87.7 0.8 fusion.46
  88.5 0.8 fusion.45
  89.3 0.8 fusion.44
  90.1 5.0 %all-to-all-start = ((bf16[8,64,3072]{2,1,0:T(8,128)(2,1)}), bf16[8,64,3072]{2,1,0:T(8,128)(2,1)S(1)}, u32[]{:S(2)}, u32[]{:S(2)}) async-start(bf16[8,64,3072]{2,1,0:T(8,128)(2,1)} %fusion.44), calls=%async_computation | async-start | bytes 6291456 | tf_op jit(solution)/shard_map/all_to_all | solution.py:113
  95.1 8.3 %fusion.2 = f32[256,2560]{1,0:T(8,128)S(1)} fusion(bf16[256,3072]{1,0:T(8,128)(2,1)} %bitcast.24, bf16[1,3072,2560]{2,1,0:T(8,128)(2,1)} %param.10), kind=kOutput, calls=%fused_computation.2 | convolution fusion | flops 4026531840 | bytes 19922944 | tf_op jit(solution)/shard_map/dot_general | solution.py:16
  103.4 5.8 %fusion.22 = bf16[256,3072]{1,0:T(8,128)(2,1)S(1)} fusion(bf16[1,1280,3072]{2,1,0:T(8,128)(2,1)} %param.11, f32[256,2560]{1,0:T(8,128)S(1)} %fusion.2), kind=kOutput, calls=%fused_computation.18 | convolution fusion | flops 2016018432 | bytes 12058624 | tf_op jit(solution)/shard_map/dot_general | solution.py:20
  109.2 0.5 collective-permute-start.9
  109.8 7.3 %fusion = f32[256,2560]{1,0:T(8,128)} fusion(bf16[256,3072]{1,0:T(8,128)(2,1)} %bitcast.26, bf16[1,3072,2560]{2,1,0:T(8,128)(2,1)S(1)} %bitcast.139), kind=kOutput, calls=%fused_computation | convolution fusion | flops 4026531840 | bytes 19922944 | tf_op jit(solution)/shard_map/dot_general | solution.py:16
  117.0 4.1 %fusion.25 = bf16[256,3072]{1,0:T(8,128)(2,1)S(1)} fusion(bf16[1,1280,3072]{2,1,0:T(8,128)(2,1)S(1)} %bitcast.145, f32[256,2560]{1,0:T(8,128)} %fusion), kind=kOutput, calls=%fused_computation.19 | convolution fusion | flops 2016018432 | bytes 12058624 | tf_op jit(solution)/shard_map/dot_general | solution.py:20
  121.1 0.4 collective-permute-start.10
  121.5 2.1 %broadcast_in_dim.38 = bf16[8,64,3072]{2,1,0:T(8,128)(2,1)} broadcast(bf16[]{:T(256)} %constant.129.clone.1), dimensions={} | broadcast | bytes 3145730 | tf_op jit(solution)/shard_map/broadcast_in_dim | solution.py:105
  123.6 0.8 slice_dynamic-update-slice_fusion.7
  124.4 0.8 slice_dynamic-update-slice_fusion.6
  125.1 0.8 slice_dynamic-update-slice_fusion.5
  125.9 0.8 slice_dynamic-update-slice_fusion.4
  126.7 0.8 slice_dynamic-update-slice_fusion.3
  127.5 0.8 slice_dynamic-update-slice_fusion.2
  128.3 0.8 slice_dynamic-update-slice_fusion.1
  129.1 0.8 slice_dynamic-update-slice_fusion
  129.8 5.6 %all-to-all-done = bf16[8,64,3072]{2,1,0:T(8,128)(2,1)S(1)} async-done(((bf16[8,64,3072]{2,1,0:T(8,128)(2,1)}), bf16[8,64,3072]{2,1,0:T(8,128)(2,1)S(1)}, u32[]{:S(2)}, u32[]{:S(2)}) %all-to-all-start) | async-done | bytes 3145760 | tf_op jit(solution)/shard_map/all_to_all | solution.py:113
  135.4 4.4 %all-to-all-start.1 = ((bf16[8,64,3072]{2,1,0:T(8,128)(2,1)}), bf16[8,64,3072]{2,1,0:T(8,128)(2,1)}, u32[]{:S(2)}, u32[]{:S(2)}) async-start(bf16[8,64,3072]{2,1,0:T(8,128)(2,1)} %slice_dynamic-update-slice_fusion), calls=%async_computation.1 | async-start | bytes 6291456 | tf_op jit(solution)/shard_map/all_to_all | solution.py:119
  139.9 0.1 copy.15
  140.0 0.1 copy.22
  140.1 0.4 select_reduce_fusion
  140.6 1.9 %convolution_bitcast_fusion.1 = f32[128,3072]{1,0:T(8,128)} fusion(bf16[8,64,3072]{2,1,0:T(8,128)(2,1)S(1)} %all-to-all-done, s32[8,64]{1,0:T(8,128)S(1)} %bitcast.134, bf16[8,128]{1,0:T(8,128)(2,1)S(1)} %get-tuple-element.44), kind=kOutput, calls=%fused_computation.25 | convolution fusion | flops 402784256 | bytes 4722688 | tf_op jit(solution)/shard_map/dot_general | solution.py:136
  142.5 36.9 %all-to-all-done.1 = bf16[8,64,3072]{2,1,0:T(8,128)(2,1)} async-done(((bf16[8,64,3072]{2,1,0:T(8,128)(2,1)}), bf16[8,64,3072]{2,1,0:T(8,128)(2,1)}, u32[]{:S(2)}, u32[]{:S(2)}) %all-to-all-start.1) | async-done | bytes 3145760 | tf_op jit(solution)/shard_map/all_to_all | solution.py:119
  179.4 3.9 %fusion.29 = bf16[128,3072]{1,0:T(8,128)(2,1)} fusion(f32[128,3072]{1,0:T(8,128)} %convolution_bitcast_fusion.1, bf16[8,64,3072]{2,1,0:T(8,128)(2,1)} %all-to-all-done.1, s32[8,64]{1,0:T(8,128)S(1)} %bitcast.135, bf16[8,128]{1,0:T(8,128)(2,1)S(1)} %get-tuple-element.43), kind=kOutput, calls=%fused_computation.27 | convolution fusion | flops 403570688 | bytes 5509120 | tf_op jit(solution)/shard_map/dot_general | solution.py:136
  (65 shorter events, 0.8 us)
Async XLA Ops:
  2.0 22.0 %collective-permute-start = (bf16[129,3072]{1,0:T(8,128)(2,1)S(1)}, bf16[129,3072]{1,0:T(8,128)(2,1)S(1)}, u32[]{:S(2)}, u32[]{:S(2)}) collective-permute-start(bf16[129,3072]{1,0:T(8,128)(2,1)S(1)} %fusion.35), channel_id=1, source_target_pairs={{0,2},{2,0},{1,3},{3,1},{4,6},{6,4},{5,7},{7,5},{8,10},{10,8},{9,1... | collective-permute-start | bytes 2377736 | tf_op jit(solution)/shard_map/ppermute | solution.py:31
  5.3 21.6 %collective-permute-start.3 = (bf16[129,3072]{1,0:T(8,128)(2,1)S(1)}, bf16[129,3072]{1,0:T(8,128)(2,1)S(1)}, u32[]{:S(2)}, u32[]{:S(2)}) collective-permute-start(bf16[129,3072]{1,0:T(8,128)(2,1)S(1)} %fusion.35), channel_id=1, source_target_pairs={{0,12},{4,0},{8,4},{12,8},{1,13},{5,1},{9,5},{13,9},{2,14},{6,2},{... | collective-permute-start | bytes 2377736 | tf_op jit(solution)/shard_map/ppermute | solution.py:27
  9.4 21.0 %collective-permute-start.1 = (bf16[129,3072]{1,0:T(8,128)(2,1)S(1)}, bf16[129,3072]{1,0:T(8,128)(2,1)S(1)}, u32[]{:S(2)}, u32[]{:S(2)}) collective-permute-start(bf16[129,3072]{1,0:T(8,128)(2,1)S(1)} %fusion.35), channel_id=1, source_target_pairs={{0,4},{4,8},{8,12},{12,0},{1,5},{5,9},{9,13},{13,1},{2,6},{6,10},{... | collective-permute-start | bytes 2377736 | tf_op jit(solution)/shard_map/ppermute | solution.py:27
  30.7 7.2 %slice-start = ((s8[15728640]{0:T(1024)(128)(4,1)}), s8[4194304]{0:T(1024)(128)(4,1)S(1)}, s32[]{:S(2)}) async-start(s8[15728640]{0:T(1024)(128)(4,1)} %bitcast.136), calls=%async_computation.2 | async-start | bytes 8388608
  30.7 7.2 %slice-start.1 = ((s8[15728640]{0:T(1024)(128)(4,1)}), s8[4194304]{0:T(1024)(128)(4,1)S(1)}, s32[]{:S(2)}) async-start(s8[15728640]{0:T(1024)(128)(4,1)} %bitcast.136), calls=%async_computation.3 | async-start | bytes 8388608
  32.4 5.5 %slice-start.2 = ((s8[15728640]{0:T(1024)(128)(4,1)}), s8[4194304]{0:T(1024)(128)(4,1)S(1)}, s32[]{:S(2)}) async-start(s8[15728640]{0:T(1024)(128)(4,1)} %bitcast.136), calls=%async_computation.4 | async-start | bytes 8388608
  32.4 5.5 %slice-start.3 = ((s8[15728640]{0:T(1024)(128)(4,1)}), s8[3145728]{0:T(1024)(128)(4,1)S(1)}, s32[]{:S(2)}) async-start(s8[15728640]{0:T(1024)(128)(4,1)} %bitcast.136), calls=%async_computation.5 | async-start | bytes 6291456
  34.4 28.6 %collective-permute-start.2 = (bf16[193,3072]{1,0:T(8,128)(2,1)S(1)}, bf16[193,3072]{1,0:T(8,128)(2,1)S(1)}, u32[]{:S(2)}, u32[]{:S(2)}) collective-permute-start(bf16[193,3072]{1,0:T(8,128)(2,1)S(1)} %pad_maximum_fusion.6), channel_id=1, source_target_pairs={{0,4},{4,8},{8,12},{12,0},{1,5},{5,9},{9,13},{13,1},{2,6},{6,10},{... | collective-permute-start | bytes 3557384 | tf_op jit(solution)/shard_map/ppermute | solution.py:27
  34.5 10.8 %slice-start.8 = ((s8[7864320]{0:T(1024)(128)(4,1)}), s8[4194304]{0:T(1024)(128)(4,1)S(1)}, s32[]{:S(2)}) async-start(s8[7864320]{0:T(1024)(128)(4,1)} %bitcast.140), calls=%async_computation.10 | async-start | bytes 8388608
  34.7 28.4 %collective-permute-start.4 = (bf16[194,3072]{1,0:T(8,128)(2,1)S(1)}, bf16[194,3072]{1,0:T(8,128)(2,1)S(1)}, u32[]{:S(2)}, u32[]{:S(2)}) collective-permute-start(bf16[194,3072]{1,0:T(8,128)(2,1)S(1)} %pad_maximum_fusion.7), channel_id=1, source_target_pairs={{0,12},{4,0},{8,4},{12,8},{1,13},{5,1},{9,5},{13,9},{2,14},{6,2},{... | collective-permute-start | bytes 3575816 | tf_op jit(solution)/shard_map/ppermute | solution.py:27
  37.9 57.1 %collective-permute-start.7 = (bf16[4,64,3072]{2,1,0:T(8,128)(2,1)}, bf16[4,64,3072]{2,1,0:T(8,128)(2,1)}, u32[]{:S(2)}, u32[]{:S(2)}) collective-permute-start(bf16[4,64,3072]{2,1,0:T(8,128)(2,1)} %convolution_convert_fusion.1), channel_id=1, source_target_pairs={{0,1},{1,0},{2,3},{3,2},{4,5},{5,4},{6,7},{7,6},{8,9},{9,8},{10,11... | collective-permute-start | bytes 4718600 | tf_op jit(solution)/shard_map/ppermute | solution.py:31
  38.0 7.3 %slice-start.9 = ((s8[7864320]{0:T(1024)(128)(4,1)}), s8[3670016]{0:T(1024)(128)(4,1)S(1)}, s32[]{:S(2)}) async-start(s8[7864320]{0:T(1024)(128)(4,1)} %bitcast.140), calls=%async_computation.11 | async-start | bytes 7340032
  63.0 9.7 %collective-permute-start.5 = (bf16[64,3072]{1,0:T(8,128)(2,1)S(1)}, bf16[64,3072]{1,0:T(8,128)(2,1)S(1)}, u32[]{:S(2)}, u32[]{:S(2)}) collective-permute-start(bf16[64,3072]{1,0:T(8,128)(2,1)S(1)} %get-tuple-element.31), channel_id=1, source_target_pairs={{0,4},{4,8},{8,12},{12,0},{1,5},{5,9},{9,13},{13,1},{2,6},{6,10},{... | collective-permute-start | bytes 1179656 | tf_op jit(solution)/shard_map/ppermute | solution.py:27
  63.2 10.2 %collective-permute-start.6 = (bf16[65,3072]{1,0:T(8,128)(2,1)S(1)}, bf16[65,3072]{1,0:T(8,128)(2,1)S(1)}, u32[]{:S(2)}, u32[]{:S(2)}) collective-permute-start(bf16[65,3072]{1,0:T(8,128)(2,1)S(1)} %get-tuple-element.33), channel_id=1, source_target_pairs={{0,12},{4,0},{8,4},{12,8},{1,13},{5,1},{9,5},{13,9},{2,14},{6,2},{... | collective-permute-start | bytes 1198088 | tf_op jit(solution)/shard_map/ppermute | solution.py:27
  75.5 8.9 %slice-start.10 = ((s8[7864320]{0:T(1024)(128)(4,1)}), s8[4194304]{0:T(1024)(128)(4,1)S(1)}, s32[]{:S(2)}) async-start(s8[7864320]{0:T(1024)(128)(4,1)} %bitcast.142), calls=%async_computation.12 | async-start | bytes 8388608
  76.3 8.2 %slice-start.11 = ((s8[7864320]{0:T(1024)(128)(4,1)}), s8[3670016]{0:T(1024)(128)(4,1)S(1)}, s32[]{:S(2)}) async-start(s8[7864320]{0:T(1024)(128)(4,1)} %bitcast.142), calls=%async_computation.13 | async-start | bytes 7340032
  86.8 8.2 %collective-permute-start.8 = (bf16[4,64,3072]{2,1,0:T(8,128)(2,1)}, bf16[4,64,3072]{2,1,0:T(8,128)(2,1)}, u32[]{:S(2)}, u32[]{:S(2)}) collective-permute-start(bf16[4,64,3072]{2,1,0:T(8,128)(2,1)} %convolution_convert_fusion), channel_id=1, source_target_pairs={{0,1},{1,0},{2,3},{3,2},{4,5},{5,4},{6,7},{7,6},{8,9},{9,8},{10,11... | collective-permute-start | bytes 4718600 | tf_op jit(solution)/shard_map/ppermute | solution.py:31
  90.1 45.3 %all-to-all-start = ((bf16[8,64,3072]{2,1,0:T(8,128)(2,1)}), bf16[8,64,3072]{2,1,0:T(8,128)(2,1)S(1)}, u32[]{:S(2)}, u32[]{:S(2)}) async-start(bf16[8,64,3072]{2,1,0:T(8,128)(2,1)} %fusion.44), calls=%async_computation | async-start | bytes 6291456 | tf_op jit(solution)/shard_map/all_to_all | solution.py:113
  95.1 14.7 %slice-start.4 = ((s8[15728640]{0:T(1024)(128)(4,1)}), s8[4194304]{0:T(1024)(128)(4,1)S(1)}, s32[]{:S(2)}) async-start(s8[15728640]{0:T(1024)(128)(4,1)} %bitcast.138), calls=%async_computation.6 | async-start | bytes 8388608
  95.1 14.7 %slice-start.5 = ((s8[15728640]{0:T(1024)(128)(4,1)}), s8[4194304]{0:T(1024)(128)(4,1)S(1)}, s32[]{:S(2)}) async-start(s8[15728640]{0:T(1024)(128)(4,1)} %bitcast.138), calls=%async_computation.7 | async-start | bytes 8388608
  95.1 14.7 %slice-start.6 = ((s8[15728640]{0:T(1024)(128)(4,1)}), s8[4194304]{0:T(1024)(128)(4,1)S(1)}, s32[]{:S(2)}) async-start(s8[15728640]{0:T(1024)(128)(4,1)} %bitcast.138), calls=%async_computation.8 | async-start | bytes 8388608
  103.4 6.4 %slice-start.7 = ((s8[15728640]{0:T(1024)(128)(4,1)}), s8[3145728]{0:T(1024)(128)(4,1)S(1)}, s32[]{:S(2)}) async-start(s8[15728640]{0:T(1024)(128)(4,1)} %bitcast.138), calls=%async_computation.9 | async-start | bytes 6291456
  103.4 13.6 %slice-start.12 = ((s8[7864320]{0:T(1024)(128)(4,1)}), s8[4194304]{0:T(1024)(128)(4,1)S(1)}, s32[]{:S(2)}) async-start(s8[7864320]{0:T(1024)(128)(4,1)} %bitcast.144), calls=%async_computation.14 | async-start | bytes 8388608
  109.2 12.3 %collective-permute-start.9 = (bf16[4,64,3072]{2,1,0:T(8,128)(2,1)S(1)}, bf16[4,64,3072]{2,1,0:T(8,128)(2,1)S(1)}, u32[]{:S(2)}, u32[]{:S(2)}) collective-permute-start(bf16[4,64,3072]{2,1,0:T(8,128)(2,1)S(1)} %bitcast.147), channel_id=1, source_target_pairs={{0,1},{1,0},{2,3},{3,2},{4,5},{5,4},{6,7},{7,6},{8,9},{9,8},{10,11... | collective-permute-start | bytes 4718600 | tf_op jit(solution)/shard_map/ppermute | solution.py:31
  109.8 7.3 %slice-start.13 = ((s8[7864320]{0:T(1024)(128)(4,1)}), s8[3670016]{0:T(1024)(128)(4,1)S(1)}, s32[]{:S(2)}) async-start(s8[7864320]{0:T(1024)(128)(4,1)} %bitcast.144), calls=%async_computation.15 | async-start | bytes 7340032
  121.1 5.6 %collective-permute-start.10 = (bf16[4,64,3072]{2,1,0:T(8,128)(2,1)S(1)}, bf16[4,64,3072]{2,1,0:T(8,128)(2,1)S(1)}, u32[]{:S(2)}, u32[]{:S(2)}) collective-permute-start(bf16[4,64,3072]{2,1,0:T(8,128)(2,1)S(1)} %bitcast.146), channel_id=1, source_target_pairs={{0,1},{1,0},{2,3},{3,2},{4,5},{5,4},{6,7},{7,6},{8,9},{9,8},{10,11... | collective-permute-start | bytes 4718600 | tf_op jit(solution)/shard_map/ppermute | solution.py:31
  129.8 10.0 %copy-start.1 = (s32[128,4]{0,1:T(4,128)S(1)}, s32[128,4]{0,1:T(4,128)}, u32[]{:S(2)}) copy-start(s32[128,4]{0,1:T(4,128)} %param.7) | copy-start | bytes 6148
  129.8 10.1 %copy-start.2 = (f32[128,4]{0,1:T(4,128)S(1)}, f32[128,4]{0,1:T(4,128)}, u32[]{:S(2)}) copy-start(f32[128,4]{0,1:T(4,128)} %param.8) | copy-start | bytes 6148
  129.8 10.7 %copy-start = (s32[1,16,64]{2,1,0:T(8,128)S(1)}, s32[1,16,64]{2,1,0:T(8,128)}, u32[]{:S(2)}) copy-start(s32[1,16,64]{2,1,0:T(8,128)} %param.9) | copy-start | bytes 12292
  135.4 44.0 %all-to-all-start.1 = ((bf16[8,64,3072]{2,1,0:T(8,128)(2,1)}), bf16[8,64,3072]{2,1,0:T(8,128)(2,1)}, u32[]{:S(2)}, u32[]{:S(2)}) async-start(bf16[8,64,3072]{2,1,0:T(8,128)(2,1)} %slice_dynamic-update-slice_fusion), calls=%async_computation.1 | async-start | bytes 6291456 | tf_op jit(solution)/shard_map/all_to_all | solution.py:119
